TPU v7x, 128 devices: a whole 4x4x4 slice. The times are simulated.
128 devices in a mesh: chain: 2 (over core), slab: 64 (over z, y, x).
Axes of the slice: x: 4, y: 4, z: 4, core: 2. Of those that a mesh axis runs over, the one named last changes fastest.
Arguments:
- coarse_states: bfloat16 [8, 4, 256, 64, 128], P('chain', None, 'slab'), may hold values from -3 to 3
- accept_flags: int32 [8, 3], P('chain'), may hold values 0 or 1
- owners: int32 [2], replicated, may hold values from 0 to 7, as said below
- kl_coeffs: float32 [2, 32, 16, 64], P('chain'), may hold values from -0.02 to 0.02
- source: float32 [512, 128, 256], P('slab'), may hold values from -18 to 18
Outputs:
- pressure: float32 [2, 512, 128, 256], P('chain', 'slab')
Inputs may be any that keep to these rules, and one draw needn't show every extreme that they name: `accept_flags`: 1 means accepted. The owners of different fine chain groups are different coarse chains.
All inputs are finite; a program needn't handle non-finite values. No bound on the sum of `accept_flags` on one device may be relied on, other than what follows from the above.
Results may differ from a plain program's by a relative error of at most 0.0007.
Values may be sent and summed in bfloat16 or wider, within the bound.
No kernel may reach another device: no remote copies, remote signals or barrier semaphores. Data moves between devices by JAX's collectives and lax.ppermute only.
A program may use at most 192 MiB of HBM per device.

v0:
```python
import numpy as np
import jax
import jax.numpy as jnp
from jax import lax
from jax.sharding import PartitionSpec as P

STEPS = 4
MZ = 32
MY = 16
MX = 64
LEVELS = 4
SWEEPS = 2
BOTTOM = 4

OMEGA = 0.8
HI = lax.Precision.HIGHEST

K0_HALO = 10
F0_HALO = 3
F1_HALO = 4
COARSE_HALO = 6


def pair_sum_matrix(n):
    m = np.zeros((n, n // 2), np.float32)
    m[np.arange(n), np.arange(n) // 2] = 1.0
    return m


def repeat_matrix(n):
    return np.ascontiguousarray(pair_sum_matrix(2 * n).T)


def prolong_matrix(n):
    m = np.zeros((n, 2 * n), np.float32)
    for i in range(n):
        m[i, 2 * i] += 0.75
        m[max(i - 1, 0), 2 * i] += 0.25
        m[i, 2 * i + 1] += 0.75
        m[min(i + 1, n - 1), 2 * i + 1] += 0.25
    return m


def along_x(values, matrix, precision=HI):
    return jnp.einsum("zyx,xw->zyw", values, jnp.asarray(matrix), precision=precision,
                      preferred_element_type=jnp.float32)


def along_y(values, matrix, precision=HI):
    return jnp.einsum("zyx,yv->zvx", values, jnp.asarray(matrix), precision=precision,
                      preferred_element_type=jnp.float32)


def restrict_sum(values):
    nz, ny, nx = values.shape
    values = values.reshape(nz // 2, 2, ny, nx).sum(axis=1)
    values = along_y(values, pair_sum_matrix(ny))
    return along_x(values, pair_sum_matrix(nx))


def copy_up(values):
    nz, ny, nx = values.shape
    values = along_x(values, repeat_matrix(nx))
    values = along_y(values, repeat_matrix(ny))
    return jnp.repeat(values, 2, axis=0)


def shift_from(block, offset):
    count = lax.axis_size("slab")
    pairs = [(i, i + offset) for i in range(count) if 0 <= i + offset < count]
    return lax.ppermute(block, "slab", pairs)


def gather_slabs(block):
    count = lax.axis_size("slab")
    flat = block.reshape(block.size // 128, 128)
    spread = jnp.broadcast_to(flat[None], (count,) + flat.shape)
    got = lax.all_to_all(spread, "slab", 0, 0, tiled=False)
    return got.reshape((count * block.shape[0],) + block.shape[1:])


def plane_mask(first_global, planes, total):
    g = first_global + jnp.arange(planes, dtype=jnp.int32)
    return ((g >= 0) & (g < total))[:, None, None]


class Level:
    def __init__(self, k, k_halo, own, first_global, total):
        self.own = own
        self.halo = k_halo - 1
        self.first = first_global + 1
        self.total = total
        faces_z = 0.5 * (k[1:] + k[:-1])
        kc = k[1:-1]
        rows = jnp.pad(kc, ((0, 0), (1, 1), (0, 0)))
        self.fy = 0.5 * (rows[:, 1:] + rows[:, :-1])
        cols = jnp.pad(kc, ((0, 0), (0, 0), (1, 1)))
        self.fx = 0.5 * (cols[:, :, 1:] + cols[:, :, :-1])
        self.fzl = faces_z[:-1]
        self.fzu = faces_z[1:]
        diag = self.fzl + self.fzu + self.fy[:, 1:] + self.fy[:, :-1]
        self.diag = diag + self.fx[:, :, 1:] + self.fx[:, :, :-1]

    def cut(self, arr, h, have):
        n = self.own + 2 * h
        return arr[have - h: have - h + n]

    def coef(self, h):
        c = self.cut
        H = self.halo
        return c(self.fzl, h, H), c(self.fzu, h, H), c(self.fy, h, H), c(self.fx, h, H), c(self.diag, h, H)

    def mask(self, u, h):
        return jnp.where(plane_mask(self.first + self.halo - h, u.shape[0], self.total), u, 0.0)

    def operate(self, u, h):
        fzl, fzu, fy, fx, diag = self.coef(h - 1)
        uc = u[1:-1]
        rows = jnp.pad(uc, ((0, 0), (1, 1), (0, 0)))
        cols = jnp.pad(uc, ((0, 0), (0, 0), (1, 1)))
        nb = fzu * u[2:] + fzl * u[:-2]
        nb = nb + fy[:, 1:] * rows[:, 2:] + fy[:, :-1] * rows[:, :-2]
        nb = nb + fx[:, :, 1:] * cols[:, :, 2:] + fx[:, :, :-1] * cols[:, :, :-2]
        return diag * uc - nb

    def sweep(self, u, f, h):
        diag = self.coef(h - 1)[4]
        new = u[1:-1] + OMEGA * (f - self.operate(u, h)) / diag
        return self.mask(new, h - 1)

    def start(self, f, h):
        return self.mask(OMEGA * f / self.coef(h)[4], h)


def mode_table(mode_count, length, positions):
    frequency = length // 2 + jnp.arange(mode_count, dtype=jnp.int32)
    phases = frequency[:, None] * (2 * positions[None, :] + 1) % (4 * length)
    return jnp.cos(jnp.pi * phases.astype(jnp.float32) / (2 * length))


def on_device(coarse_states, accept_flags, owners, kl_coeffs, source):
    slabs = lax.axis_size("slab")
    chain_index = lax.axis_index("chain")
    s = lax.axis_index("slab")
    step_numbers = jnp.arange(1, STEPS, dtype=jnp.int32)
    chosen = jnp.max(jnp.where(accept_flags == 1, step_numbers[None, :], 0), axis=1)
    local_count = coarse_states.shape[0]
    accepted = coarse_states[jnp.arange(local_count, dtype=jnp.int32), chosen]
    every_field = lax.all_gather(accepted, "chain", axis=0, tiled=True)
    own = lax.dynamic_index_in_dim(every_field, owners[chain_index], 0, keepdims=False)

    cz, cy, cx = own.shape
    fz = source.shape[0]
    fy, fx = 2 * cy, 2 * cx
    coarse_total = cz * slabs
    fine_total = fz * slabs

    far = COARSE_HALO - cz
    parts = [shift_from(own[cz - far:], 2), shift_from(own, 1), own,
             shift_from(own, -1), shift_from(own[:far], -2)]
    ext = jnp.concatenate(parts, axis=0)
    n_ext = ext.shape[0]
    g0 = s * cz - COARSE_HALO
    gidx = g0 + jnp.arange(n_ext, dtype=jnp.int32)
    lo_plane = lax.dynamic_index_in_dim(ext, jnp.maximum(-g0, 0), 0, keepdims=True)
    hi_plane = lax.dynamic_index_in_dim(ext, jnp.minimum(coarse_total - 1 - g0, n_ext - 1), 0, keepdims=True)
    ext = jnp.where((gidx < 0)[:, None, None], lo_plane, ext)
    ext = jnp.where((gidx >= coarse_total)[:, None, None], hi_plane, ext)

    pro = along_x(ext, prolong_matrix(cx).astype(jnp.bfloat16), precision=lax.Precision.DEFAULT)
    pro = along_y(pro, prolong_matrix(cy))
    inner = pro[1:-1]
    even = 0.75 * inner + 0.25 * pro[:-2]
    odd = 0.75 * inner + 0.25 * pro[2:]
    log_perm = jnp.stack((even, odd), axis=1).reshape(2 * (n_ext - 2), fy, fx)
    k0_first = 2 * (g0 + 1)
    k0_planes = log_perm.shape[0]

    positions = k0_first + jnp.arange(k0_planes, dtype=jnp.int32)
    depth_table = mode_table(MZ, fine_total, positions)
    rows_table = mode_table(MY, fy, jnp.arange(fy, dtype=jnp.int32))
    cols_table = mode_table(MX, fx, jnp.arange(fx, dtype=jnp.int32))
    along_depth = jnp.einsum("abe,az->zbe", kl_coeffs[0], depth_table, precision=HI)
    along_rows = jnp.einsum("zbe,by->zye", along_depth, rows_table, precision=HI)
    kl = jnp.dot(along_rows.reshape(k0_planes * fy, MX), cols_table,
                 precision=HI).reshape(k0_planes, fy, fx)
    k0 = jnp.exp(log_perm + kl)
    k0 = jnp.where(plane_mask(k0_first, k0_planes, fine_total), k0, 0.0)
    k0_halo = (k0_planes - fz) // 2

    k1 = 0.125 * restrict_sum(k0)
    k1_halo = k0_halo // 2
    own1 = fz // 2
    k2_own = 0.125 * restrict_sum(k1[k1_halo:k1_halo + own1])
    k2 = lax.all_gather(k2_own, "slab", axis=0, tiled=True)

    h0k = F0_HALO + 1
    lvl0 = Level(k0[k0_halo - h0k: k0_halo + fz + h0k], h0k, fz, s * fz - h0k, fine_total)
    f0 = jnp.concatenate([shift_from(source[fz - F0_HALO:], 1), source,
                          shift_from(source[:F0_HALO], -1)], axis=0)
    u = lvl0.start(f0, F0_HALO)
    u1 = lvl0.sweep(u, lvl0.cut(f0, F0_HALO - 1, F0_HALO), F0_HALO)
    res0 = f0[F0_HALO:F0_HALO + fz] - lvl0.operate(u1[1:-1], 1)
    f1_own = 0.5 * restrict_sum(res0)

    h1k = F1_HALO + 1
    lvl1 = Level(k1[k1_halo - h1k: k1_halo + own1 + h1k], h1k, own1, s * own1 - h1k,
                 fine_total // 2)
    f1 = jnp.concatenate([shift_from(f1_own, 1), f1_own, shift_from(f1_own, -1)], axis=0)
    v = lvl1.start(f1, F1_HALO)
    v1 = lvl1.sweep(v, lvl1.cut(f1, F1_HALO - 1, F1_HALO), F1_HALO)
    res1 = f1_own - lvl1.operate(v1[2:-2], 1)
    f2 = gather_slabs(0.5 * restrict_sum(res1))

    own2 = own1 // 2
    total2 = fine_total // 4
    k2_halo = 13
    f2_halo = k2_halo - 1
    pad2 = ((k2_halo, k2_halo), (0, 0), (0, 0))
    k2w = lax.dynamic_slice_in_dim(jnp.pad(k2, pad2), s * own2, own2 + 2 * k2_halo, axis=0)
    f2w = lax.dynamic_slice_in_dim(jnp.pad(f2, pad2), s * own2 + 1, own2 + 2 * f2_halo, axis=0)
    lvl2 = Level(k2w, k2_halo, own2, s * own2 - k2_halo, total2)
    w = lvl2.start(f2w, f2_halo)
    w1 = lvl2.sweep(w, lvl2.cut(f2w, f2_halo - 1, f2_halo), f2_halo)
    res2 = lvl2.cut(f2w, f2_halo - 2, f2_halo) - lvl2.operate(w1, f2_halo - 1)
    f3 = 0.5 * restrict_sum(res2)
    f3_halo = (f2_halo - 2) // 2
    k3 = 0.125 * restrict_sum(k2w[1:-1])
    lvl3 = Level(k3, f3_halo + 1, own2 // 2, s * (own2 // 2) - f3_halo - 1, total2 // 2)
    b = lvl3.start(f3, f3_halo)
    for step in range(BOTTOM - 1):
        h = f3_halo - step
        b = lvl3.sweep(b, lvl3.cut(f3, h - 1, f3_halo), h)
    e3_halo = f3_halo - (BOTTOM - 1)
    cut2 = (f2_halo - 1) - 2 * e3_halo
    w = w1[cut2:w1.shape[0] - cut2] + copy_up(b)
    h = 2 * e3_halo
    for _ in range(SWEEPS):
        w = lvl2.sweep(w, lvl2.cut(f2w, h - 1, f2_halo), h)
        h -= 1
    e2 = w

    v = v1 + copy_up(e2)[1:-1]
    v = lvl1.sweep(v, lvl1.cut(f1, 2, F1_HALO), 3)
    e1 = lvl1.sweep(v, lvl1.cut(f1, 1, F1_HALO), 2)

    u = u1 + copy_up(e1)
    u = lvl0.sweep(u, lvl0.cut(f0, 1, F0_HALO), 2)
    u = lvl0.sweep(u, source, 1)
    return u[None]


def solution(mesh):
    return jax.shard_map(
        on_device,
        mesh=mesh,
        in_specs=(
            P("chain", None, "slab", None, None),
            P("chain", None),
            P(),
            P("chain", None, None, None),
            P("slab", None, None),
        ),
        out_specs=P("chain", "slab", None, None),
        check_vma=False,
    )
```

profile of v0, /device:TPU:24, one launch (start us, length us, event | category | flops | bytes accessed | tf_op | source)
XLA Modules:
  0.0 188.6 jit_solution(6216574723588018510)
XLA Ops:
  10.7 2.2 %all_gather.6 = bf16[8,4,64,128]{3,2,1,0:T(8,128)(2,1)S(1)} all-gather(bf16[4,4,64,128]{3,2,1,0:T(8,128)(2,1)S(1)} %gather_fusion), channel_id=1, replica_groups=mesh['chain'=2,'slab'=64] {'chain'}, dimensions={0}, use_global_device_ids=true | all-gather | bytes 786432 | tf_op jit(solution)/shard_map/all_gather | solution.py:149
  13.5 4.8 %collective-permute-start.4 = (bf16[4,64,128]{2,1,0:T(8,128)(2,1)S(1)}, bf16[4,64,128]{2,1,0:T(8,128)(2,1)S(1)}, u32[]{:S(2)}, u32[]{:S(2)}) collective-permute-start(bf16[4,64,128]{2,1,0:T(8,128)(2,1)S(1)} %dynamic-slice_bitcast_fusion), channel_id=1, source_target_pairs={{1,0},{2,1},{3,2},{4,3},{5,4},{6,5},{7,6},{8,7},{9,8},{10,9},{11,1... | collective-permute-start | bytes 196616 | tf_op jit(solution)/shard_map/ppermute | solution.py:71
  20.3 4.2 %collective-permute-start.5 = (bf16[2,64,128]{2,1,0:T(8,128)(2,1)S(1)}, bf16[2,64,128]{2,1,0:T(8,128)(2,1)S(1)}, u32[]{:S(2)}, u32[]{:S(2)}) collective-permute-start(bf16[2,64,128]{2,1,0:T(8,128)(2,1)S(1)} %get-tuple-element.17), channel_id=1, source_target_pairs={{2,0},{3,1},{4,2},{5,3},{6,4},{7,5},{8,6},{9,7},{10,8},{11,9},{12,... | collective-permute-start | bytes 98312 | tf_op jit(solution)/shard_map/ppermute | solution.py:71
  24.6 3.3 %collective-permute-start.2 = (bf16[2,64,128]{2,1,0:T(8,128)(2,1)S(1)}, bf16[2,64,128]{2,1,0:T(8,128)(2,1)S(1)}, u32[]{:S(2)}, u32[]{:S(2)}) collective-permute-start(bf16[2,64,128]{2,1,0:T(8,128)(2,1)S(1)} %get-tuple-element.18), channel_id=1, source_target_pairs={{0,2},{1,3},{2,4},{3,5},{4,6},{5,7},{6,8},{7,9},{8,10},{9,11},{10,... | collective-permute-start | bytes 98312 | tf_op jit(solution)/shard_map/ppermute | solution.py:71
  28.8 6.9 %collective-permute-start.1 = (f32[3,128,256]{2,1,0:T(8,128)}, f32[3,128,256]{2,1,0:T(8,128)}, u32[]{:S(2)}, u32[]{:S(2)}) collective-permute-start(f32[3,128,256]{2,1,0:T(8,128)} %get-tuple-element.15), channel_id=1, source_target_pairs={{1,0},{2,1},{3,2},{4,3},{5,4},{6,5},{7,6},{8,7},{9,8},{10,9},{11,1... | collective-permute-start | bytes 1179656 | tf_op jit(solution)/shard_map/ppermute | solution.py:71
  41.7 3.4 %convolution_bitcast_fusion = f32[16,128,256]{1,2,0:T(8,128)S(1)} fusion(f32[16,64,256]{2,1,0:T(8,128)S(1)} %fusion.127, f32[64,128,1]{1,0,2:T(8,128)S(1)} %copy-done.41), kind=kOutput, calls=%fused_computation.41 | convolution fusion | flops 402653184 | bytes 3178496 | tf_op jit(solution)/shard_map/zyx,yv->zvx/dot_general | solution.py:50
  45.5 2.2 %pad_maximum_fusion = f32[14,2,128,256]{2,3,0,1:T(8,128)} fusion(f32[14,1,128,256]{2,3,0,1:T(8,128)S(1)} %get-tuple-element.14, f32[14,1,128,256]{2,3,0,1:T(8,128)S(1)} %get-tuple-element.13), kind=kLoop, calls=%fused_computation.1 | loop fusion | flops 917504 | bytes 7340032 | tf_op jit(solution)/shard_map/stack | solution.py:175
  47.7 5.1 %copy.29 = f32[14,2,128,256]{3,2,1,0:T(8,128)} copy(f32[14,2,128,256]{2,3,0,1:T(8,128)} %pad_maximum_fusion) | data formatting | bytes 7340032 | tf_op jit(solution)/shard_map/stack | solution.py:175
  52.8 5.8 %fusion.1 = f32[28,128,256]{2,1,0:T(8,128)S(1)} fusion(f32[14,2,128,256]{3,2,1,0:T(8,128)} %copy.29, f32[28,128,64]{1,2,0:T(8,128)S(1)} %convolution_bitcast_fusion.2, pred[28]{0:T(512)(128)(4,1)S(1)} %compare_and_fusion.12, s32[256]{0:T(256)S(1)} %multiply_add_fusion, s32[64]{0:T(128)S(1)} %iota_add_fusion), kind=kOutput, calls=%fused_computation.4 | convolution fusion | flops 706707456 | bytes 8258844 | tf_op jit(solution)/shard_map/dot_general | solution.py:185
  60.4 4.4 %reduce_sum.55 = f32[14,128,256]{2,1,0:T(8,128)} reduce(f32[14,2,128,256]{3,2,1,0:T(8,128)} %bitcast.125, f32[]{:T(128)} %constant.128.clone.1), dimensions={1}, to_apply=%region_2.3 | reduce | flops 458752 | bytes 5505028 | tf_op jit(solution)/shard_map/reduce_sum | solution.py:56
  64.8 2.8 %convolution_bitcast_fusion.1 = f32[14,64,256]{2,1,0:T(8,128)S(1)} fusion(f32[14,128,256]{2,1,0:T(8,128)} %reduce_sum.55, f32[128,64,1]{0,1,2:T(8,128)S(1)} %copy-done.35), kind=kOutput, calls=%fused_computation.64 | convolution fusion | flops 352321536 | bytes 2785280 | tf_op jit(solution)/shard_map/zyx,yv->zvx/dot_general | solution.py:50
  71.2 2.3 %fusion.3 = f32[14,128,257]{2,1,0:T(8,128)} fusion(f32[14,128,256]{2,1,0:T(8,128)S(1)} %slice.1283), kind=kLoop, calls=%fused_computation.13 | loop fusion | flops 921088 | bytes 3677184 | tf_op jit(solution)/shard_map/mul | solution.py:98
  73.5 2.3 %add_multiply_fusion = f32[14,129,256]{2,1,0:T(8,128)S(1)} fusion(f32[14,128,256]{2,1,0:T(8,128)} %copy-done.15), kind=kLoop, calls=%fused_computation.23 | loop fusion | flops 924672 | bytes 3684352 | tf_op jit(solution)/shard_map/mul | solution.py:96
  79.5 4.1 %divide_select_fusion = (f32[14,128,256]{2,1,0:T(8,128)S(1)}, f32[14,128,256]{2,1,0:T(8,128)S(1)}) fusion(f32[14,128,256]{2,1,0:T(8,128)S(1)} %constant_dynamic-update-slice_fusion, pred[14]{0:T(512)(128)(4,1)S(1)} %compare_and_fusion.13, f32[14,128,257]{2,1,0:T(8,128)} %fusion.3, f32[14,129,256]{2,1,0:T(8,128)S(1)} %add_multiply_fusion, ...), kind=kLoop, calls=%fused_computation.36 | loop fusion | flops 3670016 | bytes 16515086 | tf_op jit(solution)/shard_map/jit(_where)/select_n | solution.py:114
  83.8 2.3 %copy-done.4 = f32[14,128,257]{2,1,0:T(8,128)S(1)} copy-done((f32[14,128,257]{2,1,0:T(8,128)S(1)}, f32[14,128,257]{2,1,0:T(8,128)}, u32[]{:S(2)}) %copy-start.4) | copy-done | bytes 1842200
  86.1 2.4 %fusion.23 = f32[12,128,256]{2,1,0:T(8,128)S(1)} fusion(f32[12,128,256]{2,1,0:T(8,128)S(1)} %slice.1288, f32[14,128,257]{2,1,0:T(8,128)S(1)} %copy-done.4, f32[14,129,256]{2,1,0:T(8,128)S(1)} %add_multiply_fusion, f32[14,128,256]{2,1,0:T(8,128)S(1)} %get-tuple-element.11, f32[15,128,256]{2,1,0:T(8,128)S(1)} %copy-done.2, ...), kind=kLoop, calls=%fused_computation.61 | loop fusion | flops 7077888 | bytes 18874380 | tf_op jit(solution)/shard_map/jit(_where)/select_n | solution.py:114
  92.4 6.0 %collective-permute-start.7 = (f32[4,64,128]{2,1,0:T(8,128)S(1)}, f32[4,64,128]{2,1,0:T(8,128)S(1)}, u32[]{:S(2)}, u32[]{:S(2)}) collective-permute-start(f32[4,64,128]{2,1,0:T(8,128)S(1)} %convolution_multiply_fusion.1), channel_id=1, source_target_pairs={{1,0},{2,1},{3,2},{4,3},{5,4},{6,5},{7,6},{8,7},{9,8},{10,9},{11,1... | collective-permute-start | bytes 393224 | tf_op jit(solution)/shard_map/ppermute | solution.py:71
  101.0 6.5 %collective-permute-done.6 = f32[4,64,128]{2,1,0:T(8,128)S(1)} collective-permute-done((f32[4,64,128]{2,1,0:T(8,128)S(1)}, f32[4,64,128]{2,1,0:T(8,128)S(1)}, u32[]{:S(2)}, u32[]{:S(2)}) %collective-permute-start.6) | collective-permute-done | bytes 131104 | tf_op jit(solution)/shard_map/ppermute | solution.py:71
  110.8 16.6 %all-to-all-start = ((f32[64,32,128]{2,1,0:T(8,128)}), f32[64,32,128]{2,1,0:T(8,128)S(1)}, u32[]{:S(2)}, u32[]{:S(2)}) async-start(f32[64,32,128]{2,1,0:T(8,128)} %broadcast_in_dim.320), calls=%async_computation | async-start | bytes 2097152 | tf_op jit(solution)/shard_map/all_to_all | solution.py:78
  132.9 8.2 %all-to-all-done = f32[64,32,128]{2,1,0:T(8,128)S(1)} async-done(((f32[64,32,128]{2,1,0:T(8,128)}), f32[64,32,128]{2,1,0:T(8,128)S(1)}, u32[]{:S(2)}, u32[]{:S(2)}) %all-to-all-start) | async-done | bytes 1048608 | tf_op jit(solution)/shard_map/all_to_all | solution.py:78
  142.8 7.9 %all-gather.2.cloned.1.call-done = f32[128,32,64]{2,1,0:T(8,128)} async-done(((f32[2,32,64]{2,1,0:T(8,128)}), f32[128,32,64]{2,1,0:T(8,128)}) %all-gather.2.cloned.1.call-update) | async-done | bytes 1048592 | tf_op jit(solution)/shard_map/all_gather | solution.py:195
  171.4 2.0 %bitcast_add_fusion.1 = f32[12,128,256]{2,1,0:T(8,128)S(1)} fusion(f32[12,128,256]{2,1,0:T(8,128)} %copy-done.12, f32[6,128,256]{2,1,0:T(8,128)} %copy.32), kind=kLoop, calls=%fused_computation.60 | loop fusion | flops 393216 | bytes 3932160 | tf_op jit(solution)/shard_map/add | solution.py:247
  175.3 3.1 %fusion.38 = f32[10,128,256]{2,1,0:T(8,128)S(1)} fusion(f32[10,128,256]{2,1,0:T(8,128)S(1)} %slice.1452, f32[14,128,257]{2,1,0:T(8,128)S(1)} %copy-done.5, f32[14,129,256]{2,1,0:T(8,128)S(1)} %add_multiply_fusion, f32[12,128,256]{2,1,0:T(8,128)S(1)} %bitcast_add_fusion.1, f32[15,128,256]{2,1,0:T(8,128)S(1)} %copy-done.3, f32[14,128,256]{2,1,0:T(8,128)S(1)} %copy-done.11, ...), kind=kLoop, calls=%fused_computation.82 | loop fusion | flops 5898240 | bytes 15728650 | tf_op jit(solution)/shard_map/jit(_where)/select_n | solution.py:114
  179.6 2.2 %select_bitcast_fusion = f32[1,8,128,256]{3,2,1,0:T(8,128)} fusion(f32[8,128,256]{2,1,0:T(8,128)S(1)} %slice.1463, f32[8,128,256]{2,1,0:T(8,128)S(1)} %copy-done.20, f32[10,128,256]{2,1,0:T(8,128)S(1)} %fusion.38, f32[14,128,257]{2,1,0:T(8,128)S(1)} %copy-done.5, f32[14,129,256]{2,1,0:T(8,128)S(1)} %add_multiply_fusion, f32[15,128,256]{2,1,0:T(8,128)S(1)} %copy-done.3, ...), kind=kLoop, calls=%fused_computation.130 | loop fusion | flops 4718592 | bytes 12582920 | tf_op jit(solution)/shard_map/broadcast_in_dim | solution.py:250
  (235 shorter events, 60.9 us)
Async XLA Ops:
  6.5 21.3 %copy-start.18 = (f32[8,128,256]{2,1,0:T(8,128)S(1)}, f32[8,128,256]{2,1,0:T(8,128)}, u32[]{:S(2)}) copy-start(f32[8,128,256]{2,1,0:T(8,128)} %param.29) | copy-start | bytes 3145732
  6.5 30.4 %copy-start.38 = (f32[1,32,16,64]{3,2,1,0:T(8,128)S(1)}, f32[1,32,16,64]{3,2,1,0:T(8,128)}, u32[]{:S(2)}) copy-start(f32[1,32,16,64]{3,2,1,0:T(8,128)} %param.28) | copy-start | bytes 393220
  6.5 144.1 %all-gather.2.cloned.1.call-start = ((), (), s32[]{:S(2)}) async-start(), calls=%async_computation.1 | async-start | bytes 2129920 | tf_op jit(solution)/shard_map/all_gather | solution.py:195
  13.5 27.7 %collective-permute-start.4 = (bf16[4,64,128]{2,1,0:T(8,128)(2,1)S(1)}, bf16[4,64,128]{2,1,0:T(8,128)(2,1)S(1)}, u32[]{:S(2)}, u32[]{:S(2)}) collective-permute-start(bf16[4,64,128]{2,1,0:T(8,128)(2,1)S(1)} %dynamic-slice_bitcast_fusion), channel_id=1, source_target_pairs={{1,0},{2,1},{3,2},{4,3},{5,4},{6,5},{7,6},{8,7},{9,8},{10,9},{11,1... | collective-permute-start | bytes 196616 | tf_op jit(solution)/shard_map/ppermute | solution.py:71
  18.4 22.8 %collective-permute-start.3 = (bf16[4,64,128]{2,1,0:T(8,128)(2,1)S(1)}, bf16[4,64,128]{2,1,0:T(8,128)(2,1)S(1)}, u32[]{:S(2)}, u32[]{:S(2)}) collective-permute-start(bf16[4,64,128]{2,1,0:T(8,128)(2,1)S(1)} %dynamic-slice_bitcast_fusion), channel_id=1, source_target_pairs={{0,1},{1,2},{2,3},{3,4},{4,5},{5,6},{6,7},{7,8},{8,9},{9,10},{10,1... | collective-permute-start | bytes 196616 | tf_op jit(solution)/shard_map/ppermute | solution.py:71
  20.3 20.9 %collective-permute-start.5 = (bf16[2,64,128]{2,1,0:T(8,128)(2,1)S(1)}, bf16[2,64,128]{2,1,0:T(8,128)(2,1)S(1)}, u32[]{:S(2)}, u32[]{:S(2)}) collective-permute-start(bf16[2,64,128]{2,1,0:T(8,128)(2,1)S(1)} %get-tuple-element.17), channel_id=1, source_target_pairs={{2,0},{3,1},{4,2},{5,3},{6,4},{7,5},{8,6},{9,7},{10,8},{11,9},{12,... | collective-permute-start | bytes 98312 | tf_op jit(solution)/shard_map/ppermute | solution.py:71
  24.5 16.8 %copy-start.40 = (bf16[128,256,1]{1,0,2:T(8,128)(2,1)S(1)}, bf16[128,256,1]{1,0,2:T(8,128)(2,1)}, u32[]{:S(2)}) copy-start(bf16[128,256,1]{1,0,2:T(8,128)(2,1)} %constant.370) | copy-start | bytes 196612
  24.6 14.7 %collective-permute-start.2 = (bf16[2,64,128]{2,1,0:T(8,128)(2,1)S(1)}, bf16[2,64,128]{2,1,0:T(8,128)(2,1)S(1)}, u32[]{:S(2)}, u32[]{:S(2)}) collective-permute-start(bf16[2,64,128]{2,1,0:T(8,128)(2,1)S(1)} %get-tuple-element.18), channel_id=1, source_target_pairs={{0,2},{1,3},{2,4},{3,5},{4,6},{5,7},{6,8},{7,9},{8,10},{9,11},{10,... | collective-permute-start | bytes 98312 | tf_op jit(solution)/shard_map/ppermute | solution.py:71
  28.8 49.7 %collective-permute-start.1 = (f32[3,128,256]{2,1,0:T(8,128)}, f32[3,128,256]{2,1,0:T(8,128)}, u32[]{:S(2)}, u32[]{:S(2)}) collective-permute-start(f32[3,128,256]{2,1,0:T(8,128)} %get-tuple-element.15), channel_id=1, source_target_pairs={{1,0},{2,1},{3,2},{4,3},{5,4},{6,5},{7,6},{8,7},{9,8},{10,9},{11,1... | collective-permute-start | bytes 1179656 | tf_op jit(solution)/shard_map/ppermute | solution.py:71
  37.0 4.7 %copy-start.41 = (f32[64,128,1]{1,0,2:T(8,128)S(1)}, f32[64,128,1]{1,0,2:T(8,128)}, u32[]{:S(2)}) copy-start(f32[64,128,1]{1,0,2:T(8,128)} %constant.371) | copy-start | bytes 98308
  39.2 36.7 %collective-permute-start = (f32[3,128,256]{2,1,0:T(8,128)}, f32[3,128,256]{2,1,0:T(8,128)}, u32[]{:S(2)}, u32[]{:S(2)}) collective-permute-start(f32[3,128,256]{2,1,0:T(8,128)} %get-tuple-element.16), channel_id=1, source_target_pairs={{0,1},{1,2},{2,3},{3,4},{4,5},{5,6},{6,7},{7,8},{8,9},{9,10},{10,1... | collective-permute-start | bytes 1179656 | tf_op jit(solution)/shard_map/ppermute | solution.py:71
  60.4 10.8 %copy-start.15 = (f32[14,128,256]{2,1,0:T(8,128)}, f32[14,128,256]{2,1,0:T(8,128)S(1)}, u32[]{:S(2)}) copy-start(f32[14,128,256]{2,1,0:T(8,128)S(1)} %slice.1283) | copy-start | bytes 5505028
  60.4 4.4 %copy-start.35 = (f32[128,64,1]{0,1,2:T(8,128)S(1)}, f32[128,64,1]{0,1,2:T(8,128)}, u32[]{:S(2)}) copy-start(f32[128,64,1]{0,1,2:T(8,128)} %constant.372) | copy-start | bytes 98308
  60.4 7.2 %copy-start.36 = (f32[256,128,1]{1,0,2:T(8,128)S(1)}, f32[256,128,1]{1,0,2:T(8,128)}, u32[]{:S(2)}) copy-start(f32[256,128,1]{1,0,2:T(8,128)} %constant.373) | copy-start | bytes 393220
  68.6 40.0 %copy-start.13 = (f32[13,64,128]{2,1,0:T(8,128)}, f32[13,64,128]{2,1,0:T(8,128)S(1)}, u32[]{:S(2)}) copy-start(f32[13,64,128]{2,1,0:T(8,128)S(1)} %fusion.72) | copy-start | bytes 1277956
  75.9 32.7 %copy-start.16 = (f32[12,65,128]{2,1,0:T(8,128)}, f32[12,65,128]{2,1,0:T(8,128)S(1)}, u32[]{:S(2)}) copy-start(f32[12,65,128]{2,1,0:T(8,128)S(1)} %add_multiply_fusion.1) | copy-start | bytes 1198084
  79.5 4.3 %copy-start.21 = (f32[14,128,256]{2,1,0:T(8,128)}, f32[14,128,256]{2,1,0:T(8,128)S(1)}, u32[]{:S(2)}) copy-start(f32[14,128,256]{2,1,0:T(8,128)S(1)} %constant_dynamic-update-slice_fusion) | copy-start | bytes 5505028
  83.7 5.0 %copy-start.10 = (f32[14,128,256]{2,1,0:T(8,128)}, f32[14,128,256]{2,1,0:T(8,128)S(1)}, u32[]{:S(2)}) copy-start(f32[14,128,256]{2,1,0:T(8,128)S(1)} %get-tuple-element.12) | copy-start | bytes 5505028
  92.4 8.6 %collective-permute-start.7 = (f32[4,64,128]{2,1,0:T(8,128)S(1)}, f32[4,64,128]{2,1,0:T(8,128)S(1)}, u32[]{:S(2)}, u32[]{:S(2)}) collective-permute-start(f32[4,64,128]{2,1,0:T(8,128)S(1)} %convolution_multiply_fusion.1), channel_id=1, source_target_pairs={{1,0},{2,1},{3,2},{4,3},{5,4},{6,5},{7,6},{8,7},{9,8},{10,9},{11,1... | collective-permute-start | bytes 393224 | tf_op jit(solution)/shard_map/ppermute | solution.py:71
  98.5 9.0 %collective-permute-start.6 = (f32[4,64,128]{2,1,0:T(8,128)S(1)}, f32[4,64,128]{2,1,0:T(8,128)S(1)}, u32[]{:S(2)}, u32[]{:S(2)}) collective-permute-start(f32[4,64,128]{2,1,0:T(8,128)S(1)} %convolution_multiply_fusion.1), channel_id=1, source_target_pairs={{0,1},{1,2},{2,3},{3,4},{4,5},{5,6},{6,7},{7,8},{8,9},{9,10},{10,1... | collective-permute-start | bytes 393224 | tf_op jit(solution)/shard_map/ppermute | solution.py:71
  100.7 7.9 %copy-start.22 = (f32[12,64,129]{2,1,0:T(8,128)}, f32[12,64,129]{2,1,0:T(8,128)S(1)}, u32[]{:S(2)}) copy-start(f32[12,64,129]{2,1,0:T(8,128)S(1)} %fusion.65) | copy-start | bytes 1188868
  110.8 30.3 %all-to-all-start = ((f32[64,32,128]{2,1,0:T(8,128)}), f32[64,32,128]{2,1,0:T(8,128)S(1)}, u32[]{:S(2)}, u32[]{:S(2)}) async-start(f32[64,32,128]{2,1,0:T(8,128)} %broadcast_in_dim.320), calls=%async_computation | async-start | bytes 2097152 | tf_op jit(solution)/shard_map/all_to_all | solution.py:78
  142.8 9.0 %copy-start.42 = (f32[32,16,1]{0,1,2:T(8,128)S(1)}, f32[32,16,1]{0,1,2:T(8,128)}, u32[]{:S(2)}) copy-start(f32[32,16,1]{0,1,2:T(8,128)} %constant.375) | copy-start | bytes 6148
  160.4 4.2 %copy-start.7 = (f32[128,32,64]{2,1,0:T(8,128)S(1)}, f32[128,32,64]{2,1,0:T(8,128)}, u32[]{:S(2)}) copy-start(f32[128,32,64]{2,1,0:T(8,128)} %reshape.222) | copy-start | bytes 3145732
  (42 other events, 87.0 us)
Sparse Core Ops, SparseCore 0:
  76.0 74.6 all-gather.1
where the time goes:
time: 191 us; the launch traced here: 189 us
  starting transfers between devices  47.6 us (25%)
  other arithmetic  44.9 us (24%)
  local copies, waits for them, and re-layouts  30.6 us (16%)
  matrix products  23.8 us (12%)
  waiting for transfers between devices  23 us (12%)
  between operations  16.6 us (9%)
  blocking collectives  2.18 us (1%)
    ppermute x8, starting transfers between devices, shift_from(): return lax.ppermute(block, 'slab', pairs)  31 us
    all_to_all x1, starting transfers between devices, gather_slabs(): got = lax.all_to_all(spread, 'slab', 0, 0, tiled=False)  16.6 us
    unnamed x118, local copies, waits for them, and re-layouts  15.7 us
    select_n x11, other arithmetic, mask(): jnp.where(plane_mask(self.first + self.halo - h, u.shape[0], self.total),...  13.1 us
    dot_general x10, matrix products, along_y(): jnp.einsum('zyx,yv->zvx', values, jnp.asarray(matrix), precision=precisio...  10.4 us
    all_to_all x1, waiting for transfers between devices, gather_slabs(): got = lax.all_to_all(spread, 'slab', 0, 0, tiled=False)  8.21 us
    all_gather x1, waiting for transfers between devices, on_device(): k2 = lax.all_gather(k2_own, 'slab', axis=0, tiled=True)  7.93 us
    reduce_sum x6, other arithmetic, restrict_sum(): values = values.reshape(nz // 2, 2, ny, nx).sum(axis=1)  7.61 us
  transfers between devices with their start and end apart: 10, of which 4 were waited for; matrix products, arithmetic and copies ran while one was open for 31% of the time, Pallas kernels for 0%

commit v1 on v0

--- a/solution.py
+++ b/solution.py
@@ -71,12 +71,19 @@
     return lax.ppermute(block, "slab", pairs)
 
 
-def gather_slabs(block):
+def gather_slabs(*blocks):
     count = lax.axis_size("slab")
-    flat = block.reshape(block.size // 128, 128)
+    flat = jnp.concatenate([b.reshape(b.size // 128, 128) for b in blocks], axis=0)
     spread = jnp.broadcast_to(flat[None], (count,) + flat.shape)
     got = lax.all_to_all(spread, "slab", 0, 0, tiled=False)
-    return got.reshape((count * block.shape[0],) + block.shape[1:])
+    outs = []
+    row = 0
+    for b in blocks:
+        rows = b.size // 128
+        part = got[:, row:row + rows]
+        outs.append(part.reshape((count * b.shape[0],) + b.shape[1:]))
+        row += rows
+    return outs
 
 
 def plane_mask(first_global, planes, total):
@@ -192,7 +199,6 @@
     k1_halo = k0_halo // 2
     own1 = fz // 2
     k2_own = 0.125 * restrict_sum(k1[k1_halo:k1_halo + own1])
-    k2 = lax.all_gather(k2_own, "slab", axis=0, tiled=True)
 
     h0k = F0_HALO + 1
     lvl0 = Level(k0[k0_halo - h0k: k0_halo + fz + h0k], h0k, fz, s * fz - h0k, fine_total)
@@ -210,7 +216,7 @@
     v = lvl1.start(f1, F1_HALO)
     v1 = lvl1.sweep(v, lvl1.cut(f1, F1_HALO - 1, F1_HALO), F1_HALO)
     res1 = f1_own - lvl1.operate(v1[2:-2], 1)
-    f2 = gather_slabs(0.5 * restrict_sum(res1))
+    f2, k2 = gather_slabs(0.5 * restrict_sum(res1), k2_own)
 
     own2 = own1 // 2
     total2 = fine_total // 4

time: 191 us -> 191 us (level)
  the two profiles are of different devices: /device:TPU:24 before, /device:TPU:0 now
where the time goes in v1:
time: 191 us; the launch traced here: 190 us
  starting transfers between devices  52.9 us (28%)
  other arithmetic  47.6 us (25%)
  local copies, waits for them, and re-layouts  36.4 us (19%)
  matrix products  24.1 us (13%)
  waiting for transfers between devices  23.6 us (12%)
  between operations  3.18 us (2%)
  blocking collectives  2.18 us (1%)
    all_to_all x1, starting transfers between devices, gather_slabs(): got = lax.all_to_all(spread, 'slab', 0, 0, tiled=False)  26.8 us
    ppermute x8, starting transfers between devices, shift_from(): return lax.ppermute(block, 'slab', pairs)  26.1 us
    all_to_all x1, waiting for transfers between devices, gather_slabs(): got = lax.all_to_all(spread, 'slab', 0, 0, tiled=False)  21.4 us
    unnamed x112, local copies, waits for them, and re-layouts  15.4 us
    select_n x11, other arithmetic, mask(): jnp.where(plane_mask(self.first + self.halo - h, u.shape[0], self.total),...  15.1 us
    dot_general x10, matrix products, along_y(): jnp.einsum('zyx,yv->zvx', values, jnp.asarray(matrix), precision=precisio...  10.4 us
    reduce_sum x6, other arithmetic, restrict_sum(): values = values.reshape(nz // 2, 2, ny, nx).sum(axis=1)  7.57 us
    dot_general x1, matrix products, on_device(): jnp.dot(along_rows.reshape(k0_planes * fy, MX), cols_table, precision=HI)  5.78 us
  transfers between devices with their start and end apart: 9, of which 3 were waited for; matrix products, arithmetic and copies ran while one was open for 23% of the time, Pallas kernels for 0%

profile of v1, /device:TPU:0, one launch (start us, length us, event | category | flops | bytes accessed | tf_op | source)
XLA Modules:
  0.0 189.9 jit_solution(3612115857835921653)
XLA Ops:
  4.1 2.2 %all_gather.3 = bf16[8,4,64,128]{3,2,1,0:T(8,128)(2,1)S(1)} all-gather(bf16[4,4,64,128]{3,2,1,0:T(8,128)(2,1)S(1)} %gather_fusion), channel_id=1, replica_groups=mesh['chain'=2,'slab'=64] {'chain'}, dimensions={0}, use_global_device_ids=true | all-gather | bytes 786432 | tf_op jit(solution)/shard_map/all_gather | solution.py:156
  8.3 4.5 %collective-permute-start.3 = (bf16[4,64,128]{2,1,0:T(8,128)(2,1)S(1)}, bf16[4,64,128]{2,1,0:T(8,128)(2,1)S(1)}, u32[]{:S(2)}, u32[]{:S(2)}) collective-permute-start(bf16[4,64,128]{2,1,0:T(8,128)(2,1)S(1)} %dynamic-slice_bitcast_fusion), channel_id=1, source_target_pairs={{0,1},{1,2},{2,3},{3,4},{4,5},{5,6},{6,7},{7,8},{8,9},{9,10},{10,1... | collective-permute-start | bytes 196616 | tf_op jit(solution)/shard_map/ppermute | solution.py:71
  14.2 6.2 %collective-permute-start.2 = (bf16[2,64,128]{2,1,0:T(8,128)(2,1)S(1)}, bf16[2,64,128]{2,1,0:T(8,128)(2,1)S(1)}, u32[]{:S(2)}, u32[]{:S(2)}) collective-permute-start(bf16[2,64,128]{2,1,0:T(8,128)(2,1)S(1)} %get-tuple-element.20), channel_id=1, source_target_pairs={{0,2},{1,3},{2,4},{3,5},{4,6},{5,7},{6,8},{7,9},{8,10},{9,11},{10,... | collective-permute-start | bytes 98312 | tf_op jit(solution)/shard_map/ppermute | solution.py:71
  25.0 5.6 %collective-permute-start = (f32[3,128,256]{2,1,0:T(8,128)}, f32[3,128,256]{2,1,0:T(8,128)}, u32[]{:S(2)}, u32[]{:S(2)}) collective-permute-start(f32[3,128,256]{2,1,0:T(8,128)} %get-tuple-element.18), channel_id=1, source_target_pairs={{0,1},{1,2},{2,3},{3,4},{4,5},{5,6},{6,7},{7,8},{8,9},{9,10},{10,1... | collective-permute-start | bytes 1179656 | tf_op jit(solution)/shard_map/ppermute | solution.py:71
  31.2 3.4 %convolution_bitcast_fusion = f32[16,128,256]{1,2,0:T(8,128)S(1)} fusion(f32[16,64,256]{2,1,0:T(8,128)S(1)} %fusion.127, f32[64,128,1]{1,0,2:T(8,128)S(1)} %copy-done.42), kind=kOutput, calls=%fused_computation.41 | convolution fusion | flops 402653184 | bytes 3178496 | tf_op jit(solution)/shard_map/zyx,yv->zvx/dot_general | solution.py:50
  35.0 2.2 %pad_maximum_fusion = f32[14,2,128,256]{2,3,0,1:T(8,128)} fusion(f32[14,1,128,256]{2,3,0,1:T(8,128)S(1)} %get-tuple-element.16, f32[14,1,128,256]{2,3,0,1:T(8,128)S(1)} %get-tuple-element.15), kind=kLoop, calls=%fused_computation.1 | loop fusion | flops 917504 | bytes 7340032 | tf_op jit(solution)/shard_map/stack | solution.py:182
  37.2 5.1 %copy.29 = f32[14,2,128,256]{3,2,1,0:T(8,128)} copy(f32[14,2,128,256]{2,3,0,1:T(8,128)} %pad_maximum_fusion) | data formatting | bytes 7340032 | tf_op jit(solution)/shard_map/stack | solution.py:182
  42.3 5.8 %fusion.1 = f32[28,128,256]{2,1,0:T(8,128)S(1)} fusion(f32[14,2,128,256]{3,2,1,0:T(8,128)} %copy.29, f32[28,128,64]{1,2,0:T(8,128)S(1)} %convolution_bitcast_fusion.2, pred[28]{0:T(512)(128)(4,1)S(1)} %compare_and_fusion.12, s32[256]{0:T(256)S(1)} %multiply_add_fusion, s32[64]{0:T(128)S(1)} %iota_add_fusion), kind=kOutput, calls=%fused_computation.4 | convolution fusion | flops 706707456 | bytes 8258844 | tf_op jit(solution)/shard_map/dot_general | solution.py:192
  49.9 4.4 %reduce_sum.55 = f32[14,128,256]{2,1,0:T(8,128)} reduce(f32[14,2,128,256]{3,2,1,0:T(8,128)} %bitcast.125, f32[]{:T(128)} %constant.128.clone.1), dimensions={1}, to_apply=%region_2.3 | reduce | flops 458752 | bytes 5505028 | tf_op jit(solution)/shard_map/reduce_sum | solution.py:56
  54.3 2.8 %convolution_bitcast_fusion.1 = f32[14,64,256]{2,1,0:T(8,128)S(1)} fusion(f32[14,128,256]{2,1,0:T(8,128)} %reduce_sum.55, f32[128,64,1]{0,1,2:T(8,128)S(1)} %copy-done.36), kind=kOutput, calls=%fused_computation.64 | convolution fusion | flops 352321536 | bytes 2785280 | tf_op jit(solution)/shard_map/zyx,yv->zvx/dot_general | solution.py:50
  60.0 2.3 %fusion.3 = f32[14,128,257]{2,1,0:T(8,128)} fusion(f32[14,128,256]{2,1,0:T(8,128)S(1)} %slice.1291), kind=kLoop, calls=%fused_computation.13 | loop fusion | flops 921088 | bytes 3677184 | tf_op jit(solution)/shard_map/mul | solution.py:105
  62.3 2.3 %add_multiply_fusion = f32[14,129,256]{2,1,0:T(8,128)S(1)} fusion(f32[14,128,256]{2,1,0:T(8,128)} %copy-done.16), kind=kLoop, calls=%fused_computation.23 | loop fusion | flops 924672 | bytes 3684352 | tf_op jit(solution)/shard_map/mul | solution.py:103
  68.4 4.1 %divide_select_fusion = (f32[14,128,256]{2,1,0:T(8,128)S(1)}, f32[14,128,256]{2,1,0:T(8,128)S(1)}) fusion(f32[14,128,256]{2,1,0:T(8,128)S(1)} %constant_dynamic-update-slice_fusion, pred[14]{0:T(512)(128)(4,1)S(1)} %compare_and_fusion.13, f32[14,128,257]{2,1,0:T(8,128)} %fusion.3, f32[14,129,256]{2,1,0:T(8,128)S(1)} %add_multiply_fusion, ...), kind=kLoop, calls=%fused_computation.36 | loop fusion | flops 3670016 | bytes 16515086 | tf_op jit(solution)/shard_map/jit(_where)/select_n | solution.py:121
  72.7 2.3 %copy-done.4 = f32[14,128,257]{2,1,0:T(8,128)S(1)} copy-done((f32[14,128,257]{2,1,0:T(8,128)S(1)}, f32[14,128,257]{2,1,0:T(8,128)}, u32[]{:S(2)}) %copy-start.4) | copy-done | bytes 1842200
  75.0 2.4 %fusion.23 = f32[12,128,256]{2,1,0:T(8,128)S(1)} fusion(f32[12,128,256]{2,1,0:T(8,128)S(1)} %slice.1296, f32[14,128,257]{2,1,0:T(8,128)S(1)} %copy-done.4, f32[14,129,256]{2,1,0:T(8,128)S(1)} %add_multiply_fusion, f32[14,128,256]{2,1,0:T(8,128)S(1)} %get-tuple-element.11, f32[15,128,256]{2,1,0:T(8,128)S(1)} %copy-done.2, ...), kind=kLoop, calls=%fused_computation.61 | loop fusion | flops 7077888 | bytes 18874380 | tf_op jit(solution)/shard_map/jit(_where)/select_n | solution.py:121
  82.6 4.6 %collective-permute-start.6 = (f32[4,64,128]{2,1,0:T(8,128)S(1)}, f32[4,64,128]{2,1,0:T(8,128)S(1)}, u32[]{:S(2)}, u32[]{:S(2)}) collective-permute-start(f32[4,64,128]{2,1,0:T(8,128)S(1)} %convolution_multiply_fusion.1), channel_id=1, source_target_pairs={{0,1},{1,2},{2,3},{3,4},{4,5},{5,6},{6,7},{7,8},{8,9},{9,10},{10,1... | collective-permute-start | bytes 393224 | tf_op jit(solution)/shard_map/ppermute | solution.py:71
  93.5 26.8 %all-to-all-start = ((f32[64,64,128]{2,1,0:T(8,128)}), f32[64,64,128]{2,1,0:T(8,128)}, u32[]{:S(2)}, u32[]{:S(2)}) async-start(f32[64,64,128]{2,1,0:T(8,128)} %broadcast_in_dim.318), calls=%async_computation | async-start | bytes 4194304 | tf_op jit(solution)/shard_map/all_to_all | solution.py:78
  125.9 21.4 %all-to-all-done = f32[64,64,128]{2,1,0:T(8,128)} async-done(((f32[64,64,128]{2,1,0:T(8,128)}), f32[64,64,128]{2,1,0:T(8,128)}, u32[]{:S(2)}, u32[]{:S(2)}) %all-to-all-start) | async-done | bytes 2097184 | tf_op jit(solution)/shard_map/all_to_all | solution.py:78
  147.3 2.7 %fusion.312 = (f32[64,32,128]{2,1,0:T(8,128)S(1)}, f32[64,32,128]{2,1,0:T(8,128)}) fusion(f32[64,64,128]{2,1,0:T(8,128)} %all-to-all-done), kind=kLoop, calls=%fused_computation.533 | loop fusion | bytes 4194304 | tf_op jit(solution)/shard_map/slice | solution.py:83
  150.0 1.7 reshape.235
  157.4 2.7 %reshape.234 = f32[128,32,64]{2,1,0:T(8,128)} reshape(f32[64,32,128]{2,1,0:T(8,128)} %get-tuple-element.14) | data formatting | bytes 2097152 | tf_op jit(solution)/shard_map/reshape | solution.py:84
  179.5 2.0 %bitcast_add_fusion.1 = f32[12,128,256]{2,1,0:T(8,128)S(1)} fusion(f32[12,128,256]{2,1,0:T(8,128)} %copy-done.12, f32[6,128,256]{2,1,0:T(8,128)} %copy.32), kind=kLoop, calls=%fused_computation.60 | loop fusion | flops 393216 | bytes 3932160 | tf_op jit(solution)/shard_map/add | solution.py:253
  183.4 3.1 %fusion.38 = f32[10,128,256]{2,1,0:T(8,128)S(1)} fusion(f32[10,128,256]{2,1,0:T(8,128)S(1)} %slice.1462, f32[14,128,257]{2,1,0:T(8,128)S(1)} %copy-done.5, f32[14,129,256]{2,1,0:T(8,128)S(1)} %add_multiply_fusion, f32[12,128,256]{2,1,0:T(8,128)S(1)} %bitcast_add_fusion.1, f32[15,128,256]{2,1,0:T(8,128)S(1)} %copy-done.3, f32[14,128,256]{2,1,0:T(8,128)S(1)} %copy-done.11, ...), kind=kLoop, calls=%fused_computation.82 | loop fusion | flops 5898240 | bytes 15728650 | tf_op jit(solution)/shard_map/jit(_where)/select_n | solution.py:121
  187.7 2.2 %select_bitcast_fusion = f32[1,8,128,256]{3,2,1,0:T(8,128)} fusion(f32[8,128,256]{2,1,0:T(8,128)S(1)} %slice.1473, f32[8,128,256]{2,1,0:T(8,128)S(1)} %copy-done.21, f32[10,128,256]{2,1,0:T(8,128)S(1)} %fusion.38, f32[14,128,257]{2,1,0:T(8,128)S(1)} %copy-done.5, f32[14,129,256]{2,1,0:T(8,128)S(1)} %add_multiply_fusion, f32[15,128,256]{2,1,0:T(8,128)S(1)} %copy-done.3, ...), kind=kLoop, calls=%fused_computation.130 | loop fusion | flops 4718592 | bytes 12582920 | tf_op jit(solution)/shard_map/broadcast_in_dim | solution.py:256
  (230 shorter events, 64.0 us)
Async XLA Ops:
  0.0 20.4 %copy-start.19 = (f32[8,128,256]{2,1,0:T(8,128)S(1)}, f32[8,128,256]{2,1,0:T(8,128)}, u32[]{:S(2)}) copy-start(f32[8,128,256]{2,1,0:T(8,128)} %param.29) | copy-start | bytes 3145732
  0.0 22.7 %copy-start.39 = (f32[1,32,16,64]{3,2,1,0:T(8,128)S(1)}, f32[1,32,16,64]{3,2,1,0:T(8,128)}, u32[]{:S(2)}) copy-start(f32[1,32,16,64]{3,2,1,0:T(8,128)} %param.28) | copy-start | bytes 393220
  7.0 23.7 %collective-permute-start.4 = (bf16[4,64,128]{2,1,0:T(8,128)(2,1)S(1)}, bf16[4,64,128]{2,1,0:T(8,128)(2,1)S(1)}, u32[]{:S(2)}, u32[]{:S(2)}) collective-permute-start(bf16[4,64,128]{2,1,0:T(8,128)(2,1)S(1)} %dynamic-slice_bitcast_fusion), channel_id=1, source_target_pairs={{1,0},{2,1},{3,2},{4,3},{5,4},{6,5},{7,6},{8,7},{9,8},{10,9},{11,1... | collective-permute-start | bytes 196616 | tf_op jit(solution)/shard_map/ppermute | solution.py:71
  8.3 22.4 %collective-permute-start.3 = (bf16[4,64,128]{2,1,0:T(8,128)(2,1)S(1)}, bf16[4,64,128]{2,1,0:T(8,128)(2,1)S(1)}, u32[]{:S(2)}, u32[]{:S(2)}) collective-permute-start(bf16[4,64,128]{2,1,0:T(8,128)(2,1)S(1)} %dynamic-slice_bitcast_fusion), channel_id=1, source_target_pairs={{0,1},{1,2},{2,3},{3,4},{4,5},{5,6},{6,7},{7,8},{8,9},{9,10},{10,1... | collective-permute-start | bytes 196616 | tf_op jit(solution)/shard_map/ppermute | solution.py:71
  12.9 17.9 %collective-permute-start.5 = (bf16[2,64,128]{2,1,0:T(8,128)(2,1)S(1)}, bf16[2,64,128]{2,1,0:T(8,128)(2,1)S(1)}, u32[]{:S(2)}, u32[]{:S(2)}) collective-permute-start(bf16[2,64,128]{2,1,0:T(8,128)(2,1)S(1)} %get-tuple-element.19), channel_id=1, source_target_pairs={{2,0},{3,1},{4,2},{5,3},{6,4},{7,5},{8,6},{9,7},{10,8},{11,9},{12,... | collective-permute-start | bytes 98312 | tf_op jit(solution)/shard_map/ppermute | solution.py:71
  14.2 16.6 %copy-start.41 = (bf16[128,256,1]{1,0,2:T(8,128)(2,1)S(1)}, bf16[128,256,1]{1,0,2:T(8,128)(2,1)}, u32[]{:S(2)}) copy-start(bf16[128,256,1]{1,0,2:T(8,128)(2,1)} %constant.370) | copy-start | bytes 196612
  14.2 10.8 %collective-permute-start.2 = (bf16[2,64,128]{2,1,0:T(8,128)(2,1)S(1)}, bf16[2,64,128]{2,1,0:T(8,128)(2,1)S(1)}, u32[]{:S(2)}, u32[]{:S(2)}) collective-permute-start(bf16[2,64,128]{2,1,0:T(8,128)(2,1)S(1)} %get-tuple-element.20), channel_id=1, source_target_pairs={{0,2},{1,3},{2,4},{3,5},{4,6},{5,7},{6,8},{7,9},{8,10},{9,11},{10,... | collective-permute-start | bytes 98312 | tf_op jit(solution)/shard_map/ppermute | solution.py:71
  21.3 46.1 %collective-permute-start.1 = (f32[3,128,256]{2,1,0:T(8,128)}, f32[3,128,256]{2,1,0:T(8,128)}, u32[]{:S(2)}, u32[]{:S(2)}) collective-permute-start(f32[3,128,256]{2,1,0:T(8,128)} %get-tuple-element.17), channel_id=1, source_target_pairs={{1,0},{2,1},{3,2},{4,3},{5,4},{6,5},{7,6},{8,7},{9,8},{10,9},{11,1... | collective-permute-start | bytes 1179656 | tf_op jit(solution)/shard_map/ppermute | solution.py:71
  22.8 8.4 %copy-start.42 = (f32[64,128,1]{1,0,2:T(8,128)S(1)}, f32[64,128,1]{1,0,2:T(8,128)}, u32[]{:S(2)}) copy-start(f32[64,128,1]{1,0,2:T(8,128)} %constant.371) | copy-start | bytes 98308
  25.0 39.8 %collective-permute-start = (f32[3,128,256]{2,1,0:T(8,128)}, f32[3,128,256]{2,1,0:T(8,128)}, u32[]{:S(2)}, u32[]{:S(2)}) collective-permute-start(f32[3,128,256]{2,1,0:T(8,128)} %get-tuple-element.18), channel_id=1, source_target_pairs={{0,1},{1,2},{2,3},{3,4},{4,5},{5,6},{6,7},{7,8},{8,9},{9,10},{10,1... | collective-permute-start | bytes 1179656 | tf_op jit(solution)/shard_map/ppermute | solution.py:71
  49.9 10.1 %copy-start.16 = (f32[14,128,256]{2,1,0:T(8,128)}, f32[14,128,256]{2,1,0:T(8,128)S(1)}, u32[]{:S(2)}) copy-start(f32[14,128,256]{2,1,0:T(8,128)S(1)} %slice.1291) | copy-start | bytes 5505028
  49.9 4.4 %copy-start.36 = (f32[128,64,1]{0,1,2:T(8,128)S(1)}, f32[128,64,1]{0,1,2:T(8,128)}, u32[]{:S(2)}) copy-start(f32[128,64,1]{0,1,2:T(8,128)} %constant.372) | copy-start | bytes 98308
  49.9 7.2 %copy-start.37 = (f32[256,128,1]{1,0,2:T(8,128)S(1)}, f32[256,128,1]{1,0,2:T(8,128)}, u32[]{:S(2)}) copy-start(f32[256,128,1]{1,0,2:T(8,128)} %constant.373) | copy-start | bytes 393220
  58.0 32.7 %copy-start.14 = (f32[13,64,128]{2,1,0:T(8,128)}, f32[13,64,128]{2,1,0:T(8,128)S(1)}, u32[]{:S(2)}) copy-start(f32[13,64,128]{2,1,0:T(8,128)S(1)} %fusion.72) | copy-start | bytes 1277956
  64.8 26.0 %copy-start.17 = (f32[12,65,128]{2,1,0:T(8,128)}, f32[12,65,128]{2,1,0:T(8,128)S(1)}, u32[]{:S(2)}) copy-start(f32[12,65,128]{2,1,0:T(8,128)S(1)} %add_multiply_fusion.1) | copy-start | bytes 1198084
  68.4 4.3 %copy-start.22 = (f32[14,128,256]{2,1,0:T(8,128)}, f32[14,128,256]{2,1,0:T(8,128)S(1)}, u32[]{:S(2)}) copy-start(f32[14,128,256]{2,1,0:T(8,128)S(1)} %constant_dynamic-update-slice_fusion) | copy-start | bytes 5505028
  72.5 5.0 %copy-start.10 = (f32[14,128,256]{2,1,0:T(8,128)}, f32[14,128,256]{2,1,0:T(8,128)S(1)}, u32[]{:S(2)}) copy-start(f32[14,128,256]{2,1,0:T(8,128)S(1)} %get-tuple-element.12) | copy-start | bytes 5505028
  81.3 6.9 %collective-permute-start.7 = (f32[4,64,128]{2,1,0:T(8,128)S(1)}, f32[4,64,128]{2,1,0:T(8,128)S(1)}, u32[]{:S(2)}, u32[]{:S(2)}) collective-permute-start(f32[4,64,128]{2,1,0:T(8,128)S(1)} %convolution_multiply_fusion.1), channel_id=1, source_target_pairs={{1,0},{2,1},{3,2},{4,3},{5,4},{6,5},{7,6},{8,7},{9,8},{10,9},{11,1... | collective-permute-start | bytes 393224 | tf_op jit(solution)/shard_map/ppermute | solution.py:71
  82.6 7.1 %collective-permute-start.6 = (f32[4,64,128]{2,1,0:T(8,128)S(1)}, f32[4,64,128]{2,1,0:T(8,128)S(1)}, u32[]{:S(2)}, u32[]{:S(2)}) collective-permute-start(f32[4,64,128]{2,1,0:T(8,128)S(1)} %convolution_multiply_fusion.1), channel_id=1, source_target_pairs={{0,1},{1,2},{2,3},{3,4},{4,5},{5,6},{6,7},{7,8},{8,9},{9,10},{10,1... | collective-permute-start | bytes 393224 | tf_op jit(solution)/shard_map/ppermute | solution.py:71
  93.5 53.8 %all-to-all-start = ((f32[64,64,128]{2,1,0:T(8,128)}), f32[64,64,128]{2,1,0:T(8,128)}, u32[]{:S(2)}, u32[]{:S(2)}) async-start(f32[64,64,128]{2,1,0:T(8,128)} %broadcast_in_dim.318), calls=%async_computation | async-start | bytes 4194304 | tf_op jit(solution)/shard_map/all_to_all | solution.py:78
  163.7 7.7 %copy-start.45 = (f32[16,32,1]{1,0,2:T(8,128)S(1)}, f32[16,32,1]{1,0,2:T(8,128)}, u32[]{:S(2)}) copy-start(f32[16,32,1]{1,0,2:T(8,128)} %constant.377) | copy-start | bytes 6148
  166.6 6.1 %copy-start.7 = (f32[128,32,64]{2,1,0:T(8,128)S(1)}, f32[128,32,64]{2,1,0:T(8,128)}, u32[]{:S(2)}) copy-start(f32[128,32,64]{2,1,0:T(8,128)} %reshape.234) | copy-start | bytes 3145732
  166.6 6.1 %copy-start.28 = (f32[26,32,64]{2,1,0:T(8,128)S(1)}, f32[26,32,64]{2,1,0:T(8,128)}, u32[]{:S(2)}) copy-start(f32[26,32,64]{2,1,0:T(8,128)} %copy-done.27) | copy-start | bytes 638980
  166.6 6.1 %copy-start.49 = (pred[8]{0:T(512)(128)(4,1)S(1)}, pred[8]{0:T(512)(128)(4,1)}, u32[]{:S(2)}) copy-start(pred[8]{0:T(512)(128)(4,1)} %compare_and_fusion.6) | copy-start | bytes 28
  (38 other events, 68.4 us)

commit v2 on v0

--- a/solution.py
+++ b/solution.py
@@ -71,12 +71,10 @@
     return lax.ppermute(block, "slab", pairs)
 
 
-def gather_slabs(block):
-    count = lax.axis_size("slab")
-    flat = block.reshape(block.size // 128, 128)
-    spread = jnp.broadcast_to(flat[None], (count,) + flat.shape)
-    got = lax.all_to_all(spread, "slab", 0, 0, tiled=False)
-    return got.reshape((count * block.shape[0],) + block.shape[1:])
+def gather_window(block):
+    got = jnp.concatenate([shift_from(block[None], 1), block[None], shift_from(block[None], -1)])
+    got = jnp.concatenate([shift_from(got[:2], 2), got, shift_from(got[1:], -2)])
+    return jnp.concatenate([shift_from(got[:4], 4), got, shift_from(got[3:], -4)])
 
 
 def plane_mask(first_global, planes, total):
@@ -192,7 +190,6 @@
     k1_halo = k0_halo // 2
     own1 = fz // 2
     k2_own = 0.125 * restrict_sum(k1[k1_halo:k1_halo + own1])
-    k2 = lax.all_gather(k2_own, "slab", axis=0, tiled=True)
 
     h0k = F0_HALO + 1
     lvl0 = Level(k0[k0_halo - h0k: k0_halo + fz + h0k], h0k, fz, s * fz - h0k, fine_total)
@@ -210,15 +207,15 @@
     v = lvl1.start(f1, F1_HALO)
     v1 = lvl1.sweep(v, lvl1.cut(f1, F1_HALO - 1, F1_HALO), F1_HALO)
     res1 = f1_own - lvl1.operate(v1[2:-2], 1)
-    f2 = gather_slabs(0.5 * restrict_sum(res1))
+    both = gather_window(jnp.stack([0.5 * restrict_sum(res1), k2_own]))
 
     own2 = own1 // 2
     total2 = fine_total // 4
     k2_halo = 13
     f2_halo = k2_halo - 1
-    pad2 = ((k2_halo, k2_halo), (0, 0), (0, 0))
-    k2w = lax.dynamic_slice_in_dim(jnp.pad(k2, pad2), s * own2, own2 + 2 * k2_halo, axis=0)
-    f2w = lax.dynamic_slice_in_dim(jnp.pad(f2, pad2), s * own2 + 1, own2 + 2 * f2_halo, axis=0)
+    reach = (both.shape[0] // 2) * own2
+    f2w = both[:, 0].reshape((-1,) + both.shape[3:])[reach - f2_halo: reach + own2 + f2_halo]
+    k2w = both[:, 1].reshape((-1,) + both.shape[3:])[reach - k2_halo: reach + own2 + k2_halo]
     lvl2 = Level(k2w, k2_halo, own2, s * own2 - k2_halo, total2)
     w = lvl2.start(f2w, f2_halo)
     w1 = lvl2.sweep(w, lvl2.cut(f2w, f2_halo - 1, f2_halo), f2_halo)

time: 191 us -> 180 us (0.942)
  starting transfers between devices: 47.6 us -> 66 us
  between operations: 16.6 us -> 3.5 us
  local copies, waits for them, and re-layouts: 30.6 us -> 19.3 us
  waiting for transfers between devices: 23 us -> 20.8 us
    ppermute x8 -> x14, starting transfers between devices: 31 us -> 66 us  [shift_from(): return lax.ppermute(block, 'slab', pairs)]
    all_to_all x1 -> x0, starting transfers between devices: 16.6 us -> none  [gather_slabs(): got = lax.all_to_all(spread, 'slab', 0, 0, tiled=False)]
    ppermute x8 -> x14, waiting for transfers between devices: 6.83 us -> 20.8 us  [shift_from(): return lax.ppermute(block, 'slab', pairs)]
    all_to_all x1 -> x0, waiting for transfers between devices: 8.21 us -> none  [gather_slabs(): got = lax.all_to_all(spread, 'slab', 0, 0, tiled=False)]
    all_gather x1 -> x0, waiting for transfers between devices: 7.93 us -> none  [on_device(): k2 = lax.all_gather(k2_own, 'slab', axis=0, tiled=True)]
    unnamed x118 -> x131, local copies, waits for them, and re-layouts: 15.7 us -> 9.29 us
    and x17, other arithmetic: 6.62 us -> 8.96 us  [plane_mask(): return ((g >= 0) & (g < total))[:, None, None]]
    select_n x11, other arithmetic: 13.1 us -> 10.9 us  [mask(): jnp.where(plane_mask(self.first + self.halo - h, u.shape[0], self.total),...]
  transfers between devices with their start and end apart: 10 -> 14, of which waited for: 4 -> 7; matrix products, arithmetic and copies ran while one was open for 31% -> 25% of each run, Pallas kernels for 0% -> 0%
where the time goes in v2:
time: 180 us; the launch traced here: 178 us
  starting transfers between devices  66 us (37%)
  other arithmetic  43.7 us (24%)
  matrix products  23 us (13%)
  waiting for transfers between devices  20.8 us (12%)
  local copies, waits for them, and re-layouts  19.3 us (11%)
  between operations  3.5 us (2%)
  blocking collectives  2.18 us (1%)
    ppermute x14, starting transfers between devices, shift_from(): return lax.ppermute(block, 'slab', pairs)  66 us
    ppermute x14, waiting for transfers between devices, shift_from(): return lax.ppermute(block, 'slab', pairs)  20.8 us
    select_n x11, other arithmetic, mask(): jnp.where(plane_mask(self.first + self.halo - h, u.shape[0], self.total),...  10.9 us
    dot_general x10, matrix products, along_y(): jnp.einsum('zyx,yv->zvx', values, jnp.asarray(matrix), precision=precisio...  10.4 us
    unnamed x131, local copies, waits for them, and re-layouts  9.29 us
    and x17, other arithmetic, plane_mask(): return ((g >= 0) & (g < total))[:, None, None]  8.96 us
    reduce_sum x6, other arithmetic, restrict_sum(): values = values.reshape(nz // 2, 2, ny, nx).sum(axis=1)  7.7 us
    dot_general x1, matrix products, on_device(): jnp.dot(along_rows.reshape(k0_planes * fy, MX), cols_table, precision=HI)  5.78 us
  transfers between devices with their start and end apart: 14, of which 7 were waited for; matrix products, arithmetic and copies ran while one was open for 25% of the time, Pallas kernels for 0%

profile of v2, /device:TPU:24, one launch (start us, length us, event | category | flops | bytes accessed | tf_op | source)
XLA Modules:
  0.0 178.5 jit_solution(13736307521427045772)
XLA Ops:
  4.1 2.2 %all_gather.3 = bf16[8,4,64,128]{3,2,1,0:T(8,128)(2,1)S(1)} all-gather(bf16[4,4,64,128]{3,2,1,0:T(8,128)(2,1)S(1)} %gather_fusion), channel_id=1, replica_groups=mesh['chain'=2,'slab'=64] {'chain'}, dimensions={0}, use_global_device_ids=true | all-gather | bytes 786432 | tf_op jit(solution)/shard_map/all_gather | solution.py:147
  7.0 4.8 %collective-permute-start.4 = (bf16[4,64,128]{2,1,0:T(8,128)(2,1)S(1)}, bf16[4,64,128]{2,1,0:T(8,128)(2,1)S(1)}, u32[]{:S(2)}, u32[]{:S(2)}) collective-permute-start(bf16[4,64,128]{2,1,0:T(8,128)(2,1)S(1)} %dynamic-slice_bitcast_fusion), channel_id=1, source_target_pairs={{1,0},{2,1},{3,2},{4,3},{5,4},{6,5},{7,6},{8,7},{9,8},{10,9},{11,1... | collective-permute-start | bytes 196616 | tf_op jit(solution)/shard_map/ppermute | solution.py:71
  11.9 1.9 %collective-permute-start.3 = (bf16[4,64,128]{2,1,0:T(8,128)(2,1)S(1)}, bf16[4,64,128]{2,1,0:T(8,128)(2,1)S(1)}, u32[]{:S(2)}, u32[]{:S(2)}) collective-permute-start(bf16[4,64,128]{2,1,0:T(8,128)(2,1)S(1)} %dynamic-slice_bitcast_fusion), channel_id=1, source_target_pairs={{0,1},{1,2},{2,3},{3,4},{4,5},{5,6},{6,7},{7,8},{8,9},{9,10},{10,1... | collective-permute-start | bytes 196616 | tf_op jit(solution)/shard_map/ppermute | solution.py:71
  13.8 4.2 %collective-permute-start.5 = (bf16[2,64,128]{2,1,0:T(8,128)(2,1)S(1)}, bf16[2,64,128]{2,1,0:T(8,128)(2,1)S(1)}, u32[]{:S(2)}, u32[]{:S(2)}) collective-permute-start(bf16[2,64,128]{2,1,0:T(8,128)(2,1)S(1)} %get-tuple-element.20), channel_id=1, source_target_pairs={{2,0},{3,1},{4,2},{5,3},{6,4},{7,5},{8,6},{9,7},{10,8},{11,9},{12,... | collective-permute-start | bytes 98312 | tf_op jit(solution)/shard_map/ppermute | solution.py:71
  18.0 3.3 %collective-permute-start.2 = (bf16[2,64,128]{2,1,0:T(8,128)(2,1)S(1)}, bf16[2,64,128]{2,1,0:T(8,128)(2,1)S(1)}, u32[]{:S(2)}, u32[]{:S(2)}) collective-permute-start(bf16[2,64,128]{2,1,0:T(8,128)(2,1)S(1)} %get-tuple-element.21), channel_id=1, source_target_pairs={{0,2},{1,3},{2,4},{3,5},{4,6},{5,7},{6,8},{7,9},{8,10},{9,11},{10,... | collective-permute-start | bytes 98312 | tf_op jit(solution)/shard_map/ppermute | solution.py:71
  22.3 6.9 %collective-permute-start.1 = (f32[3,128,256]{2,1,0:T(8,128)}, f32[3,128,256]{2,1,0:T(8,128)S(1)}, u32[]{:S(2)}, u32[]{:S(2)}) collective-permute-start(f32[3,128,256]{2,1,0:T(8,128)} %get-tuple-element.15), channel_id=1, source_target_pairs={{1,0},{2,1},{3,2},{4,3},{5,4},{6,5},{7,6},{8,7},{9,8},{10,9},{11,1... | collective-permute-start | bytes 1179656 | tf_op jit(solution)/shard_map/ppermute | solution.py:71
  41.1 3.4 %convolution_bitcast_fusion = f32[16,128,256]{1,2,0:T(8,128)S(1)} fusion(f32[16,64,256]{2,1,0:T(8,128)S(1)} %fusion.125, f32[64,128,1]{1,0,2:T(8,128)S(1)} %copy-done.41), kind=kOutput, calls=%fused_computation.33 | convolution fusion | flops 402653184 | bytes 3178496 | tf_op jit(solution)/shard_map/zyx,yv->zvx/dot_general | solution.py:50
  45.0 2.2 %pad_maximum_fusion = f32[14,2,128,256]{2,3,0,1:T(8,128)} fusion(f32[14,1,128,256]{2,3,0,1:T(8,128)S(1)} %get-tuple-element.14, f32[14,1,128,256]{2,3,0,1:T(8,128)S(1)} %get-tuple-element.13), kind=kLoop, calls=%fused_computation.1 | loop fusion | flops 917504 | bytes 7340032 | tf_op jit(solution)/shard_map/stack | solution.py:173
  47.2 5.1 %copy.29 = f32[14,2,128,256]{3,2,1,0:T(8,128)} copy(f32[14,2,128,256]{2,3,0,1:T(8,128)} %pad_maximum_fusion) | data formatting | bytes 7340032 | tf_op jit(solution)/shard_map/stack | solution.py:173
  52.3 5.8 %fusion.1 = f32[28,128,256]{2,1,0:T(8,128)S(1)} fusion(f32[14,2,128,256]{3,2,1,0:T(8,128)} %copy.29, f32[28,128,64]{1,2,0:T(8,128)S(1)} %convolution_bitcast_fusion.2, pred[28]{0:T(512)(128)(4,1)S(1)} %compare_and_fusion.12, s32[256]{0:T(256)S(1)} %multiply_add_fusion, s32[64]{0:T(128)S(1)} %iota_add_fusion), kind=kOutput, calls=%fused_computation.4 | convolution fusion | flops 706707456 | bytes 8258844 | tf_op jit(solution)/shard_map/dot_general | solution.py:183
  59.9 4.4 %reduce_sum.55 = f32[14,128,256]{2,1,0:T(8,128)} reduce(f32[14,2,128,256]{3,2,1,0:T(8,128)} %bitcast.140, f32[]{:T(128)} %constant.127.clone.1), dimensions={1}, to_apply=%region_2.3 | reduce | flops 458752 | bytes 5505028 | tf_op jit(solution)/shard_map/reduce_sum | solution.py:56
  64.3 2.8 %convolution_bitcast_fusion.1 = f32[14,64,256]{2,1,0:T(8,128)S(1)} fusion(f32[14,128,256]{2,1,0:T(8,128)} %reduce_sum.55, f32[128,64,1]{0,1,2:T(8,128)S(1)} %copy-done.33), kind=kOutput, calls=%fused_computation.56 | convolution fusion | flops 352321536 | bytes 2785280 | tf_op jit(solution)/shard_map/zyx,yv->zvx/dot_general | solution.py:50
  69.3 3.1 %add_multiply_fusion = f32[14,129,256]{2,1,0:T(8,128)S(1)} fusion(f32[14,128,256]{2,1,0:T(8,128)} %copy-done.13), kind=kLoop, calls=%fused_computation.15 | loop fusion | flops 924672 | bytes 3684352 | tf_op jit(solution)/shard_map/mul | solution.py:94
  75.8 2.4 %fusion.23 = f32[12,128,256]{2,1,0:T(8,128)S(1)} fusion(f32[12,128,256]{2,1,0:T(8,128)S(1)} %slice.1330, f32[14,128,257]{2,1,0:T(8,128)S(1)} %fusion.3, f32[14,129,256]{2,1,0:T(8,128)S(1)} %add_multiply_fusion, f32[14,128,256]{2,1,0:T(8,128)S(1)} %get-tuple-element.11, f32[15,128,256]{2,1,0:T(8,128)S(1)} %fusion.4, ...), kind=kLoop, calls=%fused_computation.53 | loop fusion | flops 7077888 | bytes 18874380 | tf_op jit(solution)/shard_map/jit(_where)/select_n | solution.py:112
  80.5 6.0 %collective-permute-start.7 = (f32[4,64,128]{2,1,0:T(8,128)S(1)}, f32[4,64,128]{2,1,0:T(8,128)S(1)}, u32[]{:S(2)}, u32[]{:S(2)}) collective-permute-start(f32[4,64,128]{2,1,0:T(8,128)S(1)} %convolution_multiply_fusion.1), channel_id=1, source_target_pairs={{1,0},{2,1},{3,2},{4,3},{5,4},{6,5},{7,6},{8,7},{9,8},{10,9},{11,1... | collective-permute-start | bytes 393224 | tf_op jit(solution)/shard_map/ppermute | solution.py:71
  89.0 6.5 %collective-permute-done.6 = f32[4,64,128]{2,1,0:T(8,128)S(1)} collective-permute-done((f32[4,64,128]{2,1,0:T(8,128)S(1)}, f32[4,64,128]{2,1,0:T(8,128)S(1)}, u32[]{:S(2)}, u32[]{:S(2)}) %collective-permute-start.6) | collective-permute-done | bytes 131104 | tf_op jit(solution)/shard_map/ppermute | solution.py:71
  99.6 3.9 %collective-permute-start.8 = (f32[1,2,2,32,64]{4,3,2,1,0:T(8,128)S(1)}, f32[1,2,2,32,64]{4,3,2,1,0:T(8,128)S(1)}, u32[]{:S(2)}, u32[]{:S(2)}) collective-permute-start(f32[1,2,2,32,64]{4,3,2,1,0:T(8,128)S(1)} %maximum_bitcast_fusion), channel_id=1, source_target_pairs={{0,1},{1,2},{2,3},{3,4},{4,5},{5,6},{6,7},{7,8},{8,9},{9,10},{10,1... | collective-permute-start | bytes 98312 | tf_op jit(solution)/shard_map/ppermute | solution.py:71
  104.1 3.7 %collective-permute-done.8 = f32[1,2,2,32,64]{4,3,2,1,0:T(8,128)S(1)} collective-permute-done((f32[1,2,2,32,64]{4,3,2,1,0:T(8,128)S(1)}, f32[1,2,2,32,64]{4,3,2,1,0:T(8,128)S(1)}, u32[]{:S(2)}, u32[]{:S(2)}) %collective-permute-start.8) | collective-permute-done | bytes 32800 | tf_op jit(solution)/shard_map/ppermute | solution.py:71
  109.8 7.3 %collective-permute-start.9 = (f32[2,2,2,32,64]{4,3,2,1,0:T(8,128)S(1)}, f32[2,2,2,32,64]{4,3,2,1,0:T(8,128)S(1)}, u32[]{:S(2)}, u32[]{:S(2)}) collective-permute-start(f32[2,2,2,32,64]{4,3,2,1,0:T(8,128)S(1)} %get-tuple-element.29), channel_id=1, source_target_pairs={{0,2},{1,3},{2,4},{3,5},{4,6},{5,7},{6,8},{7,9},{8,10},{9,11},{10,... | collective-permute-start | bytes 196616 | tf_op jit(solution)/shard_map/ppermute | solution.py:71
  119.7 18.0 %collective-permute-start.10 = (f32[4,2,2,32,64]{4,3,2,1,0:T(8,128)S(1)}, f32[4,2,2,32,64]{4,3,2,1,0:T(8,128)S(1)}, u32[]{:S(2)}, u32[]{:S(2)}) collective-permute-start(f32[4,2,2,32,64]{4,3,2,1,0:T(8,128)S(1)} %get-tuple-element.27), channel_id=1, source_target_pairs={{0,4},{1,5},{2,6},{3,7},{4,8},{5,9},{6,10},{7,11},{8,12},{9,13},{1... | collective-permute-start | bytes 393224 | tf_op jit(solution)/shard_map/ppermute | solution.py:71
  141.7 7.6 %collective-permute-done.13 = f32[4,2,2,32,64]{4,3,2,1,0:T(8,128)S(1)} collective-permute-done((f32[4,2,2,32,64]{4,3,2,1,0:T(8,128)S(1)}, f32[4,2,2,32,64]{4,3,2,1,0:T(8,128)S(1)}, u32[]{:S(2)}, u32[]{:S(2)}) %collective-permute-start.13) | collective-permute-done | bytes 131104 | tf_op jit(solution)/shard_map/ppermute | solution.py:71
  168.1 2.0 %bitcast_add_fusion.1 = f32[12,128,256]{2,1,0:T(8,128)S(1)} fusion(f32[12,128,256]{2,1,0:T(8,128)} %copy-done.10, f32[6,128,256]{2,1,0:T(8,128)} %copy.32), kind=kLoop, calls=%fused_computation.52 | loop fusion | flops 393216 | bytes 3932160 | tf_op jit(solution)/shard_map/add | solution.py:244
  171.9 3.1 %fusion.38 = f32[10,128,256]{2,1,0:T(8,128)S(1)} fusion(f32[10,128,256]{2,1,0:T(8,128)S(1)} %slice.1502, f32[14,128,257]{2,1,0:T(8,128)S(1)} %copy-done.5, f32[14,129,256]{2,1,0:T(8,128)S(1)} %add_multiply_fusion, f32[12,128,256]{2,1,0:T(8,128)S(1)} %bitcast_add_fusion.1, f32[15,128,256]{2,1,0:T(8,128)S(1)} %copy-done.3, f32[14,128,256]{2,1,0:T(8,128)S(1)} %copy-done.9, ...), kind=kLoop, calls=%fused_computation.74 | loop fusion | flops 5898240 | bytes 15728650 | tf_op jit(solution)/shard_map/jit(_where)/select_n | solution.py:112
  176.3 2.2 %select_bitcast_fusion = f32[1,8,128,256]{3,2,1,0:T(8,128)} fusion(f32[8,128,256]{2,1,0:T(8,128)S(1)} %slice.1513, f32[8,128,256]{2,1,0:T(8,128)S(1)} %copy-done.18, f32[10,128,256]{2,1,0:T(8,128)S(1)} %fusion.38, f32[14,128,257]{2,1,0:T(8,128)S(1)} %copy-done.5, f32[14,129,256]{2,1,0:T(8,128)S(1)} %add_multiply_fusion, f32[15,128,256]{2,1,0:T(8,128)S(1)} %copy-done.3, ...), kind=kLoop, calls=%fused_computation.124 | loop fusion | flops 4718592 | bytes 12582920 | tf_op jit(solution)/shard_map/broadcast_in_dim | solution.py:247
  (260 shorter events, 62.0 us)
Async XLA Ops:
  0.0 21.3 %copy-start.16 = (f32[8,128,256]{2,1,0:T(8,128)S(1)}, f32[8,128,256]{2,1,0:T(8,128)}, u32[]{:S(2)}) copy-start(f32[8,128,256]{2,1,0:T(8,128)} %param.29) | copy-start | bytes 3145732
  0.0 35.9 %copy-start.38 = (f32[1,32,16,64]{3,2,1,0:T(8,128)S(1)}, f32[1,32,16,64]{3,2,1,0:T(8,128)}, u32[]{:S(2)}) copy-start(f32[1,32,16,64]{3,2,1,0:T(8,128)} %param.28) | copy-start | bytes 393220
  7.0 33.7 %collective-permute-start.4 = (bf16[4,64,128]{2,1,0:T(8,128)(2,1)S(1)}, bf16[4,64,128]{2,1,0:T(8,128)(2,1)S(1)}, u32[]{:S(2)}, u32[]{:S(2)}) collective-permute-start(bf16[4,64,128]{2,1,0:T(8,128)(2,1)S(1)} %dynamic-slice_bitcast_fusion), channel_id=1, source_target_pairs={{1,0},{2,1},{3,2},{4,3},{5,4},{6,5},{7,6},{8,7},{9,8},{10,9},{11,1... | collective-permute-start | bytes 196616 | tf_op jit(solution)/shard_map/ppermute | solution.py:71
  11.9 28.8 %collective-permute-start.3 = (bf16[4,64,128]{2,1,0:T(8,128)(2,1)S(1)}, bf16[4,64,128]{2,1,0:T(8,128)(2,1)S(1)}, u32[]{:S(2)}, u32[]{:S(2)}) collective-permute-start(bf16[4,64,128]{2,1,0:T(8,128)(2,1)S(1)} %dynamic-slice_bitcast_fusion), channel_id=1, source_target_pairs={{0,1},{1,2},{2,3},{3,4},{4,5},{5,6},{6,7},{7,8},{8,9},{9,10},{10,1... | collective-permute-start | bytes 196616 | tf_op jit(solution)/shard_map/ppermute | solution.py:71
  13.8 26.9 %collective-permute-start.5 = (bf16[2,64,128]{2,1,0:T(8,128)(2,1)S(1)}, bf16[2,64,128]{2,1,0:T(8,128)(2,1)S(1)}, u32[]{:S(2)}, u32[]{:S(2)}) collective-permute-start(bf16[2,64,128]{2,1,0:T(8,128)(2,1)S(1)} %get-tuple-element.20), channel_id=1, source_target_pairs={{2,0},{3,1},{4,2},{5,3},{6,4},{7,5},{8,6},{9,7},{10,8},{11,9},{12,... | collective-permute-start | bytes 98312 | tf_op jit(solution)/shard_map/ppermute | solution.py:71
  18.0 22.8 %copy-start.40 = (bf16[128,256,1]{1,0,2:T(8,128)(2,1)S(1)}, bf16[128,256,1]{1,0,2:T(8,128)(2,1)}, u32[]{:S(2)}) copy-start(bf16[128,256,1]{1,0,2:T(8,128)(2,1)} %constant.362) | copy-start | bytes 196612
  18.0 20.7 %collective-permute-start.2 = (bf16[2,64,128]{2,1,0:T(8,128)(2,1)S(1)}, bf16[2,64,128]{2,1,0:T(8,128)(2,1)S(1)}, u32[]{:S(2)}, u32[]{:S(2)}) collective-permute-start(bf16[2,64,128]{2,1,0:T(8,128)(2,1)S(1)} %get-tuple-element.21), channel_id=1, source_target_pairs={{0,2},{1,3},{2,4},{3,5},{4,6},{5,7},{6,8},{7,9},{8,10},{9,11},{10,... | collective-permute-start | bytes 98312 | tf_op jit(solution)/shard_map/ppermute | solution.py:71
  22.3 51.7 %collective-permute-start.1 = (f32[3,128,256]{2,1,0:T(8,128)}, f32[3,128,256]{2,1,0:T(8,128)S(1)}, u32[]{:S(2)}, u32[]{:S(2)}) collective-permute-start(f32[3,128,256]{2,1,0:T(8,128)} %get-tuple-element.15), channel_id=1, source_target_pairs={{1,0},{2,1},{3,2},{4,3},{5,4},{6,5},{7,6},{8,7},{9,8},{10,9},{11,1... | collective-permute-start | bytes 1179656 | tf_op jit(solution)/shard_map/ppermute | solution.py:71
  38.7 34.0 %collective-permute-start = (f32[3,128,256]{2,1,0:T(8,128)}, f32[3,128,256]{2,1,0:T(8,128)}, u32[]{:S(2)}, u32[]{:S(2)}) collective-permute-start(f32[3,128,256]{2,1,0:T(8,128)} %get-tuple-element.16), channel_id=1, source_target_pairs={{0,1},{1,2},{2,3},{3,4},{4,5},{5,6},{6,7},{7,8},{8,9},{9,10},{10,1... | collective-permute-start | bytes 1179656 | tf_op jit(solution)/shard_map/ppermute | solution.py:71
  59.9 8.4 %copy-start.13 = (f32[14,128,256]{2,1,0:T(8,128)}, f32[14,128,256]{2,1,0:T(8,128)S(1)}, u32[]{:S(2)}) copy-start(f32[14,128,256]{2,1,0:T(8,128)S(1)} %slice.1325) | copy-start | bytes 5505028
  68.1 28.4 %copy-start.11 = (f32[13,64,128]{2,1,0:T(8,128)}, f32[13,64,128]{2,1,0:T(8,128)S(1)}, u32[]{:S(2)}) copy-start(f32[13,64,128]{2,1,0:T(8,128)S(1)} %fusion.71) | copy-start | bytes 1277956
  68.3 10.1 %copy-start.2 = (f32[15,128,256]{2,1,0:T(8,128)}, f32[15,128,256]{2,1,0:T(8,128)S(1)}, u32[]{:S(2)}) copy-start(f32[15,128,256]{2,1,0:T(8,128)S(1)} %fusion.4) | copy-start | bytes 5898244
  69.1 9.3 %copy-start.4 = (f32[14,128,257]{2,1,0:T(8,128)}, f32[14,128,257]{2,1,0:T(8,128)S(1)}, u32[]{:S(2)}) copy-start(f32[14,128,257]{2,1,0:T(8,128)S(1)} %fusion.3) | copy-start | bytes 5526532
  72.7 23.9 %copy-start.14 = (f32[12,65,128]{2,1,0:T(8,128)}, f32[12,65,128]{2,1,0:T(8,128)S(1)}, u32[]{:S(2)}) copy-start(f32[12,65,128]{2,1,0:T(8,128)S(1)} %add_multiply_fusion.1) | copy-start | bytes 1198084
  79.6 15.8 %copy-start.53 = (pred[12]{0:T(512)(128)(4,1)S(1)}, pred[12]{0:T(512)(128)(4,1)}, u32[]{:S(2)}) copy-start(pred[12]{0:T(512)(128)(4,1)} %compare_and_fusion.8) | copy-start | bytes 40
  80.5 8.5 %collective-permute-start.7 = (f32[4,64,128]{2,1,0:T(8,128)S(1)}, f32[4,64,128]{2,1,0:T(8,128)S(1)}, u32[]{:S(2)}, u32[]{:S(2)}) collective-permute-start(f32[4,64,128]{2,1,0:T(8,128)S(1)} %convolution_multiply_fusion.1), channel_id=1, source_target_pairs={{1,0},{2,1},{3,2},{4,3},{5,4},{6,5},{7,6},{8,7},{9,8},{10,9},{11,1... | collective-permute-start | bytes 393224 | tf_op jit(solution)/shard_map/ppermute | solution.py:71
  86.5 9.0 %collective-permute-start.6 = (f32[4,64,128]{2,1,0:T(8,128)S(1)}, f32[4,64,128]{2,1,0:T(8,128)S(1)}, u32[]{:S(2)}, u32[]{:S(2)}) collective-permute-start(f32[4,64,128]{2,1,0:T(8,128)S(1)} %convolution_multiply_fusion.1), channel_id=1, source_target_pairs={{0,1},{1,2},{2,3},{3,4},{4,5},{5,6},{6,7},{7,8},{8,9},{9,10},{10,1... | collective-permute-start | bytes 393224 | tf_op jit(solution)/shard_map/ppermute | solution.py:71
  88.7 7.9 %copy-start.20 = (f32[12,64,129]{2,1,0:T(8,128)}, f32[12,64,129]{2,1,0:T(8,128)S(1)}, u32[]{:S(2)}) copy-start(f32[12,64,129]{2,1,0:T(8,128)S(1)} %fusion.67) | copy-start | bytes 1188868
  97.6 6.5 %collective-permute-start.11 = (f32[1,2,2,32,64]{4,3,2,1,0:T(8,128)S(1)}, f32[1,2,2,32,64]{4,3,2,1,0:T(8,128)S(1)}, u32[]{:S(2)}, u32[]{:S(2)}) collective-permute-start(f32[1,2,2,32,64]{4,3,2,1,0:T(8,128)S(1)} %maximum_bitcast_fusion), channel_id=1, source_target_pairs={{1,0},{2,1},{3,2},{4,3},{5,4},{6,5},{7,6},{8,7},{9,8},{10,9},{11,1... | collective-permute-start | bytes 98312 | tf_op jit(solution)/shard_map/ppermute | solution.py:71
  99.6 8.3 %collective-permute-start.8 = (f32[1,2,2,32,64]{4,3,2,1,0:T(8,128)S(1)}, f32[1,2,2,32,64]{4,3,2,1,0:T(8,128)S(1)}, u32[]{:S(2)}, u32[]{:S(2)}) collective-permute-start(f32[1,2,2,32,64]{4,3,2,1,0:T(8,128)S(1)} %maximum_bitcast_fusion), channel_id=1, source_target_pairs={{0,1},{1,2},{2,3},{3,4},{4,5},{5,6},{6,7},{7,8},{8,9},{9,10},{10,1... | collective-permute-start | bytes 98312 | tf_op jit(solution)/shard_map/ppermute | solution.py:71
  107.9 10.3 %collective-permute-start.12 = (f32[2,2,2,32,64]{4,3,2,1,0:T(8,128)S(1)}, f32[2,2,2,32,64]{4,3,2,1,0:T(8,128)S(1)}, u32[]{:S(2)}, u32[]{:S(2)}) collective-permute-start(f32[2,2,2,32,64]{4,3,2,1,0:T(8,128)S(1)} %get-tuple-element.28), channel_id=1, source_target_pairs={{2,0},{3,1},{4,2},{5,3},{6,4},{7,5},{8,6},{9,7},{10,8},{11,9},{12,... | collective-permute-start | bytes 196616 | tf_op jit(solution)/shard_map/ppermute | solution.py:71
  109.8 9.8 %collective-permute-start.9 = (f32[2,2,2,32,64]{4,3,2,1,0:T(8,128)S(1)}, f32[2,2,2,32,64]{4,3,2,1,0:T(8,128)S(1)}, u32[]{:S(2)}, u32[]{:S(2)}) collective-permute-start(f32[2,2,2,32,64]{4,3,2,1,0:T(8,128)S(1)} %get-tuple-element.29), channel_id=1, source_target_pairs={{0,2},{1,3},{2,4},{3,5},{4,6},{5,7},{6,8},{7,9},{8,10},{9,11},{10,... | collective-permute-start | bytes 196616 | tf_op jit(solution)/shard_map/ppermute | solution.py:71
  119.7 21.9 %collective-permute-start.10 = (f32[4,2,2,32,64]{4,3,2,1,0:T(8,128)S(1)}, f32[4,2,2,32,64]{4,3,2,1,0:T(8,128)S(1)}, u32[]{:S(2)}, u32[]{:S(2)}) collective-permute-start(f32[4,2,2,32,64]{4,3,2,1,0:T(8,128)S(1)} %get-tuple-element.27), channel_id=1, source_target_pairs={{0,4},{1,5},{2,6},{3,7},{4,8},{5,9},{6,10},{7,11},{8,12},{9,13},{1... | collective-permute-start | bytes 393224 | tf_op jit(solution)/shard_map/ppermute | solution.py:71
  138.9 10.4 %collective-permute-start.13 = (f32[4,2,2,32,64]{4,3,2,1,0:T(8,128)S(1)}, f32[4,2,2,32,64]{4,3,2,1,0:T(8,128)S(1)}, u32[]{:S(2)}, u32[]{:S(2)}) collective-permute-start(f32[4,2,2,32,64]{4,3,2,1,0:T(8,128)S(1)} %get-tuple-element.26), channel_id=1, source_target_pairs={{4,0},{5,1},{6,2},{7,3},{8,4},{9,5},{10,6},{11,7},{12,8},{13,9},{1... | collective-permute-start | bytes 393224 | tf_op jit(solution)/shard_map/ppermute | solution.py:71
  (50 other events, 116.1 us)

commit v3 on v2

--- a/solution.py
+++ b/solution.py
@@ -97,7 +97,13 @@
         self.fzl = faces_z[:-1]
         self.fzu = faces_z[1:]
         diag = self.fzl + self.fzu + self.fy[:, 1:] + self.fy[:, :-1]
-        self.diag = diag + self.fx[:, :, 1:] + self.fx[:, :, :-1]
+        diag = diag + self.fx[:, :, 1:] + self.fx[:, :, :-1]
+        inside = plane_mask(self.first, kc.shape[0], total)
+        self.fzl = jnp.where(inside, self.fzl, 0.0)
+        self.fzu = jnp.where(inside, self.fzu, 0.0)
+        self.fy = jnp.where(inside, self.fy, 0.0)
+        self.fx = jnp.where(inside, self.fx, 0.0)
+        self.diag = jnp.where(inside, diag, 1.0)
 
     def cut(self, arr, h, have):
         n = self.own + 2 * h
@@ -107,9 +113,6 @@
         c = self.cut
         H = self.halo
         return c(self.fzl, h, H), c(self.fzu, h, H), c(self.fy, h, H), c(self.fx, h, H), c(self.diag, h, H)
-
-    def mask(self, u, h):
-        return jnp.where(plane_mask(self.first + self.halo - h, u.shape[0], self.total), u, 0.0)
 
     def operate(self, u, h):
         fzl, fzu, fy, fx, diag = self.coef(h - 1)
@@ -123,11 +126,10 @@
 
     def sweep(self, u, f, h):
         diag = self.coef(h - 1)[4]
-        new = u[1:-1] + OMEGA * (f - self.operate(u, h)) / diag
-        return self.mask(new, h - 1)
+        return u[1:-1] + OMEGA * (f - self.operate(u, h)) / diag
 
     def start(self, f, h):
-        return self.mask(OMEGA * f / self.coef(h)[4], h)
+        return OMEGA * f / self.coef(h)[4]
 
 
 def mode_table(mode_count, length, positions):

time: 180 us -> 190 us (1.056)
  local copies, waits for them, and re-layouts: 19.3 us -> 26.5 us
    add x1 -> x9, other arithmetic: 0.15 us -> 10.9 us  [sweep(): return u[1:-1] + OMEGA * (f - self.operate(u, h)) / diag]
    and x17 -> x5, other arithmetic: 8.96 us -> 0.04 us  [plane_mask(): return ((g >= 0) & (g < total))[:, None, None]]
    unnamed x131 -> x133, local copies, waits for them, and re-layouts: 9.29 us -> 15.3 us
    mul x8 -> x0, other arithmetic: 5.26 us -> none  [the longest x4 3.94 us: __init__(): self.fy = 0.5 * (rows[:, 1:] + rows[:, :-1])]
    div x0 -> x3, other arithmetic: none -> 4.7 us  [start(): return OMEGA * f / self.coef(h)[4]]
    mul x4, other arithmetic: 0.23 us -> 2.34 us  [__init__(): faces_z = 0.5 * (k[1:] + k[:-1])]
    select_n x11 -> x8, other arithmetic: 10.9 us -> 9.32 us  [the longest x4 5.79 us: __init__(): self.fx = jnp.where(inside, self.fx, 0.0)]
  transfers between devices with their start and end apart: 14 -> 14, of which waited for: 7 -> 8; matrix products, arithmetic and copies ran while one was open for 25% -> 22% of each run, Pallas kernels for 0% -> 0%
where the time goes in v3:
time: 190 us; the launch traced here: 189 us
  starting transfers between devices  66 us (35%)
  other arithmetic  45.1 us (24%)
  local copies, waits for them, and re-layouts  26.5 us (14%)
  matrix products  23.9 us (13%)
  waiting for transfers between devices  21.8 us (11%)
  between operations  3.46 us (2%)
  blocking collectives  2.18 us (1%)
    ppermute x14, starting transfers between devices, shift_from(): return lax.ppermute(block, 'slab', pairs)  66 us
    ppermute x14, waiting for transfers between devices, shift_from(): return lax.ppermute(block, 'slab', pairs)  21.8 us
    unnamed x133, local copies, waits for them, and re-layouts  15.3 us
    add x9, other arithmetic, sweep(): return u[1:-1] + OMEGA * (f - self.operate(u, h)) / diag  10.9 us
    dot_general x10, matrix products, along_y(): jnp.einsum('zyx,yv->zvx', values, jnp.asarray(matrix), precision=precisio...  10.3 us
    reduce_sum x6, other arithmetic, restrict_sum(): values = values.reshape(nz // 2, 2, ny, nx).sum(axis=1)  7.21 us
    dot_general x1, matrix products, on_device(): jnp.dot(along_rows.reshape(k0_planes * fy, MX), cols_table, precision=HI)  5.83 us
    select_n x4, other arithmetic, __init__(): self.fx = jnp.where(inside, self.fx, 0.0)  5.79 us
  transfers between devices with their start and end apart: 14, of which 8 were waited for; matrix products, arithmetic and copies ran while one was open for 22% of the time, Pallas kernels for 0%

profile of v3, /device:TPU:24, one launch (start us, length us, event | category | flops | bytes accessed | tf_op | source)
XLA Modules:
  0.0 189.0 jit_solution(10672747948672115944)
XLA Ops:
  7.0 4.8 %collective-permute-start.4 = (bf16[4,64,128]{2,1,0:T(8,128)(2,1)S(1)}, bf16[4,64,128]{2,1,0:T(8,128)(2,1)S(1)}, u32[]{:S(2)}, u32[]{:S(2)}) collective-permute-start(bf16[4,64,128]{2,1,0:T(8,128)(2,1)S(1)} %dynamic-slice_bitcast_fusion), channel_id=1, source_target_pairs={{1,0},{2,1},{3,2},{4,3},{5,4},{6,5},{7,6},{8,7},{9,8},{10,9},{11,1... | collective-permute-start | bytes 196616 | tf_op jit(solution)/shard_map/ppermute | solution.py:71
  13.8 4.2 %collective-permute-start.5 = (bf16[2,64,128]{2,1,0:T(8,128)(2,1)S(1)}, bf16[2,64,128]{2,1,0:T(8,128)(2,1)S(1)}, u32[]{:S(2)}, u32[]{:S(2)}) collective-permute-start(bf16[2,64,128]{2,1,0:T(8,128)(2,1)S(1)} %get-tuple-element.38), channel_id=1, source_target_pairs={{2,0},{3,1},{4,2},{5,3},{6,4},{7,5},{8,6},{9,7},{10,8},{11,9},{12,... | collective-permute-start | bytes 98312 | tf_op jit(solution)/shard_map/ppermute | solution.py:71
  18.0 3.3 %collective-permute-start.2 = (bf16[2,64,128]{2,1,0:T(8,128)(2,1)S(1)}, bf16[2,64,128]{2,1,0:T(8,128)(2,1)S(1)}, u32[]{:S(2)}, u32[]{:S(2)}) collective-permute-start(bf16[2,64,128]{2,1,0:T(8,128)(2,1)S(1)} %get-tuple-element.39), channel_id=1, source_target_pairs={{0,2},{1,3},{2,4},{3,5},{4,6},{5,7},{6,8},{7,9},{8,10},{9,11},{10,... | collective-permute-start | bytes 98312 | tf_op jit(solution)/shard_map/ppermute | solution.py:71
  22.3 6.9 %collective-permute-start.1 = (f32[3,128,256]{2,1,0:T(8,128)}, f32[3,128,256]{2,1,0:T(8,128)}, u32[]{:S(2)}, u32[]{:S(2)}) collective-permute-start(f32[3,128,256]{2,1,0:T(8,128)} %get-tuple-element.33), channel_id=1, source_target_pairs={{1,0},{2,1},{3,2},{4,3},{5,4},{6,5},{7,6},{8,7},{9,8},{10,9},{11,1... | collective-permute-start | bytes 1179656 | tf_op jit(solution)/shard_map/ppermute | solution.py:71
  29.9 2.6 %convolution_bitcast_fusion.2 = f32[28,128,64]{1,2,0:T(8,128)} fusion(f32[28,16,64]{2,0,1:T(8,128)S(1)} %fusion.123, s32[128]{0:T(128)S(1)} %multiply_add_fusion.2, s32[16]{0:T(128)S(1)} %iota_add_fusion.2), kind=kOutput, calls=%fused_computation.59 | convolution fusion | flops 44068864 | bytes 1032768 | tf_op jit(solution)/shard_map/zbe,by->zye/dot_general | solution.py:184
  34.9 3.4 %convolution_bitcast_fusion = f32[16,128,256]{1,2,0:T(8,128)S(1)} fusion(f32[16,64,256]{2,1,0:T(8,128)S(1)} %fusion.125, f32[64,128,1]{1,0,2:T(8,128)S(1)} %copy-done.53), kind=kOutput, calls=%fused_computation.35 | convolution fusion | flops 402653184 | bytes 3178496 | tf_op jit(solution)/shard_map/zyx,yv->zvx/dot_general | solution.py:50
  38.8 2.2 %pad_maximum_fusion = f32[14,2,128,256]{2,3,0,1:T(8,128)} fusion(f32[14,1,128,256]{2,3,0,1:T(8,128)S(1)} %get-tuple-element.30, f32[14,1,128,256]{2,3,0,1:T(8,128)S(1)} %get-tuple-element.29), kind=kLoop, calls=%fused_computation.1 | loop fusion | flops 917504 | bytes 7340032 | tf_op jit(solution)/shard_map/stack | solution.py:175
  41.0 5.2 %copy.29 = f32[14,2,128,256]{3,2,1,0:T(8,128)} copy(f32[14,2,128,256]{2,3,0,1:T(8,128)} %pad_maximum_fusion) | data formatting | bytes 7340032 | tf_op jit(solution)/shard_map/stack | solution.py:175
  46.3 5.8 %fusion.1 = f32[28,128,256]{2,1,0:T(8,128)S(1)} fusion(f32[14,2,128,256]{3,2,1,0:T(8,128)} %copy.29, f32[28,128,64]{1,2,0:T(8,128)S(1)} %copy-done.29, pred[28]{0:T(512)(128)(4,1)S(1)} %compare_and_fusion.3, s32[256]{0:T(256)S(1)} %multiply_add_fusion, s32[64]{0:T(128)S(1)} %iota_add_fusion), kind=kOutput, calls=%fused_computation.4 | convolution fusion | flops 706707456 | bytes 8258844 | tf_op jit(solution)/shard_map/dot_general | solution.py:185
  57.1 3.4 %broadcast_select_fusion = (f32[14,128,257]{2,1,0:T(8,128)}, f32[14,128,257]{2,1,0:T(8,128)}) fusion(pred[14]{0:T(512)(128)(4,1)S(1)} %compare_and_fusion.4, f32[14,128,256]{2,1,0:T(8,128)S(1)} %slice.1297), kind=kLoop, calls=%fused_computation.55 | loop fusion | flops 1381632 | bytes 5519374 | tf_op jit(solution)/shard_map/jit(_where)/select_n | solution.py:105
  60.5 3.8 %reduce_sum.55 = f32[14,128,256]{2,1,0:T(8,128)} reduce(f32[14,2,128,256]{3,2,1,0:T(8,128)} %bitcast.141, f32[]{:T(128)} %constant.95.clone.1), dimensions={1}, to_apply=%region_2.3 | reduce | flops 458752 | bytes 5505028 | tf_op jit(solution)/shard_map/reduce_sum | solution.py:56
  64.2 2.7 %convolution_bitcast_fusion.1 = f32[14,64,256]{2,1,0:T(8,128)S(1)} fusion(f32[14,128,256]{2,1,0:T(8,128)} %reduce_sum.55, f32[128,64,1]{0,1,2:T(8,128)S(1)} %copy-done.44), kind=kOutput, calls=%fused_computation.58 | convolution fusion | flops 352321536 | bytes 2785280 | tf_op jit(solution)/shard_map/zyx,yv->zvx/dot_general | solution.py:50
  74.7 4.1 %multiply_divide_fusion = (f32[14,128,256]{2,1,0:T(8,128)S(1)}, f32[14,128,256]{2,1,0:T(8,128)S(1)}, f32[14,128,256]{2,1,0:T(8,128)S(1)}, f32[14,128,256]{2,1,0:T(8,128)S(1)}) fusion(f32[14,128,256]{2,1,0:T(8,128)} %copy-done.17, f32[14,128,257]{2,1,0:T(8,128)} %get-tuple-element.26, f32[14,129,256]{2,1,0:T(8,128)S(1)} %copy-done.12, ...), kind=kLoop, calls=%fused_computation.28 | loop fusion | flops 4587520 | bytes 20185102 | tf_op jit(solution)/shard_map/div | solution.py:132
  79.0 3.6 %copy-done.2 = f32[14,128,257]{2,1,0:T(8,128)S(1)} copy-done((f32[14,128,257]{2,1,0:T(8,128)S(1)}, f32[14,128,257]{2,1,0:T(8,128)}, u32[]{:S(2)}) %copy-start.2) | copy-done | bytes 1842200
  82.6 3.7 %fusion.19 = f32[12,128,256]{2,1,0:T(8,128)S(1)} fusion(f32[12,128,256]{2,1,0:T(8,128)S(1)} %slice.1302, f32[14,128,257]{2,1,0:T(8,128)S(1)} %copy-done.2, f32[14,129,256]{2,1,0:T(8,128)S(1)} %get-tuple-element.23, f32[14,128,256]{2,1,0:T(8,128)S(1)} %get-tuple-element.27, f32[14,128,256]{2,1,0:T(8,128)S(1)} %get-tuple-element.32, ...), kind=kLoop, calls=%fused_computation.47 | loop fusion | flops 6684672 | bytes 18874368 | tf_op jit(solution)/shard_map/add | solution.py:129
  88.8 6.0 %collective-permute-start.7 = (f32[4,64,128]{2,1,0:T(8,128)S(1)}, f32[4,64,128]{2,1,0:T(8,128)S(1)}, u32[]{:S(2)}, u32[]{:S(2)}) collective-permute-start(f32[4,64,128]{2,1,0:T(8,128)S(1)} %convolution_multiply_fusion.1), channel_id=1, source_target_pairs={{1,0},{2,1},{3,2},{4,3},{5,4},{6,5},{7,6},{8,7},{9,8},{10,9},{11,1... | collective-permute-start | bytes 393224 | tf_op jit(solution)/shard_map/ppermute | solution.py:71
  97.3 6.5 %collective-permute-done.6 = f32[4,64,128]{2,1,0:T(8,128)S(1)} collective-permute-done((f32[4,64,128]{2,1,0:T(8,128)S(1)}, f32[4,64,128]{2,1,0:T(8,128)S(1)}, u32[]{:S(2)}, u32[]{:S(2)}) %collective-permute-start.6) | collective-permute-done | bytes 131104 | tf_op jit(solution)/shard_map/ppermute | solution.py:71
  109.2 3.9 %collective-permute-start.8 = (f32[1,2,2,32,64]{4,3,2,1,0:T(8,128)S(1)}, f32[1,2,2,32,64]{4,3,2,1,0:T(8,128)S(1)}, u32[]{:S(2)}, u32[]{:S(2)}) collective-permute-start(f32[1,2,2,32,64]{4,3,2,1,0:T(8,128)S(1)} %maximum_bitcast_fusion), channel_id=1, source_target_pairs={{0,1},{1,2},{2,3},{3,4},{4,5},{5,6},{6,7},{7,8},{8,9},{9,10},{10,1... | collective-permute-start | bytes 98312 | tf_op jit(solution)/shard_map/ppermute | solution.py:71
  113.4 4.0 %collective-permute-done.8 = f32[1,2,2,32,64]{4,3,2,1,0:T(8,128)S(1)} collective-permute-done((f32[1,2,2,32,64]{4,3,2,1,0:T(8,128)S(1)}, f32[1,2,2,32,64]{4,3,2,1,0:T(8,128)S(1)}, u32[]{:S(2)}, u32[]{:S(2)}) %collective-permute-start.8) | collective-permute-done | bytes 32800 | tf_op jit(solution)/shard_map/ppermute | solution.py:71
  119.4 7.3 %collective-permute-start.9 = (f32[2,2,2,32,64]{4,3,2,1,0:T(8,128)S(1)}, f32[2,2,2,32,64]{4,3,2,1,0:T(8,128)S(1)}, u32[]{:S(2)}, u32[]{:S(2)}) collective-permute-start(f32[2,2,2,32,64]{4,3,2,1,0:T(8,128)S(1)} %get-tuple-element.53), channel_id=1, source_target_pairs={{0,2},{1,3},{2,4},{3,5},{4,6},{5,7},{6,8},{7,9},{8,10},{9,11},{10,... | collective-permute-start | bytes 196616 | tf_op jit(solution)/shard_map/ppermute | solution.py:71
  129.3 18.0 %collective-permute-start.10 = (f32[4,2,2,32,64]{4,3,2,1,0:T(8,128)S(1)}, f32[4,2,2,32,64]{4,3,2,1,0:T(8,128)S(1)}, u32[]{:S(2)}, u32[]{:S(2)}) collective-permute-start(f32[4,2,2,32,64]{4,3,2,1,0:T(8,128)S(1)} %get-tuple-element.51), channel_id=1, source_target_pairs={{0,4},{1,5},{2,6},{3,7},{4,8},{5,9},{6,10},{7,11},{8,12},{9,13},{1... | collective-permute-start | bytes 393224 | tf_op jit(solution)/shard_map/ppermute | solution.py:71
  151.3 7.1 %collective-permute-done.13 = f32[4,2,2,32,64]{4,3,2,1,0:T(8,128)S(1)} collective-permute-done((f32[4,2,2,32,64]{4,3,2,1,0:T(8,128)S(1)}, f32[4,2,2,32,64]{4,3,2,1,0:T(8,128)S(1)}, u32[]{:S(2)}, u32[]{:S(2)}) %collective-permute-start.13) | collective-permute-done | bytes 131104 | tf_op jit(solution)/shard_map/ppermute | solution.py:71
  181.9 3.4 %fusion.33 = f32[10,128,256]{2,1,0:T(8,128)S(1)} fusion(f32[10,128,256]{2,1,0:T(8,128)S(1)} %slice.1474, f32[14,128,257]{2,1,0:T(8,128)S(1)} %copy-done.3, f32[14,129,256]{2,1,0:T(8,128)S(1)} %get-tuple-element.23, f32[12,128,256]{2,1,0:T(8,128)S(1)} %bitcast_add_fusion.1, f32[14,128,256]{2,1,0:T(8,128)} %copy-done.9, f32[14,128,256]{2,1,0:T(8,128)S(1)} %copy-done.8, ...), kind=kLoop, calls=%fused_computation.69 | loop fusion | flops 5570560 | bytes 15728640 | tf_op jit(solution)/shard_map/add | solution.py:129
  186.8 2.2 %fusion.65 = f32[1,8,128,256]{3,2,1,0:T(8,128)} fusion(f32[8,128,256]{2,1,0:T(8,128)S(1)} %slice.1485, f32[8,128,256]{2,1,0:T(8,128)S(1)} %copy-done.16, f32[10,128,256]{2,1,0:T(8,128)S(1)} %fusion.33, f32[14,128,257]{2,1,0:T(8,128)S(1)} %copy-done.3, f32[14,129,256]{2,1,0:T(8,128)S(1)} %get-tuple-element.23, f32[14,128,256]{2,1,0:T(8,128)S(1)} %copy-done.10, ...), kind=kLoop, calls=%fused_computation.125 | loop fusion | flops 4456448 | bytes 12582912 | tf_op jit(solution)/shard_map/broadcast_in_dim | solution.py:249
  (250 shorter events, 67.4 us)
Async XLA Ops:
  0.0 21.3 %copy-start.14 = (f32[8,128,256]{2,1,0:T(8,128)S(1)}, f32[8,128,256]{2,1,0:T(8,128)}, u32[]{:S(2)}) copy-start(f32[8,128,256]{2,1,0:T(8,128)} %param.29) | copy-start | bytes 3145732
  0.0 29.3 %copy-start.50 = (f32[1,32,16,64]{3,2,1,0:T(8,128)S(1)}, f32[1,32,16,64]{3,2,1,0:T(8,128)}, u32[]{:S(2)}) copy-start(f32[1,32,16,64]{3,2,1,0:T(8,128)} %param.28) | copy-start | bytes 393220
  7.0 27.5 %collective-permute-start.4 = (bf16[4,64,128]{2,1,0:T(8,128)(2,1)S(1)}, bf16[4,64,128]{2,1,0:T(8,128)(2,1)S(1)}, u32[]{:S(2)}, u32[]{:S(2)}) collective-permute-start(bf16[4,64,128]{2,1,0:T(8,128)(2,1)S(1)} %dynamic-slice_bitcast_fusion), channel_id=1, source_target_pairs={{1,0},{2,1},{3,2},{4,3},{5,4},{6,5},{7,6},{8,7},{9,8},{10,9},{11,1... | collective-permute-start | bytes 196616 | tf_op jit(solution)/shard_map/ppermute | solution.py:71
  11.9 22.6 %collective-permute-start.3 = (bf16[4,64,128]{2,1,0:T(8,128)(2,1)S(1)}, bf16[4,64,128]{2,1,0:T(8,128)(2,1)S(1)}, u32[]{:S(2)}, u32[]{:S(2)}) collective-permute-start(bf16[4,64,128]{2,1,0:T(8,128)(2,1)S(1)} %dynamic-slice_bitcast_fusion), channel_id=1, source_target_pairs={{0,1},{1,2},{2,3},{3,4},{4,5},{5,6},{6,7},{7,8},{8,9},{9,10},{10,1... | collective-permute-start | bytes 196616 | tf_op jit(solution)/shard_map/ppermute | solution.py:71
  13.8 20.7 %collective-permute-start.5 = (bf16[2,64,128]{2,1,0:T(8,128)(2,1)S(1)}, bf16[2,64,128]{2,1,0:T(8,128)(2,1)S(1)}, u32[]{:S(2)}, u32[]{:S(2)}) collective-permute-start(bf16[2,64,128]{2,1,0:T(8,128)(2,1)S(1)} %get-tuple-element.38), channel_id=1, source_target_pairs={{2,0},{3,1},{4,2},{5,3},{6,4},{7,5},{8,6},{9,7},{10,8},{11,9},{12,... | collective-permute-start | bytes 98312 | tf_op jit(solution)/shard_map/ppermute | solution.py:71
  18.0 16.5 %copy-start.52 = (bf16[128,256,1]{1,0,2:T(8,128)(2,1)S(1)}, bf16[128,256,1]{1,0,2:T(8,128)(2,1)}, u32[]{:S(2)}) copy-start(bf16[128,256,1]{1,0,2:T(8,128)(2,1)} %constant.313) | copy-start | bytes 196612
  18.0 14.5 %collective-permute-start.2 = (bf16[2,64,128]{2,1,0:T(8,128)(2,1)S(1)}, bf16[2,64,128]{2,1,0:T(8,128)(2,1)S(1)}, u32[]{:S(2)}, u32[]{:S(2)}) collective-permute-start(bf16[2,64,128]{2,1,0:T(8,128)(2,1)S(1)} %get-tuple-element.39), channel_id=1, source_target_pairs={{0,2},{1,3},{2,4},{3,5},{4,6},{5,7},{6,8},{7,9},{8,10},{9,11},{10,... | collective-permute-start | bytes 98312 | tf_op jit(solution)/shard_map/ppermute | solution.py:71
  22.3 50.1 %collective-permute-start.1 = (f32[3,128,256]{2,1,0:T(8,128)}, f32[3,128,256]{2,1,0:T(8,128)}, u32[]{:S(2)}, u32[]{:S(2)}) collective-permute-start(f32[3,128,256]{2,1,0:T(8,128)} %get-tuple-element.33), channel_id=1, source_target_pairs={{1,0},{2,1},{3,2},{4,3},{5,4},{6,5},{7,6},{8,7},{9,8},{10,9},{11,1... | collective-permute-start | bytes 1179656 | tf_op jit(solution)/shard_map/ppermute | solution.py:71
  32.5 36.8 %copy-start.57 = (pred[12]{0:T(512)(128)(4,1)}, pred[12]{0:T(512)(128)(4,1)S(1)}, u32[]{:S(2)}) copy-start(pred[12]{0:T(512)(128)(4,1)S(1)} %compare_and_fusion.2) | copy-start | bytes 40
  32.5 38.7 %collective-permute-start = (f32[3,128,256]{2,1,0:T(8,128)}, f32[3,128,256]{2,1,0:T(8,128)}, u32[]{:S(2)}, u32[]{:S(2)}) collective-permute-start(f32[3,128,256]{2,1,0:T(8,128)} %get-tuple-element.34), channel_id=1, source_target_pairs={{0,1},{1,2},{2,3},{3,4},{4,5},{5,6},{6,7},{7,8},{8,9},{9,10},{10,1... | collective-permute-start | bytes 1179656 | tf_op jit(solution)/shard_map/ppermute | solution.py:71
  86.5 17.3 %copy-start.40 = (f32[12,64,129]{2,1,0:T(8,128)S(1)}, f32[12,64,129]{2,1,0:T(8,128)}, u32[]{:S(2)}) copy-start(f32[12,64,129]{2,1,0:T(8,128)} %get-tuple-element.20) | copy-start | bytes 1188868
  86.5 17.3 %copy-start.58 = (pred[12]{0:T(512)(128)(4,1)S(1)}, pred[12]{0:T(512)(128)(4,1)}, u32[]{:S(2)}) copy-start(pred[12]{0:T(512)(128)(4,1)} %copy-done.57) | copy-start | bytes 40
  88.0 15.8 %copy-start.30 = (f32[13,64,128]{2,1,0:T(8,128)S(1)}, f32[13,64,128]{2,1,0:T(8,128)}, u32[]{:S(2)}) copy-start(f32[13,64,128]{2,1,0:T(8,128)} %fusion.72) | copy-start | bytes 1277956
  88.0 15.8 %copy-start.31 = (f32[12,65,128]{2,1,0:T(8,128)S(1)}, f32[12,65,128]{2,1,0:T(8,128)}, u32[]{:S(2)}) copy-start(f32[12,65,128]{2,1,0:T(8,128)} %get-tuple-element.18) | copy-start | bytes 1198084
  88.8 8.5 %collective-permute-start.7 = (f32[4,64,128]{2,1,0:T(8,128)S(1)}, f32[4,64,128]{2,1,0:T(8,128)S(1)}, u32[]{:S(2)}, u32[]{:S(2)}) collective-permute-start(f32[4,64,128]{2,1,0:T(8,128)S(1)} %convolution_multiply_fusion.1), channel_id=1, source_target_pairs={{1,0},{2,1},{3,2},{4,3},{5,4},{6,5},{7,6},{8,7},{9,8},{10,9},{11,1... | collective-permute-start | bytes 393224 | tf_op jit(solution)/shard_map/ppermute | solution.py:71
  94.8 9.0 %collective-permute-start.6 = (f32[4,64,128]{2,1,0:T(8,128)S(1)}, f32[4,64,128]{2,1,0:T(8,128)S(1)}, u32[]{:S(2)}, u32[]{:S(2)}) collective-permute-start(f32[4,64,128]{2,1,0:T(8,128)S(1)} %convolution_multiply_fusion.1), channel_id=1, source_target_pairs={{0,1},{1,2},{2,3},{3,4},{4,5},{5,6},{6,7},{7,8},{8,9},{9,10},{10,1... | collective-permute-start | bytes 393224 | tf_op jit(solution)/shard_map/ppermute | solution.py:71
  107.3 6.1 %collective-permute-start.11 = (f32[1,2,2,32,64]{4,3,2,1,0:T(8,128)S(1)}, f32[1,2,2,32,64]{4,3,2,1,0:T(8,128)S(1)}, u32[]{:S(2)}, u32[]{:S(2)}) collective-permute-start(f32[1,2,2,32,64]{4,3,2,1,0:T(8,128)S(1)} %maximum_bitcast_fusion), channel_id=1, source_target_pairs={{1,0},{2,1},{3,2},{4,3},{5,4},{6,5},{7,6},{8,7},{9,8},{10,9},{11,1... | collective-permute-start | bytes 98312 | tf_op jit(solution)/shard_map/ppermute | solution.py:71
  109.2 8.3 %collective-permute-start.8 = (f32[1,2,2,32,64]{4,3,2,1,0:T(8,128)S(1)}, f32[1,2,2,32,64]{4,3,2,1,0:T(8,128)S(1)}, u32[]{:S(2)}, u32[]{:S(2)}) collective-permute-start(f32[1,2,2,32,64]{4,3,2,1,0:T(8,128)S(1)} %maximum_bitcast_fusion), channel_id=1, source_target_pairs={{0,1},{1,2},{2,3},{3,4},{4,5},{5,6},{6,7},{7,8},{8,9},{9,10},{10,1... | collective-permute-start | bytes 98312 | tf_op jit(solution)/shard_map/ppermute | solution.py:71
  113.1 38.1 %copy-start.48 = (f32[1,2,32,64]{3,2,1,0:T(8,128)S(1)}, f32[1,2,32,64]{3,2,1,0:T(8,128)}, u32[]{:S(2)}) copy-start(f32[1,2,32,64]{3,2,1,0:T(8,128)} %copy-done.47) | copy-start | bytes 49156
  117.5 10.3 %collective-permute-start.12 = (f32[2,2,2,32,64]{4,3,2,1,0:T(8,128)S(1)}, f32[2,2,2,32,64]{4,3,2,1,0:T(8,128)S(1)}, u32[]{:S(2)}, u32[]{:S(2)}) collective-permute-start(f32[2,2,2,32,64]{4,3,2,1,0:T(8,128)S(1)} %get-tuple-element.52), channel_id=1, source_target_pairs={{2,0},{3,1},{4,2},{5,3},{6,4},{7,5},{8,6},{9,7},{10,8},{11,9},{12,... | collective-permute-start | bytes 196616 | tf_op jit(solution)/shard_map/ppermute | solution.py:71
  119.4 9.8 %collective-permute-start.9 = (f32[2,2,2,32,64]{4,3,2,1,0:T(8,128)S(1)}, f32[2,2,2,32,64]{4,3,2,1,0:T(8,128)S(1)}, u32[]{:S(2)}, u32[]{:S(2)}) collective-permute-start(f32[2,2,2,32,64]{4,3,2,1,0:T(8,128)S(1)} %get-tuple-element.53), channel_id=1, source_target_pairs={{0,2},{1,3},{2,4},{3,5},{4,6},{5,7},{6,8},{7,9},{8,10},{9,11},{10,... | collective-permute-start | bytes 196616 | tf_op jit(solution)/shard_map/ppermute | solution.py:71
  129.3 21.9 %collective-permute-start.10 = (f32[4,2,2,32,64]{4,3,2,1,0:T(8,128)S(1)}, f32[4,2,2,32,64]{4,3,2,1,0:T(8,128)S(1)}, u32[]{:S(2)}, u32[]{:S(2)}) collective-permute-start(f32[4,2,2,32,64]{4,3,2,1,0:T(8,128)S(1)} %get-tuple-element.51), channel_id=1, source_target_pairs={{0,4},{1,5},{2,6},{3,7},{4,8},{5,9},{6,10},{7,11},{8,12},{9,13},{1... | collective-permute-start | bytes 393224 | tf_op jit(solution)/shard_map/ppermute | solution.py:71
  147.4 13.0 %copy-start.59 = (pred[11]{0:T(512)(128)(4,1)}, pred[11]{0:T(512)(128)(4,1)S(1)}, u32[]{:S(2)}) copy-start(pred[11]{0:T(512)(128)(4,1)S(1)} %compare_and_fusion) | copy-start | bytes 37
  148.0 10.4 %collective-permute-start.13 = (f32[4,2,2,32,64]{4,3,2,1,0:T(8,128)S(1)}, f32[4,2,2,32,64]{4,3,2,1,0:T(8,128)S(1)}, u32[]{:S(2)}, u32[]{:S(2)}) collective-permute-start(f32[4,2,2,32,64]{4,3,2,1,0:T(8,128)S(1)} %get-tuple-element.50), channel_id=1, source_target_pairs={{4,0},{5,1},{6,2},{7,3},{8,4},{9,5},{10,6},{11,7},{12,8},{13,9},{1... | collective-permute-start | bytes 393224 | tf_op jit(solution)/shard_map/ppermute | solution.py:71
  (51 other events, 145.3 us)

commit v4 on v2

--- a/solution.py
+++ b/solution.py
@@ -15,10 +15,9 @@
 OMEGA = 0.8
 HI = lax.Precision.HIGHEST
 
-K0_HALO = 10
 F0_HALO = 3
 F1_HALO = 4
-COARSE_HALO = 6
+COARSE_HALO = 4
 
 
 def pair_sum_matrix(n):
@@ -153,10 +152,7 @@
     coarse_total = cz * slabs
     fine_total = fz * slabs
 
-    far = COARSE_HALO - cz
-    parts = [shift_from(own[cz - far:], 2), shift_from(own, 1), own,
-             shift_from(own, -1), shift_from(own[:far], -2)]
-    ext = jnp.concatenate(parts, axis=0)
+    ext = jnp.concatenate([shift_from(own, 1), own, shift_from(own, -1)], axis=0)
     n_ext = ext.shape[0]
     g0 = s * cz - COARSE_HALO
     gidx = g0 + jnp.arange(n_ext, dtype=jnp.int32)
@@ -201,9 +197,12 @@
     f1_own = 0.5 * restrict_sum(res0)
 
     h1k = F1_HALO + 1
-    lvl1 = Level(k1[k1_halo - h1k: k1_halo + own1 + h1k], h1k, own1, s * own1 - h1k,
-                 fine_total // 2)
-    f1 = jnp.concatenate([shift_from(f1_own, 1), f1_own, shift_from(f1_own, -1)], axis=0)
+    extra = h1k - k1_halo
+    from_left = shift_from(jnp.concatenate([k1[own1 - extra: own1], f1_own]), 1)
+    from_right = shift_from(jnp.concatenate([f1_own, k1[2 * k1_halo: 2 * k1_halo + extra]]), -1)
+    k1_ext = jnp.concatenate([from_left[:extra], k1, from_right[own1:]], axis=0)
+    f1 = jnp.concatenate([from_left[extra:], f1_own, from_right[:own1]], axis=0)
+    lvl1 = Level(k1_ext, h1k, own1, s * own1 - h1k, fine_total // 2)
     v = lvl1.start(f1, F1_HALO)
     v1 = lvl1.sweep(v, lvl1.cut(f1, F1_HALO - 1, F1_HALO), F1_HALO)
     res1 = f1_own - lvl1.operate(v1[2:-2], 1)

time: 180 us -> 158 us (0.88)
  other arithmetic: 43.7 us -> 34.8 us
  starting transfers between devices: 66 us -> 58.8 us
  matrix products: 23 us -> 20.7 us
  waiting for transfers between devices: 20.8 us -> 18.8 us
    ppermute x14 -> x12, starting transfers between devices: 66 us -> 58.8 us  [shift_from(): return lax.ppermute(block, 'slab', pairs)]
    reduce_sum x6, other arithmetic: 7.7 us -> 4.75 us  [restrict_sum(): values = values.reshape(nz // 2, 2, ny, nx).sum(axis=1)]
    mul x4, other arithmetic: 3.94 us -> 1.06 us  [__init__(): self.fy = 0.5 * (rows[:, 1:] + rows[:, :-1])]
    another operation x1, local copies, waits for them, and re-layouts: 5.13 us -> 2.26 us  [on_device(): log_perm = jnp.stack((even, odd), axis=1).reshape(2 * (n_ext - 2), fy, fx)]
    and x17, other arithmetic: 8.96 us -> 6.85 us  [plane_mask(): return ((g >= 0) & (g < total))[:, None, None]]
    another operation x2, other arithmetic: 2.6 us -> 0.5 us  [on_device(): log_perm = jnp.stack((even, odd), axis=1).reshape(2 * (n_ext - 2), fy, fx)]
    ppermute x14 -> x12, waiting for transfers between devices: 20.8 us -> 18.8 us  [shift_from(): return lax.ppermute(block, 'slab', pairs)]
    unnamed x131 -> x113, local copies, waits for them, and re-layouts: 9.29 us -> 9.95 us
  transfers between devices with their start and end apart: 14 -> 12, of which waited for: 7 -> 7; matrix products, arithmetic and copies ran while one was open for 25% -> 21% of each run, Pallas kernels for 0% -> 0%
where the time goes in v4:
time: 158 us; the launch traced here: 157 us
  starting transfers between devices  58.8 us (37%)
  other arithmetic  34.8 us (22%)
  matrix products  20.7 us (13%)
  waiting for transfers between devices  18.8 us (12%)
  local copies, waits for them, and re-layouts  18.5 us (12%)
  between operations  3.35 us (2%)
  blocking collectives  2.31 us (1%)
    ppermute x12, starting transfers between devices, shift_from(): return lax.ppermute(block, 'slab', pairs)  58.8 us
    ppermute x12, waiting for transfers between devices, shift_from(): return lax.ppermute(block, 'slab', pairs)  18.8 us
    select_n x11, other arithmetic, mask(): jnp.where(plane_mask(self.first + self.halo - h, u.shape[0], self.total),...  10.6 us
    unnamed x113, local copies, waits for them, and re-layouts  9.95 us
    dot_general x10, matrix products, along_y(): jnp.einsum('zyx,yv->zvx', values, jnp.asarray(matrix), precision=precisio...  9.13 us
    and x17, other arithmetic, plane_mask(): return ((g >= 0) & (g < total))[:, None, None]  6.85 us
    reduce_sum x6, other arithmetic, restrict_sum(): values = values.reshape(nz // 2, 2, ny, nx).sum(axis=1)  4.75 us
    dot_general x1, matrix products, on_device(): jnp.dot(along_rows.reshape(k0_planes * fy, MX), cols_table, precision=HI)  4.67 us
  transfers between devices with their start and end apart: 12, of which 7 were waited for; matrix products, arithmetic and copies ran while one was open for 21% of the time, Pallas kernels for 0%

profile of v4, /device:TPU:24, one launch (start us, length us, event | category | flops | bytes accessed | tf_op | source)
XLA Modules:
  0.0 157.3 jit_solution(11864039209649756971)
XLA Ops:
  4.1 2.3 %all_gather.3 = bf16[8,4,64,128]{3,2,1,0:T(8,128)(2,1)S(1)} all-gather(bf16[4,4,64,128]{3,2,1,0:T(8,128)(2,1)S(1)} %gather_fusion), channel_id=1, replica_groups=mesh['chain'=2,'slab'=64] {'chain'}, dimensions={0}, use_global_device_ids=true | all-gather | bytes 786432 | tf_op jit(solution)/shard_map/all_gather | solution.py:146
  7.1 5.0 %collective-permute-start.3 = (bf16[4,64,128]{2,1,0:T(8,128)(2,1)S(1)}, bf16[4,64,128]{2,1,0:T(8,128)(2,1)S(1)}, u32[]{:S(2)}, u32[]{:S(2)}) collective-permute-start(bf16[4,64,128]{2,1,0:T(8,128)(2,1)S(1)} %dynamic-slice_bitcast_fusion), channel_id=1, source_target_pairs={{1,0},{2,1},{3,2},{4,3},{5,4},{6,5},{7,6},{8,7},{9,8},{10,9},{11,1... | collective-permute-start | bytes 196616 | tf_op jit(solution)/shard_map/ppermute | solution.py:70
  12.1 1.9 %collective-permute-start.2 = (bf16[4,64,128]{2,1,0:T(8,128)(2,1)S(1)}, bf16[4,64,128]{2,1,0:T(8,128)(2,1)S(1)}, u32[]{:S(2)}, u32[]{:S(2)}) collective-permute-start(bf16[4,64,128]{2,1,0:T(8,128)(2,1)S(1)} %dynamic-slice_bitcast_fusion), channel_id=1, source_target_pairs={{0,1},{1,2},{2,3},{3,4},{4,5},{5,6},{6,7},{7,8},{8,9},{9,10},{10,1... | collective-permute-start | bytes 196616 | tf_op jit(solution)/shard_map/ppermute | solution.py:70
  15.0 6.2 %collective-permute-start.1 = (f32[3,128,256]{2,1,0:T(8,128)}, f32[3,128,256]{2,1,0:T(8,128)S(1)}, u32[]{:S(2)}, u32[]{:S(2)}) collective-permute-start(f32[3,128,256]{2,1,0:T(8,128)} %get-tuple-element.15), channel_id=1, source_target_pairs={{1,0},{2,1},{3,2},{4,3},{5,4},{6,5},{7,6},{8,7},{9,8},{10,9},{11,1... | collective-permute-start | bytes 1179656 | tf_op jit(solution)/shard_map/ppermute | solution.py:70
  21.2 1.9 %collective-permute-start = (f32[3,128,256]{2,1,0:T(8,128)}, f32[3,128,256]{2,1,0:T(8,128)}, u32[]{:S(2)}, u32[]{:S(2)}) collective-permute-start(f32[3,128,256]{2,1,0:T(8,128)} %get-tuple-element.16), channel_id=1, source_target_pairs={{0,1},{1,2},{2,3},{3,4},{4,5},{5,6},{6,7},{7,8},{8,9},{9,10},{10,1... | collective-permute-start | bytes 1179656 | tf_op jit(solution)/shard_map/ppermute | solution.py:70
  28.3 2.1 %convolution_bitcast_fusion.3 = f32[20,128,64]{1,2,0:T(8,128)} fusion(f32[20,16,64]{2,0,1:T(8,128)S(1)} %fusion.123, s32[128]{0:T(128)S(1)} %multiply_add_fusion.2, s32[16]{0:T(128)S(1)} %iota_add_fusion.2), kind=kOutput, calls=%fused_computation.75 | convolution fusion | flops 31485952 | bytes 737856 | tf_op jit(solution)/shard_map/zbe,by->zye/dot_general | solution.py:178
  31.4 2.6 %convolution_bitcast_fusion = f32[12,128,256]{1,2,0:T(8,128)S(1)} fusion(f32[12,64,256]{2,1,0:T(8,128)S(1)} %fusion.142, f32[64,128,1]{1,0,2:T(8,128)S(1)} %copy-done.38), kind=kOutput, calls=%fused_computation.46 | convolution fusion | flops 301989888 | bytes 2392064 | tf_op jit(solution)/shard_map/zyx,yv->zvx/dot_general | solution.py:49
  34.5 2.3 %copy.29 = f32[10,2,128,256]{3,2,1,0:T(8,128)} copy(f32[10,2,128,256]{2,3,0,1:T(8,128)S(1)} %pad_maximum_fusion) | data formatting | bytes 5242880 | tf_op jit(solution)/shard_map/stack | solution.py:169
  36.8 4.7 %fusion.3 = f32[20,128,256]{2,1,0:T(8,128)S(1)} fusion(f32[10,2,128,256]{3,2,1,0:T(8,128)} %copy.29, f32[20,128,64]{1,2,0:T(8,128)} %convolution_bitcast_fusion.3, pred[20]{0:T(512)(128)(4,1)S(1)} %compare_and_fusion.12, s32[256]{0:T(256)S(1)} %multiply_add_fusion, s32[64]{0:T(128)S(1)} %iota_add_fusion), kind=kOutput, calls=%fused_computation.8 | convolution fusion | flops 504856576 | bytes 5899540 | tf_op jit(solution)/shard_map/dot_general | solution.py:179
  45.9 2.3 %convolution_bitcast_fusion.2 = f32[10,64,256]{2,1,0:T(8,128)S(1)} fusion(f32[10,128,256]{2,1,0:T(8,128)} %reduce_sum.54, f32[128,64,1]{0,1,2:T(8,128)S(1)} %copy-done.31), kind=kOutput, calls=%fused_computation.74 | convolution fusion | flops 251658240 | bytes 1998848 | tf_op jit(solution)/shard_map/zyx,yv->zvx/dot_general | solution.py:49
  50.1 2.0 %constant_dynamic-update-slice_fusion.2 = f32[14,128,256]{2,1,0:T(8,128)S(1)} fusion(f32[3,128,256]{2,1,0:T(8,128)} %collective-permute-done), kind=kLoop, calls=%fused_computation.435 | loop fusion | bytes 786432
  54.9 2.1 %fusion.19 = f32[12,128,256]{2,1,0:T(8,128)S(1)} fusion(f32[12,128,256]{2,1,0:T(8,128)S(1)} %slice.1338, f32[14,128,257]{2,1,0:T(8,128)S(1)} %fusion.1, f32[14,129,256]{2,1,0:T(8,128)S(1)} %add_multiply_fusion, f32[14,128,256]{2,1,0:T(8,128)S(1)} %get-tuple-element.11, f32[15,128,256]{2,1,0:T(8,128)S(1)} %copy-done.2, ...), kind=kLoop, calls=%fused_computation.45 | loop fusion | flops 7077888 | bytes 18874380 | tf_op jit(solution)/shard_map/jit(_where)/select_n | solution.py:111
  59.4 1.9 %collective-permute-start.4 = (f32[6,64,128]{2,1,0:T(8,128)S(1)}, f32[6,64,128]{2,1,0:T(8,128)S(1)}, u32[]{:S(2)}, u32[]{:S(2)}) collective-permute-start(f32[6,64,128]{2,1,0:T(8,128)S(1)} %get-tuple-element.25), channel_id=1, source_target_pairs={{0,1},{1,2},{2,3},{3,4},{4,5},{5,6},{6,7},{7,8},{8,9},{9,10},{10,1... | collective-permute-start | bytes 589832 | tf_op jit(solution)/shard_map/ppermute | solution.py:70
  61.3 6.3 %collective-permute-start.5 = (f32[6,64,128]{2,1,0:T(8,128)S(1)}, f32[6,64,128]{2,1,0:T(8,128)S(1)}, u32[]{:S(2)}, u32[]{:S(2)}) collective-permute-start(f32[6,64,128]{2,1,0:T(8,128)S(1)} %get-tuple-element.26), channel_id=1, source_target_pairs={{1,0},{2,1},{3,2},{4,3},{5,4},{6,5},{7,6},{8,7},{9,8},{10,9},{11,1... | collective-permute-start | bytes 589832 | tf_op jit(solution)/shard_map/ppermute | solution.py:70
  73.3 6.5 %collective-permute-start.9 = (f32[1,2,2,32,64]{4,3,2,1,0:T(8,128)S(1)}, f32[1,2,2,32,64]{4,3,2,1,0:T(8,128)S(1)}, u32[]{:S(2)}, u32[]{:S(2)}) collective-permute-start(f32[1,2,2,32,64]{4,3,2,1,0:T(8,128)S(1)} %maximum_bitcast_fusion), channel_id=1, source_target_pairs={{1,0},{2,1},{3,2},{4,3},{5,4},{6,5},{7,6},{8,7},{9,8},{10,9},{11,1... | collective-permute-start | bytes 98312 | tf_op jit(solution)/shard_map/ppermute | solution.py:70
  79.8 3.2 %collective-permute-start.6 = (f32[1,2,2,32,64]{4,3,2,1,0:T(8,128)S(1)}, f32[1,2,2,32,64]{4,3,2,1,0:T(8,128)S(1)}, u32[]{:S(2)}, u32[]{:S(2)}) collective-permute-start(f32[1,2,2,32,64]{4,3,2,1,0:T(8,128)S(1)} %maximum_bitcast_fusion), channel_id=1, source_target_pairs={{0,1},{1,2},{2,3},{3,4},{4,5},{5,6},{6,7},{7,8},{8,9},{9,10},{10,1... | collective-permute-start | bytes 98312 | tf_op jit(solution)/shard_map/ppermute | solution.py:70
  83.6 4.5 %collective-permute-done.6 = f32[1,2,2,32,64]{4,3,2,1,0:T(8,128)S(1)} collective-permute-done((f32[1,2,2,32,64]{4,3,2,1,0:T(8,128)S(1)}, f32[1,2,2,32,64]{4,3,2,1,0:T(8,128)S(1)}, u32[]{:S(2)}, u32[]{:S(2)}) %collective-permute-start.6) | collective-permute-done | bytes 32800 | tf_op jit(solution)/shard_map/ppermute | solution.py:70
  90.1 5.4 %collective-permute-start.7 = (f32[2,2,2,32,64]{4,3,2,1,0:T(8,128)S(1)}, f32[2,2,2,32,64]{4,3,2,1,0:T(8,128)S(1)}, u32[]{:S(2)}, u32[]{:S(2)}) collective-permute-start(f32[2,2,2,32,64]{4,3,2,1,0:T(8,128)S(1)} %get-tuple-element.31), channel_id=1, source_target_pairs={{0,2},{1,3},{2,4},{3,5},{4,6},{5,7},{6,8},{7,9},{8,10},{9,11},{10,... | collective-permute-start | bytes 196616 | tf_op jit(solution)/shard_map/ppermute | solution.py:70
  96.6 2.7 %collective-permute-done.7 = f32[2,2,2,32,64]{4,3,2,1,0:T(8,128)S(1)} collective-permute-done((f32[2,2,2,32,64]{4,3,2,1,0:T(8,128)S(1)}, f32[2,2,2,32,64]{4,3,2,1,0:T(8,128)S(1)}, u32[]{:S(2)}, u32[]{:S(2)}) %collective-permute-start.7) | collective-permute-done | bytes 65568 | tf_op jit(solution)/shard_map/ppermute | solution.py:70
  99.4 16.7 %collective-permute-start.8 = (f32[4,2,2,32,64]{4,3,2,1,0:T(8,128)S(1)}, f32[4,2,2,32,64]{4,3,2,1,0:T(8,128)S(1)}, u32[]{:S(2)}, u32[]{:S(2)}) collective-permute-start(f32[4,2,2,32,64]{4,3,2,1,0:T(8,128)S(1)} %get-tuple-element.29), channel_id=1, source_target_pairs={{0,4},{1,5},{2,6},{3,7},{4,8},{5,9},{6,10},{7,11},{8,12},{9,13},{1... | collective-permute-start | bytes 393224 | tf_op jit(solution)/shard_map/ppermute | solution.py:70
  120.0 7.6 %collective-permute-done.11 = f32[4,2,2,32,64]{4,3,2,1,0:T(8,128)S(1)} collective-permute-done((f32[4,2,2,32,64]{4,3,2,1,0:T(8,128)S(1)}, f32[4,2,2,32,64]{4,3,2,1,0:T(8,128)S(1)}, u32[]{:S(2)}, u32[]{:S(2)}) %collective-permute-start.11) | collective-permute-done | bytes 131104 | tf_op jit(solution)/shard_map/ppermute | solution.py:70
  146.9 2.0 %bitcast_add_fusion.1 = f32[12,128,256]{2,1,0:T(8,128)S(1)} fusion(f32[12,128,256]{2,1,0:T(8,128)} %copy-done.8, f32[6,128,256]{2,1,0:T(8,128)} %copy.32), kind=kLoop, calls=%fused_computation.44 | loop fusion | flops 393216 | bytes 3932160 | tf_op jit(solution)/shard_map/add | solution.py:243
  150.8 3.1 %fusion.38 = f32[10,128,256]{2,1,0:T(8,128)S(1)} fusion(f32[10,128,256]{2,1,0:T(8,128)S(1)} %slice.1516, f32[14,128,257]{2,1,0:T(8,128)S(1)} %copy-done.5, f32[14,129,256]{2,1,0:T(8,128)S(1)} %add_multiply_fusion, f32[12,128,256]{2,1,0:T(8,128)S(1)} %bitcast_add_fusion.1, f32[15,128,256]{2,1,0:T(8,128)S(1)} %copy-done.3, f32[14,128,256]{2,1,0:T(8,128)S(1)} %copy-done.7, ...), kind=kLoop, calls=%fused_computation.72 | loop fusion | flops 5898240 | bytes 15728650 | tf_op jit(solution)/shard_map/jit(_where)/select_n | solution.py:111
  155.1 2.2 %select_bitcast_fusion = f32[1,8,128,256]{3,2,1,0:T(8,128)} fusion(f32[8,128,256]{2,1,0:T(8,128)S(1)} %slice.1527, f32[8,128,256]{2,1,0:T(8,128)S(1)} %copy-done.16, f32[10,128,256]{2,1,0:T(8,128)S(1)} %fusion.38, f32[14,128,257]{2,1,0:T(8,128)S(1)} %copy-done.5, f32[14,129,256]{2,1,0:T(8,128)S(1)} %add_multiply_fusion, f32[15,128,256]{2,1,0:T(8,128)S(1)} %copy-done.3, ...), kind=kLoop, calls=%fused_computation.124 | loop fusion | flops 4718592 | bytes 12582920 | tf_op jit(solution)/shard_map/broadcast_in_dim | solution.py:246
  (244 shorter events, 56.5 us)
Async XLA Ops:
  0.0 3.5 %copy-start = (bf16[4,4,4,64,128]{4,3,2,1,0:T(8,128)(2,1)S(1)}, bf16[4,4,4,64,128]{4,3,2,1,0:T(8,128)(2,1)}, u32[]{:S(2)}) copy-start(bf16[4,4,4,64,128]{4,3,2,1,0:T(8,128)(2,1)} %param.25) | copy-start | bytes 3145732
  0.0 14.1 %copy-start.14 = (f32[8,128,256]{2,1,0:T(8,128)S(1)}, f32[8,128,256]{2,1,0:T(8,128)}, u32[]{:S(2)}) copy-start(f32[8,128,256]{2,1,0:T(8,128)} %param.29) | copy-start | bytes 3145732
  4.1 23.7 %copy-start.35 = (f32[1,32,16,64]{3,2,1,0:T(8,128)S(1)}, f32[1,32,16,64]{3,2,1,0:T(8,128)}, u32[]{:S(2)}) copy-start(f32[1,32,16,64]{3,2,1,0:T(8,128)} %param.28) | copy-start | bytes 393220
  7.1 23.9 %copy-start.37 = (bf16[128,256,1]{1,0,2:T(8,128)(2,1)S(1)}, bf16[128,256,1]{1,0,2:T(8,128)(2,1)}, u32[]{:S(2)}) copy-start(bf16[128,256,1]{1,0,2:T(8,128)(2,1)} %constant.357) | copy-start | bytes 196612
  7.1 23.9 %collective-permute-start.3 = (bf16[4,64,128]{2,1,0:T(8,128)(2,1)S(1)}, bf16[4,64,128]{2,1,0:T(8,128)(2,1)S(1)}, u32[]{:S(2)}, u32[]{:S(2)}) collective-permute-start(bf16[4,64,128]{2,1,0:T(8,128)(2,1)S(1)} %dynamic-slice_bitcast_fusion), channel_id=1, source_target_pairs={{1,0},{2,1},{3,2},{4,3},{5,4},{6,5},{7,6},{8,7},{9,8},{10,9},{11,1... | collective-permute-start | bytes 196616 | tf_op jit(solution)/shard_map/ppermute | solution.py:70
  12.1 18.9 %collective-permute-start.2 = (bf16[4,64,128]{2,1,0:T(8,128)(2,1)S(1)}, bf16[4,64,128]{2,1,0:T(8,128)(2,1)S(1)}, u32[]{:S(2)}, u32[]{:S(2)}) collective-permute-start(bf16[4,64,128]{2,1,0:T(8,128)(2,1)S(1)} %dynamic-slice_bitcast_fusion), channel_id=1, source_target_pairs={{0,1},{1,2},{2,3},{3,4},{4,5},{5,6},{6,7},{7,8},{8,9},{9,10},{10,1... | collective-permute-start | bytes 196616 | tf_op jit(solution)/shard_map/ppermute | solution.py:70
  15.0 16.4 %copy-start.38 = (f32[64,128,1]{1,0,2:T(8,128)S(1)}, f32[64,128,1]{1,0,2:T(8,128)}, u32[]{:S(2)}) copy-start(f32[64,128,1]{1,0,2:T(8,128)} %constant.358) | copy-start | bytes 98308
  15.0 37.2 %collective-permute-start.1 = (f32[3,128,256]{2,1,0:T(8,128)}, f32[3,128,256]{2,1,0:T(8,128)S(1)}, u32[]{:S(2)}, u32[]{:S(2)}) collective-permute-start(f32[3,128,256]{2,1,0:T(8,128)} %get-tuple-element.15), channel_id=1, source_target_pairs={{1,0},{2,1},{3,2},{4,3},{5,4},{6,5},{7,6},{8,7},{9,8},{10,9},{11,1... | collective-permute-start | bytes 1179656 | tf_op jit(solution)/shard_map/ppermute | solution.py:70
  21.2 28.9 %collective-permute-start = (f32[3,128,256]{2,1,0:T(8,128)}, f32[3,128,256]{2,1,0:T(8,128)}, u32[]{:S(2)}, u32[]{:S(2)}) collective-permute-start(f32[3,128,256]{2,1,0:T(8,128)} %get-tuple-element.16), channel_id=1, source_target_pairs={{0,1},{1,2},{2,3},{3,4},{4,5},{5,6},{6,7},{7,8},{8,9},{9,10},{10,1... | collective-permute-start | bytes 1179656 | tf_op jit(solution)/shard_map/ppermute | solution.py:70
  49.7 7.4 %copy-start.4 = (f32[14,128,257]{2,1,0:T(8,128)}, f32[14,128,257]{2,1,0:T(8,128)S(1)}, u32[]{:S(2)}) copy-start(f32[14,128,257]{2,1,0:T(8,128)S(1)} %fusion.1) | copy-start | bytes 5526532
  58.5 9.0 %copy-start.34 = (f32[64,32,1]{0,1,2:T(8,128)S(1)}, f32[64,32,1]{0,1,2:T(8,128)}, u32[]{:S(2)}) copy-start(f32[64,32,1]{0,1,2:T(8,128)} %constant.361) | copy-start | bytes 24580
  59.4 10.1 %collective-permute-start.4 = (f32[6,64,128]{2,1,0:T(8,128)S(1)}, f32[6,64,128]{2,1,0:T(8,128)S(1)}, u32[]{:S(2)}, u32[]{:S(2)}) collective-permute-start(f32[6,64,128]{2,1,0:T(8,128)S(1)} %get-tuple-element.25), channel_id=1, source_target_pairs={{0,1},{1,2},{2,3},{3,4},{4,5},{5,6},{6,7},{7,8},{8,9},{9,10},{10,1... | collective-permute-start | bytes 589832 | tf_op jit(solution)/shard_map/ppermute | solution.py:70
  61.3 9.4 %collective-permute-start.5 = (f32[6,64,128]{2,1,0:T(8,128)S(1)}, f32[6,64,128]{2,1,0:T(8,128)S(1)}, u32[]{:S(2)}, u32[]{:S(2)}) collective-permute-start(f32[6,64,128]{2,1,0:T(8,128)S(1)} %get-tuple-element.26), channel_id=1, source_target_pairs={{1,0},{2,1},{3,2},{4,3},{5,4},{6,5},{7,6},{8,7},{9,8},{10,9},{11,1... | collective-permute-start | bytes 589832 | tf_op jit(solution)/shard_map/ppermute | solution.py:70
  73.3 10.3 %collective-permute-start.9 = (f32[1,2,2,32,64]{4,3,2,1,0:T(8,128)S(1)}, f32[1,2,2,32,64]{4,3,2,1,0:T(8,128)S(1)}, u32[]{:S(2)}, u32[]{:S(2)}) collective-permute-start(f32[1,2,2,32,64]{4,3,2,1,0:T(8,128)S(1)} %maximum_bitcast_fusion), channel_id=1, source_target_pairs={{1,0},{2,1},{3,2},{4,3},{5,4},{6,5},{7,6},{8,7},{9,8},{10,9},{11,1... | collective-permute-start | bytes 98312 | tf_op jit(solution)/shard_map/ppermute | solution.py:70
  79.8 8.3 %collective-permute-start.6 = (f32[1,2,2,32,64]{4,3,2,1,0:T(8,128)S(1)}, f32[1,2,2,32,64]{4,3,2,1,0:T(8,128)S(1)}, u32[]{:S(2)}, u32[]{:S(2)}) collective-permute-start(f32[1,2,2,32,64]{4,3,2,1,0:T(8,128)S(1)} %maximum_bitcast_fusion), channel_id=1, source_target_pairs={{0,1},{1,2},{2,3},{3,4},{4,5},{5,6},{6,7},{7,8},{8,9},{9,10},{10,1... | collective-permute-start | bytes 98312 | tf_op jit(solution)/shard_map/ppermute | solution.py:70
  88.1 8.5 %collective-permute-start.10 = (f32[2,2,2,32,64]{4,3,2,1,0:T(8,128)S(1)}, f32[2,2,2,32,64]{4,3,2,1,0:T(8,128)S(1)}, u32[]{:S(2)}, u32[]{:S(2)}) collective-permute-start(f32[2,2,2,32,64]{4,3,2,1,0:T(8,128)S(1)} %get-tuple-element.30), channel_id=1, source_target_pairs={{2,0},{3,1},{4,2},{5,3},{6,4},{7,5},{8,6},{9,7},{10,8},{11,9},{12,... | collective-permute-start | bytes 196616 | tf_op jit(solution)/shard_map/ppermute | solution.py:70
  90.1 9.3 %collective-permute-start.7 = (f32[2,2,2,32,64]{4,3,2,1,0:T(8,128)S(1)}, f32[2,2,2,32,64]{4,3,2,1,0:T(8,128)S(1)}, u32[]{:S(2)}, u32[]{:S(2)}) collective-permute-start(f32[2,2,2,32,64]{4,3,2,1,0:T(8,128)S(1)} %get-tuple-element.31), channel_id=1, source_target_pairs={{0,2},{1,3},{2,4},{3,5},{4,6},{5,7},{6,8},{7,9},{8,10},{9,11},{10,... | collective-permute-start | bytes 196616 | tf_op jit(solution)/shard_map/ppermute | solution.py:70
  99.4 20.6 %collective-permute-start.8 = (f32[4,2,2,32,64]{4,3,2,1,0:T(8,128)S(1)}, f32[4,2,2,32,64]{4,3,2,1,0:T(8,128)S(1)}, u32[]{:S(2)}, u32[]{:S(2)}) collective-permute-start(f32[4,2,2,32,64]{4,3,2,1,0:T(8,128)S(1)} %get-tuple-element.29), channel_id=1, source_target_pairs={{0,4},{1,5},{2,6},{3,7},{4,8},{5,9},{6,10},{7,11},{8,12},{9,13},{1... | collective-permute-start | bytes 393224 | tf_op jit(solution)/shard_map/ppermute | solution.py:70
  117.3 10.4 %collective-permute-start.11 = (f32[4,2,2,32,64]{4,3,2,1,0:T(8,128)S(1)}, f32[4,2,2,32,64]{4,3,2,1,0:T(8,128)S(1)}, u32[]{:S(2)}, u32[]{:S(2)}) collective-permute-start(f32[4,2,2,32,64]{4,3,2,1,0:T(8,128)S(1)} %get-tuple-element.28), channel_id=1, source_target_pairs={{4,0},{5,1},{6,2},{7,3},{8,4},{9,5},{10,6},{11,7},{12,8},{13,9},{1... | collective-permute-start | bytes 393224 | tf_op jit(solution)/shard_map/ppermute | solution.py:70
  134.5 3.6 %copy-start.30 = (f32[11,17,32]{2,1,0:T(8,128)S(1)}, f32[11,17,32]{2,1,0:T(8,128)}, u32[]{:S(2)}) copy-start(f32[11,17,32]{2,1,0:T(8,128)} %fusion.150) | copy-start | bytes 71812
  134.5 3.6 %copy-start.48 = (pred[7]{0:T(512)(128)(4,1)S(1)}, pred[7]{0:T(512)(128)(4,1)}, u32[]{:S(2)}) copy-start(pred[7]{0:T(512)(128)(4,1)} %compare_and_fusion.2) | copy-start | bytes 25
  134.5 3.8 %copy-start.40 = (f32[32,64,1]{1,0,2:T(8,128)S(1)}, f32[32,64,1]{1,0,2:T(8,128)}, u32[]{:S(2)}) copy-start(f32[32,64,1]{1,0,2:T(8,128)} %constant.363) | copy-start | bytes 24580
  134.5 3.8 %copy-start.52 = (pred[5]{0:T(512)(128)(4,1)S(1)}, pred[5]{0:T(512)(128)(4,1)}, u32[]{:S(2)}) copy-start(pred[5]{0:T(512)(128)(4,1)} %compare_and_fusion.3) | copy-start | bytes 19
  145.7 3.2 %copy-start.42 = (pred[10]{0:T(512)(128)(4,1)S(1)}, pred[10]{0:T(512)(128)(4,1)}, u32[]{:S(2)}) copy-start(pred[10]{0:T(512)(128)(4,1)} %compare_and_fusion.15) | copy-start | bytes 34
  (41 other events, 66.5 us)

commit v5 on v4

--- a/solution.py
+++ b/solution.py
@@ -152,7 +152,17 @@
     coarse_total = cz * slabs
     fine_total = fz * slabs
 
-    ext = jnp.concatenate([shift_from(own, 1), own, shift_from(own, -1)], axis=0)
+    crow = cz * cy * cx // fx
+
+    def pack(source_part):
+        return jnp.concatenate([own.astype(jnp.float32).reshape(crow, fx),
+                                source_part.reshape(-1, fx)], axis=0)
+
+    got_l = shift_from(pack(source[fz - F0_HALO:]), 1)
+    got_r = shift_from(pack(source[:F0_HALO]), -1)
+    coarse_l = got_l[:crow].reshape(cz, cy, cx).astype(own.dtype)
+    coarse_r = got_r[:crow].reshape(cz, cy, cx).astype(own.dtype)
+    ext = jnp.concatenate([coarse_l, own, coarse_r], axis=0)
     n_ext = ext.shape[0]
     g0 = s * cz - COARSE_HALO
     gidx = g0 + jnp.arange(n_ext, dtype=jnp.int32)
@@ -189,8 +199,8 @@
 
     h0k = F0_HALO + 1
     lvl0 = Level(k0[k0_halo - h0k: k0_halo + fz + h0k], h0k, fz, s * fz - h0k, fine_total)
-    f0 = jnp.concatenate([shift_from(source[fz - F0_HALO:], 1), source,
-                          shift_from(source[:F0_HALO], -1)], axis=0)
+    f0 = jnp.concatenate([got_l[crow:].reshape(F0_HALO, fy, fx), source,
+                          got_r[crow:].reshape(F0_HALO, fy, fx)], axis=0)
     u = lvl0.start(f0, F0_HALO)
     u1 = lvl0.sweep(u, lvl0.cut(f0, F0_HALO - 1, F0_HALO), F0_HALO)
     res0 = f0[F0_HALO:F0_HALO + fz] - lvl0.operate(u1[1:-1], 1)

time: 158 us -> 150 us (0.949)
  starting transfers between devices: 58.8 us -> 48.4 us
  waiting for transfers between devices: 18.8 us -> 24.1 us
  local copies, waits for them, and re-layouts: 18.5 us -> 16.8 us
    ppermute x12 -> x10, starting transfers between devices: 58.8 us -> 48.4 us  [shift_from(): return lax.ppermute(block, 'slab', pairs)]
    ppermute x12 -> x10, waiting for transfers between devices: 18.8 us -> 24.1 us  [shift_from(): return lax.ppermute(block, 'slab', pairs)]
    and x17 -> x15, other arithmetic: 6.85 us -> 6.19 us  [plane_mask(): return ((g >= 0) & (g < total))[:, None, None]]
    unnamed x113 -> x119, local copies, waits for them, and re-layouts: 9.95 us -> 9.59 us
  transfers between devices with their start and end apart: 12 -> 10, of which waited for: 7 -> 9; matrix products, arithmetic and copies ran while one was open for 21% -> 7% of each run, Pallas kernels for 0% -> 0%
where the time goes in v5:
time: 150 us; the launch traced here: 149 us
  starting transfers between devices  48.4 us (32%)
  other arithmetic  33.5 us (22%)
  waiting for transfers between devices  24.1 us (16%)
  matrix products  20.6 us (14%)
  local copies, waits for them, and re-layouts  16.8 us (11%)
  between operations  3.4 us (2%)
  blocking collectives  2.18 us (1%)
    ppermute x10, starting transfers between devices, shift_from(): return lax.ppermute(block, 'slab', pairs)  48.4 us
    ppermute x10, waiting for transfers between devices, shift_from(): return lax.ppermute(block, 'slab', pairs)  24.1 us
    select_n x11, other arithmetic, mask(): jnp.where(plane_mask(self.first + self.halo - h, u.shape[0], self.total),...  11.2 us
    unnamed x119, local copies, waits for them, and re-layouts  9.59 us
    dot_general x10, matrix products, along_y(): jnp.einsum('zyx,yv->zvx', values, jnp.asarray(matrix), precision=precisio...  9.03 us
    and x15, other arithmetic, plane_mask(): return ((g >= 0) & (g < total))[:, None, None]  6.19 us
    reduce_sum x6, other arithmetic, restrict_sum(): values = values.reshape(nz // 2, 2, ny, nx).sum(axis=1)  4.78 us
    dot_general x1, matrix products, on_device(): jnp.dot(along_rows.reshape(k0_planes * fy, MX), cols_table, precision=HI)  4.67 us
  transfers between devices with their start and end apart: 10, of which 9 were waited for; matrix products, arithmetic and copies ran while one was open for 7% of the time, Pallas kernels for 0%

profile of v5, /device:TPU:24, one launch (start us, length us, event | category | flops | bytes accessed | tf_op | source)
XLA Modules:
  0.0 148.9 jit_solution(79704125385860443)
XLA Ops:
  4.1 2.2 %all_gather.3 = bf16[8,4,64,128]{3,2,1,0:T(8,128)(2,1)S(1)} all-gather(bf16[4,4,64,128]{3,2,1,0:T(8,128)(2,1)S(1)} %gather_fusion), channel_id=1, replica_groups=mesh['chain'=2,'slab'=64] {'chain'}, dimensions={0}, use_global_device_ids=true | all-gather | bytes 786432 | tf_op jit(solution)/shard_map/all_gather | solution.py:146
  7.2 3.5 %collective-permute-start = (f32[512,256]{1,0:T(8,128)S(1)}, f32[512,256]{1,0:T(8,128)S(1)}, u32[]{:S(2)}, u32[]{:S(2)}) collective-permute-start(f32[512,256]{1,0:T(8,128)S(1)} %get-tuple-element.30), channel_id=1, source_target_pairs={{0,1},{1,2},{2,3},{3,4},{4,5},{5,6},{6,7},{7,8},{8,9},{9,10},{10,1... | collective-permute-start | bytes 1572872 | tf_op jit(solution)/shard_map/ppermute | solution.py:70
  10.8 4.6 %collective-permute-start.1 = (f32[512,256]{1,0:T(8,128)S(1)}, f32[512,256]{1,0:T(8,128)S(1)}, u32[]{:S(2)}, u32[]{:S(2)}) collective-permute-start(f32[512,256]{1,0:T(8,128)S(1)} %get-tuple-element.31), channel_id=1, source_target_pairs={{1,0},{2,1},{3,2},{4,3},{5,4},{6,5},{7,6},{8,7},{9,8},{10,9},{11,1... | collective-permute-start | bytes 1572872 | tf_op jit(solution)/shard_map/ppermute | solution.py:70
  20.4 2.1 %convolution_bitcast_fusion.3 = f32[20,128,64]{1,2,0:T(8,128)} fusion(f32[20,16,64]{2,0,1:T(8,128)S(1)} %fusion.123, s32[128]{0:T(128)S(1)} %multiply_add_fusion.2, s32[16]{0:T(128)S(1)} %iota_add_fusion.2), kind=kOutput, calls=%fused_computation.76 | convolution fusion | flops 31485952 | bytes 737856 | tf_op jit(solution)/shard_map/zbe,by->zye/dot_general | solution.py:188
  22.4 2.9 %collective-permute-done = f32[512,256]{1,0:T(8,128)S(1)} collective-permute-done((f32[512,256]{1,0:T(8,128)S(1)}, f32[512,256]{1,0:T(8,128)S(1)}, u32[]{:S(2)}, u32[]{:S(2)}) %collective-permute-start) | collective-permute-done | bytes 524320 | tf_op jit(solution)/shard_map/ppermute | solution.py:70
  27.7 2.6 %convolution_bitcast_fusion = f32[12,128,256]{1,2,0:T(8,128)S(1)} fusion(f32[12,64,256]{2,1,0:T(8,128)S(1)} %fusion.142, f32[64,128,1]{1,0,2:T(8,128)S(1)} %copy-done.42), kind=kOutput, calls=%fused_computation.47 | convolution fusion | flops 301989888 | bytes 2392064 | tf_op jit(solution)/shard_map/zyx,yv->zvx/dot_general | solution.py:49
  30.8 2.3 %copy.29 = f32[10,2,128,256]{3,2,1,0:T(8,128)} copy(f32[10,2,128,256]{2,3,0,1:T(8,128)S(1)} %pad_maximum_fusion) | data formatting | bytes 5242880 | tf_op jit(solution)/shard_map/stack | solution.py:179
  33.1 4.7 %fusion.3 = f32[20,128,256]{2,1,0:T(8,128)S(1)} fusion(f32[10,2,128,256]{3,2,1,0:T(8,128)} %copy.29, f32[20,128,64]{1,2,0:T(8,128)} %convolution_bitcast_fusion.3, pred[20]{0:T(512)(128)(4,1)S(1)} %compare_and_fusion.12, s32[256]{0:T(256)S(1)} %multiply_add_fusion, s32[64]{0:T(128)S(1)} %iota_add_fusion), kind=kOutput, calls=%fused_computation.8 | convolution fusion | flops 504856576 | bytes 5899540 | tf_op jit(solution)/shard_map/dot_general | solution.py:189
  39.2 2.2 %convolution_bitcast_fusion.2 = f32[10,64,256]{2,1,0:T(8,128)S(1)} fusion(f32[10,128,256]{2,1,0:T(8,128)} %reduce_sum.54, f32[128,64,1]{0,1,2:T(8,128)S(1)} %copy-done.30), kind=kOutput, calls=%fused_computation.75 | convolution fusion | flops 251658240 | bytes 1998848 | tf_op jit(solution)/shard_map/zyx,yv->zvx/dot_general | solution.py:49
  48.4 2.3 %fusion.19 = f32[12,128,256]{2,1,0:T(8,128)S(1)} fusion(f32[12,128,256]{2,1,0:T(8,128)S(1)} %slice.1360, f32[14,128,257]{2,1,0:T(8,128)S(1)} %fusion.1, f32[14,129,256]{2,1,0:T(8,128)S(1)} %add_multiply_fusion, f32[14,128,256]{2,1,0:T(8,128)S(1)} %get-tuple-element.11, f32[15,128,256]{2,1,0:T(8,128)S(1)} %fusion.4, ...), kind=kLoop, calls=%fused_computation.46 | loop fusion | flops 7077888 | bytes 18874380 | tf_op jit(solution)/shard_map/jit(_where)/select_n | solution.py:111
  53.2 3.2 %collective-permute-start.2 = (f32[6,64,128]{2,1,0:T(8,128)S(1)}, f32[6,64,128]{2,1,0:T(8,128)S(1)}, u32[]{:S(2)}, u32[]{:S(2)}) collective-permute-start(f32[6,64,128]{2,1,0:T(8,128)S(1)} %get-tuple-element.28), channel_id=1, source_target_pairs={{0,1},{1,2},{2,3},{3,4},{4,5},{5,6},{6,7},{7,8},{8,9},{9,10},{10,1... | collective-permute-start | bytes 589832 | tf_op jit(solution)/shard_map/ppermute | solution.py:70
  56.4 5.4 %collective-permute-start.3 = (f32[6,64,128]{2,1,0:T(8,128)S(1)}, f32[6,64,128]{2,1,0:T(8,128)S(1)}, u32[]{:S(2)}, u32[]{:S(2)}) collective-permute-start(f32[6,64,128]{2,1,0:T(8,128)S(1)} %get-tuple-element.29), channel_id=1, source_target_pairs={{1,0},{2,1},{3,2},{4,3},{5,4},{6,5},{7,6},{8,7},{9,8},{10,9},{11,1... | collective-permute-start | bytes 589832 | tf_op jit(solution)/shard_map/ppermute | solution.py:70
  67.6 6.5 %collective-permute-start.7 = (f32[1,2,2,32,64]{4,3,2,1,0:T(8,128)S(1)}, f32[1,2,2,32,64]{4,3,2,1,0:T(8,128)S(1)}, u32[]{:S(2)}, u32[]{:S(2)}) collective-permute-start(f32[1,2,2,32,64]{4,3,2,1,0:T(8,128)S(1)} %maximum_bitcast_fusion), channel_id=1, source_target_pairs={{1,0},{2,1},{3,2},{4,3},{5,4},{6,5},{7,6},{8,7},{9,8},{10,9},{11,1... | collective-permute-start | bytes 98312 | tf_op jit(solution)/shard_map/ppermute | solution.py:70
  74.1 1.9 %collective-permute-start.4 = (f32[1,2,2,32,64]{4,3,2,1,0:T(8,128)S(1)}, f32[1,2,2,32,64]{4,3,2,1,0:T(8,128)S(1)}, u32[]{:S(2)}, u32[]{:S(2)}) collective-permute-start(f32[1,2,2,32,64]{4,3,2,1,0:T(8,128)S(1)} %maximum_bitcast_fusion), channel_id=1, source_target_pairs={{0,1},{1,2},{2,3},{3,4},{4,5},{5,6},{6,7},{7,8},{8,9},{9,10},{10,1... | collective-permute-start | bytes 98312 | tf_op jit(solution)/shard_map/ppermute | solution.py:70
  76.6 5.7 %collective-permute-done.4 = f32[1,2,2,32,64]{4,3,2,1,0:T(8,128)S(1)} collective-permute-done((f32[1,2,2,32,64]{4,3,2,1,0:T(8,128)S(1)}, f32[1,2,2,32,64]{4,3,2,1,0:T(8,128)S(1)}, u32[]{:S(2)}, u32[]{:S(2)}) %collective-permute-start.4) | collective-permute-done | bytes 32800 | tf_op jit(solution)/shard_map/ppermute | solution.py:70
  82.4 1.9 %collective-permute-start.8 = (f32[2,2,2,32,64]{4,3,2,1,0:T(8,128)S(1)}, f32[2,2,2,32,64]{4,3,2,1,0:T(8,128)S(1)}, u32[]{:S(2)}, u32[]{:S(2)}) collective-permute-start(f32[2,2,2,32,64]{4,3,2,1,0:T(8,128)S(1)} %get-tuple-element.35), channel_id=1, source_target_pairs={{2,0},{3,1},{4,2},{5,3},{6,4},{7,5},{8,6},{9,7},{10,8},{11,9},{12,... | collective-permute-start | bytes 196616 | tf_op jit(solution)/shard_map/ppermute | solution.py:70
  84.3 5.4 %collective-permute-start.5 = (f32[2,2,2,32,64]{4,3,2,1,0:T(8,128)S(1)}, f32[2,2,2,32,64]{4,3,2,1,0:T(8,128)S(1)}, u32[]{:S(2)}, u32[]{:S(2)}) collective-permute-start(f32[2,2,2,32,64]{4,3,2,1,0:T(8,128)S(1)} %get-tuple-element.36), channel_id=1, source_target_pairs={{0,2},{1,3},{2,4},{3,5},{4,6},{5,7},{6,8},{7,9},{8,10},{9,11},{10,... | collective-permute-start | bytes 196616 | tf_op jit(solution)/shard_map/ppermute | solution.py:70
  90.8 2.8 %collective-permute-done.5 = f32[2,2,2,32,64]{4,3,2,1,0:T(8,128)S(1)} collective-permute-done((f32[2,2,2,32,64]{4,3,2,1,0:T(8,128)S(1)}, f32[2,2,2,32,64]{4,3,2,1,0:T(8,128)S(1)}, u32[]{:S(2)}, u32[]{:S(2)}) %collective-permute-start.5) | collective-permute-done | bytes 65568 | tf_op jit(solution)/shard_map/ppermute | solution.py:70
  93.7 14.0 %collective-permute-start.6 = (f32[4,2,2,32,64]{4,3,2,1,0:T(8,128)S(1)}, f32[4,2,2,32,64]{4,3,2,1,0:T(8,128)S(1)}, u32[]{:S(2)}, u32[]{:S(2)}) collective-permute-start(f32[4,2,2,32,64]{4,3,2,1,0:T(8,128)S(1)} %get-tuple-element.34), channel_id=1, source_target_pairs={{0,4},{1,5},{2,6},{3,7},{4,8},{5,9},{6,10},{7,11},{8,12},{9,13},{1... | collective-permute-start | bytes 393224 | tf_op jit(solution)/shard_map/ppermute | solution.py:70
  109.0 1.9 %collective-permute-start.9 = (f32[4,2,2,32,64]{4,3,2,1,0:T(8,128)S(1)}, f32[4,2,2,32,64]{4,3,2,1,0:T(8,128)S(1)}, u32[]{:S(2)}, u32[]{:S(2)}) collective-permute-start(f32[4,2,2,32,64]{4,3,2,1,0:T(8,128)S(1)} %get-tuple-element.33), channel_id=1, source_target_pairs={{4,0},{5,1},{6,2},{7,3},{8,4},{9,5},{10,6},{11,7},{12,8},{13,9},{1... | collective-permute-start | bytes 393224 | tf_op jit(solution)/shard_map/ppermute | solution.py:70
  111.7 7.6 %collective-permute-done.9 = f32[4,2,2,32,64]{4,3,2,1,0:T(8,128)S(1)} collective-permute-done((f32[4,2,2,32,64]{4,3,2,1,0:T(8,128)S(1)}, f32[4,2,2,32,64]{4,3,2,1,0:T(8,128)S(1)}, u32[]{:S(2)}, u32[]{:S(2)}) %collective-permute-start.9) | collective-permute-done | bytes 131104 | tf_op jit(solution)/shard_map/ppermute | solution.py:70
  138.5 2.0 %bitcast_add_fusion.1 = f32[12,128,256]{2,1,0:T(8,128)S(1)} fusion(f32[12,128,256]{2,1,0:T(8,128)} %copy-done.8, f32[6,128,256]{2,1,0:T(8,128)} %copy.32), kind=kLoop, calls=%fused_computation.45 | loop fusion | flops 393216 | bytes 3932160 | tf_op jit(solution)/shard_map/add | solution.py:253
  142.4 3.1 %fusion.38 = f32[10,128,256]{2,1,0:T(8,128)S(1)} fusion(f32[10,128,256]{2,1,0:T(8,128)S(1)} %slice.1538, f32[14,128,257]{2,1,0:T(8,128)S(1)} %copy-done.5, f32[14,129,256]{2,1,0:T(8,128)S(1)} %add_multiply_fusion, f32[12,128,256]{2,1,0:T(8,128)S(1)} %bitcast_add_fusion.1, f32[15,128,256]{2,1,0:T(8,128)S(1)} %copy-done.3, f32[14,128,256]{2,1,0:T(8,128)S(1)} %copy-done.7, ...), kind=kLoop, calls=%fused_computation.73 | loop fusion | flops 5898240 | bytes 15728650 | tf_op jit(solution)/shard_map/jit(_where)/select_n | solution.py:111
  146.7 2.2 %select_bitcast_fusion = f32[1,8,128,256]{3,2,1,0:T(8,128)} fusion(f32[8,128,256]{2,1,0:T(8,128)S(1)} %slice.1549, f32[8,128,256]{2,1,0:T(8,128)S(1)} %copy-done.15, f32[10,128,256]{2,1,0:T(8,128)S(1)} %fusion.38, f32[14,128,257]{2,1,0:T(8,128)S(1)} %copy-done.5, f32[14,129,256]{2,1,0:T(8,128)S(1)} %add_multiply_fusion, f32[15,128,256]{2,1,0:T(8,128)S(1)} %copy-done.3, ...), kind=kLoop, calls=%fused_computation.125 | loop fusion | flops 4718592 | bytes 12582920 | tf_op jit(solution)/shard_map/broadcast_in_dim | solution.py:256
  (251 shorter events, 52.3 us)
Async XLA Ops:
  0.0 3.5 %copy-start = (bf16[4,4,4,64,128]{4,3,2,1,0:T(8,128)(2,1)S(1)}, bf16[4,4,4,64,128]{4,3,2,1,0:T(8,128)(2,1)}, u32[]{:S(2)}) copy-start(bf16[4,4,4,64,128]{4,3,2,1,0:T(8,128)(2,1)} %param.25) | copy-start | bytes 3145732
  0.0 7.0 %copy-start.13 = (f32[8,128,256]{2,1,0:T(8,128)S(1)}, f32[8,128,256]{2,1,0:T(8,128)}, u32[]{:S(2)}) copy-start(f32[8,128,256]{2,1,0:T(8,128)} %param.29) | copy-start | bytes 3145732
  7.1 12.8 %copy-start.38 = (f32[1,32,16,64]{3,2,1,0:T(8,128)S(1)}, f32[1,32,16,64]{3,2,1,0:T(8,128)}, u32[]{:S(2)}) copy-start(f32[1,32,16,64]{3,2,1,0:T(8,128)} %param.28) | copy-start | bytes 393220
  7.2 20.1 %copy-start.41 = (bf16[128,256,1]{1,0,2:T(8,128)(2,1)S(1)}, bf16[128,256,1]{1,0,2:T(8,128)(2,1)}, u32[]{:S(2)}) copy-start(bf16[128,256,1]{1,0,2:T(8,128)(2,1)} %constant.357) | copy-start | bytes 196612
  7.2 18.1 %collective-permute-start = (f32[512,256]{1,0:T(8,128)S(1)}, f32[512,256]{1,0:T(8,128)S(1)}, u32[]{:S(2)}, u32[]{:S(2)}) collective-permute-start(f32[512,256]{1,0:T(8,128)S(1)} %get-tuple-element.30), channel_id=1, source_target_pairs={{0,1},{1,2},{2,3},{3,4},{4,5},{5,6},{6,7},{7,8},{8,9},{9,10},{10,1... | collective-permute-start | bytes 1572872 | tf_op jit(solution)/shard_map/ppermute | solution.py:70
  10.8 15.7 %collective-permute-start.1 = (f32[512,256]{1,0:T(8,128)S(1)}, f32[512,256]{1,0:T(8,128)S(1)}, u32[]{:S(2)}, u32[]{:S(2)}) collective-permute-start(f32[512,256]{1,0:T(8,128)S(1)} %get-tuple-element.31), channel_id=1, source_target_pairs={{1,0},{2,1},{3,2},{4,3},{5,4},{6,5},{7,6},{8,7},{9,8},{10,9},{11,1... | collective-permute-start | bytes 1572872 | tf_op jit(solution)/shard_map/ppermute | solution.py:70
  19.9 7.8 %copy-start.42 = (f32[64,128,1]{1,0,2:T(8,128)S(1)}, f32[64,128,1]{1,0,2:T(8,128)}, u32[]{:S(2)}) copy-start(f32[64,128,1]{1,0,2:T(8,128)} %constant.358) | copy-start | bytes 98308
  43.0 7.8 %copy-start.2 = (f32[15,128,256]{2,1,0:T(8,128)}, f32[15,128,256]{2,1,0:T(8,128)S(1)}, u32[]{:S(2)}) copy-start(f32[15,128,256]{2,1,0:T(8,128)S(1)} %fusion.4) | copy-start | bytes 5898244
  44.7 6.2 %copy-start.4 = (f32[14,128,257]{2,1,0:T(8,128)}, f32[14,128,257]{2,1,0:T(8,128)S(1)}, u32[]{:S(2)}) copy-start(f32[14,128,257]{2,1,0:T(8,128)S(1)} %fusion.1) | copy-start | bytes 5526532
  52.3 9.5 %copy-start.37 = (f32[64,32,1]{0,1,2:T(8,128)S(1)}, f32[64,32,1]{0,1,2:T(8,128)}, u32[]{:S(2)}) copy-start(f32[64,32,1]{0,1,2:T(8,128)} %constant.361) | copy-start | bytes 24580
  53.2 10.6 %collective-permute-start.2 = (f32[6,64,128]{2,1,0:T(8,128)S(1)}, f32[6,64,128]{2,1,0:T(8,128)S(1)}, u32[]{:S(2)}, u32[]{:S(2)}) collective-permute-start(f32[6,64,128]{2,1,0:T(8,128)S(1)} %get-tuple-element.28), channel_id=1, source_target_pairs={{0,1},{1,2},{2,3},{3,4},{4,5},{5,6},{6,7},{7,8},{8,9},{9,10},{10,1... | collective-permute-start | bytes 589832 | tf_op jit(solution)/shard_map/ppermute | solution.py:70
  56.4 8.5 %collective-permute-start.3 = (f32[6,64,128]{2,1,0:T(8,128)S(1)}, f32[6,64,128]{2,1,0:T(8,128)S(1)}, u32[]{:S(2)}, u32[]{:S(2)}) collective-permute-start(f32[6,64,128]{2,1,0:T(8,128)S(1)} %get-tuple-element.29), channel_id=1, source_target_pairs={{1,0},{2,1},{3,2},{4,3},{5,4},{6,5},{7,6},{8,7},{9,8},{10,9},{11,1... | collective-permute-start | bytes 589832 | tf_op jit(solution)/shard_map/ppermute | solution.py:70
  67.6 9.0 %collective-permute-start.7 = (f32[1,2,2,32,64]{4,3,2,1,0:T(8,128)S(1)}, f32[1,2,2,32,64]{4,3,2,1,0:T(8,128)S(1)}, u32[]{:S(2)}, u32[]{:S(2)}) collective-permute-start(f32[1,2,2,32,64]{4,3,2,1,0:T(8,128)S(1)} %maximum_bitcast_fusion), channel_id=1, source_target_pairs={{1,0},{2,1},{3,2},{4,3},{5,4},{6,5},{7,6},{8,7},{9,8},{10,9},{11,1... | collective-permute-start | bytes 98312 | tf_op jit(solution)/shard_map/ppermute | solution.py:70
  74.1 8.3 %collective-permute-start.4 = (f32[1,2,2,32,64]{4,3,2,1,0:T(8,128)S(1)}, f32[1,2,2,32,64]{4,3,2,1,0:T(8,128)S(1)}, u32[]{:S(2)}, u32[]{:S(2)}) collective-permute-start(f32[1,2,2,32,64]{4,3,2,1,0:T(8,128)S(1)} %maximum_bitcast_fusion), channel_id=1, source_target_pairs={{0,1},{1,2},{2,3},{3,4},{4,5},{5,6},{6,7},{7,8},{8,9},{9,10},{10,1... | collective-permute-start | bytes 98312 | tf_op jit(solution)/shard_map/ppermute | solution.py:70
  82.4 8.4 %collective-permute-start.8 = (f32[2,2,2,32,64]{4,3,2,1,0:T(8,128)S(1)}, f32[2,2,2,32,64]{4,3,2,1,0:T(8,128)S(1)}, u32[]{:S(2)}, u32[]{:S(2)}) collective-permute-start(f32[2,2,2,32,64]{4,3,2,1,0:T(8,128)S(1)} %get-tuple-element.35), channel_id=1, source_target_pairs={{2,0},{3,1},{4,2},{5,3},{6,4},{7,5},{8,6},{9,7},{10,8},{11,9},{12,... | collective-permute-start | bytes 196616 | tf_op jit(solution)/shard_map/ppermute | solution.py:70
  84.3 9.3 %collective-permute-start.5 = (f32[2,2,2,32,64]{4,3,2,1,0:T(8,128)S(1)}, f32[2,2,2,32,64]{4,3,2,1,0:T(8,128)S(1)}, u32[]{:S(2)}, u32[]{:S(2)}) collective-permute-start(f32[2,2,2,32,64]{4,3,2,1,0:T(8,128)S(1)} %get-tuple-element.36), channel_id=1, source_target_pairs={{0,2},{1,3},{2,4},{3,5},{4,6},{5,7},{6,8},{7,9},{8,10},{9,11},{10,... | collective-permute-start | bytes 196616 | tf_op jit(solution)/shard_map/ppermute | solution.py:70
  93.7 17.9 %collective-permute-start.6 = (f32[4,2,2,32,64]{4,3,2,1,0:T(8,128)S(1)}, f32[4,2,2,32,64]{4,3,2,1,0:T(8,128)S(1)}, u32[]{:S(2)}, u32[]{:S(2)}) collective-permute-start(f32[4,2,2,32,64]{4,3,2,1,0:T(8,128)S(1)} %get-tuple-element.34), channel_id=1, source_target_pairs={{0,4},{1,5},{2,6},{3,7},{4,8},{5,9},{6,10},{7,11},{8,12},{9,13},{1... | collective-permute-start | bytes 393224 | tf_op jit(solution)/shard_map/ppermute | solution.py:70
  109.0 10.4 %collective-permute-start.9 = (f32[4,2,2,32,64]{4,3,2,1,0:T(8,128)S(1)}, f32[4,2,2,32,64]{4,3,2,1,0:T(8,128)S(1)}, u32[]{:S(2)}, u32[]{:S(2)}) collective-permute-start(f32[4,2,2,32,64]{4,3,2,1,0:T(8,128)S(1)} %get-tuple-element.33), channel_id=1, source_target_pairs={{4,0},{5,1},{6,2},{7,3},{8,4},{9,5},{10,6},{11,7},{12,8},{13,9},{1... | collective-permute-start | bytes 393224 | tf_op jit(solution)/shard_map/ppermute | solution.py:70
  126.1 3.6 %copy-start.29 = (f32[11,17,32]{2,1,0:T(8,128)S(1)}, f32[11,17,32]{2,1,0:T(8,128)}, u32[]{:S(2)}) copy-start(f32[11,17,32]{2,1,0:T(8,128)} %fusion.150) | copy-start | bytes 71812
  126.1 3.6 %copy-start.53 = (pred[7]{0:T(512)(128)(4,1)S(1)}, pred[7]{0:T(512)(128)(4,1)}, u32[]{:S(2)}) copy-start(pred[7]{0:T(512)(128)(4,1)} %compare_and_fusion.2) | copy-start | bytes 25
  126.1 3.8 %copy-start.44 = (f32[32,64,1]{1,0,2:T(8,128)S(1)}, f32[32,64,1]{1,0,2:T(8,128)}, u32[]{:S(2)}) copy-start(f32[32,64,1]{1,0,2:T(8,128)} %constant.363) | copy-start | bytes 24580
  126.1 3.8 %copy-start.56 = (pred[5]{0:T(512)(128)(4,1)S(1)}, pred[5]{0:T(512)(128)(4,1)}, u32[]{:S(2)}) copy-start(pred[5]{0:T(512)(128)(4,1)} %compare_and_fusion.3) | copy-start | bytes 19
  128.5 2.9 %copy-start.21 = (f32[26,32,64]{2,1,0:T(8,128)S(1)}, f32[26,32,64]{2,1,0:T(8,128)}, u32[]{:S(2)}) copy-start(f32[26,32,64]{2,1,0:T(8,128)} %copy-done.20) | copy-start | bytes 638980
  138.5 3.0 %copy-start.7 = (f32[14,128,256]{2,1,0:T(8,128)S(1)}, f32[14,128,256]{2,1,0:T(8,128)}, u32[]{:S(2)}) copy-start(f32[14,128,256]{2,1,0:T(8,128)} %copy-done.6) | copy-start | bytes 5505028
  (43 other events, 66.3 us)

commit v6 on v5

--- a/solution.py
+++ b/solution.py
@@ -188,6 +188,7 @@
     along_rows = jnp.einsum("zbe,by->zye", along_depth, rows_table, precision=HI)
     kl = jnp.dot(along_rows.reshape(k0_planes * fy, MX), cols_table,
                  precision=HI).reshape(k0_planes, fy, fx)
+    kl = lax.optimization_barrier(kl)
     k0 = jnp.exp(log_perm + kl)
     k0 = jnp.where(plane_mask(k0_first, k0_planes, fine_total), k0, 0.0)
     k0_halo = (k0_planes - fz) // 2

time: 150 us -> 152 us (1.013)
  other arithmetic: 33.5 us -> 40.5 us
  waiting for transfers between devices: 24.1 us -> 20.8 us
    select_n x11, other arithmetic: 11.2 us -> 14.6 us  [mask(): jnp.where(plane_mask(self.first + self.halo - h, u.shape[0], self.total),...]
    ppermute x10, waiting for transfers between devices: 24.1 us -> 20.8 us  [shift_from(): return lax.ppermute(block, 'slab', pairs)]
    select_n x0 -> x1, other arithmetic: none -> 3.09 us  [on_device(): k0 = jnp.where(plane_mask(k0_first, k0_planes, fine_total), k0, 0.0)]
    unnamed x119 -> x113, local copies, waits for them, and re-layouts: 9.59 us -> 7.94 us
  transfers between devices with their start and end apart: 10 -> 10, of which waited for: 9 -> 8; matrix products, arithmetic and copies ran while one was open for 7% -> 9% of each run, Pallas kernels for 0% -> 0%
where the time goes in v6:
time: 152 us; the launch traced here: 151 us
  starting transfers between devices  48.3 us (32%)
  other arithmetic  40.5 us (27%)
  waiting for transfers between devices  20.8 us (14%)
  matrix products  20 us (13%)
  local copies, waits for them, and re-layouts  15.8 us (10%)
  between operations  3.41 us (2%)
  blocking collectives  2.18 us (1%)
    ppermute x10, starting transfers between devices, shift_from(): return lax.ppermute(block, 'slab', pairs)  48.3 us
    ppermute x10, waiting for transfers between devices, shift_from(): return lax.ppermute(block, 'slab', pairs)  20.8 us
    select_n x11, other arithmetic, mask(): jnp.where(plane_mask(self.first + self.halo - h, u.shape[0], self.total),...  14.6 us
    dot_general x10, matrix products, along_y(): jnp.einsum('zyx,yv->zvx', values, jnp.asarray(matrix), precision=precisio...  9.03 us
    unnamed x113, local copies, waits for them, and re-layouts  7.94 us
    and x15, other arithmetic, plane_mask(): return ((g >= 0) & (g < total))[:, None, None]  6.3 us
    dot_general x10, matrix products, along_x(): jnp.einsum('zyx,xw->zyw', values, jnp.asarray(matrix), precision=precisio...  5.26 us
    reduce_sum x6, other arithmetic, restrict_sum(): values = values.reshape(nz // 2, 2, ny, nx).sum(axis=1)  4.6 us
  transfers between devices with their start and end apart: 10, of which 8 were waited for; matrix products, arithmetic and copies ran while one was open for 9% of the time, Pallas kernels for 0%

profile of v6, /device:TPU:24, one launch (start us, length us, event | category | flops | bytes accessed | tf_op | source)
XLA Modules:
  0.0 151.0 jit_solution(12175617952327691204)
XLA Ops:
  4.1 2.2 %all_gather.3 = bf16[8,4,64,128]{3,2,1,0:T(8,128)(2,1)S(1)} all-gather(bf16[4,4,64,128]{3,2,1,0:T(8,128)(2,1)S(1)} %gather_fusion), channel_id=1, replica_groups=mesh['chain'=2,'slab'=64] {'chain'}, dimensions={0}, use_global_device_ids=true | all-gather | bytes 786432 | tf_op jit(solution)/shard_map/all_gather | solution.py:146
  7.2 3.4 %collective-permute-start = (f32[512,256]{1,0:T(8,128)S(1)}, f32[512,256]{1,0:T(8,128)S(1)}, u32[]{:S(2)}, u32[]{:S(2)}) collective-permute-start(f32[512,256]{1,0:T(8,128)S(1)} %get-tuple-element.30), channel_id=1, source_target_pairs={{0,1},{1,2},{2,3},{3,4},{4,5},{5,6},{6,7},{7,8},{8,9},{9,10},{10,1... | collective-permute-start | bytes 1572872 | tf_op jit(solution)/shard_map/ppermute | solution.py:70
  10.6 4.6 %collective-permute-start.1 = (f32[512,256]{1,0:T(8,128)S(1)}, f32[512,256]{1,0:T(8,128)S(1)}, u32[]{:S(2)}, u32[]{:S(2)}) collective-permute-start(f32[512,256]{1,0:T(8,128)S(1)} %get-tuple-element.31), channel_id=1, source_target_pairs={{1,0},{2,1},{3,2},{4,3},{5,4},{6,5},{7,6},{8,7},{9,8},{10,9},{11,1... | collective-permute-start | bytes 1572872 | tf_op jit(solution)/shard_map/ppermute | solution.py:70
  19.4 4.0 %fusion.212 = f32[20,128,256]{2,1,0:T(8,128)} fusion(f32[20,128,64]{1,2,0:T(8,128)S(1)} %convolution_bitcast_fusion.3, s32[256]{0:T(256)S(1)} %multiply_add_fusion, s32[64]{0:T(128)S(1)} %iota_add_fusion), kind=kOutput, calls=%fused_computation.385 | convolution fusion | flops 503545856 | bytes 3278080 | tf_op jit(solution)/shard_map/dot_general | solution.py:189
  26.8 2.6 %convolution_bitcast_fusion = f32[12,128,256]{1,2,0:T(8,128)S(1)} fusion(f32[12,64,256]{2,1,0:T(8,128)S(1)} %fusion.142, f32[64,128,1]{1,0,2:T(8,128)S(1)} %copy-done.40), kind=kOutput, calls=%fused_computation.47 | convolution fusion | flops 301989888 | bytes 2392064 | tf_op jit(solution)/shard_map/zyx,yv->zvx/dot_general | solution.py:49
  30.0 2.3 %copy.29 = f32[10,2,128,256]{3,2,1,0:T(8,128)} copy(f32[10,2,128,256]{2,3,0,1:T(8,128)S(1)} %pad_maximum_fusion) | data formatting | bytes 5242880 | tf_op jit(solution)/shard_map/stack | solution.py:179
  32.3 3.1 %fusion.3 = f32[20,128,256]{2,1,0:T(8,128)S(1)} fusion(f32[20,128,256]{2,1,0:T(8,128)} %fusion.212, f32[10,2,128,256]{3,2,1,0:T(8,128)} %copy.29, pred[20]{0:T(512)(128)(4,1)S(1)} %compare_and_fusion.12), kind=kLoop, calls=%fused_computation.8 | loop fusion | flops 1310720 | bytes 7864340 | tf_op jit(solution)/shard_map/jit(_where)/select_n | solution.py:193
  36.8 2.2 %convolution_bitcast_fusion.2 = f32[10,64,256]{2,1,0:T(8,128)S(1)} fusion(f32[10,128,256]{2,1,0:T(8,128)} %reduce_sum.54, f32[128,64,1]{0,1,2:T(8,128)S(1)} %copy-done.31), kind=kOutput, calls=%fused_computation.75 | convolution fusion | flops 251658240 | bytes 1998848 | tf_op jit(solution)/shard_map/zyx,yv->zvx/dot_general | solution.py:49
  44.1 2.4 %divide_select_fusion = (f32[14,128,256]{2,1,0:T(8,128)S(1)}, f32[14,128,256]{2,1,0:T(8,128)S(1)}, f32[14,128,256]{2,1,0:T(8,128)}) fusion(pred[14]{0:T(512)(128)(4,1)S(1)} %compare_and_fusion.13, f32[3,128,256]{2,1,0:T(8,128)S(1)} %bitcast.149, f32[8,128,256]{2,1,0:T(8,128)S(1)} %copy-done.14, f32[3,128,256]{2,1,0:T(8,128)S(1)} %bitcast.148, ...), kind=kLoop, calls=%fused_computation.22 | loop fusion | flops 4587520 | bytes 18350094 | tf_op jit(solution)/shard_map/jit(_where)/select_n | solution.py:111
  46.5 3.9 %fusion.19 = f32[12,128,256]{2,1,0:T(8,128)S(1)} fusion(f32[12,128,256]{2,1,0:T(8,128)S(1)} %slice.1360, f32[14,128,257]{2,1,0:T(8,128)S(1)} %fusion.1, f32[14,129,256]{2,1,0:T(8,128)S(1)} %add_multiply_fusion, f32[14,128,256]{2,1,0:T(8,128)S(1)} %get-tuple-element.11, f32[15,128,256]{2,1,0:T(8,128)S(1)} %fusion.4, ...), kind=kLoop, calls=%fused_computation.46 | loop fusion | flops 7077888 | bytes 18874380 | tf_op jit(solution)/shard_map/jit(_where)/select_n | solution.py:111
  52.7 3.2 %collective-permute-start.2 = (f32[6,64,128]{2,1,0:T(8,128)S(1)}, f32[6,64,128]{2,1,0:T(8,128)S(1)}, u32[]{:S(2)}, u32[]{:S(2)}) collective-permute-start(f32[6,64,128]{2,1,0:T(8,128)S(1)} %get-tuple-element.28), channel_id=1, source_target_pairs={{0,1},{1,2},{2,3},{3,4},{4,5},{5,6},{6,7},{7,8},{8,9},{9,10},{10,1... | collective-permute-start | bytes 589832 | tf_op jit(solution)/shard_map/ppermute | solution.py:70
  56.0 5.2 %collective-permute-start.3 = (f32[6,64,128]{2,1,0:T(8,128)S(1)}, f32[6,64,128]{2,1,0:T(8,128)S(1)}, u32[]{:S(2)}, u32[]{:S(2)}) collective-permute-start(f32[6,64,128]{2,1,0:T(8,128)S(1)} %get-tuple-element.29), channel_id=1, source_target_pairs={{1,0},{2,1},{3,2},{4,3},{5,4},{6,5},{7,6},{8,7},{9,8},{10,9},{11,1... | collective-permute-start | bytes 589832 | tf_op jit(solution)/shard_map/ppermute | solution.py:70
  67.1 6.5 %collective-permute-start.7 = (f32[1,2,2,32,64]{4,3,2,1,0:T(8,128)S(1)}, f32[1,2,2,32,64]{4,3,2,1,0:T(8,128)S(1)}, u32[]{:S(2)}, u32[]{:S(2)}) collective-permute-start(f32[1,2,2,32,64]{4,3,2,1,0:T(8,128)S(1)} %maximum_bitcast_fusion), channel_id=1, source_target_pairs={{1,0},{2,1},{3,2},{4,3},{5,4},{6,5},{7,6},{8,7},{9,8},{10,9},{11,1... | collective-permute-start | bytes 98312 | tf_op jit(solution)/shard_map/ppermute | solution.py:70
  73.6 1.9 %collective-permute-start.4 = (f32[1,2,2,32,64]{4,3,2,1,0:T(8,128)S(1)}, f32[1,2,2,32,64]{4,3,2,1,0:T(8,128)S(1)}, u32[]{:S(2)}, u32[]{:S(2)}) collective-permute-start(f32[1,2,2,32,64]{4,3,2,1,0:T(8,128)S(1)} %maximum_bitcast_fusion), channel_id=1, source_target_pairs={{0,1},{1,2},{2,3},{3,4},{4,5},{5,6},{6,7},{7,8},{8,9},{9,10},{10,1... | collective-permute-start | bytes 98312 | tf_op jit(solution)/shard_map/ppermute | solution.py:70
  76.1 5.8 %collective-permute-done.4 = f32[1,2,2,32,64]{4,3,2,1,0:T(8,128)S(1)} collective-permute-done((f32[1,2,2,32,64]{4,3,2,1,0:T(8,128)S(1)}, f32[1,2,2,32,64]{4,3,2,1,0:T(8,128)S(1)}, u32[]{:S(2)}, u32[]{:S(2)}) %collective-permute-start.4) | collective-permute-done | bytes 32800 | tf_op jit(solution)/shard_map/ppermute | solution.py:70
  81.9 1.9 %collective-permute-start.8 = (f32[2,2,2,32,64]{4,3,2,1,0:T(8,128)S(1)}, f32[2,2,2,32,64]{4,3,2,1,0:T(8,128)S(1)}, u32[]{:S(2)}, u32[]{:S(2)}) collective-permute-start(f32[2,2,2,32,64]{4,3,2,1,0:T(8,128)S(1)} %get-tuple-element.35), channel_id=1, source_target_pairs={{2,0},{3,1},{4,2},{5,3},{6,4},{7,5},{8,6},{9,7},{10,8},{11,9},{12,... | collective-permute-start | bytes 196616 | tf_op jit(solution)/shard_map/ppermute | solution.py:70
  83.9 5.4 %collective-permute-start.5 = (f32[2,2,2,32,64]{4,3,2,1,0:T(8,128)S(1)}, f32[2,2,2,32,64]{4,3,2,1,0:T(8,128)S(1)}, u32[]{:S(2)}, u32[]{:S(2)}) collective-permute-start(f32[2,2,2,32,64]{4,3,2,1,0:T(8,128)S(1)} %get-tuple-element.36), channel_id=1, source_target_pairs={{0,2},{1,3},{2,4},{3,5},{4,6},{5,7},{6,8},{7,9},{8,10},{9,11},{10,... | collective-permute-start | bytes 196616 | tf_op jit(solution)/shard_map/ppermute | solution.py:70
  90.3 2.8 %collective-permute-done.5 = f32[2,2,2,32,64]{4,3,2,1,0:T(8,128)S(1)} collective-permute-done((f32[2,2,2,32,64]{4,3,2,1,0:T(8,128)S(1)}, f32[2,2,2,32,64]{4,3,2,1,0:T(8,128)S(1)}, u32[]{:S(2)}, u32[]{:S(2)}) %collective-permute-start.5) | collective-permute-done | bytes 65568 | tf_op jit(solution)/shard_map/ppermute | solution.py:70
  93.2 14.0 %collective-permute-start.6 = (f32[4,2,2,32,64]{4,3,2,1,0:T(8,128)S(1)}, f32[4,2,2,32,64]{4,3,2,1,0:T(8,128)S(1)}, u32[]{:S(2)}, u32[]{:S(2)}) collective-permute-start(f32[4,2,2,32,64]{4,3,2,1,0:T(8,128)S(1)} %get-tuple-element.34), channel_id=1, source_target_pairs={{0,4},{1,5},{2,6},{3,7},{4,8},{5,9},{6,10},{7,11},{8,12},{9,13},{1... | collective-permute-start | bytes 393224 | tf_op jit(solution)/shard_map/ppermute | solution.py:70
  108.4 2.1 %collective-permute-start.9 = (f32[4,2,2,32,64]{4,3,2,1,0:T(8,128)S(1)}, f32[4,2,2,32,64]{4,3,2,1,0:T(8,128)S(1)}, u32[]{:S(2)}, u32[]{:S(2)}) collective-permute-start(f32[4,2,2,32,64]{4,3,2,1,0:T(8,128)S(1)} %get-tuple-element.33), channel_id=1, source_target_pairs={{4,0},{5,1},{6,2},{7,3},{8,4},{9,5},{10,6},{11,7},{12,8},{13,9},{1... | collective-permute-start | bytes 393224 | tf_op jit(solution)/shard_map/ppermute | solution.py:70
  111.2 7.6 %collective-permute-done.9 = f32[4,2,2,32,64]{4,3,2,1,0:T(8,128)S(1)} collective-permute-done((f32[4,2,2,32,64]{4,3,2,1,0:T(8,128)S(1)}, f32[4,2,2,32,64]{4,3,2,1,0:T(8,128)S(1)}, u32[]{:S(2)}, u32[]{:S(2)}) %collective-permute-start.9) | collective-permute-done | bytes 131104 | tf_op jit(solution)/shard_map/ppermute | solution.py:70
  140.6 2.0 %bitcast_add_fusion.1 = f32[12,128,256]{2,1,0:T(8,128)S(1)} fusion(f32[12,128,256]{2,1,0:T(8,128)} %copy-done.8, f32[6,128,256]{2,1,0:T(8,128)} %copy.32), kind=kLoop, calls=%fused_computation.45 | loop fusion | flops 393216 | bytes 3932160 | tf_op jit(solution)/shard_map/add | solution.py:254
  144.4 3.1 %fusion.38 = f32[10,128,256]{2,1,0:T(8,128)S(1)} fusion(f32[10,128,256]{2,1,0:T(8,128)S(1)} %slice.1538, f32[14,128,257]{2,1,0:T(8,128)S(1)} %copy-done.5, f32[14,129,256]{2,1,0:T(8,128)S(1)} %add_multiply_fusion, f32[12,128,256]{2,1,0:T(8,128)S(1)} %bitcast_add_fusion.1, f32[15,128,256]{2,1,0:T(8,128)S(1)} %copy-done.3, f32[14,128,256]{2,1,0:T(8,128)S(1)} %copy-done.7, ...), kind=kLoop, calls=%fused_computation.73 | loop fusion | flops 5898240 | bytes 15728650 | tf_op jit(solution)/shard_map/jit(_where)/select_n | solution.py:111
  148.8 2.2 %select_bitcast_fusion = f32[1,8,128,256]{3,2,1,0:T(8,128)} fusion(f32[8,128,256]{2,1,0:T(8,128)S(1)} %slice.1549, f32[8,128,256]{2,1,0:T(8,128)S(1)} %copy-done.15, f32[10,128,256]{2,1,0:T(8,128)S(1)} %fusion.38, f32[14,128,257]{2,1,0:T(8,128)S(1)} %copy-done.5, f32[14,129,256]{2,1,0:T(8,128)S(1)} %add_multiply_fusion, f32[15,128,256]{2,1,0:T(8,128)S(1)} %copy-done.3, ...), kind=kLoop, calls=%fused_computation.125 | loop fusion | flops 4718592 | bytes 12582920 | tf_op jit(solution)/shard_map/broadcast_in_dim | solution.py:257
  (248 shorter events, 53.1 us)
Async XLA Ops:
  0.0 7.0 %copy-start.13 = (f32[8,128,256]{2,1,0:T(8,128)S(1)}, f32[8,128,256]{2,1,0:T(8,128)}, u32[]{:S(2)}) copy-start(f32[8,128,256]{2,1,0:T(8,128)} %param.29) | copy-start | bytes 3145732
  7.1 10.6 %copy-start.35 = (f32[1,32,16,64]{3,2,1,0:T(8,128)S(1)}, f32[1,32,16,64]{3,2,1,0:T(8,128)}, u32[]{:S(2)}) copy-start(f32[1,32,16,64]{3,2,1,0:T(8,128)} %param.28) | copy-start | bytes 393220
  7.2 18.5 %collective-permute-start = (f32[512,256]{1,0:T(8,128)S(1)}, f32[512,256]{1,0:T(8,128)S(1)}, u32[]{:S(2)}, u32[]{:S(2)}) collective-permute-start(f32[512,256]{1,0:T(8,128)S(1)} %get-tuple-element.30), channel_id=1, source_target_pairs={{0,1},{1,2},{2,3},{3,4},{4,5},{5,6},{6,7},{7,8},{8,9},{9,10},{10,1... | collective-permute-start | bytes 1572872 | tf_op jit(solution)/shard_map/ppermute | solution.py:70
  10.6 15.7 %collective-permute-start.1 = (f32[512,256]{1,0:T(8,128)S(1)}, f32[512,256]{1,0:T(8,128)S(1)}, u32[]{:S(2)}, u32[]{:S(2)}) collective-permute-start(f32[512,256]{1,0:T(8,128)S(1)} %get-tuple-element.31), channel_id=1, source_target_pairs={{1,0},{2,1},{3,2},{4,3},{5,4},{6,5},{7,6},{8,7},{9,8},{10,9},{11,1... | collective-permute-start | bytes 1572872 | tf_op jit(solution)/shard_map/ppermute | solution.py:70
  19.3 7.1 %copy-start.39 = (bf16[128,256,1]{1,0,2:T(8,128)(2,1)S(1)}, bf16[128,256,1]{1,0,2:T(8,128)(2,1)}, u32[]{:S(2)}) copy-start(bf16[128,256,1]{1,0,2:T(8,128)(2,1)} %constant.357) | copy-start | bytes 196612
  25.7 3.8 %copy-start.29 = (f32[512,256]{1,0:T(8,128)}, f32[512,256]{1,0:T(8,128)S(1)}, u32[]{:S(2)}) copy-start(f32[512,256]{1,0:T(8,128)S(1)} %collective-permute-done) | copy-start | bytes 1572868
  40.6 9.9 %copy-start.2 = (f32[15,128,256]{2,1,0:T(8,128)}, f32[15,128,256]{2,1,0:T(8,128)S(1)}, u32[]{:S(2)}) copy-start(f32[15,128,256]{2,1,0:T(8,128)S(1)} %fusion.4) | copy-start | bytes 5898244
  41.7 8.9 %copy-start.4 = (f32[14,128,257]{2,1,0:T(8,128)}, f32[14,128,257]{2,1,0:T(8,128)S(1)}, u32[]{:S(2)}) copy-start(f32[14,128,257]{2,1,0:T(8,128)S(1)} %fusion.1) | copy-start | bytes 5526532
  46.4 4.2 %copy-start.6 = (f32[14,128,256]{2,1,0:T(8,128)}, f32[14,128,256]{2,1,0:T(8,128)S(1)}, u32[]{:S(2)}) copy-start(f32[14,128,256]{2,1,0:T(8,128)S(1)} %get-tuple-element.12) | copy-start | bytes 5505028
  51.8 9.3 %copy-start.34 = (f32[64,32,1]{0,1,2:T(8,128)S(1)}, f32[64,32,1]{0,1,2:T(8,128)}, u32[]{:S(2)}) copy-start(f32[64,32,1]{0,1,2:T(8,128)} %constant.361) | copy-start | bytes 24580
  52.7 10.5 %collective-permute-start.2 = (f32[6,64,128]{2,1,0:T(8,128)S(1)}, f32[6,64,128]{2,1,0:T(8,128)S(1)}, u32[]{:S(2)}, u32[]{:S(2)}) collective-permute-start(f32[6,64,128]{2,1,0:T(8,128)S(1)} %get-tuple-element.28), channel_id=1, source_target_pairs={{0,1},{1,2},{2,3},{3,4},{4,5},{5,6},{6,7},{7,8},{8,9},{9,10},{10,1... | collective-permute-start | bytes 589832 | tf_op jit(solution)/shard_map/ppermute | solution.py:70
  56.0 8.5 %collective-permute-start.3 = (f32[6,64,128]{2,1,0:T(8,128)S(1)}, f32[6,64,128]{2,1,0:T(8,128)S(1)}, u32[]{:S(2)}, u32[]{:S(2)}) collective-permute-start(f32[6,64,128]{2,1,0:T(8,128)S(1)} %get-tuple-element.29), channel_id=1, source_target_pairs={{1,0},{2,1},{3,2},{4,3},{5,4},{6,5},{7,6},{8,7},{9,8},{10,9},{11,1... | collective-permute-start | bytes 589832 | tf_op jit(solution)/shard_map/ppermute | solution.py:70
  67.1 8.9 %collective-permute-start.7 = (f32[1,2,2,32,64]{4,3,2,1,0:T(8,128)S(1)}, f32[1,2,2,32,64]{4,3,2,1,0:T(8,128)S(1)}, u32[]{:S(2)}, u32[]{:S(2)}) collective-permute-start(f32[1,2,2,32,64]{4,3,2,1,0:T(8,128)S(1)} %maximum_bitcast_fusion), channel_id=1, source_target_pairs={{1,0},{2,1},{3,2},{4,3},{5,4},{6,5},{7,6},{8,7},{9,8},{10,9},{11,1... | collective-permute-start | bytes 98312 | tf_op jit(solution)/shard_map/ppermute | solution.py:70
  73.6 8.3 %collective-permute-start.4 = (f32[1,2,2,32,64]{4,3,2,1,0:T(8,128)S(1)}, f32[1,2,2,32,64]{4,3,2,1,0:T(8,128)S(1)}, u32[]{:S(2)}, u32[]{:S(2)}) collective-permute-start(f32[1,2,2,32,64]{4,3,2,1,0:T(8,128)S(1)} %maximum_bitcast_fusion), channel_id=1, source_target_pairs={{0,1},{1,2},{2,3},{3,4},{4,5},{5,6},{6,7},{7,8},{8,9},{9,10},{10,1... | collective-permute-start | bytes 98312 | tf_op jit(solution)/shard_map/ppermute | solution.py:70
  81.9 8.4 %collective-permute-start.8 = (f32[2,2,2,32,64]{4,3,2,1,0:T(8,128)S(1)}, f32[2,2,2,32,64]{4,3,2,1,0:T(8,128)S(1)}, u32[]{:S(2)}, u32[]{:S(2)}) collective-permute-start(f32[2,2,2,32,64]{4,3,2,1,0:T(8,128)S(1)} %get-tuple-element.35), channel_id=1, source_target_pairs={{2,0},{3,1},{4,2},{5,3},{6,4},{7,5},{8,6},{9,7},{10,8},{11,9},{12,... | collective-permute-start | bytes 196616 | tf_op jit(solution)/shard_map/ppermute | solution.py:70
  83.9 9.3 %collective-permute-start.5 = (f32[2,2,2,32,64]{4,3,2,1,0:T(8,128)S(1)}, f32[2,2,2,32,64]{4,3,2,1,0:T(8,128)S(1)}, u32[]{:S(2)}, u32[]{:S(2)}) collective-permute-start(f32[2,2,2,32,64]{4,3,2,1,0:T(8,128)S(1)} %get-tuple-element.36), channel_id=1, source_target_pairs={{0,2},{1,3},{2,4},{3,5},{4,6},{5,7},{6,8},{7,9},{8,10},{9,11},{10,... | collective-permute-start | bytes 196616 | tf_op jit(solution)/shard_map/ppermute | solution.py:70
  93.2 17.9 %collective-permute-start.6 = (f32[4,2,2,32,64]{4,3,2,1,0:T(8,128)S(1)}, f32[4,2,2,32,64]{4,3,2,1,0:T(8,128)S(1)}, u32[]{:S(2)}, u32[]{:S(2)}) collective-permute-start(f32[4,2,2,32,64]{4,3,2,1,0:T(8,128)S(1)} %get-tuple-element.34), channel_id=1, source_target_pairs={{0,4},{1,5},{2,6},{3,7},{4,8},{5,9},{6,10},{7,11},{8,12},{9,13},{1... | collective-permute-start | bytes 393224 | tf_op jit(solution)/shard_map/ppermute | solution.py:70
  108.4 10.4 %collective-permute-start.9 = (f32[4,2,2,32,64]{4,3,2,1,0:T(8,128)S(1)}, f32[4,2,2,32,64]{4,3,2,1,0:T(8,128)S(1)}, u32[]{:S(2)}, u32[]{:S(2)}) collective-permute-start(f32[4,2,2,32,64]{4,3,2,1,0:T(8,128)S(1)} %get-tuple-element.33), channel_id=1, source_target_pairs={{4,0},{5,1},{6,2},{7,3},{8,4},{9,5},{10,6},{11,7},{12,8},{13,9},{1... | collective-permute-start | bytes 393224 | tf_op jit(solution)/shard_map/ppermute | solution.py:70
  126.3 3.8 %copy-start.28 = (f32[11,17,32]{2,1,0:T(8,128)S(1)}, f32[11,17,32]{2,1,0:T(8,128)}, u32[]{:S(2)}) copy-start(f32[11,17,32]{2,1,0:T(8,128)} %fusion.150) | copy-start | bytes 71812
  126.3 4.8 %copy-start.42 = (f32[32,64,1]{1,0,2:T(8,128)S(1)}, f32[32,64,1]{1,0,2:T(8,128)}, u32[]{:S(2)}) copy-start(f32[32,64,1]{1,0,2:T(8,128)} %constant.363) | copy-start | bytes 24580
  126.3 4.8 %copy-start.53 = (pred[5]{0:T(512)(128)(4,1)S(1)}, pred[5]{0:T(512)(128)(4,1)}, u32[]{:S(2)}) copy-start(pred[5]{0:T(512)(128)(4,1)} %compare_and_fusion.3) | copy-start | bytes 19
  127.5 4.8 %copy-start.43 = (f32[16,32,1]{1,0,2:T(8,128)S(1)}, f32[16,32,1]{1,0,2:T(8,128)}, u32[]{:S(2)}) copy-start(f32[16,32,1]{1,0,2:T(8,128)} %constant.364) | copy-start | bytes 6148
  128.8 4.7 %copy-start.20 = (f32[26,32,64]{2,1,0:T(8,128)S(1)}, f32[26,32,64]{2,1,0:T(8,128)}, u32[]{:S(2)}) copy-start(f32[26,32,64]{2,1,0:T(8,128)} %copy-done.19) | copy-start | bytes 638980
  128.8 4.7 %copy-start.48 = (pred[8]{0:T(512)(128)(4,1)S(1)}, pred[8]{0:T(512)(128)(4,1)}, u32[]{:S(2)}) copy-start(pred[8]{0:T(512)(128)(4,1)} %compare_and_fusion.6) | copy-start | bytes 28
  (42 other events, 70.1 us)

commit v7 on v5

--- a/solution.py
+++ b/solution.py
@@ -142,9 +142,14 @@
     step_numbers = jnp.arange(1, STEPS, dtype=jnp.int32)
     chosen = jnp.max(jnp.where(accept_flags == 1, step_numbers[None, :], 0), axis=1)
     local_count = coarse_states.shape[0]
-    accepted = coarse_states[jnp.arange(local_count, dtype=jnp.int32), chosen]
-    every_field = lax.all_gather(accepted, "chain", axis=0, tiled=True)
-    own = lax.dynamic_index_in_dim(every_field, owners[chain_index], 0, keepdims=False)
+    def local_state(owner):
+        pick = owner % local_count
+        return coarse_states[pick, chosen[pick]]
+
+    other = owners[1 - chain_index]
+    sent = lax.ppermute(local_state(other), "chain", [(0, 1), (1, 0)])
+    target = owners[chain_index]
+    own = jnp.where(target // local_count == chain_index, local_state(target), sent)
 
     cz, cy, cx = own.shape
     fz = source.shape[0]

time: 150 us -> 164 us (1.093)
  between operations: 3.4 us -> 9.3 us
  waiting for transfers between devices: 24.1 us -> 29.6 us
  other arithmetic: 33.5 us -> 36.5 us
  local copies, waits for them, and re-layouts: 16.8 us -> 19.2 us
  blocking collectives: 2.18 us -> 0 us
    ppermute x10, waiting for transfers between devices: 24.1 us -> 29.6 us  [shift_from(): return lax.ppermute(block, 'slab', pairs)]
    all_gather x1 -> x0, blocking collectives: 2.18 us -> none  [on_device(): every_field = lax.all_gather(accepted, 'chain', axis=0, tiled=True)]
    unnamed x119 -> x115, local copies, waits for them, and re-layouts: 9.59 us -> 10.1 us
  transfers between devices with their start and end apart: 10 -> 11, of which waited for: 9 -> 9; matrix products, arithmetic and copies ran while one was open for 7% -> 7% of each run, Pallas kernels for 0% -> 0%
where the time goes in v7:
time: 164 us; the launch traced here: 163 us
  starting transfers between devices  48.4 us (30%)
  other arithmetic  36.5 us (22%)
  waiting for transfers between devices  29.6 us (18%)
  matrix products  19.7 us (12%)
  local copies, waits for them, and re-layouts  19.2 us (12%)
  between operations  9.3 us (6%)
    ppermute x10, starting transfers between devices, shift_from(): return lax.ppermute(block, 'slab', pairs)  48.4 us
    ppermute x10, waiting for transfers between devices, shift_from(): return lax.ppermute(block, 'slab', pairs)  29.6 us
    select_n x11, other arithmetic, mask(): jnp.where(plane_mask(self.first + self.halo - h, u.shape[0], self.total),...  11.9 us
    unnamed x115, local copies, waits for them, and re-layouts  10.1 us
    dot_general x10, matrix products, along_y(): jnp.einsum('zyx,yv->zvx', values, jnp.asarray(matrix), precision=precisio...  9.14 us
    and x15, other arithmetic, plane_mask(): return ((g >= 0) & (g < total))[:, None, None]  6.79 us
    reduce_sum x6, other arithmetic, restrict_sum(): values = values.reshape(nz // 2, 2, ny, nx).sum(axis=1)  4.48 us
    dot_general x1, matrix products, on_device(): jnp.dot(along_rows.reshape(k0_planes * fy, MX), cols_table, precision=HI)  4.45 us
  transfers between devices with their start and end apart: 11, of which 9 were waited for; matrix products, arithmetic and copies ran while one was open for 7% of the time, Pallas kernels for 0%

profile of v7, /device:TPU:24, one launch (start us, length us, event | category | flops | bytes accessed | tf_op | source)
XLA Modules:
  0.0 162.7 jit_solution(13682861352668313873)
XLA Ops:
  20.1 3.5 %collective-permute-start.1 = (f32[512,256]{1,0:T(8,128)S(1)}, f32[512,256]{1,0:T(8,128)S(1)}, u32[]{:S(2)}, u32[]{:S(2)}) collective-permute-start(f32[512,256]{1,0:T(8,128)S(1)} %get-tuple-element.28), channel_id=1, source_target_pairs={{0,1},{1,2},{2,3},{3,4},{4,5},{5,6},{6,7},{7,8},{8,9},{9,10},{10,1... | collective-permute-start | bytes 1572872 | tf_op jit(solution)/shard_map/ppermute | solution.py:70
  23.6 4.6 %collective-permute-start.2 = (f32[512,256]{1,0:T(8,128)S(1)}, f32[512,256]{1,0:T(8,128)S(1)}, u32[]{:S(2)}, u32[]{:S(2)}) collective-permute-start(f32[512,256]{1,0:T(8,128)S(1)} %get-tuple-element.29), channel_id=1, source_target_pairs={{1,0},{2,1},{3,2},{4,3},{5,4},{6,5},{7,6},{8,7},{9,8},{10,9},{11,1... | collective-permute-start | bytes 1572872 | tf_op jit(solution)/shard_map/ppermute | solution.py:70
  30.4 8.1 %collective-permute-done.1 = f32[512,256]{1,0:T(8,128)S(1)} collective-permute-done((f32[512,256]{1,0:T(8,128)S(1)}, f32[512,256]{1,0:T(8,128)S(1)}, u32[]{:S(2)}, u32[]{:S(2)}) %collective-permute-start.1) | collective-permute-done | bytes 524320 | tf_op jit(solution)/shard_map/ppermute | solution.py:70
  40.1 2.6 %convolution_bitcast_fusion = f32[12,128,256]{1,2,0:T(8,128)S(1)} fusion(f32[12,64,256]{2,1,0:T(8,128)S(1)} %fusion.142, f32[64,128,1]{1,0,2:T(8,128)S(1)} %copy-done.38), kind=kOutput, calls=%fused_computation.46 | convolution fusion | flops 301989888 | bytes 2392064 | tf_op jit(solution)/shard_map/zyx,yv->zvx/dot_general | solution.py:49
  43.3 2.3 %copy.27 = f32[10,2,128,256]{3,2,1,0:T(8,128)} copy(f32[10,2,128,256]{2,3,0,1:T(8,128)S(1)} %pad_maximum_fusion) | data formatting | bytes 5242880 | tf_op jit(solution)/shard_map/stack | solution.py:184
  45.6 4.5 %fusion.3 = f32[20,128,256]{2,1,0:T(8,128)S(1)} fusion(f32[10,2,128,256]{3,2,1,0:T(8,128)} %copy.27, f32[20,128,64]{1,2,0:T(8,128)S(1)} %convolution_bitcast_fusion.3, pred[20]{0:T(512)(128)(4,1)S(1)} %copy-done.50, s32[256]{0:T(256)S(1)} %copy-done.41, s32[64]{0:T(128)S(1)} %copy-done.51), kind=kOutput, calls=%fused_computation.7 | convolution fusion | flops 504856576 | bytes 5899540 | tf_op jit(solution)/shard_map/dot_general | solution.py:194
  51.5 2.2 %convolution_bitcast_fusion.2 = f32[10,64,256]{2,1,0:T(8,128)S(1)} fusion(f32[10,128,256]{2,1,0:T(8,128)} %reduce_sum.54, f32[128,64,1]{0,1,2:T(8,128)S(1)} %copy-done.31), kind=kOutput, calls=%fused_computation.74 | convolution fusion | flops 251658240 | bytes 1998848 | tf_op jit(solution)/shard_map/zyx,yv->zvx/dot_general | solution.py:49
  58.2 2.4 %divide_select_fusion = (f32[14,128,256]{2,1,0:T(8,128)S(1)}, f32[14,128,256]{2,1,0:T(8,128)S(1)}, f32[14,128,256]{2,1,0:T(8,128)}) fusion(pred[14]{0:T(512)(128)(4,1)S(1)} %copy-done.48, f32[3,128,256]{2,1,0:T(8,128)S(1)} %bitcast.147, f32[8,128,256]{2,1,0:T(8,128)S(1)} %copy-done.13, f32[3,128,256]{2,1,0:T(8,128)S(1)} %bitcast.146, ...), kind=kLoop, calls=%fused_computation.21 | loop fusion | flops 4587520 | bytes 18350094 | tf_op jit(solution)/shard_map/jit(_where)/select_n | solution.py:111
  60.6 2.1 %copy-done.15 = f32[14,128,256]{2,1,0:T(8,128)S(1)} copy-done((f32[14,128,256]{2,1,0:T(8,128)S(1)}, f32[14,128,256]{2,1,0:T(8,128)}, u32[]{:S(2)}) %copy-start.15) | copy-done | bytes 1835032
  62.7 2.1 %fusion.19 = f32[12,128,256]{2,1,0:T(8,128)S(1)} fusion(f32[12,128,256]{2,1,0:T(8,128)S(1)} %slice.1358, f32[14,128,257]{2,1,0:T(8,128)S(1)} %fusion.1, f32[14,129,256]{2,1,0:T(8,128)S(1)} %add_multiply_fusion, f32[14,128,256]{2,1,0:T(8,128)S(1)} %get-tuple-element.11, f32[15,128,256]{2,1,0:T(8,128)S(1)} %fusion.4, ...), kind=kLoop, calls=%fused_computation.45 | loop fusion | flops 7077888 | bytes 18874380 | tf_op jit(solution)/shard_map/jit(_where)/select_n | solution.py:111
  66.9 3.2 %collective-permute-start.3 = (f32[6,64,128]{2,1,0:T(8,128)S(1)}, f32[6,64,128]{2,1,0:T(8,128)S(1)}, u32[]{:S(2)}, u32[]{:S(2)}) collective-permute-start(f32[6,64,128]{2,1,0:T(8,128)S(1)} %get-tuple-element.26), channel_id=1, source_target_pairs={{0,1},{1,2},{2,3},{3,4},{4,5},{5,6},{6,7},{7,8},{8,9},{9,10},{10,1... | collective-permute-start | bytes 589832 | tf_op jit(solution)/shard_map/ppermute | solution.py:70
  70.1 5.4 %collective-permute-start.4 = (f32[6,64,128]{2,1,0:T(8,128)S(1)}, f32[6,64,128]{2,1,0:T(8,128)S(1)}, u32[]{:S(2)}, u32[]{:S(2)}) collective-permute-start(f32[6,64,128]{2,1,0:T(8,128)S(1)} %get-tuple-element.27), channel_id=1, source_target_pairs={{1,0},{2,1},{3,2},{4,3},{5,4},{6,5},{7,6},{8,7},{9,8},{10,9},{11,1... | collective-permute-start | bytes 589832 | tf_op jit(solution)/shard_map/ppermute | solution.py:70
  81.9 6.5 %collective-permute-start.8 = (f32[1,2,2,32,64]{4,3,2,1,0:T(8,128)S(1)}, f32[1,2,2,32,64]{4,3,2,1,0:T(8,128)S(1)}, u32[]{:S(2)}, u32[]{:S(2)}) collective-permute-start(f32[1,2,2,32,64]{4,3,2,1,0:T(8,128)S(1)} %maximum_bitcast_fusion), channel_id=1, source_target_pairs={{1,0},{2,1},{3,2},{4,3},{5,4},{6,5},{7,6},{8,7},{9,8},{10,9},{11,1... | collective-permute-start | bytes 98312 | tf_op jit(solution)/shard_map/ppermute | solution.py:70
  88.4 1.9 %collective-permute-start.5 = (f32[1,2,2,32,64]{4,3,2,1,0:T(8,128)S(1)}, f32[1,2,2,32,64]{4,3,2,1,0:T(8,128)S(1)}, u32[]{:S(2)}, u32[]{:S(2)}) collective-permute-start(f32[1,2,2,32,64]{4,3,2,1,0:T(8,128)S(1)} %maximum_bitcast_fusion), channel_id=1, source_target_pairs={{0,1},{1,2},{2,3},{3,4},{4,5},{5,6},{6,7},{7,8},{8,9},{9,10},{10,1... | collective-permute-start | bytes 98312 | tf_op jit(solution)/shard_map/ppermute | solution.py:70
  90.9 5.8 %collective-permute-done.5 = f32[1,2,2,32,64]{4,3,2,1,0:T(8,128)S(1)} collective-permute-done((f32[1,2,2,32,64]{4,3,2,1,0:T(8,128)S(1)}, f32[1,2,2,32,64]{4,3,2,1,0:T(8,128)S(1)}, u32[]{:S(2)}, u32[]{:S(2)}) %collective-permute-start.5) | collective-permute-done | bytes 32800 | tf_op jit(solution)/shard_map/ppermute | solution.py:70
  96.7 1.9 %collective-permute-start.9 = (f32[2,2,2,32,64]{4,3,2,1,0:T(8,128)S(1)}, f32[2,2,2,32,64]{4,3,2,1,0:T(8,128)S(1)}, u32[]{:S(2)}, u32[]{:S(2)}) collective-permute-start(f32[2,2,2,32,64]{4,3,2,1,0:T(8,128)S(1)} %get-tuple-element.33), channel_id=1, source_target_pairs={{2,0},{3,1},{4,2},{5,3},{6,4},{7,5},{8,6},{9,7},{10,8},{11,9},{12,... | collective-permute-start | bytes 196616 | tf_op jit(solution)/shard_map/ppermute | solution.py:70
  98.6 5.4 %collective-permute-start.6 = (f32[2,2,2,32,64]{4,3,2,1,0:T(8,128)S(1)}, f32[2,2,2,32,64]{4,3,2,1,0:T(8,128)S(1)}, u32[]{:S(2)}, u32[]{:S(2)}) collective-permute-start(f32[2,2,2,32,64]{4,3,2,1,0:T(8,128)S(1)} %get-tuple-element.34), channel_id=1, source_target_pairs={{0,2},{1,3},{2,4},{3,5},{4,6},{5,7},{6,8},{7,9},{8,10},{9,11},{10,... | collective-permute-start | bytes 196616 | tf_op jit(solution)/shard_map/ppermute | solution.py:70
  105.0 2.8 %collective-permute-done.6 = f32[2,2,2,32,64]{4,3,2,1,0:T(8,128)S(1)} collective-permute-done((f32[2,2,2,32,64]{4,3,2,1,0:T(8,128)S(1)}, f32[2,2,2,32,64]{4,3,2,1,0:T(8,128)S(1)}, u32[]{:S(2)}, u32[]{:S(2)}) %collective-permute-start.6) | collective-permute-done | bytes 65568 | tf_op jit(solution)/shard_map/ppermute | solution.py:70
  107.9 14.0 %collective-permute-start.7 = (f32[4,2,2,32,64]{4,3,2,1,0:T(8,128)S(1)}, f32[4,2,2,32,64]{4,3,2,1,0:T(8,128)S(1)}, u32[]{:S(2)}, u32[]{:S(2)}) collective-permute-start(f32[4,2,2,32,64]{4,3,2,1,0:T(8,128)S(1)} %get-tuple-element.32), channel_id=1, source_target_pairs={{0,4},{1,5},{2,6},{3,7},{4,8},{5,9},{6,10},{7,11},{8,12},{9,13},{1... | collective-permute-start | bytes 393224 | tf_op jit(solution)/shard_map/ppermute | solution.py:70
  122.6 1.9 %collective-permute-start.10 = (f32[4,2,2,32,64]{4,3,2,1,0:T(8,128)S(1)}, f32[4,2,2,32,64]{4,3,2,1,0:T(8,128)S(1)}, u32[]{:S(2)}, u32[]{:S(2)}) collective-permute-start(f32[4,2,2,32,64]{4,3,2,1,0:T(8,128)S(1)} %get-tuple-element.31), channel_id=1, source_target_pairs={{4,0},{5,1},{6,2},{7,3},{8,4},{9,5},{10,6},{11,7},{12,8},{13,9},{1... | collective-permute-start | bytes 393224 | tf_op jit(solution)/shard_map/ppermute | solution.py:70
  125.9 7.0 %collective-permute-done.10 = f32[4,2,2,32,64]{4,3,2,1,0:T(8,128)S(1)} collective-permute-done((f32[4,2,2,32,64]{4,3,2,1,0:T(8,128)S(1)}, f32[4,2,2,32,64]{4,3,2,1,0:T(8,128)S(1)}, u32[]{:S(2)}, u32[]{:S(2)}) %collective-permute-start.10) | collective-permute-done | bytes 131104 | tf_op jit(solution)/shard_map/ppermute | solution.py:70
  152.4 2.0 %bitcast_add_fusion.1 = f32[12,128,256]{2,1,0:T(8,128)S(1)} fusion(f32[12,128,256]{2,1,0:T(8,128)} %copy-done.8, f32[6,128,256]{2,1,0:T(8,128)} %copy.28), kind=kLoop, calls=%fused_computation.44 | loop fusion | flops 393216 | bytes 3932160 | tf_op jit(solution)/shard_map/add | solution.py:258
  156.2 3.1 %fusion.38 = f32[10,128,256]{2,1,0:T(8,128)S(1)} fusion(f32[10,128,256]{2,1,0:T(8,128)S(1)} %slice.1536, f32[14,128,257]{2,1,0:T(8,128)S(1)} %copy-done.5, f32[14,129,256]{2,1,0:T(8,128)S(1)} %add_multiply_fusion, f32[12,128,256]{2,1,0:T(8,128)S(1)} %bitcast_add_fusion.1, f32[15,128,256]{2,1,0:T(8,128)S(1)} %copy-done.3, f32[14,128,256]{2,1,0:T(8,128)S(1)} %copy-done.7, ...), kind=kLoop, calls=%fused_computation.72 | loop fusion | flops 5898240 | bytes 15728650 | tf_op jit(solution)/shard_map/jit(_where)/select_n | solution.py:111
  160.6 2.2 %select_bitcast_fusion = f32[1,8,128,256]{3,2,1,0:T(8,128)} fusion(f32[8,128,256]{2,1,0:T(8,128)S(1)} %slice.1547, f32[8,128,256]{2,1,0:T(8,128)S(1)} %copy-done.14, f32[10,128,256]{2,1,0:T(8,128)S(1)} %fusion.38, f32[14,128,257]{2,1,0:T(8,128)S(1)} %copy-done.5, f32[14,129,256]{2,1,0:T(8,128)S(1)} %add_multiply_fusion, f32[15,128,256]{2,1,0:T(8,128)S(1)} %copy-done.3, ...), kind=kLoop, calls=%fused_computation.124 | loop fusion | flops 4718592 | bytes 12582920 | tf_op jit(solution)/shard_map/broadcast_in_dim | solution.py:261
  (250 shorter events, 56.0 us)
Async XLA Ops:
  0.0 28.6 %copy-start = (f32[1,32,16,64]{3,2,1,0:T(8,128)S(1)}, f32[1,32,16,64]{3,2,1,0:T(8,128)}, u32[]{:S(2)}) copy-start(f32[1,32,16,64]{3,2,1,0:T(8,128)} %param.28) | copy-start | bytes 393220
  9.0 10.1 %collective-permute-start = (bf16[4,64,128]{2,1,0:T(8,128)(2,1)S(1)}, bf16[4,64,128]{2,1,0:T(8,128)(2,1)S(1)}, u32[]{:S(2)}, u32[]{:S(2)}) collective-permute-start(bf16[4,64,128]{2,1,0:T(8,128)(2,1)S(1)} %dynamic-slice_bitcast_fusion), channel_id=1, source_target_pairs={{0,64},{64,0},{1,65},{65,1},{2,66},{66,2},{3,67},{67,3},{4,68},{68... | collective-permute-start | bytes 196616 | tf_op jit(solution)/shard_map/ppermute | solution.py:150
  20.0 19.8 %copy-start.36 = (bf16[128,256,1]{1,0,2:T(8,128)(2,1)S(1)}, bf16[128,256,1]{1,0,2:T(8,128)(2,1)}, u32[]{:S(2)}) copy-start(bf16[128,256,1]{1,0,2:T(8,128)(2,1)} %constant.362) | copy-start | bytes 196612
  20.1 18.5 %collective-permute-start.1 = (f32[512,256]{1,0:T(8,128)S(1)}, f32[512,256]{1,0:T(8,128)S(1)}, u32[]{:S(2)}, u32[]{:S(2)}) collective-permute-start(f32[512,256]{1,0:T(8,128)S(1)} %get-tuple-element.28), channel_id=1, source_target_pairs={{0,1},{1,2},{2,3},{3,4},{4,5},{5,6},{6,7},{7,8},{8,9},{9,10},{10,1... | collective-permute-start | bytes 1572872 | tf_op jit(solution)/shard_map/ppermute | solution.py:70
  23.6 16.1 %collective-permute-start.2 = (f32[512,256]{1,0:T(8,128)S(1)}, f32[512,256]{1,0:T(8,128)S(1)}, u32[]{:S(2)}, u32[]{:S(2)}) collective-permute-start(f32[512,256]{1,0:T(8,128)S(1)} %get-tuple-element.29), channel_id=1, source_target_pairs={{1,0},{2,1},{3,2},{4,3},{5,4},{6,5},{7,6},{8,7},{9,8},{10,9},{11,1... | collective-permute-start | bytes 1572872 | tf_op jit(solution)/shard_map/ppermute | solution.py:70
  28.6 11.5 %copy-start.38 = (f32[64,128,1]{1,0,2:T(8,128)S(1)}, f32[64,128,1]{1,0,2:T(8,128)}, u32[]{:S(2)}) copy-start(f32[64,128,1]{1,0,2:T(8,128)} %constant.363) | copy-start | bytes 98308
  38.5 4.3 %copy-start.29 = (f32[512,256]{1,0:T(8,128)}, f32[512,256]{1,0:T(8,128)S(1)}, u32[]{:S(2)}) copy-start(f32[512,256]{1,0:T(8,128)S(1)} %collective-permute-done.1) | copy-start | bytes 1572868
  39.7 3.1 %copy-start.30 = (f32[512,256]{1,0:T(8,128)}, f32[512,256]{1,0:T(8,128)S(1)}, u32[]{:S(2)}) copy-start(f32[512,256]{1,0:T(8,128)S(1)} %collective-permute-done.2) | copy-start | bytes 1572868
  54.7 10.2 %copy-start.2 = (f32[15,128,256]{2,1,0:T(8,128)}, f32[15,128,256]{2,1,0:T(8,128)S(1)}, u32[]{:S(2)}) copy-start(f32[15,128,256]{2,1,0:T(8,128)S(1)} %fusion.4) | copy-start | bytes 5898244
  55.8 9.1 %copy-start.4 = (f32[14,128,257]{2,1,0:T(8,128)}, f32[14,128,257]{2,1,0:T(8,128)S(1)}, u32[]{:S(2)}) copy-start(f32[14,128,257]{2,1,0:T(8,128)S(1)} %fusion.1) | copy-start | bytes 5526532
  60.5 4.4 %copy-start.6 = (f32[14,128,256]{2,1,0:T(8,128)}, f32[14,128,256]{2,1,0:T(8,128)S(1)}, u32[]{:S(2)}) copy-start(f32[14,128,256]{2,1,0:T(8,128)S(1)} %get-tuple-element.12) | copy-start | bytes 5505028
  66.0 9.5 %copy-start.34 = (f32[64,32,1]{0,1,2:T(8,128)S(1)}, f32[64,32,1]{0,1,2:T(8,128)}, u32[]{:S(2)}) copy-start(f32[64,32,1]{0,1,2:T(8,128)} %constant.366) | copy-start | bytes 24580
  66.9 10.9 %collective-permute-start.3 = (f32[6,64,128]{2,1,0:T(8,128)S(1)}, f32[6,64,128]{2,1,0:T(8,128)S(1)}, u32[]{:S(2)}, u32[]{:S(2)}) collective-permute-start(f32[6,64,128]{2,1,0:T(8,128)S(1)} %get-tuple-element.26), channel_id=1, source_target_pairs={{0,1},{1,2},{2,3},{3,4},{4,5},{5,6},{6,7},{7,8},{8,9},{9,10},{10,1... | collective-permute-start | bytes 589832 | tf_op jit(solution)/shard_map/ppermute | solution.py:70
  70.1 8.9 %collective-permute-start.4 = (f32[6,64,128]{2,1,0:T(8,128)S(1)}, f32[6,64,128]{2,1,0:T(8,128)S(1)}, u32[]{:S(2)}, u32[]{:S(2)}) collective-permute-start(f32[6,64,128]{2,1,0:T(8,128)S(1)} %get-tuple-element.27), channel_id=1, source_target_pairs={{1,0},{2,1},{3,2},{4,3},{5,4},{6,5},{7,6},{8,7},{9,8},{10,9},{11,1... | collective-permute-start | bytes 589832 | tf_op jit(solution)/shard_map/ppermute | solution.py:70
  81.9 9.0 %collective-permute-start.8 = (f32[1,2,2,32,64]{4,3,2,1,0:T(8,128)S(1)}, f32[1,2,2,32,64]{4,3,2,1,0:T(8,128)S(1)}, u32[]{:S(2)}, u32[]{:S(2)}) collective-permute-start(f32[1,2,2,32,64]{4,3,2,1,0:T(8,128)S(1)} %maximum_bitcast_fusion), channel_id=1, source_target_pairs={{1,0},{2,1},{3,2},{4,3},{5,4},{6,5},{7,6},{8,7},{9,8},{10,9},{11,1... | collective-permute-start | bytes 98312 | tf_op jit(solution)/shard_map/ppermute | solution.py:70
  88.4 8.3 %collective-permute-start.5 = (f32[1,2,2,32,64]{4,3,2,1,0:T(8,128)S(1)}, f32[1,2,2,32,64]{4,3,2,1,0:T(8,128)S(1)}, u32[]{:S(2)}, u32[]{:S(2)}) collective-permute-start(f32[1,2,2,32,64]{4,3,2,1,0:T(8,128)S(1)} %maximum_bitcast_fusion), channel_id=1, source_target_pairs={{0,1},{1,2},{2,3},{3,4},{4,5},{5,6},{6,7},{7,8},{8,9},{9,10},{10,1... | collective-permute-start | bytes 98312 | tf_op jit(solution)/shard_map/ppermute | solution.py:70
  96.7 8.4 %collective-permute-start.9 = (f32[2,2,2,32,64]{4,3,2,1,0:T(8,128)S(1)}, f32[2,2,2,32,64]{4,3,2,1,0:T(8,128)S(1)}, u32[]{:S(2)}, u32[]{:S(2)}) collective-permute-start(f32[2,2,2,32,64]{4,3,2,1,0:T(8,128)S(1)} %get-tuple-element.33), channel_id=1, source_target_pairs={{2,0},{3,1},{4,2},{5,3},{6,4},{7,5},{8,6},{9,7},{10,8},{11,9},{12,... | collective-permute-start | bytes 196616 | tf_op jit(solution)/shard_map/ppermute | solution.py:70
  98.6 9.3 %collective-permute-start.6 = (f32[2,2,2,32,64]{4,3,2,1,0:T(8,128)S(1)}, f32[2,2,2,32,64]{4,3,2,1,0:T(8,128)S(1)}, u32[]{:S(2)}, u32[]{:S(2)}) collective-permute-start(f32[2,2,2,32,64]{4,3,2,1,0:T(8,128)S(1)} %get-tuple-element.34), channel_id=1, source_target_pairs={{0,2},{1,3},{2,4},{3,5},{4,6},{5,7},{6,8},{7,9},{8,10},{9,11},{10,... | collective-permute-start | bytes 196616 | tf_op jit(solution)/shard_map/ppermute | solution.py:70
  107.9 17.9 %collective-permute-start.7 = (f32[4,2,2,32,64]{4,3,2,1,0:T(8,128)S(1)}, f32[4,2,2,32,64]{4,3,2,1,0:T(8,128)S(1)}, u32[]{:S(2)}, u32[]{:S(2)}) collective-permute-start(f32[4,2,2,32,64]{4,3,2,1,0:T(8,128)S(1)} %get-tuple-element.32), channel_id=1, source_target_pairs={{0,4},{1,5},{2,6},{3,7},{4,8},{5,9},{6,10},{7,11},{8,12},{9,13},{1... | collective-permute-start | bytes 393224 | tf_op jit(solution)/shard_map/ppermute | solution.py:70
  122.6 10.4 %collective-permute-start.10 = (f32[4,2,2,32,64]{4,3,2,1,0:T(8,128)S(1)}, f32[4,2,2,32,64]{4,3,2,1,0:T(8,128)S(1)}, u32[]{:S(2)}, u32[]{:S(2)}) collective-permute-start(f32[4,2,2,32,64]{4,3,2,1,0:T(8,128)S(1)} %get-tuple-element.31), channel_id=1, source_target_pairs={{4,0},{5,1},{6,2},{7,3},{8,4},{9,5},{10,6},{11,7},{12,8},{13,9},{1... | collective-permute-start | bytes 393224 | tf_op jit(solution)/shard_map/ppermute | solution.py:70
  138.3 5.4 %copy-start.49 = (pred[7]{0:T(512)(128)(4,1)S(1)}, pred[7]{0:T(512)(128)(4,1)}, u32[]{:S(2)}) copy-start(pred[7]{0:T(512)(128)(4,1)} %compare_and_fusion.2) | copy-start | bytes 25
  138.3 5.6 %copy-start.39 = (f32[32,64,1]{1,0,2:T(8,128)S(1)}, f32[32,64,1]{1,0,2:T(8,128)}, u32[]{:S(2)}) copy-start(f32[32,64,1]{1,0,2:T(8,128)} %constant.368) | copy-start | bytes 24580
  140.0 3.7 %copy-start.28 = (f32[11,17,32]{2,1,0:T(8,128)S(1)}, f32[11,17,32]{2,1,0:T(8,128)}, u32[]{:S(2)}) copy-start(f32[11,17,32]{2,1,0:T(8,128)} %fusion.150) | copy-start | bytes 71812
  140.0 3.9 %copy-start.54 = (pred[5]{0:T(512)(128)(4,1)S(1)}, pred[5]{0:T(512)(128)(4,1)}, u32[]{:S(2)}) copy-start(pred[5]{0:T(512)(128)(4,1)} %compare_and_fusion.3) | copy-start | bytes 19
  (44 other events, 74.9 us)

commit v8 on v5

--- a/solution.py
+++ b/solution.py
@@ -97,6 +97,7 @@
         self.fzu = faces_z[1:]
         diag = self.fzl + self.fzu + self.fy[:, 1:] + self.fy[:, :-1]
         self.diag = diag + self.fx[:, :, 1:] + self.fx[:, :, :-1]
+        self.valid = plane_mask(self.first, kc.shape[0], total)
 
     def cut(self, arr, h, have):
         n = self.own + 2 * h
@@ -108,7 +109,7 @@
         return c(self.fzl, h, H), c(self.fzu, h, H), c(self.fy, h, H), c(self.fx, h, H), c(self.diag, h, H)
 
     def mask(self, u, h):
-        return jnp.where(plane_mask(self.first + self.halo - h, u.shape[0], self.total), u, 0.0)
+        return jnp.where(self.cut(self.valid, h, self.halo), u, 0.0)
 
     def operate(self, u, h):
         fzl, fzu, fy, fx, diag = self.coef(h - 1)

time: 150 us -> 154 us (1.027)
  other arithmetic: 33.5 us -> 27.3 us
  local copies, waits for them, and re-layouts: 16.8 us -> 22.1 us
  waiting for transfers between devices: 24.1 us -> 29.4 us
    and x15 -> x5, other arithmetic: 6.19 us -> 0.04 us  [plane_mask(): return ((g >= 0) & (g < total))[:, None, None]]
    slice x1 -> x13, local copies, waits for them, and re-layouts: 0.03 us -> 5.87 us  [cut(): return arr[have - h:have - h + n]]
    ppermute x10, waiting for transfers between devices: 24.1 us -> 29.4 us  [shift_from(): return lax.ppermute(block, 'slab', pairs)]
    unnamed x119 -> x117, local copies, waits for them, and re-layouts: 9.59 us -> 9.09 us
  transfers between devices with their start and end apart: 10 -> 10, of which waited for: 9 -> 8; matrix products, arithmetic and copies ran while one was open for 7% -> 6% of each run, Pallas kernels for 0% -> 0%
where the time goes in v8:
time: 154 us; the launch traced here: 153 us
  starting transfers between devices  48.4 us (31%)
  waiting for transfers between devices  29.4 us (19%)
  other arithmetic  27.3 us (18%)
  local copies, waits for them, and re-layouts  22.1 us (14%)
  matrix products  20.6 us (13%)
  between operations  3.45 us (2%)
  blocking collectives  2.18 us (1%)
    ppermute x10, starting transfers between devices, shift_from(): return lax.ppermute(block, 'slab', pairs)  48.4 us
    ppermute x10, waiting for transfers between devices, shift_from(): return lax.ppermute(block, 'slab', pairs)  29.4 us
    select_n x11, other arithmetic, mask(): return jnp.where(self.cut(self.valid, h, self.halo), u, 0.0)  11.2 us
    unnamed x117, local copies, waits for them, and re-layouts  9.09 us
    dot_general x10, matrix products, along_y(): jnp.einsum('zyx,yv->zvx', values, jnp.asarray(matrix), precision=precisio...  9.02 us
    slice x13, local copies, waits for them, and re-layouts, cut(): return arr[have - h:have - h + n]  5.87 us
    reduce_sum x6, other arithmetic, restrict_sum(): values = values.reshape(nz // 2, 2, ny, nx).sum(axis=1)  4.78 us
    dot_general x1, matrix products, on_device(): jnp.dot(along_rows.reshape(k0_planes * fy, MX), cols_table, precision=HI)  4.67 us
  transfers between devices with their start and end apart: 10, of which 8 were waited for; matrix products, arithmetic and copies ran while one was open for 6% of the time, Pallas kernels for 0%

profile of v8, /device:TPU:24, one launch (start us, length us, event | category | flops | bytes accessed | tf_op | source)
XLA Modules:
  0.0 153.5 jit_solution(1785411334696592843)
XLA Ops:
  4.1 2.2 %all_gather.3 = bf16[8,4,64,128]{3,2,1,0:T(8,128)(2,1)S(1)} all-gather(bf16[4,4,64,128]{3,2,1,0:T(8,128)(2,1)S(1)} %gather_fusion), channel_id=1, replica_groups=mesh['chain'=2,'slab'=64] {'chain'}, dimensions={0}, use_global_device_ids=true | all-gather | bytes 786432 | tf_op jit(solution)/shard_map/all_gather | solution.py:147
  7.2 3.5 %collective-permute-start = (f32[512,256]{1,0:T(8,128)S(1)}, f32[512,256]{1,0:T(8,128)S(1)}, u32[]{:S(2)}, u32[]{:S(2)}) collective-permute-start(f32[512,256]{1,0:T(8,128)S(1)} %get-tuple-element.30), channel_id=1, source_target_pairs={{0,1},{1,2},{2,3},{3,4},{4,5},{5,6},{6,7},{7,8},{8,9},{9,10},{10,1... | collective-permute-start | bytes 1572872 | tf_op jit(solution)/shard_map/ppermute | solution.py:70
  10.8 4.6 %collective-permute-start.1 = (f32[512,256]{1,0:T(8,128)S(1)}, f32[512,256]{1,0:T(8,128)S(1)}, u32[]{:S(2)}, u32[]{:S(2)}) collective-permute-start(f32[512,256]{1,0:T(8,128)S(1)} %get-tuple-element.31), channel_id=1, source_target_pairs={{1,0},{2,1},{3,2},{4,3},{5,4},{6,5},{7,6},{8,7},{9,8},{10,9},{11,1... | collective-permute-start | bytes 1572872 | tf_op jit(solution)/shard_map/ppermute | solution.py:70
  16.1 2.1 %convolution_bitcast_fusion.3 = f32[20,128,64]{1,2,0:T(8,128)} fusion(f32[20,16,64]{2,0,1:T(8,128)S(1)} %fusion.123, s32[128]{0:T(128)S(1)} %multiply_add_fusion.2, s32[16]{0:T(128)S(1)} %iota_add_fusion.2), kind=kOutput, calls=%fused_computation.76 | convolution fusion | flops 31485952 | bytes 737856 | tf_op jit(solution)/shard_map/zbe,by->zye/dot_general | solution.py:189
  18.2 7.1 %collective-permute-done = f32[512,256]{1,0:T(8,128)S(1)} collective-permute-done((f32[512,256]{1,0:T(8,128)S(1)}, f32[512,256]{1,0:T(8,128)S(1)}, u32[]{:S(2)}, u32[]{:S(2)}) %collective-permute-start) | collective-permute-done | bytes 524320 | tf_op jit(solution)/shard_map/ppermute | solution.py:70
  27.7 2.6 %convolution_bitcast_fusion = f32[12,128,256]{1,2,0:T(8,128)S(1)} fusion(f32[12,64,256]{2,1,0:T(8,128)S(1)} %fusion.142, f32[64,128,1]{1,0,2:T(8,128)S(1)} %copy-done.42), kind=kOutput, calls=%fused_computation.47 | convolution fusion | flops 301989888 | bytes 2392064 | tf_op jit(solution)/shard_map/zyx,yv->zvx/dot_general | solution.py:49
  30.8 2.3 %copy.29 = f32[10,2,128,256]{3,2,1,0:T(8,128)} copy(f32[10,2,128,256]{2,3,0,1:T(8,128)S(1)} %pad_maximum_fusion) | data formatting | bytes 5242880 | tf_op jit(solution)/shard_map/stack | solution.py:180
  33.1 4.7 %fusion.3 = f32[20,128,256]{2,1,0:T(8,128)S(1)} fusion(f32[10,2,128,256]{3,2,1,0:T(8,128)} %copy.29, f32[20,128,64]{1,2,0:T(8,128)} %convolution_bitcast_fusion.3, pred[20]{0:T(512)(128)(4,1)S(1)} %compare_and_fusion.3, s32[256]{0:T(256)S(1)} %multiply_add_fusion, s32[64]{0:T(128)S(1)} %iota_add_fusion), kind=kOutput, calls=%fused_computation.8 | convolution fusion | flops 504856576 | bytes 5899540 | tf_op jit(solution)/shard_map/dot_general | solution.py:190
  39.2 2.2 %convolution_bitcast_fusion.2 = f32[10,64,256]{2,1,0:T(8,128)S(1)} fusion(f32[10,128,256]{2,1,0:T(8,128)} %reduce_sum.54, f32[128,64,1]{0,1,2:T(8,128)S(1)} %copy-done.30), kind=kOutput, calls=%fused_computation.75 | convolution fusion | flops 251658240 | bytes 1998848 | tf_op jit(solution)/shard_map/zyx,yv->zvx/dot_general | solution.py:49
  48.4 2.3 %fusion.19 = f32[12,128,256]{2,1,0:T(8,128)S(1)} fusion(f32[12,128,256]{2,1,0:T(8,128)S(1)} %slice.1420, f32[14,128,257]{2,1,0:T(8,128)S(1)} %fusion.1, f32[14,129,256]{2,1,0:T(8,128)S(1)} %add_multiply_fusion, f32[14,128,256]{2,1,0:T(8,128)S(1)} %get-tuple-element.11, f32[15,128,256]{2,1,0:T(8,128)S(1)} %fusion.4, ...), kind=kLoop, calls=%fused_computation.46 | loop fusion | flops 7077888 | bytes 18874380 | tf_op jit(solution)/shard_map/jit(_where)/select_n | solution.py:112
  53.2 3.2 %collective-permute-start.2 = (f32[6,64,128]{2,1,0:T(8,128)S(1)}, f32[6,64,128]{2,1,0:T(8,128)S(1)}, u32[]{:S(2)}, u32[]{:S(2)}) collective-permute-start(f32[6,64,128]{2,1,0:T(8,128)S(1)} %get-tuple-element.28), channel_id=1, source_target_pairs={{0,1},{1,2},{2,3},{3,4},{4,5},{5,6},{6,7},{7,8},{8,9},{9,10},{10,1... | collective-permute-start | bytes 589832 | tf_op jit(solution)/shard_map/ppermute | solution.py:70
  56.4 5.4 %collective-permute-start.3 = (f32[6,64,128]{2,1,0:T(8,128)S(1)}, f32[6,64,128]{2,1,0:T(8,128)S(1)}, u32[]{:S(2)}, u32[]{:S(2)}) collective-permute-start(f32[6,64,128]{2,1,0:T(8,128)S(1)} %get-tuple-element.29), channel_id=1, source_target_pairs={{1,0},{2,1},{3,2},{4,3},{5,4},{6,5},{7,6},{8,7},{9,8},{10,9},{11,1... | collective-permute-start | bytes 589832 | tf_op jit(solution)/shard_map/ppermute | solution.py:70
  67.6 6.5 %collective-permute-start.7 = (f32[1,2,2,32,64]{4,3,2,1,0:T(8,128)S(1)}, f32[1,2,2,32,64]{4,3,2,1,0:T(8,128)S(1)}, u32[]{:S(2)}, u32[]{:S(2)}) collective-permute-start(f32[1,2,2,32,64]{4,3,2,1,0:T(8,128)S(1)} %maximum_bitcast_fusion), channel_id=1, source_target_pairs={{1,0},{2,1},{3,2},{4,3},{5,4},{6,5},{7,6},{8,7},{9,8},{10,9},{11,1... | collective-permute-start | bytes 98312 | tf_op jit(solution)/shard_map/ppermute | solution.py:70
  74.1 1.9 %collective-permute-start.4 = (f32[1,2,2,32,64]{4,3,2,1,0:T(8,128)S(1)}, f32[1,2,2,32,64]{4,3,2,1,0:T(8,128)S(1)}, u32[]{:S(2)}, u32[]{:S(2)}) collective-permute-start(f32[1,2,2,32,64]{4,3,2,1,0:T(8,128)S(1)} %maximum_bitcast_fusion), channel_id=1, source_target_pairs={{0,1},{1,2},{2,3},{3,4},{4,5},{5,6},{6,7},{7,8},{8,9},{9,10},{10,1... | collective-permute-start | bytes 98312 | tf_op jit(solution)/shard_map/ppermute | solution.py:70
  76.0 6.3 %collective-permute-done.4 = f32[1,2,2,32,64]{4,3,2,1,0:T(8,128)S(1)} collective-permute-done((f32[1,2,2,32,64]{4,3,2,1,0:T(8,128)S(1)}, f32[1,2,2,32,64]{4,3,2,1,0:T(8,128)S(1)}, u32[]{:S(2)}, u32[]{:S(2)}) %collective-permute-start.4) | collective-permute-done | bytes 32800 | tf_op jit(solution)/shard_map/ppermute | solution.py:70
  82.4 1.9 %collective-permute-start.8 = (f32[2,2,2,32,64]{4,3,2,1,0:T(8,128)S(1)}, f32[2,2,2,32,64]{4,3,2,1,0:T(8,128)S(1)}, u32[]{:S(2)}, u32[]{:S(2)}) collective-permute-start(f32[2,2,2,32,64]{4,3,2,1,0:T(8,128)S(1)} %get-tuple-element.35), channel_id=1, source_target_pairs={{2,0},{3,1},{4,2},{5,3},{6,4},{7,5},{8,6},{9,7},{10,8},{11,9},{12,... | collective-permute-start | bytes 196616 | tf_op jit(solution)/shard_map/ppermute | solution.py:70
  84.3 5.4 %collective-permute-start.5 = (f32[2,2,2,32,64]{4,3,2,1,0:T(8,128)S(1)}, f32[2,2,2,32,64]{4,3,2,1,0:T(8,128)S(1)}, u32[]{:S(2)}, u32[]{:S(2)}) collective-permute-start(f32[2,2,2,32,64]{4,3,2,1,0:T(8,128)S(1)} %get-tuple-element.36), channel_id=1, source_target_pairs={{0,2},{1,3},{2,4},{3,5},{4,6},{5,7},{6,8},{7,9},{8,10},{9,11},{10,... | collective-permute-start | bytes 196616 | tf_op jit(solution)/shard_map/ppermute | solution.py:70
  90.8 2.8 %collective-permute-done.5 = f32[2,2,2,32,64]{4,3,2,1,0:T(8,128)S(1)} collective-permute-done((f32[2,2,2,32,64]{4,3,2,1,0:T(8,128)S(1)}, f32[2,2,2,32,64]{4,3,2,1,0:T(8,128)S(1)}, u32[]{:S(2)}, u32[]{:S(2)}) %collective-permute-start.5) | collective-permute-done | bytes 65568 | tf_op jit(solution)/shard_map/ppermute | solution.py:70
  93.6 14.0 %collective-permute-start.6 = (f32[4,2,2,32,64]{4,3,2,1,0:T(8,128)S(1)}, f32[4,2,2,32,64]{4,3,2,1,0:T(8,128)S(1)}, u32[]{:S(2)}, u32[]{:S(2)}) collective-permute-start(f32[4,2,2,32,64]{4,3,2,1,0:T(8,128)S(1)} %get-tuple-element.34), channel_id=1, source_target_pairs={{0,4},{1,5},{2,6},{3,7},{4,8},{5,9},{6,10},{7,11},{8,12},{9,13},{1... | collective-permute-start | bytes 393224 | tf_op jit(solution)/shard_map/ppermute | solution.py:70
  114.1 1.9 %collective-permute-start.9 = (f32[4,2,2,32,64]{4,3,2,1,0:T(8,128)S(1)}, f32[4,2,2,32,64]{4,3,2,1,0:T(8,128)S(1)}, u32[]{:S(2)}, u32[]{:S(2)}) collective-permute-start(f32[4,2,2,32,64]{4,3,2,1,0:T(8,128)S(1)} %get-tuple-element.33), channel_id=1, source_target_pairs={{4,0},{5,1},{6,2},{7,3},{8,4},{9,5},{10,6},{11,7},{12,8},{13,9},{1... | collective-permute-start | bytes 393224 | tf_op jit(solution)/shard_map/ppermute | solution.py:70
  116.1 8.3 %collective-permute-done.9 = f32[4,2,2,32,64]{4,3,2,1,0:T(8,128)S(1)} collective-permute-done((f32[4,2,2,32,64]{4,3,2,1,0:T(8,128)S(1)}, f32[4,2,2,32,64]{4,3,2,1,0:T(8,128)S(1)}, u32[]{:S(2)}, u32[]{:S(2)}) %collective-permute-start.9) | collective-permute-done | bytes 131104 | tf_op jit(solution)/shard_map/ppermute | solution.py:70
  143.1 2.0 %bitcast_add_fusion.1 = f32[12,128,256]{2,1,0:T(8,128)S(1)} fusion(f32[12,128,256]{2,1,0:T(8,128)} %copy-done.8, f32[6,128,256]{2,1,0:T(8,128)} %copy.32), kind=kLoop, calls=%fused_computation.45 | loop fusion | flops 393216 | bytes 3932160 | tf_op jit(solution)/shard_map/add | solution.py:254
  147.0 3.1 %fusion.38 = f32[10,128,256]{2,1,0:T(8,128)S(1)} fusion(f32[10,128,256]{2,1,0:T(8,128)S(1)} %slice.1598, f32[14,128,257]{2,1,0:T(8,128)S(1)} %copy-done.5, f32[14,129,256]{2,1,0:T(8,128)S(1)} %add_multiply_fusion, f32[12,128,256]{2,1,0:T(8,128)S(1)} %bitcast_add_fusion.1, f32[15,128,256]{2,1,0:T(8,128)S(1)} %copy-done.3, f32[14,128,256]{2,1,0:T(8,128)S(1)} %copy-done.7, ...), kind=kLoop, calls=%fused_computation.73 | loop fusion | flops 5898240 | bytes 15728650 | tf_op jit(solution)/shard_map/jit(_where)/select_n | solution.py:112
  151.3 2.2 %select_bitcast_fusion = f32[1,8,128,256]{3,2,1,0:T(8,128)} fusion(f32[8,128,256]{2,1,0:T(8,128)S(1)} %slice.1609, f32[8,128,256]{2,1,0:T(8,128)S(1)} %copy-done.15, f32[10,128,256]{2,1,0:T(8,128)S(1)} %fusion.38, f32[14,128,257]{2,1,0:T(8,128)S(1)} %copy-done.5, f32[14,129,256]{2,1,0:T(8,128)S(1)} %add_multiply_fusion, f32[15,128,256]{2,1,0:T(8,128)S(1)} %copy-done.3, ...), kind=kLoop, calls=%fused_computation.125 | loop fusion | flops 4718592 | bytes 12582920 | tf_op jit(solution)/shard_map/broadcast_in_dim | solution.py:257
  (251 shorter events, 51.4 us)
Async XLA Ops:
  0.0 3.5 %copy-start = (bf16[4,4,4,64,128]{4,3,2,1,0:T(8,128)(2,1)S(1)}, bf16[4,4,4,64,128]{4,3,2,1,0:T(8,128)(2,1)}, u32[]{:S(2)}) copy-start(bf16[4,4,4,64,128]{4,3,2,1,0:T(8,128)(2,1)} %param.25) | copy-start | bytes 3145732
  0.0 7.0 %copy-start.13 = (f32[8,128,256]{2,1,0:T(8,128)S(1)}, f32[8,128,256]{2,1,0:T(8,128)}, u32[]{:S(2)}) copy-start(f32[8,128,256]{2,1,0:T(8,128)} %param.29) | copy-start | bytes 3145732
  7.1 8.6 %copy-start.38 = (f32[1,32,16,64]{3,2,1,0:T(8,128)S(1)}, f32[1,32,16,64]{3,2,1,0:T(8,128)}, u32[]{:S(2)}) copy-start(f32[1,32,16,64]{3,2,1,0:T(8,128)} %param.28) | copy-start | bytes 393220
  7.2 20.1 %copy-start.41 = (bf16[128,256,1]{1,0,2:T(8,128)(2,1)S(1)}, bf16[128,256,1]{1,0,2:T(8,128)(2,1)}, u32[]{:S(2)}) copy-start(bf16[128,256,1]{1,0,2:T(8,128)(2,1)} %constant.307) | copy-start | bytes 196612
  7.2 18.1 %collective-permute-start = (f32[512,256]{1,0:T(8,128)S(1)}, f32[512,256]{1,0:T(8,128)S(1)}, u32[]{:S(2)}, u32[]{:S(2)}) collective-permute-start(f32[512,256]{1,0:T(8,128)S(1)} %get-tuple-element.30), channel_id=1, source_target_pairs={{0,1},{1,2},{2,3},{3,4},{4,5},{5,6},{6,7},{7,8},{8,9},{9,10},{10,1... | collective-permute-start | bytes 1572872 | tf_op jit(solution)/shard_map/ppermute | solution.py:70
  10.8 15.7 %collective-permute-start.1 = (f32[512,256]{1,0:T(8,128)S(1)}, f32[512,256]{1,0:T(8,128)S(1)}, u32[]{:S(2)}, u32[]{:S(2)}) collective-permute-start(f32[512,256]{1,0:T(8,128)S(1)} %get-tuple-element.31), channel_id=1, source_target_pairs={{1,0},{2,1},{3,2},{4,3},{5,4},{6,5},{7,6},{8,7},{9,8},{10,9},{11,1... | collective-permute-start | bytes 1572872 | tf_op jit(solution)/shard_map/ppermute | solution.py:70
  15.6 12.0 %copy-start.42 = (f32[64,128,1]{1,0,2:T(8,128)S(1)}, f32[64,128,1]{1,0,2:T(8,128)}, u32[]{:S(2)}) copy-start(f32[64,128,1]{1,0,2:T(8,128)} %constant.308) | copy-start | bytes 98308
  43.0 7.8 %copy-start.2 = (f32[15,128,256]{2,1,0:T(8,128)}, f32[15,128,256]{2,1,0:T(8,128)S(1)}, u32[]{:S(2)}) copy-start(f32[15,128,256]{2,1,0:T(8,128)S(1)} %fusion.4) | copy-start | bytes 5898244
  44.7 6.2 %copy-start.4 = (f32[14,128,257]{2,1,0:T(8,128)}, f32[14,128,257]{2,1,0:T(8,128)S(1)}, u32[]{:S(2)}) copy-start(f32[14,128,257]{2,1,0:T(8,128)S(1)} %fusion.1) | copy-start | bytes 5526532
  52.3 9.5 %copy-start.37 = (f32[64,32,1]{0,1,2:T(8,128)S(1)}, f32[64,32,1]{0,1,2:T(8,128)}, u32[]{:S(2)}) copy-start(f32[64,32,1]{0,1,2:T(8,128)} %constant.311) | copy-start | bytes 24580
  53.2 10.6 %collective-permute-start.2 = (f32[6,64,128]{2,1,0:T(8,128)S(1)}, f32[6,64,128]{2,1,0:T(8,128)S(1)}, u32[]{:S(2)}, u32[]{:S(2)}) collective-permute-start(f32[6,64,128]{2,1,0:T(8,128)S(1)} %get-tuple-element.28), channel_id=1, source_target_pairs={{0,1},{1,2},{2,3},{3,4},{4,5},{5,6},{6,7},{7,8},{8,9},{9,10},{10,1... | collective-permute-start | bytes 589832 | tf_op jit(solution)/shard_map/ppermute | solution.py:70
  56.4 8.5 %collective-permute-start.3 = (f32[6,64,128]{2,1,0:T(8,128)S(1)}, f32[6,64,128]{2,1,0:T(8,128)S(1)}, u32[]{:S(2)}, u32[]{:S(2)}) collective-permute-start(f32[6,64,128]{2,1,0:T(8,128)S(1)} %get-tuple-element.29), channel_id=1, source_target_pairs={{1,0},{2,1},{3,2},{4,3},{5,4},{6,5},{7,6},{8,7},{9,8},{10,9},{11,1... | collective-permute-start | bytes 589832 | tf_op jit(solution)/shard_map/ppermute | solution.py:70
  67.6 8.4 %collective-permute-start.7 = (f32[1,2,2,32,64]{4,3,2,1,0:T(8,128)S(1)}, f32[1,2,2,32,64]{4,3,2,1,0:T(8,128)S(1)}, u32[]{:S(2)}, u32[]{:S(2)}) collective-permute-start(f32[1,2,2,32,64]{4,3,2,1,0:T(8,128)S(1)} %maximum_bitcast_fusion), channel_id=1, source_target_pairs={{1,0},{2,1},{3,2},{4,3},{5,4},{6,5},{7,6},{8,7},{9,8},{10,9},{11,1... | collective-permute-start | bytes 98312 | tf_op jit(solution)/shard_map/ppermute | solution.py:70
  74.1 8.3 %collective-permute-start.4 = (f32[1,2,2,32,64]{4,3,2,1,0:T(8,128)S(1)}, f32[1,2,2,32,64]{4,3,2,1,0:T(8,128)S(1)}, u32[]{:S(2)}, u32[]{:S(2)}) collective-permute-start(f32[1,2,2,32,64]{4,3,2,1,0:T(8,128)S(1)} %maximum_bitcast_fusion), channel_id=1, source_target_pairs={{0,1},{1,2},{2,3},{3,4},{4,5},{5,6},{6,7},{7,8},{8,9},{9,10},{10,1... | collective-permute-start | bytes 98312 | tf_op jit(solution)/shard_map/ppermute | solution.py:70
  82.4 8.4 %collective-permute-start.8 = (f32[2,2,2,32,64]{4,3,2,1,0:T(8,128)S(1)}, f32[2,2,2,32,64]{4,3,2,1,0:T(8,128)S(1)}, u32[]{:S(2)}, u32[]{:S(2)}) collective-permute-start(f32[2,2,2,32,64]{4,3,2,1,0:T(8,128)S(1)} %get-tuple-element.35), channel_id=1, source_target_pairs={{2,0},{3,1},{4,2},{5,3},{6,4},{7,5},{8,6},{9,7},{10,8},{11,9},{12,... | collective-permute-start | bytes 196616 | tf_op jit(solution)/shard_map/ppermute | solution.py:70
  84.3 9.3 %collective-permute-start.5 = (f32[2,2,2,32,64]{4,3,2,1,0:T(8,128)S(1)}, f32[2,2,2,32,64]{4,3,2,1,0:T(8,128)S(1)}, u32[]{:S(2)}, u32[]{:S(2)}) collective-permute-start(f32[2,2,2,32,64]{4,3,2,1,0:T(8,128)S(1)} %get-tuple-element.36), channel_id=1, source_target_pairs={{0,2},{1,3},{2,4},{3,5},{4,6},{5,7},{6,8},{7,9},{8,10},{9,11},{10,... | collective-permute-start | bytes 196616 | tf_op jit(solution)/shard_map/ppermute | solution.py:70
  93.6 22.3 %collective-permute-start.6 = (f32[4,2,2,32,64]{4,3,2,1,0:T(8,128)S(1)}, f32[4,2,2,32,64]{4,3,2,1,0:T(8,128)S(1)}, u32[]{:S(2)}, u32[]{:S(2)}) collective-permute-start(f32[4,2,2,32,64]{4,3,2,1,0:T(8,128)S(1)} %get-tuple-element.34), channel_id=1, source_target_pairs={{0,4},{1,5},{2,6},{3,7},{4,8},{5,9},{6,10},{7,11},{8,12},{9,13},{1... | collective-permute-start | bytes 393224 | tf_op jit(solution)/shard_map/ppermute | solution.py:70
  107.7 16.8 %copy-start.51 = (pred[11]{0:T(512)(128)(4,1)}, pred[11]{0:T(512)(128)(4,1)S(1)}, u32[]{:S(2)}) copy-start(pred[11]{0:T(512)(128)(4,1)S(1)} %compare_and_fusion) | copy-start | bytes 37
  114.1 10.4 %collective-permute-start.9 = (f32[4,2,2,32,64]{4,3,2,1,0:T(8,128)S(1)}, f32[4,2,2,32,64]{4,3,2,1,0:T(8,128)S(1)}, u32[]{:S(2)}, u32[]{:S(2)}) collective-permute-start(f32[4,2,2,32,64]{4,3,2,1,0:T(8,128)S(1)} %get-tuple-element.33), channel_id=1, source_target_pairs={{4,0},{5,1},{6,2},{7,3},{8,4},{9,5},{10,6},{11,7},{12,8},{13,9},{1... | collective-permute-start | bytes 393224 | tf_op jit(solution)/shard_map/ppermute | solution.py:70
  130.7 3.6 %copy-start.29 = (f32[11,17,32]{2,1,0:T(8,128)S(1)}, f32[11,17,32]{2,1,0:T(8,128)}, u32[]{:S(2)}) copy-start(f32[11,17,32]{2,1,0:T(8,128)} %fusion.150) | copy-start | bytes 71812
  130.7 3.6 %copy-start.50 = (pred[7]{0:T(512)(128)(4,1)S(1)}, pred[7]{0:T(512)(128)(4,1)}, u32[]{:S(2)}) copy-start(pred[7]{0:T(512)(128)(4,1)} %slice.1242) | copy-start | bytes 25
  130.7 3.8 %copy-start.44 = (f32[32,64,1]{1,0,2:T(8,128)S(1)}, f32[32,64,1]{1,0,2:T(8,128)}, u32[]{:S(2)}) copy-start(f32[32,64,1]{1,0,2:T(8,128)} %constant.313) | copy-start | bytes 24580
  130.7 3.8 %copy-start.55 = (pred[5]{0:T(512)(128)(4,1)S(1)}, pred[5]{0:T(512)(128)(4,1)}, u32[]{:S(2)}) copy-start(pred[5]{0:T(512)(128)(4,1)} %slice.1241) | copy-start | bytes 19
  141.9 3.2 %copy-start.46 = (pred[10]{0:T(512)(128)(4,1)S(1)}, pred[10]{0:T(512)(128)(4,1)}, u32[]{:S(2)}) copy-start(pred[10]{0:T(512)(128)(4,1)} %slice.1100) | copy-start | bytes 34
  (42 other events, 68.7 us)

commit v9 on v5

--- a/solution.py
+++ b/solution.py
@@ -14,6 +14,7 @@
 
 OMEGA = 0.8
 HI = lax.Precision.HIGHEST
+GRID = lax.Precision.HIGH
 
 F0_HALO = 3
 F1_HALO = 4
@@ -53,14 +54,14 @@
 def restrict_sum(values):
     nz, ny, nx = values.shape
     values = values.reshape(nz // 2, 2, ny, nx).sum(axis=1)
-    values = along_y(values, pair_sum_matrix(ny))
-    return along_x(values, pair_sum_matrix(nx))
+    values = along_y(values, pair_sum_matrix(ny), GRID)
+    return along_x(values, pair_sum_matrix(nx), GRID)
 
 
 def copy_up(values):
     nz, ny, nx = values.shape
-    values = along_x(values, repeat_matrix(nx))
-    values = along_y(values, repeat_matrix(ny))
+    values = along_x(values, repeat_matrix(nx), GRID)
+    values = along_y(values, repeat_matrix(ny), GRID)
     return jnp.repeat(values, 2, axis=0)
 
 
@@ -172,7 +173,7 @@
     ext = jnp.where((gidx >= coarse_total)[:, None, None], hi_plane, ext)
 
     pro = along_x(ext, prolong_matrix(cx).astype(jnp.bfloat16), precision=lax.Precision.DEFAULT)
-    pro = along_y(pro, prolong_matrix(cy))
+    pro = along_y(pro, prolong_matrix(cy), GRID)
     inner = pro[1:-1]
     even = 0.75 * inner + 0.25 * pro[:-2]
     odd = 0.75 * inner + 0.25 * pro[2:]

time: 150 us -> 147 us (0.980)
  matrix products: 20.6 us -> 17.3 us
    dot_general x10, matrix products: 9.03 us -> 6.39 us  [along_y(): jnp.einsum('zyx,yv->zvx', values, jnp.asarray(matrix), precision=precisio...]
where the time goes in v9:
time: 147 us; the launch traced here: 146 us
  starting transfers between devices  48.4 us (33%)
  other arithmetic  33.5 us (23%)
  waiting for transfers between devices  24.1 us (16%)
  matrix products  17.3 us (12%)
  local copies, waits for them, and re-layouts  16.9 us (11%)
  between operations  3.39 us (2%)
  blocking collectives  2.18 us (1%)
    ppermute x10, starting transfers between devices, shift_from(): return lax.ppermute(block, 'slab', pairs)  48.4 us
    ppermute x10, waiting for transfers between devices, shift_from(): return lax.ppermute(block, 'slab', pairs)  24.1 us
    select_n x11, other arithmetic, mask(): jnp.where(plane_mask(self.first + self.halo - h, u.shape[0], self.total),...  11.2 us
    unnamed x119, local copies, waits for them, and re-layouts  9.73 us
    dot_general x10, matrix products, along_y(): jnp.einsum('zyx,yv->zvx', values, jnp.asarray(matrix), precision=precisio...  6.39 us
    and x15, other arithmetic, plane_mask(): return ((g >= 0) & (g < total))[:, None, None]  6.19 us
    reduce_sum x6, other arithmetic, restrict_sum(): values = values.reshape(nz // 2, 2, ny, nx).sum(axis=1)  4.78 us
    dot_general x1, matrix products, on_device(): jnp.dot(along_rows.reshape(k0_planes * fy, MX), cols_table, precision=HI)  4.67 us
  transfers between devices with their start and end apart: 10, of which 9 were waited for; matrix products, arithmetic and copies ran while one was open for 7% of the time, Pallas kernels for 0%

profile of v9, /device:TPU:24, one launch (start us, length us, event | category | flops | bytes accessed | tf_op | source)
XLA Modules:
  0.0 145.7 jit_solution(14382610429726404722)
XLA Ops:
  4.1 2.2 %all_gather.3 = bf16[8,4,64,128]{3,2,1,0:T(8,128)(2,1)S(1)} all-gather(bf16[4,4,64,128]{3,2,1,0:T(8,128)(2,1)S(1)} %gather_fusion), channel_id=1, replica_groups=mesh['chain'=2,'slab'=64] {'chain'}, dimensions={0}, use_global_device_ids=true | all-gather | bytes 786432 | tf_op jit(solution)/shard_map/all_gather | solution.py:147
  7.2 3.5 %collective-permute-start = (f32[512,256]{1,0:T(8,128)S(1)}, f32[512,256]{1,0:T(8,128)S(1)}, u32[]{:S(2)}, u32[]{:S(2)}) collective-permute-start(f32[512,256]{1,0:T(8,128)S(1)} %get-tuple-element.30), channel_id=1, source_target_pairs={{0,1},{1,2},{2,3},{3,4},{4,5},{5,6},{6,7},{7,8},{8,9},{9,10},{10,1... | collective-permute-start | bytes 1572872 | tf_op jit(solution)/shard_map/ppermute | solution.py:71
  10.8 4.6 %collective-permute-start.1 = (f32[512,256]{1,0:T(8,128)S(1)}, f32[512,256]{1,0:T(8,128)S(1)}, u32[]{:S(2)}, u32[]{:S(2)}) collective-permute-start(f32[512,256]{1,0:T(8,128)S(1)} %get-tuple-element.31), channel_id=1, source_target_pairs={{1,0},{2,1},{3,2},{4,3},{5,4},{6,5},{7,6},{8,7},{9,8},{10,9},{11,1... | collective-permute-start | bytes 1572872 | tf_op jit(solution)/shard_map/ppermute | solution.py:71
  20.4 2.1 %convolution_bitcast_fusion.3 = f32[20,128,64]{1,2,0:T(8,128)} fusion(f32[20,16,64]{2,0,1:T(8,128)S(1)} %fusion.123, s32[128]{0:T(128)S(1)} %multiply_add_fusion.2, s32[16]{0:T(128)S(1)} %iota_add_fusion.2), kind=kOutput, calls=%fused_computation.76 | convolution fusion | flops 31485952 | bytes 737856 | tf_op jit(solution)/shard_map/zbe,by->zye/dot_general | solution.py:189
  22.4 2.9 %collective-permute-done = f32[512,256]{1,0:T(8,128)S(1)} collective-permute-done((f32[512,256]{1,0:T(8,128)S(1)}, f32[512,256]{1,0:T(8,128)S(1)}, u32[]{:S(2)}, u32[]{:S(2)}) %collective-permute-start) | collective-permute-done | bytes 524320 | tf_op jit(solution)/shard_map/ppermute | solution.py:71
  29.6 2.3 %copy.29 = f32[10,2,128,256]{3,2,1,0:T(8,128)} copy(f32[10,2,128,256]{2,3,0,1:T(8,128)S(1)} %pad_maximum_fusion) | data formatting | bytes 5242880 | tf_op jit(solution)/shard_map/stack | solution.py:180
  31.9 4.7 %fusion.3 = f32[20,128,256]{2,1,0:T(8,128)S(1)} fusion(f32[10,2,128,256]{3,2,1,0:T(8,128)} %copy.29, f32[20,128,64]{1,2,0:T(8,128)} %convolution_bitcast_fusion.3, pred[20]{0:T(512)(128)(4,1)S(1)} %compare_and_fusion.12, s32[256]{0:T(256)S(1)} %multiply_add_fusion, s32[64]{0:T(128)S(1)} %iota_add_fusion), kind=kOutput, calls=%fused_computation.8 | convolution fusion | flops 504856576 | bytes 5899540 | tf_op jit(solution)/shard_map/dot_general | solution.py:190
  37.9 1.8 %convolution_bitcast_fusion.2 = f32[10,64,256]{2,1,0:T(8,128)S(1)} fusion(f32[10,128,256]{2,1,0:T(8,128)} %reduce_sum.54, f32[128,64,1]{0,1,2:T(8,128)S(1)} %copy-done.30), kind=kOutput, calls=%fused_computation.75 | convolution fusion | flops 125829120 | bytes 1998848 | tf_op jit(solution)/shard_map/zyx,yv->zvx/dot_general | solution.py:50
  46.6 2.3 %fusion.19 = f32[12,128,256]{2,1,0:T(8,128)S(1)} fusion(f32[12,128,256]{2,1,0:T(8,128)S(1)} %slice.1360, f32[14,128,257]{2,1,0:T(8,128)S(1)} %fusion.1, f32[14,129,256]{2,1,0:T(8,128)S(1)} %add_multiply_fusion, f32[14,128,256]{2,1,0:T(8,128)S(1)} %get-tuple-element.11, f32[15,128,256]{2,1,0:T(8,128)S(1)} %fusion.4, ...), kind=kLoop, calls=%fused_computation.46 | loop fusion | flops 7077888 | bytes 18874380 | tf_op jit(solution)/shard_map/jit(_where)/select_n | solution.py:112
  51.1 3.2 %collective-permute-start.2 = (f32[6,64,128]{2,1,0:T(8,128)S(1)}, f32[6,64,128]{2,1,0:T(8,128)S(1)}, u32[]{:S(2)}, u32[]{:S(2)}) collective-permute-start(f32[6,64,128]{2,1,0:T(8,128)S(1)} %get-tuple-element.28), channel_id=1, source_target_pairs={{0,1},{1,2},{2,3},{3,4},{4,5},{5,6},{6,7},{7,8},{8,9},{9,10},{10,1... | collective-permute-start | bytes 589832 | tf_op jit(solution)/shard_map/ppermute | solution.py:71
  54.3 5.2 %collective-permute-start.3 = (f32[6,64,128]{2,1,0:T(8,128)S(1)}, f32[6,64,128]{2,1,0:T(8,128)S(1)}, u32[]{:S(2)}, u32[]{:S(2)}) collective-permute-start(f32[6,64,128]{2,1,0:T(8,128)S(1)} %get-tuple-element.29), channel_id=1, source_target_pairs={{1,0},{2,1},{3,2},{4,3},{5,4},{6,5},{7,6},{8,7},{9,8},{10,9},{11,1... | collective-permute-start | bytes 589832 | tf_op jit(solution)/shard_map/ppermute | solution.py:71
  59.8 1.8 %collective-permute-done.2 = f32[6,64,128]{2,1,0:T(8,128)S(1)} collective-permute-done((f32[6,64,128]{2,1,0:T(8,128)S(1)}, f32[6,64,128]{2,1,0:T(8,128)S(1)}, u32[]{:S(2)}, u32[]{:S(2)}) %collective-permute-start.2) | collective-permute-done | bytes 196640 | tf_op jit(solution)/shard_map/ppermute | solution.py:71
  65.5 6.5 %collective-permute-start.7 = (f32[1,2,2,32,64]{4,3,2,1,0:T(8,128)S(1)}, f32[1,2,2,32,64]{4,3,2,1,0:T(8,128)S(1)}, u32[]{:S(2)}, u32[]{:S(2)}) collective-permute-start(f32[1,2,2,32,64]{4,3,2,1,0:T(8,128)S(1)} %maximum_bitcast_fusion), channel_id=1, source_target_pairs={{1,0},{2,1},{3,2},{4,3},{5,4},{6,5},{7,6},{8,7},{9,8},{10,9},{11,1... | collective-permute-start | bytes 98312 | tf_op jit(solution)/shard_map/ppermute | solution.py:71
  72.0 1.9 %collective-permute-start.4 = (f32[1,2,2,32,64]{4,3,2,1,0:T(8,128)S(1)}, f32[1,2,2,32,64]{4,3,2,1,0:T(8,128)S(1)}, u32[]{:S(2)}, u32[]{:S(2)}) collective-permute-start(f32[1,2,2,32,64]{4,3,2,1,0:T(8,128)S(1)} %maximum_bitcast_fusion), channel_id=1, source_target_pairs={{0,1},{1,2},{2,3},{3,4},{4,5},{5,6},{6,7},{7,8},{8,9},{9,10},{10,1... | collective-permute-start | bytes 98312 | tf_op jit(solution)/shard_map/ppermute | solution.py:71
  74.5 5.7 %collective-permute-done.4 = f32[1,2,2,32,64]{4,3,2,1,0:T(8,128)S(1)} collective-permute-done((f32[1,2,2,32,64]{4,3,2,1,0:T(8,128)S(1)}, f32[1,2,2,32,64]{4,3,2,1,0:T(8,128)S(1)}, u32[]{:S(2)}, u32[]{:S(2)}) %collective-permute-start.4) | collective-permute-done | bytes 32800 | tf_op jit(solution)/shard_map/ppermute | solution.py:71
  80.3 1.9 %collective-permute-start.8 = (f32[2,2,2,32,64]{4,3,2,1,0:T(8,128)S(1)}, f32[2,2,2,32,64]{4,3,2,1,0:T(8,128)S(1)}, u32[]{:S(2)}, u32[]{:S(2)}) collective-permute-start(f32[2,2,2,32,64]{4,3,2,1,0:T(8,128)S(1)} %get-tuple-element.35), channel_id=1, source_target_pairs={{2,0},{3,1},{4,2},{5,3},{6,4},{7,5},{8,6},{9,7},{10,8},{11,9},{12,... | collective-permute-start | bytes 196616 | tf_op jit(solution)/shard_map/ppermute | solution.py:71
  82.2 5.4 %collective-permute-start.5 = (f32[2,2,2,32,64]{4,3,2,1,0:T(8,128)S(1)}, f32[2,2,2,32,64]{4,3,2,1,0:T(8,128)S(1)}, u32[]{:S(2)}, u32[]{:S(2)}) collective-permute-start(f32[2,2,2,32,64]{4,3,2,1,0:T(8,128)S(1)} %get-tuple-element.36), channel_id=1, source_target_pairs={{0,2},{1,3},{2,4},{3,5},{4,6},{5,7},{6,8},{7,9},{8,10},{9,11},{10,... | collective-permute-start | bytes 196616 | tf_op jit(solution)/shard_map/ppermute | solution.py:71
  88.6 2.8 %collective-permute-done.5 = f32[2,2,2,32,64]{4,3,2,1,0:T(8,128)S(1)} collective-permute-done((f32[2,2,2,32,64]{4,3,2,1,0:T(8,128)S(1)}, f32[2,2,2,32,64]{4,3,2,1,0:T(8,128)S(1)}, u32[]{:S(2)}, u32[]{:S(2)}) %collective-permute-start.5) | collective-permute-done | bytes 65568 | tf_op jit(solution)/shard_map/ppermute | solution.py:71
  91.5 14.0 %collective-permute-start.6 = (f32[4,2,2,32,64]{4,3,2,1,0:T(8,128)S(1)}, f32[4,2,2,32,64]{4,3,2,1,0:T(8,128)S(1)}, u32[]{:S(2)}, u32[]{:S(2)}) collective-permute-start(f32[4,2,2,32,64]{4,3,2,1,0:T(8,128)S(1)} %get-tuple-element.34), channel_id=1, source_target_pairs={{0,4},{1,5},{2,6},{3,7},{4,8},{5,9},{6,10},{7,11},{8,12},{9,13},{1... | collective-permute-start | bytes 393224 | tf_op jit(solution)/shard_map/ppermute | solution.py:71
  106.8 2.1 %collective-permute-start.9 = (f32[4,2,2,32,64]{4,3,2,1,0:T(8,128)S(1)}, f32[4,2,2,32,64]{4,3,2,1,0:T(8,128)S(1)}, u32[]{:S(2)}, u32[]{:S(2)}) collective-permute-start(f32[4,2,2,32,64]{4,3,2,1,0:T(8,128)S(1)} %get-tuple-element.33), channel_id=1, source_target_pairs={{4,0},{5,1},{6,2},{7,3},{8,4},{9,5},{10,6},{11,7},{12,8},{13,9},{1... | collective-permute-start | bytes 393224 | tf_op jit(solution)/shard_map/ppermute | solution.py:71
  109.5 7.6 %collective-permute-done.9 = f32[4,2,2,32,64]{4,3,2,1,0:T(8,128)S(1)} collective-permute-done((f32[4,2,2,32,64]{4,3,2,1,0:T(8,128)S(1)}, f32[4,2,2,32,64]{4,3,2,1,0:T(8,128)S(1)}, u32[]{:S(2)}, u32[]{:S(2)}) %collective-permute-start.9) | collective-permute-done | bytes 131104 | tf_op jit(solution)/shard_map/ppermute | solution.py:71
  135.3 2.0 %bitcast_add_fusion.1 = f32[12,128,256]{2,1,0:T(8,128)S(1)} fusion(f32[12,128,256]{2,1,0:T(8,128)} %copy-done.8, f32[6,128,256]{2,1,0:T(8,128)} %copy.32), kind=kLoop, calls=%fused_computation.45 | loop fusion | flops 393216 | bytes 3932160 | tf_op jit(solution)/shard_map/add | solution.py:254
  139.2 3.1 %fusion.38 = f32[10,128,256]{2,1,0:T(8,128)S(1)} fusion(f32[10,128,256]{2,1,0:T(8,128)S(1)} %slice.1538, f32[14,128,257]{2,1,0:T(8,128)S(1)} %copy-done.5, f32[14,129,256]{2,1,0:T(8,128)S(1)} %add_multiply_fusion, f32[12,128,256]{2,1,0:T(8,128)S(1)} %bitcast_add_fusion.1, f32[15,128,256]{2,1,0:T(8,128)S(1)} %copy-done.3, f32[14,128,256]{2,1,0:T(8,128)S(1)} %copy-done.7, ...), kind=kLoop, calls=%fused_computation.73 | loop fusion | flops 5898240 | bytes 15728650 | tf_op jit(solution)/shard_map/jit(_where)/select_n | solution.py:112
  143.6 2.2 %select_bitcast_fusion = f32[1,8,128,256]{3,2,1,0:T(8,128)} fusion(f32[8,128,256]{2,1,0:T(8,128)S(1)} %slice.1549, f32[8,128,256]{2,1,0:T(8,128)S(1)} %copy-done.15, f32[10,128,256]{2,1,0:T(8,128)S(1)} %fusion.38, f32[14,128,257]{2,1,0:T(8,128)S(1)} %copy-done.5, f32[14,129,256]{2,1,0:T(8,128)S(1)} %add_multiply_fusion, f32[15,128,256]{2,1,0:T(8,128)S(1)} %copy-done.3, ...), kind=kLoop, calls=%fused_computation.125 | loop fusion | flops 4718592 | bytes 12582920 | tf_op jit(solution)/shard_map/broadcast_in_dim | solution.py:257
  (251 shorter events, 50.4 us)
Async XLA Ops:
  0.0 3.5 %copy-start = (bf16[4,4,4,64,128]{4,3,2,1,0:T(8,128)(2,1)S(1)}, bf16[4,4,4,64,128]{4,3,2,1,0:T(8,128)(2,1)}, u32[]{:S(2)}) copy-start(bf16[4,4,4,64,128]{4,3,2,1,0:T(8,128)(2,1)} %param.25) | copy-start | bytes 3145732
  0.0 7.0 %copy-start.13 = (f32[8,128,256]{2,1,0:T(8,128)S(1)}, f32[8,128,256]{2,1,0:T(8,128)}, u32[]{:S(2)}) copy-start(f32[8,128,256]{2,1,0:T(8,128)} %param.29) | copy-start | bytes 3145732
  7.1 12.8 %copy-start.38 = (f32[1,32,16,64]{3,2,1,0:T(8,128)S(1)}, f32[1,32,16,64]{3,2,1,0:T(8,128)}, u32[]{:S(2)}) copy-start(f32[1,32,16,64]{3,2,1,0:T(8,128)} %param.28) | copy-start | bytes 393220
  7.2 20.1 %copy-start.41 = (bf16[128,256,1]{1,0,2:T(8,128)(2,1)S(1)}, bf16[128,256,1]{1,0,2:T(8,128)(2,1)}, u32[]{:S(2)}) copy-start(bf16[128,256,1]{1,0,2:T(8,128)(2,1)} %constant.357) | copy-start | bytes 196612
  7.2 18.1 %collective-permute-start = (f32[512,256]{1,0:T(8,128)S(1)}, f32[512,256]{1,0:T(8,128)S(1)}, u32[]{:S(2)}, u32[]{:S(2)}) collective-permute-start(f32[512,256]{1,0:T(8,128)S(1)} %get-tuple-element.30), channel_id=1, source_target_pairs={{0,1},{1,2},{2,3},{3,4},{4,5},{5,6},{6,7},{7,8},{8,9},{9,10},{10,1... | collective-permute-start | bytes 1572872 | tf_op jit(solution)/shard_map/ppermute | solution.py:71
  10.8 15.7 %collective-permute-start.1 = (f32[512,256]{1,0:T(8,128)S(1)}, f32[512,256]{1,0:T(8,128)S(1)}, u32[]{:S(2)}, u32[]{:S(2)}) collective-permute-start(f32[512,256]{1,0:T(8,128)S(1)} %get-tuple-element.31), channel_id=1, source_target_pairs={{1,0},{2,1},{3,2},{4,3},{5,4},{6,5},{7,6},{8,7},{9,8},{10,9},{11,1... | collective-permute-start | bytes 1572872 | tf_op jit(solution)/shard_map/ppermute | solution.py:71
  19.9 7.8 %copy-start.42 = (f32[64,128,1]{1,0,2:T(8,128)S(1)}, f32[64,128,1]{1,0,2:T(8,128)}, u32[]{:S(2)}) copy-start(f32[64,128,1]{1,0,2:T(8,128)} %constant.358) | copy-start | bytes 98308
  41.2 7.8 %copy-start.2 = (f32[15,128,256]{2,1,0:T(8,128)}, f32[15,128,256]{2,1,0:T(8,128)S(1)}, u32[]{:S(2)}) copy-start(f32[15,128,256]{2,1,0:T(8,128)S(1)} %fusion.4) | copy-start | bytes 5898244
  42.9 6.2 %copy-start.4 = (f32[14,128,257]{2,1,0:T(8,128)}, f32[14,128,257]{2,1,0:T(8,128)S(1)}, u32[]{:S(2)}) copy-start(f32[14,128,257]{2,1,0:T(8,128)S(1)} %fusion.1) | copy-start | bytes 5526532
  50.5 9.1 %copy-start.37 = (f32[64,32,1]{0,1,2:T(8,128)S(1)}, f32[64,32,1]{0,1,2:T(8,128)}, u32[]{:S(2)}) copy-start(f32[64,32,1]{0,1,2:T(8,128)} %constant.361) | copy-start | bytes 24580
  51.1 10.6 %collective-permute-start.2 = (f32[6,64,128]{2,1,0:T(8,128)S(1)}, f32[6,64,128]{2,1,0:T(8,128)S(1)}, u32[]{:S(2)}, u32[]{:S(2)}) collective-permute-start(f32[6,64,128]{2,1,0:T(8,128)S(1)} %get-tuple-element.28), channel_id=1, source_target_pairs={{0,1},{1,2},{2,3},{3,4},{4,5},{5,6},{6,7},{7,8},{8,9},{9,10},{10,1... | collective-permute-start | bytes 589832 | tf_op jit(solution)/shard_map/ppermute | solution.py:71
  54.3 8.5 %collective-permute-start.3 = (f32[6,64,128]{2,1,0:T(8,128)S(1)}, f32[6,64,128]{2,1,0:T(8,128)S(1)}, u32[]{:S(2)}, u32[]{:S(2)}) collective-permute-start(f32[6,64,128]{2,1,0:T(8,128)S(1)} %get-tuple-element.29), channel_id=1, source_target_pairs={{1,0},{2,1},{3,2},{4,3},{5,4},{6,5},{7,6},{8,7},{9,8},{10,9},{11,1... | collective-permute-start | bytes 589832 | tf_op jit(solution)/shard_map/ppermute | solution.py:71
  65.5 9.0 %collective-permute-start.7 = (f32[1,2,2,32,64]{4,3,2,1,0:T(8,128)S(1)}, f32[1,2,2,32,64]{4,3,2,1,0:T(8,128)S(1)}, u32[]{:S(2)}, u32[]{:S(2)}) collective-permute-start(f32[1,2,2,32,64]{4,3,2,1,0:T(8,128)S(1)} %maximum_bitcast_fusion), channel_id=1, source_target_pairs={{1,0},{2,1},{3,2},{4,3},{5,4},{6,5},{7,6},{8,7},{9,8},{10,9},{11,1... | collective-permute-start | bytes 98312 | tf_op jit(solution)/shard_map/ppermute | solution.py:71
  72.0 8.3 %collective-permute-start.4 = (f32[1,2,2,32,64]{4,3,2,1,0:T(8,128)S(1)}, f32[1,2,2,32,64]{4,3,2,1,0:T(8,128)S(1)}, u32[]{:S(2)}, u32[]{:S(2)}) collective-permute-start(f32[1,2,2,32,64]{4,3,2,1,0:T(8,128)S(1)} %maximum_bitcast_fusion), channel_id=1, source_target_pairs={{0,1},{1,2},{2,3},{3,4},{4,5},{5,6},{6,7},{7,8},{8,9},{9,10},{10,1... | collective-permute-start | bytes 98312 | tf_op jit(solution)/shard_map/ppermute | solution.py:71
  80.3 8.4 %collective-permute-start.8 = (f32[2,2,2,32,64]{4,3,2,1,0:T(8,128)S(1)}, f32[2,2,2,32,64]{4,3,2,1,0:T(8,128)S(1)}, u32[]{:S(2)}, u32[]{:S(2)}) collective-permute-start(f32[2,2,2,32,64]{4,3,2,1,0:T(8,128)S(1)} %get-tuple-element.35), channel_id=1, source_target_pairs={{2,0},{3,1},{4,2},{5,3},{6,4},{7,5},{8,6},{9,7},{10,8},{11,9},{12,... | collective-permute-start | bytes 196616 | tf_op jit(solution)/shard_map/ppermute | solution.py:71
  82.2 9.3 %collective-permute-start.5 = (f32[2,2,2,32,64]{4,3,2,1,0:T(8,128)S(1)}, f32[2,2,2,32,64]{4,3,2,1,0:T(8,128)S(1)}, u32[]{:S(2)}, u32[]{:S(2)}) collective-permute-start(f32[2,2,2,32,64]{4,3,2,1,0:T(8,128)S(1)} %get-tuple-element.36), channel_id=1, source_target_pairs={{0,2},{1,3},{2,4},{3,5},{4,6},{5,7},{6,8},{7,9},{8,10},{9,11},{10,... | collective-permute-start | bytes 196616 | tf_op jit(solution)/shard_map/ppermute | solution.py:71
  91.5 17.9 %collective-permute-start.6 = (f32[4,2,2,32,64]{4,3,2,1,0:T(8,128)S(1)}, f32[4,2,2,32,64]{4,3,2,1,0:T(8,128)S(1)}, u32[]{:S(2)}, u32[]{:S(2)}) collective-permute-start(f32[4,2,2,32,64]{4,3,2,1,0:T(8,128)S(1)} %get-tuple-element.34), channel_id=1, source_target_pairs={{0,4},{1,5},{2,6},{3,7},{4,8},{5,9},{6,10},{7,11},{8,12},{9,13},{1... | collective-permute-start | bytes 393224 | tf_op jit(solution)/shard_map/ppermute | solution.py:71
  106.8 10.4 %collective-permute-start.9 = (f32[4,2,2,32,64]{4,3,2,1,0:T(8,128)S(1)}, f32[4,2,2,32,64]{4,3,2,1,0:T(8,128)S(1)}, u32[]{:S(2)}, u32[]{:S(2)}) collective-permute-start(f32[4,2,2,32,64]{4,3,2,1,0:T(8,128)S(1)} %get-tuple-element.33), channel_id=1, source_target_pairs={{4,0},{5,1},{6,2},{7,3},{8,4},{9,5},{10,6},{11,7},{12,8},{13,9},{1... | collective-permute-start | bytes 393224 | tf_op jit(solution)/shard_map/ppermute | solution.py:71
  123.8 3.5 %copy-start.29 = (f32[11,17,32]{2,1,0:T(8,128)S(1)}, f32[11,17,32]{2,1,0:T(8,128)}, u32[]{:S(2)}) copy-start(f32[11,17,32]{2,1,0:T(8,128)} %fusion.150) | copy-start | bytes 71812
  123.8 3.5 %copy-start.53 = (pred[7]{0:T(512)(128)(4,1)S(1)}, pred[7]{0:T(512)(128)(4,1)}, u32[]{:S(2)}) copy-start(pred[7]{0:T(512)(128)(4,1)} %compare_and_fusion.2) | copy-start | bytes 25
  123.8 3.7 %copy-start.44 = (f32[32,64,1]{1,0,2:T(8,128)S(1)}, f32[32,64,1]{1,0,2:T(8,128)}, u32[]{:S(2)}) copy-start(f32[32,64,1]{1,0,2:T(8,128)} %constant.363) | copy-start | bytes 24580
  123.8 3.7 %copy-start.56 = (pred[5]{0:T(512)(128)(4,1)S(1)}, pred[5]{0:T(512)(128)(4,1)}, u32[]{:S(2)}) copy-start(pred[5]{0:T(512)(128)(4,1)} %compare_and_fusion.3) | copy-start | bytes 19
  126.1 2.9 %copy-start.21 = (f32[26,32,64]{2,1,0:T(8,128)S(1)}, f32[26,32,64]{2,1,0:T(8,128)}, u32[]{:S(2)}) copy-start(f32[26,32,64]{2,1,0:T(8,128)} %copy-done.20) | copy-start | bytes 638980
  135.3 3.0 %copy-start.7 = (f32[14,128,256]{2,1,0:T(8,128)S(1)}, f32[14,128,256]{2,1,0:T(8,128)}, u32[]{:S(2)}) copy-start(f32[14,128,256]{2,1,0:T(8,128)} %copy-done.6) | copy-start | bytes 5505028
  (43 other events, 65.4 us)

commit v10 on v9

--- a/solution.py
+++ b/solution.py
@@ -185,10 +185,10 @@
     depth_table = mode_table(MZ, fine_total, positions)
     rows_table = mode_table(MY, fy, jnp.arange(fy, dtype=jnp.int32))
     cols_table = mode_table(MX, fx, jnp.arange(fx, dtype=jnp.int32))
-    along_depth = jnp.einsum("abe,az->zbe", kl_coeffs[0], depth_table, precision=HI)
-    along_rows = jnp.einsum("zbe,by->zye", along_depth, rows_table, precision=HI)
+    along_depth = jnp.einsum("abe,az->zbe", kl_coeffs[0], depth_table, precision=GRID)
+    along_rows = jnp.einsum("zbe,by->zye", along_depth, rows_table, precision=GRID)
     kl = jnp.dot(along_rows.reshape(k0_planes * fy, MX), cols_table,
-                 precision=HI).reshape(k0_planes, fy, fx)
+                 precision=GRID).reshape(k0_planes, fy, fx)
     k0 = jnp.exp(log_perm + kl)
     k0 = jnp.where(plane_mask(k0_first, k0_planes, fine_total), k0, 0.0)
     k0_halo = (k0_planes - fz) // 2

time: 147 us -> 145 us (0.986)
  matrix products: 17.3 us -> 15.6 us
    dot_general x3, matrix products: 7.21 us -> 5.57 us  [the longest x1 3.62 us: on_device(): jnp.dot(along_rows.reshape(k0_planes * fy, MX), cols_table, precision=GRID)]
  transfers between devices with their start and end apart: 10 -> 10, of which waited for: 9 -> 9; matrix products, arithmetic and copies ran while one was open for 7% -> 6% of each run, Pallas kernels for 0% -> 0%
where the time goes in v10:
time: 145 us
  starting transfers between devices  48.4 us (33%)
  other arithmetic  33.5 us (23%)
  waiting for transfers between devices  24.7 us (17%)
  local copies, waits for them, and re-layouts  16.7 us (12%)
  matrix products  15.6 us (11%)
  between operations  3.39 us (2%)
  blocking collectives  2.18 us (2%)
    ppermute x10, starting transfers between devices, shift_from(): return lax.ppermute(block, 'slab', pairs)  48.4 us
    ppermute x10, waiting for transfers between devices, shift_from(): return lax.ppermute(block, 'slab', pairs)  24.7 us
    select_n x11, other arithmetic, mask(): jnp.where(plane_mask(self.first + self.halo - h, u.shape[0], self.total),...  11.2 us
    unnamed x119, local copies, waits for them, and re-layouts  9.73 us
    dot_general x10, matrix products, along_y(): jnp.einsum('zyx,yv->zvx', values, jnp.asarray(matrix), precision=precisio...  6.4 us
    and x15, other arithmetic, plane_mask(): return ((g >= 0) & (g < total))[:, None, None]  6.19 us
    reduce_sum x6, other arithmetic, restrict_sum(): values = values.reshape(nz // 2, 2, ny, nx).sum(axis=1)  4.78 us
    dot_general x10, matrix products, along_x(): jnp.einsum('zyx,xw->zyw', values, jnp.asarray(matrix), precision=precisio...  3.65 us
  transfers between devices with their start and end apart: 10, of which 9 were waited for; matrix products, arithmetic and copies ran while one was open for 6% of the time, Pallas kernels for 0%

profile of v10, /device:TPU:24, one launch (start us, length us, event | category | flops | bytes accessed | tf_op | source)
XLA Modules:
  0.0 144.5 jit_solution(14648776884460450937)
XLA Ops:
  4.1 2.2 %all_gather.3 = bf16[8,4,64,128]{3,2,1,0:T(8,128)(2,1)S(1)} all-gather(bf16[4,4,64,128]{3,2,1,0:T(8,128)(2,1)S(1)} %gather_fusion), channel_id=1, replica_groups=mesh['chain'=2,'slab'=64] {'chain'}, dimensions={0}, use_global_device_ids=true | all-gather | bytes 786432 | tf_op jit(solution)/shard_map/all_gather | solution.py:147
  7.2 3.5 %collective-permute-start = (f32[512,256]{1,0:T(8,128)S(1)}, f32[512,256]{1,0:T(8,128)S(1)}, u32[]{:S(2)}, u32[]{:S(2)}) collective-permute-start(f32[512,256]{1,0:T(8,128)S(1)} %get-tuple-element.30), channel_id=1, source_target_pairs={{0,1},{1,2},{2,3},{3,4},{4,5},{5,6},{6,7},{7,8},{8,9},{9,10},{10,1... | collective-permute-start | bytes 1572872 | tf_op jit(solution)/shard_map/ppermute | solution.py:71
  10.8 4.6 %collective-permute-start.1 = (f32[512,256]{1,0:T(8,128)S(1)}, f32[512,256]{1,0:T(8,128)S(1)}, u32[]{:S(2)}, u32[]{:S(2)}) collective-permute-start(f32[512,256]{1,0:T(8,128)S(1)} %get-tuple-element.31), channel_id=1, source_target_pairs={{1,0},{2,1},{3,2},{4,3},{5,4},{6,5},{7,6},{8,7},{9,8},{10,9},{11,1... | collective-permute-start | bytes 1572872 | tf_op jit(solution)/shard_map/ppermute | solution.py:71
  21.8 3.5 %collective-permute-done = f32[512,256]{1,0:T(8,128)S(1)} collective-permute-done((f32[512,256]{1,0:T(8,128)S(1)}, f32[512,256]{1,0:T(8,128)S(1)}, u32[]{:S(2)}, u32[]{:S(2)}) %collective-permute-start) | collective-permute-done | bytes 524320 | tf_op jit(solution)/shard_map/ppermute | solution.py:71
  29.6 2.1 %copy.29 = f32[10,2,128,256]{3,2,1,0:T(8,128)} copy(f32[10,2,128,256]{2,3,0,1:T(8,128)S(1)} %pad_maximum_fusion) | data formatting | bytes 5242880 | tf_op jit(solution)/shard_map/stack | solution.py:180
  31.7 3.6 %fusion.3 = f32[20,128,256]{2,1,0:T(8,128)S(1)} fusion(f32[10,2,128,256]{3,2,1,0:T(8,128)} %copy.29, f32[20,128,64]{1,2,0:T(8,128)} %convolution_bitcast_fusion.3, pred[20]{0:T(512)(128)(4,1)S(1)} %compare_and_fusion.12, s32[256]{0:T(256)S(1)} %multiply_add_fusion, s32[64]{0:T(128)S(1)} %iota_add_fusion), kind=kOutput, calls=%fused_computation.8 | convolution fusion | flops 253198336 | bytes 5899540 | tf_op jit(solution)/shard_map/dot_general | solution.py:190
  36.7 1.8 %convolution_bitcast_fusion.2 = f32[10,64,256]{2,1,0:T(8,128)S(1)} fusion(f32[10,128,256]{2,1,0:T(8,128)} %reduce_sum.54, f32[128,64,1]{0,1,2:T(8,128)S(1)} %copy-done.30), kind=kOutput, calls=%fused_computation.75 | convolution fusion | flops 125829120 | bytes 1998848 | tf_op jit(solution)/shard_map/zyx,yv->zvx/dot_general | solution.py:50
  41.9 1.8 %copy-done.14 = f32[8,128,256]{2,1,0:T(8,128)S(1)} copy-done((f32[8,128,256]{2,1,0:T(8,128)S(1)}, f32[8,128,256]{2,1,0:T(8,128)}, u32[]{:S(2)}) %copy-start.14) | copy-done | bytes 1048600
  45.3 2.3 %fusion.19 = f32[12,128,256]{2,1,0:T(8,128)S(1)} fusion(f32[12,128,256]{2,1,0:T(8,128)S(1)} %slice.1360, f32[14,128,257]{2,1,0:T(8,128)S(1)} %fusion.1, f32[14,129,256]{2,1,0:T(8,128)S(1)} %add_multiply_fusion, f32[14,128,256]{2,1,0:T(8,128)S(1)} %get-tuple-element.11, f32[15,128,256]{2,1,0:T(8,128)S(1)} %fusion.4, ...), kind=kLoop, calls=%fused_computation.46 | loop fusion | flops 7077888 | bytes 18874380 | tf_op jit(solution)/shard_map/jit(_where)/select_n | solution.py:112
  49.9 3.2 %collective-permute-start.2 = (f32[6,64,128]{2,1,0:T(8,128)S(1)}, f32[6,64,128]{2,1,0:T(8,128)S(1)}, u32[]{:S(2)}, u32[]{:S(2)}) collective-permute-start(f32[6,64,128]{2,1,0:T(8,128)S(1)} %get-tuple-element.28), channel_id=1, source_target_pairs={{0,1},{1,2},{2,3},{3,4},{4,5},{5,6},{6,7},{7,8},{8,9},{9,10},{10,1... | collective-permute-start | bytes 589832 | tf_op jit(solution)/shard_map/ppermute | solution.py:71
  53.1 5.4 %collective-permute-start.3 = (f32[6,64,128]{2,1,0:T(8,128)S(1)}, f32[6,64,128]{2,1,0:T(8,128)S(1)}, u32[]{:S(2)}, u32[]{:S(2)}) collective-permute-start(f32[6,64,128]{2,1,0:T(8,128)S(1)} %get-tuple-element.29), channel_id=1, source_target_pairs={{1,0},{2,1},{3,2},{4,3},{5,4},{6,5},{7,6},{8,7},{9,8},{10,9},{11,1... | collective-permute-start | bytes 589832 | tf_op jit(solution)/shard_map/ppermute | solution.py:71
  64.2 6.5 %collective-permute-start.7 = (f32[1,2,2,32,64]{4,3,2,1,0:T(8,128)S(1)}, f32[1,2,2,32,64]{4,3,2,1,0:T(8,128)S(1)}, u32[]{:S(2)}, u32[]{:S(2)}) collective-permute-start(f32[1,2,2,32,64]{4,3,2,1,0:T(8,128)S(1)} %maximum_bitcast_fusion), channel_id=1, source_target_pairs={{1,0},{2,1},{3,2},{4,3},{5,4},{6,5},{7,6},{8,7},{9,8},{10,9},{11,1... | collective-permute-start | bytes 98312 | tf_op jit(solution)/shard_map/ppermute | solution.py:71
  70.7 1.9 %collective-permute-start.4 = (f32[1,2,2,32,64]{4,3,2,1,0:T(8,128)S(1)}, f32[1,2,2,32,64]{4,3,2,1,0:T(8,128)S(1)}, u32[]{:S(2)}, u32[]{:S(2)}) collective-permute-start(f32[1,2,2,32,64]{4,3,2,1,0:T(8,128)S(1)} %maximum_bitcast_fusion), channel_id=1, source_target_pairs={{0,1},{1,2},{2,3},{3,4},{4,5},{5,6},{6,7},{7,8},{8,9},{9,10},{10,1... | collective-permute-start | bytes 98312 | tf_op jit(solution)/shard_map/ppermute | solution.py:71
  73.3 5.7 %collective-permute-done.4 = f32[1,2,2,32,64]{4,3,2,1,0:T(8,128)S(1)} collective-permute-done((f32[1,2,2,32,64]{4,3,2,1,0:T(8,128)S(1)}, f32[1,2,2,32,64]{4,3,2,1,0:T(8,128)S(1)}, u32[]{:S(2)}, u32[]{:S(2)}) %collective-permute-start.4) | collective-permute-done | bytes 32800 | tf_op jit(solution)/shard_map/ppermute | solution.py:71
  79.0 1.9 %collective-permute-start.8 = (f32[2,2,2,32,64]{4,3,2,1,0:T(8,128)S(1)}, f32[2,2,2,32,64]{4,3,2,1,0:T(8,128)S(1)}, u32[]{:S(2)}, u32[]{:S(2)}) collective-permute-start(f32[2,2,2,32,64]{4,3,2,1,0:T(8,128)S(1)} %get-tuple-element.35), channel_id=1, source_target_pairs={{2,0},{3,1},{4,2},{5,3},{6,4},{7,5},{8,6},{9,7},{10,8},{11,9},{12,... | collective-permute-start | bytes 196616 | tf_op jit(solution)/shard_map/ppermute | solution.py:71
  81.0 5.4 %collective-permute-start.5 = (f32[2,2,2,32,64]{4,3,2,1,0:T(8,128)S(1)}, f32[2,2,2,32,64]{4,3,2,1,0:T(8,128)S(1)}, u32[]{:S(2)}, u32[]{:S(2)}) collective-permute-start(f32[2,2,2,32,64]{4,3,2,1,0:T(8,128)S(1)} %get-tuple-element.36), channel_id=1, source_target_pairs={{0,2},{1,3},{2,4},{3,5},{4,6},{5,7},{6,8},{7,9},{8,10},{9,11},{10,... | collective-permute-start | bytes 196616 | tf_op jit(solution)/shard_map/ppermute | solution.py:71
  87.4 2.8 %collective-permute-done.5 = f32[2,2,2,32,64]{4,3,2,1,0:T(8,128)S(1)} collective-permute-done((f32[2,2,2,32,64]{4,3,2,1,0:T(8,128)S(1)}, f32[2,2,2,32,64]{4,3,2,1,0:T(8,128)S(1)}, u32[]{:S(2)}, u32[]{:S(2)}) %collective-permute-start.5) | collective-permute-done | bytes 65568 | tf_op jit(solution)/shard_map/ppermute | solution.py:71
  90.3 14.0 %collective-permute-start.6 = (f32[4,2,2,32,64]{4,3,2,1,0:T(8,128)S(1)}, f32[4,2,2,32,64]{4,3,2,1,0:T(8,128)S(1)}, u32[]{:S(2)}, u32[]{:S(2)}) collective-permute-start(f32[4,2,2,32,64]{4,3,2,1,0:T(8,128)S(1)} %get-tuple-element.34), channel_id=1, source_target_pairs={{0,4},{1,5},{2,6},{3,7},{4,8},{5,9},{6,10},{7,11},{8,12},{9,13},{1... | collective-permute-start | bytes 393224 | tf_op jit(solution)/shard_map/ppermute | solution.py:71
  105.6 1.9 %collective-permute-start.9 = (f32[4,2,2,32,64]{4,3,2,1,0:T(8,128)S(1)}, f32[4,2,2,32,64]{4,3,2,1,0:T(8,128)S(1)}, u32[]{:S(2)}, u32[]{:S(2)}) collective-permute-start(f32[4,2,2,32,64]{4,3,2,1,0:T(8,128)S(1)} %get-tuple-element.33), channel_id=1, source_target_pairs={{4,0},{5,1},{6,2},{7,3},{8,4},{9,5},{10,6},{11,7},{12,8},{13,9},{1... | collective-permute-start | bytes 393224 | tf_op jit(solution)/shard_map/ppermute | solution.py:71
  108.3 7.6 %collective-permute-done.9 = f32[4,2,2,32,64]{4,3,2,1,0:T(8,128)S(1)} collective-permute-done((f32[4,2,2,32,64]{4,3,2,1,0:T(8,128)S(1)}, f32[4,2,2,32,64]{4,3,2,1,0:T(8,128)S(1)}, u32[]{:S(2)}, u32[]{:S(2)}) %collective-permute-start.9) | collective-permute-done | bytes 131104 | tf_op jit(solution)/shard_map/ppermute | solution.py:71
  120.9 1.7 %reduce_sum.58 = f32[11,32,64]{2,1,0:T(8,128)} reduce(f32[11,2,32,64]{3,2,1,0:T(8,128)} %bitcast.150, f32[]{:T(128)} %constant.129.clone.1), dimensions={1}, to_apply=%region_5.6 | reduce | flops 22528 | bytes 270340 | tf_op jit(solution)/shard_map/reduce_sum | solution.py:56
  134.1 2.0 %bitcast_add_fusion.1 = f32[12,128,256]{2,1,0:T(8,128)S(1)} fusion(f32[12,128,256]{2,1,0:T(8,128)} %copy-done.8, f32[6,128,256]{2,1,0:T(8,128)} %copy.32), kind=kLoop, calls=%fused_computation.45 | loop fusion | flops 393216 | bytes 3932160 | tf_op jit(solution)/shard_map/add | solution.py:254
  138.0 3.1 %fusion.38 = f32[10,128,256]{2,1,0:T(8,128)S(1)} fusion(f32[10,128,256]{2,1,0:T(8,128)S(1)} %slice.1538, f32[14,128,257]{2,1,0:T(8,128)S(1)} %copy-done.5, f32[14,129,256]{2,1,0:T(8,128)S(1)} %add_multiply_fusion, f32[12,128,256]{2,1,0:T(8,128)S(1)} %bitcast_add_fusion.1, f32[15,128,256]{2,1,0:T(8,128)S(1)} %copy-done.3, f32[14,128,256]{2,1,0:T(8,128)S(1)} %copy-done.7, ...), kind=kLoop, calls=%fused_computation.73 | loop fusion | flops 5898240 | bytes 15728650 | tf_op jit(solution)/shard_map/jit(_where)/select_n | solution.py:112
  142.3 2.2 %select_bitcast_fusion = f32[1,8,128,256]{3,2,1,0:T(8,128)} fusion(f32[8,128,256]{2,1,0:T(8,128)S(1)} %slice.1549, f32[8,128,256]{2,1,0:T(8,128)S(1)} %copy-done.15, f32[10,128,256]{2,1,0:T(8,128)S(1)} %fusion.38, f32[14,128,257]{2,1,0:T(8,128)S(1)} %copy-done.5, f32[14,129,256]{2,1,0:T(8,128)S(1)} %add_multiply_fusion, f32[15,128,256]{2,1,0:T(8,128)S(1)} %copy-done.3, ...), kind=kLoop, calls=%fused_computation.125 | loop fusion | flops 4718592 | bytes 12582920 | tf_op jit(solution)/shard_map/broadcast_in_dim | solution.py:257
  (251 shorter events, 50.2 us)
Async XLA Ops:
  0.0 3.5 %copy-start = (bf16[4,4,4,64,128]{4,3,2,1,0:T(8,128)(2,1)S(1)}, bf16[4,4,4,64,128]{4,3,2,1,0:T(8,128)(2,1)}, u32[]{:S(2)}) copy-start(bf16[4,4,4,64,128]{4,3,2,1,0:T(8,128)(2,1)} %param.25) | copy-start | bytes 3145732
  0.0 7.0 %copy-start.13 = (f32[8,128,256]{2,1,0:T(8,128)S(1)}, f32[8,128,256]{2,1,0:T(8,128)}, u32[]{:S(2)}) copy-start(f32[8,128,256]{2,1,0:T(8,128)} %param.29) | copy-start | bytes 3145732
  7.1 12.8 %copy-start.38 = (f32[1,32,16,64]{3,2,1,0:T(8,128)S(1)}, f32[1,32,16,64]{3,2,1,0:T(8,128)}, u32[]{:S(2)}) copy-start(f32[1,32,16,64]{3,2,1,0:T(8,128)} %param.28) | copy-start | bytes 393220
  7.2 20.1 %copy-start.41 = (bf16[128,256,1]{1,0,2:T(8,128)(2,1)S(1)}, bf16[128,256,1]{1,0,2:T(8,128)(2,1)}, u32[]{:S(2)}) copy-start(bf16[128,256,1]{1,0,2:T(8,128)(2,1)} %constant.357) | copy-start | bytes 196612
  7.2 18.1 %collective-permute-start = (f32[512,256]{1,0:T(8,128)S(1)}, f32[512,256]{1,0:T(8,128)S(1)}, u32[]{:S(2)}, u32[]{:S(2)}) collective-permute-start(f32[512,256]{1,0:T(8,128)S(1)} %get-tuple-element.30), channel_id=1, source_target_pairs={{0,1},{1,2},{2,3},{3,4},{4,5},{5,6},{6,7},{7,8},{8,9},{9,10},{10,1... | collective-permute-start | bytes 1572872 | tf_op jit(solution)/shard_map/ppermute | solution.py:71
  10.8 15.7 %collective-permute-start.1 = (f32[512,256]{1,0:T(8,128)S(1)}, f32[512,256]{1,0:T(8,128)S(1)}, u32[]{:S(2)}, u32[]{:S(2)}) collective-permute-start(f32[512,256]{1,0:T(8,128)S(1)} %get-tuple-element.31), channel_id=1, source_target_pairs={{1,0},{2,1},{3,2},{4,3},{5,4},{6,5},{7,6},{8,7},{9,8},{10,9},{11,1... | collective-permute-start | bytes 1572872 | tf_op jit(solution)/shard_map/ppermute | solution.py:71
  19.9 7.8 %copy-start.42 = (f32[64,128,1]{1,0,2:T(8,128)S(1)}, f32[64,128,1]{1,0,2:T(8,128)}, u32[]{:S(2)}) copy-start(f32[64,128,1]{1,0,2:T(8,128)} %constant.358) | copy-start | bytes 98308
  40.0 7.8 %copy-start.2 = (f32[15,128,256]{2,1,0:T(8,128)}, f32[15,128,256]{2,1,0:T(8,128)S(1)}, u32[]{:S(2)}) copy-start(f32[15,128,256]{2,1,0:T(8,128)S(1)} %fusion.4) | copy-start | bytes 5898244
  41.7 6.2 %copy-start.4 = (f32[14,128,257]{2,1,0:T(8,128)}, f32[14,128,257]{2,1,0:T(8,128)S(1)}, u32[]{:S(2)}) copy-start(f32[14,128,257]{2,1,0:T(8,128)S(1)} %fusion.1) | copy-start | bytes 5526532
  49.2 9.2 %copy-start.37 = (f32[64,32,1]{0,1,2:T(8,128)S(1)}, f32[64,32,1]{0,1,2:T(8,128)}, u32[]{:S(2)}) copy-start(f32[64,32,1]{0,1,2:T(8,128)} %constant.361) | copy-start | bytes 24580
  49.9 10.6 %collective-permute-start.2 = (f32[6,64,128]{2,1,0:T(8,128)S(1)}, f32[6,64,128]{2,1,0:T(8,128)S(1)}, u32[]{:S(2)}, u32[]{:S(2)}) collective-permute-start(f32[6,64,128]{2,1,0:T(8,128)S(1)} %get-tuple-element.28), channel_id=1, source_target_pairs={{0,1},{1,2},{2,3},{3,4},{4,5},{5,6},{6,7},{7,8},{8,9},{9,10},{10,1... | collective-permute-start | bytes 589832 | tf_op jit(solution)/shard_map/ppermute | solution.py:71
  53.1 8.5 %collective-permute-start.3 = (f32[6,64,128]{2,1,0:T(8,128)S(1)}, f32[6,64,128]{2,1,0:T(8,128)S(1)}, u32[]{:S(2)}, u32[]{:S(2)}) collective-permute-start(f32[6,64,128]{2,1,0:T(8,128)S(1)} %get-tuple-element.29), channel_id=1, source_target_pairs={{1,0},{2,1},{3,2},{4,3},{5,4},{6,5},{7,6},{8,7},{9,8},{10,9},{11,1... | collective-permute-start | bytes 589832 | tf_op jit(solution)/shard_map/ppermute | solution.py:71
  64.2 9.0 %collective-permute-start.7 = (f32[1,2,2,32,64]{4,3,2,1,0:T(8,128)S(1)}, f32[1,2,2,32,64]{4,3,2,1,0:T(8,128)S(1)}, u32[]{:S(2)}, u32[]{:S(2)}) collective-permute-start(f32[1,2,2,32,64]{4,3,2,1,0:T(8,128)S(1)} %maximum_bitcast_fusion), channel_id=1, source_target_pairs={{1,0},{2,1},{3,2},{4,3},{5,4},{6,5},{7,6},{8,7},{9,8},{10,9},{11,1... | collective-permute-start | bytes 98312 | tf_op jit(solution)/shard_map/ppermute | solution.py:71
  70.7 8.3 %collective-permute-start.4 = (f32[1,2,2,32,64]{4,3,2,1,0:T(8,128)S(1)}, f32[1,2,2,32,64]{4,3,2,1,0:T(8,128)S(1)}, u32[]{:S(2)}, u32[]{:S(2)}) collective-permute-start(f32[1,2,2,32,64]{4,3,2,1,0:T(8,128)S(1)} %maximum_bitcast_fusion), channel_id=1, source_target_pairs={{0,1},{1,2},{2,3},{3,4},{4,5},{5,6},{6,7},{7,8},{8,9},{9,10},{10,1... | collective-permute-start | bytes 98312 | tf_op jit(solution)/shard_map/ppermute | solution.py:71
  79.0 8.4 %collective-permute-start.8 = (f32[2,2,2,32,64]{4,3,2,1,0:T(8,128)S(1)}, f32[2,2,2,32,64]{4,3,2,1,0:T(8,128)S(1)}, u32[]{:S(2)}, u32[]{:S(2)}) collective-permute-start(f32[2,2,2,32,64]{4,3,2,1,0:T(8,128)S(1)} %get-tuple-element.35), channel_id=1, source_target_pairs={{2,0},{3,1},{4,2},{5,3},{6,4},{7,5},{8,6},{9,7},{10,8},{11,9},{12,... | collective-permute-start | bytes 196616 | tf_op jit(solution)/shard_map/ppermute | solution.py:71
  81.0 9.3 %collective-permute-start.5 = (f32[2,2,2,32,64]{4,3,2,1,0:T(8,128)S(1)}, f32[2,2,2,32,64]{4,3,2,1,0:T(8,128)S(1)}, u32[]{:S(2)}, u32[]{:S(2)}) collective-permute-start(f32[2,2,2,32,64]{4,3,2,1,0:T(8,128)S(1)} %get-tuple-element.36), channel_id=1, source_target_pairs={{0,2},{1,3},{2,4},{3,5},{4,6},{5,7},{6,8},{7,9},{8,10},{9,11},{10,... | collective-permute-start | bytes 196616 | tf_op jit(solution)/shard_map/ppermute | solution.py:71
  90.3 17.9 %collective-permute-start.6 = (f32[4,2,2,32,64]{4,3,2,1,0:T(8,128)S(1)}, f32[4,2,2,32,64]{4,3,2,1,0:T(8,128)S(1)}, u32[]{:S(2)}, u32[]{:S(2)}) collective-permute-start(f32[4,2,2,32,64]{4,3,2,1,0:T(8,128)S(1)} %get-tuple-element.34), channel_id=1, source_target_pairs={{0,4},{1,5},{2,6},{3,7},{4,8},{5,9},{6,10},{7,11},{8,12},{9,13},{1... | collective-permute-start | bytes 393224 | tf_op jit(solution)/shard_map/ppermute | solution.py:71
  105.6 10.4 %collective-permute-start.9 = (f32[4,2,2,32,64]{4,3,2,1,0:T(8,128)S(1)}, f32[4,2,2,32,64]{4,3,2,1,0:T(8,128)S(1)}, u32[]{:S(2)}, u32[]{:S(2)}) collective-permute-start(f32[4,2,2,32,64]{4,3,2,1,0:T(8,128)S(1)} %get-tuple-element.33), channel_id=1, source_target_pairs={{4,0},{5,1},{6,2},{7,3},{8,4},{9,5},{10,6},{11,7},{12,8},{13,9},{1... | collective-permute-start | bytes 393224 | tf_op jit(solution)/shard_map/ppermute | solution.py:71
  122.6 3.5 %copy-start.29 = (f32[11,17,32]{2,1,0:T(8,128)S(1)}, f32[11,17,32]{2,1,0:T(8,128)}, u32[]{:S(2)}) copy-start(f32[11,17,32]{2,1,0:T(8,128)} %fusion.150) | copy-start | bytes 71812
  122.6 3.5 %copy-start.53 = (pred[7]{0:T(512)(128)(4,1)S(1)}, pred[7]{0:T(512)(128)(4,1)}, u32[]{:S(2)}) copy-start(pred[7]{0:T(512)(128)(4,1)} %compare_and_fusion.2) | copy-start | bytes 25
  122.6 3.7 %copy-start.44 = (f32[32,64,1]{1,0,2:T(8,128)S(1)}, f32[32,64,1]{1,0,2:T(8,128)}, u32[]{:S(2)}) copy-start(f32[32,64,1]{1,0,2:T(8,128)} %constant.363) | copy-start | bytes 24580
  122.6 3.7 %copy-start.56 = (pred[5]{0:T(512)(128)(4,1)S(1)}, pred[5]{0:T(512)(128)(4,1)}, u32[]{:S(2)}) copy-start(pred[5]{0:T(512)(128)(4,1)} %compare_and_fusion.3) | copy-start | bytes 19
  124.9 2.9 %copy-start.21 = (f32[26,32,64]{2,1,0:T(8,128)S(1)}, f32[26,32,64]{2,1,0:T(8,128)}, u32[]{:S(2)}) copy-start(f32[26,32,64]{2,1,0:T(8,128)} %copy-done.20) | copy-start | bytes 638980
  134.1 3.0 %copy-start.7 = (f32[14,128,256]{2,1,0:T(8,128)S(1)}, f32[14,128,256]{2,1,0:T(8,128)}, u32[]{:S(2)}) copy-start(f32[14,128,256]{2,1,0:T(8,128)} %copy-done.6) | copy-start | bytes 5505028
  (43 other events, 65.4 us)

commit v11 on v10

--- a/solution.py
+++ b/solution.py
@@ -54,14 +54,14 @@
 def restrict_sum(values):
     nz, ny, nx = values.shape
     values = values.reshape(nz // 2, 2, ny, nx).sum(axis=1)
-    values = along_y(values, pair_sum_matrix(ny), GRID)
-    return along_x(values, pair_sum_matrix(nx), GRID)
+    values = along_x(values, pair_sum_matrix(nx), GRID)
+    return along_y(values, pair_sum_matrix(ny), GRID)
 
 
 def copy_up(values):
     nz, ny, nx = values.shape
+    values = along_y(values, repeat_matrix(ny), GRID)
     values = along_x(values, repeat_matrix(nx), GRID)
-    values = along_y(values, repeat_matrix(ny), GRID)
     return jnp.repeat(values, 2, axis=0)
 
 

time: 145 us -> 142 us (0.979)
  other arithmetic: 33.5 us -> 30.6 us
    dot_general x10, matrix products: 3.65 us -> 5.55 us  [along_x(): jnp.einsum('zyx,xw->zyw', values, jnp.asarray(matrix), precision=precisio...]
    add x1, other arithmetic: 1.97 us -> 0.15 us  [on_device(): u = u1 + copy_up(e1)]
    unnamed x119 -> x123, local copies, waits for them, and re-layouts: 9.73 us -> 10.1 us
  transfers between devices with their start and end apart: 10 -> 10, of which waited for: 9 -> 9; matrix products, arithmetic and copies ran while one was open for 6% -> 7% of each run, Pallas kernels for 0% -> 0%
where the time goes in v11:
time: 142 us; the launch traced here: 141 us
  starting transfers between devices  48.4 us (34%)
  other arithmetic  30.6 us (22%)
  waiting for transfers between devices  24.7 us (17%)
  matrix products  16.1 us (11%)
  local copies, waits for them, and re-layouts  15.9 us (11%)
  between operations  3.42 us (2%)
  blocking collectives  2.18 us (2%)
    ppermute x10, starting transfers between devices, shift_from(): return lax.ppermute(block, 'slab', pairs)  48.4 us
    ppermute x10, waiting for transfers between devices, shift_from(): return lax.ppermute(block, 'slab', pairs)  24.7 us
    unnamed x123, local copies, waits for them, and re-layouts  10.1 us
    select_n x11, other arithmetic, mask(): jnp.where(plane_mask(self.first + self.halo - h, u.shape[0], self.total),...  10.1 us
    and x15, other arithmetic, plane_mask(): return ((g >= 0) & (g < total))[:, None, None]  6.22 us
    dot_general x10, matrix products, along_x(): jnp.einsum('zyx,xw->zyw', values, jnp.asarray(matrix), precision=precisio...  5.55 us
    dot_general x10, matrix products, along_y(): jnp.einsum('zyx,yv->zvx', values, jnp.asarray(matrix), precision=precisio...  5.03 us
    reduce_sum x6, other arithmetic, restrict_sum(): values = values.reshape(nz // 2, 2, ny, nx).sum(axis=1)  4.77 us
  transfers between devices with their start and end apart: 10, of which 9 were waited for; matrix products, arithmetic and copies ran while one was open for 7% of the time, Pallas kernels for 0%

profile of v11, /device:TPU:24, one launch (start us, length us, event | category | flops | bytes accessed | tf_op | source)
XLA Modules:
  0.0 141.3 jit_solution(8757072301757125401)
XLA Ops:
  4.1 2.2 %all_gather.3 = bf16[8,4,64,128]{3,2,1,0:T(8,128)(2,1)S(1)} all-gather(bf16[4,4,64,128]{3,2,1,0:T(8,128)(2,1)S(1)} %gather_fusion), channel_id=1, replica_groups=mesh['chain'=2,'slab'=64] {'chain'}, dimensions={0}, use_global_device_ids=true | all-gather | bytes 786432 | tf_op jit(solution)/shard_map/all_gather | solution.py:147
  7.2 3.5 %collective-permute-start = (f32[512,256]{1,0:T(8,128)S(1)}, f32[512,256]{1,0:T(8,128)S(1)}, u32[]{:S(2)}, u32[]{:S(2)}) collective-permute-start(f32[512,256]{1,0:T(8,128)S(1)} %get-tuple-element.30), channel_id=1, source_target_pairs={{0,1},{1,2},{2,3},{3,4},{4,5},{5,6},{6,7},{7,8},{8,9},{9,10},{10,1... | collective-permute-start | bytes 1572872 | tf_op jit(solution)/shard_map/ppermute | solution.py:71
  10.8 4.6 %collective-permute-start.1 = (f32[512,256]{1,0:T(8,128)S(1)}, f32[512,256]{1,0:T(8,128)S(1)}, u32[]{:S(2)}, u32[]{:S(2)}) collective-permute-start(f32[512,256]{1,0:T(8,128)S(1)} %get-tuple-element.31), channel_id=1, source_target_pairs={{1,0},{2,1},{3,2},{4,3},{5,4},{6,5},{7,6},{8,7},{9,8},{10,9},{11,1... | collective-permute-start | bytes 1572872 | tf_op jit(solution)/shard_map/ppermute | solution.py:71
  21.9 3.4 %collective-permute-done = f32[512,256]{1,0:T(8,128)S(1)} collective-permute-done((f32[512,256]{1,0:T(8,128)S(1)}, f32[512,256]{1,0:T(8,128)S(1)}, u32[]{:S(2)}, u32[]{:S(2)}) %collective-permute-start) | collective-permute-done | bytes 524320 | tf_op jit(solution)/shard_map/ppermute | solution.py:71
  29.6 2.1 %copy.27 = f32[10,2,128,256]{3,2,1,0:T(8,128)} copy(f32[10,2,128,256]{2,3,0,1:T(8,128)S(1)} %pad_maximum_fusion) | data formatting | bytes 5242880 | tf_op jit(solution)/shard_map/stack | solution.py:180
  31.7 3.6 %fusion.3 = f32[20,128,256]{2,1,0:T(8,128)S(1)} fusion(f32[10,2,128,256]{3,2,1,0:T(8,128)} %copy.27, f32[20,128,64]{1,2,0:T(8,128)} %convolution_bitcast_fusion.1, pred[20]{0:T(512)(128)(4,1)S(1)} %compare_and_fusion.12, s32[256]{0:T(256)S(1)} %multiply_add_fusion, s32[64]{0:T(128)S(1)} %iota_add_fusion), kind=kOutput, calls=%fused_computation.8 | convolution fusion | flops 253198336 | bytes 5899540 | tf_op jit(solution)/shard_map/dot_general | solution.py:190
  36.7 2.0 %fusion.312 = f32[10,128,128]{2,1,0:T(8,128)S(1)} fusion(f32[10,128,256]{2,1,0:T(8,128)} %reduce_sum.54, f32[256,128,1]{1,0,2:T(8,128)S(1)} %copy-done.32), kind=kOutput, calls=%fused_computation.535 | convolution fusion | flops 251658240 | bytes 2097152 | tf_op jit(solution)/shard_map/zyx,xw->zyw/dot_general | solution.py:45
  41.9 1.8 %copy-done.15 = f32[8,128,256]{2,1,0:T(8,128)S(1)} copy-done((f32[8,128,256]{2,1,0:T(8,128)S(1)}, f32[8,128,256]{2,1,0:T(8,128)}, u32[]{:S(2)}) %copy-start.15) | copy-done | bytes 1048600
  45.4 2.4 %fusion.19 = f32[12,128,256]{2,1,0:T(8,128)S(1)} fusion(f32[12,128,256]{2,1,0:T(8,128)S(1)} %slice.1360, f32[14,128,257]{2,1,0:T(8,128)S(1)} %fusion.1, f32[14,129,256]{2,1,0:T(8,128)S(1)} %add_multiply_fusion, f32[14,128,256]{2,1,0:T(8,128)S(1)} %get-tuple-element.11, f32[15,128,256]{2,1,0:T(8,128)S(1)} %fusion.4, ...), kind=kLoop, calls=%fused_computation.46 | loop fusion | flops 7077888 | bytes 18874380 | tf_op jit(solution)/shard_map/jit(_where)/select_n | solution.py:112
  50.0 3.2 %collective-permute-start.2 = (f32[6,64,128]{2,1,0:T(8,128)S(1)}, f32[6,64,128]{2,1,0:T(8,128)S(1)}, u32[]{:S(2)}, u32[]{:S(2)}) collective-permute-start(f32[6,64,128]{2,1,0:T(8,128)S(1)} %get-tuple-element.28), channel_id=1, source_target_pairs={{0,1},{1,2},{2,3},{3,4},{4,5},{5,6},{6,7},{7,8},{8,9},{9,10},{10,1... | collective-permute-start | bytes 589832 | tf_op jit(solution)/shard_map/ppermute | solution.py:71
  53.2 5.4 %collective-permute-start.3 = (f32[6,64,128]{2,1,0:T(8,128)S(1)}, f32[6,64,128]{2,1,0:T(8,128)S(1)}, u32[]{:S(2)}, u32[]{:S(2)}) collective-permute-start(f32[6,64,128]{2,1,0:T(8,128)S(1)} %get-tuple-element.29), channel_id=1, source_target_pairs={{1,0},{2,1},{3,2},{4,3},{5,4},{6,5},{7,6},{8,7},{9,8},{10,9},{11,1... | collective-permute-start | bytes 589832 | tf_op jit(solution)/shard_map/ppermute | solution.py:71
  58.9 1.6 %collective-permute-done.2 = f32[6,64,128]{2,1,0:T(8,128)S(1)} collective-permute-done((f32[6,64,128]{2,1,0:T(8,128)S(1)}, f32[6,64,128]{2,1,0:T(8,128)S(1)}, u32[]{:S(2)}, u32[]{:S(2)}) %collective-permute-start.2) | collective-permute-done | bytes 196640 | tf_op jit(solution)/shard_map/ppermute | solution.py:71
  64.4 6.5 %collective-permute-start.7 = (f32[1,2,2,32,64]{4,3,2,1,0:T(8,128)S(1)}, f32[1,2,2,32,64]{4,3,2,1,0:T(8,128)S(1)}, u32[]{:S(2)}, u32[]{:S(2)}) collective-permute-start(f32[1,2,2,32,64]{4,3,2,1,0:T(8,128)S(1)} %maximum_bitcast_fusion), channel_id=1, source_target_pairs={{1,0},{2,1},{3,2},{4,3},{5,4},{6,5},{7,6},{8,7},{9,8},{10,9},{11,1... | collective-permute-start | bytes 98312 | tf_op jit(solution)/shard_map/ppermute | solution.py:71
  70.9 1.9 %collective-permute-start.4 = (f32[1,2,2,32,64]{4,3,2,1,0:T(8,128)S(1)}, f32[1,2,2,32,64]{4,3,2,1,0:T(8,128)S(1)}, u32[]{:S(2)}, u32[]{:S(2)}) collective-permute-start(f32[1,2,2,32,64]{4,3,2,1,0:T(8,128)S(1)} %maximum_bitcast_fusion), channel_id=1, source_target_pairs={{0,1},{1,2},{2,3},{3,4},{4,5},{5,6},{6,7},{7,8},{8,9},{9,10},{10,1... | collective-permute-start | bytes 98312 | tf_op jit(solution)/shard_map/ppermute | solution.py:71
  73.4 5.7 %collective-permute-done.4 = f32[1,2,2,32,64]{4,3,2,1,0:T(8,128)S(1)} collective-permute-done((f32[1,2,2,32,64]{4,3,2,1,0:T(8,128)S(1)}, f32[1,2,2,32,64]{4,3,2,1,0:T(8,128)S(1)}, u32[]{:S(2)}, u32[]{:S(2)}) %collective-permute-start.4) | collective-permute-done | bytes 32800 | tf_op jit(solution)/shard_map/ppermute | solution.py:71
  79.2 1.9 %collective-permute-start.8 = (f32[2,2,2,32,64]{4,3,2,1,0:T(8,128)S(1)}, f32[2,2,2,32,64]{4,3,2,1,0:T(8,128)S(1)}, u32[]{:S(2)}, u32[]{:S(2)}) collective-permute-start(f32[2,2,2,32,64]{4,3,2,1,0:T(8,128)S(1)} %get-tuple-element.34), channel_id=1, source_target_pairs={{2,0},{3,1},{4,2},{5,3},{6,4},{7,5},{8,6},{9,7},{10,8},{11,9},{12,... | collective-permute-start | bytes 196616 | tf_op jit(solution)/shard_map/ppermute | solution.py:71
  81.1 5.4 %collective-permute-start.5 = (f32[2,2,2,32,64]{4,3,2,1,0:T(8,128)S(1)}, f32[2,2,2,32,64]{4,3,2,1,0:T(8,128)S(1)}, u32[]{:S(2)}, u32[]{:S(2)}) collective-permute-start(f32[2,2,2,32,64]{4,3,2,1,0:T(8,128)S(1)} %get-tuple-element.35), channel_id=1, source_target_pairs={{0,2},{1,3},{2,4},{3,5},{4,6},{5,7},{6,8},{7,9},{8,10},{9,11},{10,... | collective-permute-start | bytes 196616 | tf_op jit(solution)/shard_map/ppermute | solution.py:71
  87.5 2.8 %collective-permute-done.5 = f32[2,2,2,32,64]{4,3,2,1,0:T(8,128)S(1)} collective-permute-done((f32[2,2,2,32,64]{4,3,2,1,0:T(8,128)S(1)}, f32[2,2,2,32,64]{4,3,2,1,0:T(8,128)S(1)}, u32[]{:S(2)}, u32[]{:S(2)}) %collective-permute-start.5) | collective-permute-done | bytes 65568 | tf_op jit(solution)/shard_map/ppermute | solution.py:71
  90.4 14.0 %collective-permute-start.6 = (f32[4,2,2,32,64]{4,3,2,1,0:T(8,128)S(1)}, f32[4,2,2,32,64]{4,3,2,1,0:T(8,128)S(1)}, u32[]{:S(2)}, u32[]{:S(2)}) collective-permute-start(f32[4,2,2,32,64]{4,3,2,1,0:T(8,128)S(1)} %get-tuple-element.33), channel_id=1, source_target_pairs={{0,4},{1,5},{2,6},{3,7},{4,8},{5,9},{6,10},{7,11},{8,12},{9,13},{1... | collective-permute-start | bytes 393224 | tf_op jit(solution)/shard_map/ppermute | solution.py:71
  105.7 1.9 %collective-permute-start.9 = (f32[4,2,2,32,64]{4,3,2,1,0:T(8,128)S(1)}, f32[4,2,2,32,64]{4,3,2,1,0:T(8,128)S(1)}, u32[]{:S(2)}, u32[]{:S(2)}) collective-permute-start(f32[4,2,2,32,64]{4,3,2,1,0:T(8,128)S(1)} %get-tuple-element.32), channel_id=1, source_target_pairs={{4,0},{5,1},{6,2},{7,3},{8,4},{9,5},{10,6},{11,7},{12,8},{13,9},{1... | collective-permute-start | bytes 393224 | tf_op jit(solution)/shard_map/ppermute | solution.py:71
  108.4 7.6 %collective-permute-done.9 = f32[4,2,2,32,64]{4,3,2,1,0:T(8,128)S(1)} collective-permute-done((f32[4,2,2,32,64]{4,3,2,1,0:T(8,128)S(1)}, f32[4,2,2,32,64]{4,3,2,1,0:T(8,128)S(1)}, u32[]{:S(2)}, u32[]{:S(2)}) %collective-permute-start.9) | collective-permute-done | bytes 131104 | tf_op jit(solution)/shard_map/ppermute | solution.py:71
  120.8 1.7 %reduce_sum.58 = f32[11,32,64]{2,1,0:T(8,128)} reduce(f32[11,2,32,64]{3,2,1,0:T(8,128)} %bitcast.154, f32[]{:T(128)} %constant.129.clone.1), dimensions={1}, to_apply=%region_5.6 | reduce | flops 22528 | bytes 270340 | tf_op jit(solution)/shard_map/reduce_sum | solution.py:56
  135.9 2.0 %fusion.38 = f32[10,128,256]{2,1,0:T(8,128)S(1)} fusion(f32[10,128,256]{2,1,0:T(8,128)S(1)} %slice.1538, f32[14,128,257]{2,1,0:T(8,128)S(1)} %copy-done.5, f32[14,129,256]{2,1,0:T(8,128)S(1)} %add_multiply_fusion, f32[12,128,256]{2,1,0:T(8,128)S(1)} %bitcast_add_fusion.1, f32[15,128,256]{2,1,0:T(8,128)S(1)} %copy-done.3, f32[14,128,256]{2,1,0:T(8,128)S(1)} %copy-done.7, ...), kind=kLoop, calls=%fused_computation.73 | loop fusion | flops 5898240 | bytes 15728650 | tf_op jit(solution)/shard_map/jit(_where)/select_n | solution.py:112
  139.1 2.2 %select_bitcast_fusion = f32[1,8,128,256]{3,2,1,0:T(8,128)} fusion(f32[8,128,256]{2,1,0:T(8,128)S(1)} %slice.1549, f32[8,128,256]{2,1,0:T(8,128)S(1)} %copy-done.16, f32[10,128,256]{2,1,0:T(8,128)S(1)} %fusion.38, f32[14,128,257]{2,1,0:T(8,128)S(1)} %copy-done.5, f32[14,129,256]{2,1,0:T(8,128)S(1)} %add_multiply_fusion, f32[15,128,256]{2,1,0:T(8,128)S(1)} %copy-done.3, ...), kind=kLoop, calls=%fused_computation.122 | loop fusion | flops 4718592 | bytes 12582920 | tf_op jit(solution)/shard_map/broadcast_in_dim | solution.py:257
  (255 shorter events, 48.4 us)
Async XLA Ops:
  0.0 3.5 %copy-start = (bf16[4,4,4,64,128]{4,3,2,1,0:T(8,128)(2,1)S(1)}, bf16[4,4,4,64,128]{4,3,2,1,0:T(8,128)(2,1)}, u32[]{:S(2)}) copy-start(bf16[4,4,4,64,128]{4,3,2,1,0:T(8,128)(2,1)} %param.25) | copy-start | bytes 3145732
  0.0 7.0 %copy-start.14 = (f32[8,128,256]{2,1,0:T(8,128)S(1)}, f32[8,128,256]{2,1,0:T(8,128)}, u32[]{:S(2)}) copy-start(f32[8,128,256]{2,1,0:T(8,128)} %param.29) | copy-start | bytes 3145732
  7.1 12.9 %copy-start.40 = (f32[1,32,16,64]{3,2,1,0:T(8,128)S(1)}, f32[1,32,16,64]{3,2,1,0:T(8,128)}, u32[]{:S(2)}) copy-start(f32[1,32,16,64]{3,2,1,0:T(8,128)} %param.28) | copy-start | bytes 393220
  7.2 20.1 %copy-start.43 = (bf16[128,256,1]{1,0,2:T(8,128)(2,1)S(1)}, bf16[128,256,1]{1,0,2:T(8,128)(2,1)}, u32[]{:S(2)}) copy-start(bf16[128,256,1]{1,0,2:T(8,128)(2,1)} %constant.357) | copy-start | bytes 196612
  7.2 18.1 %collective-permute-start = (f32[512,256]{1,0:T(8,128)S(1)}, f32[512,256]{1,0:T(8,128)S(1)}, u32[]{:S(2)}, u32[]{:S(2)}) collective-permute-start(f32[512,256]{1,0:T(8,128)S(1)} %get-tuple-element.30), channel_id=1, source_target_pairs={{0,1},{1,2},{2,3},{3,4},{4,5},{5,6},{6,7},{7,8},{8,9},{9,10},{10,1... | collective-permute-start | bytes 1572872 | tf_op jit(solution)/shard_map/ppermute | solution.py:71
  10.8 15.7 %collective-permute-start.1 = (f32[512,256]{1,0:T(8,128)S(1)}, f32[512,256]{1,0:T(8,128)S(1)}, u32[]{:S(2)}, u32[]{:S(2)}) collective-permute-start(f32[512,256]{1,0:T(8,128)S(1)} %get-tuple-element.31), channel_id=1, source_target_pairs={{1,0},{2,1},{3,2},{4,3},{5,4},{6,5},{7,6},{8,7},{9,8},{10,9},{11,1... | collective-permute-start | bytes 1572872 | tf_op jit(solution)/shard_map/ppermute | solution.py:71
  20.0 7.7 %copy-start.45 = (f32[64,128,1]{1,0,2:T(8,128)S(1)}, f32[64,128,1]{1,0,2:T(8,128)}, u32[]{:S(2)}) copy-start(f32[64,128,1]{1,0,2:T(8,128)} %constant.358) | copy-start | bytes 98308
  40.0 7.9 %copy-start.2 = (f32[15,128,256]{2,1,0:T(8,128)}, f32[15,128,256]{2,1,0:T(8,128)S(1)}, u32[]{:S(2)}) copy-start(f32[15,128,256]{2,1,0:T(8,128)S(1)} %fusion.4) | copy-start | bytes 5898244
  41.7 6.2 %copy-start.4 = (f32[14,128,257]{2,1,0:T(8,128)}, f32[14,128,257]{2,1,0:T(8,128)S(1)}, u32[]{:S(2)}) copy-start(f32[14,128,257]{2,1,0:T(8,128)S(1)} %fusion.1) | copy-start | bytes 5526532
  49.3 9.5 %copy-start.39 = (f32[64,32,1]{0,1,2:T(8,128)S(1)}, f32[64,32,1]{0,1,2:T(8,128)}, u32[]{:S(2)}) copy-start(f32[64,32,1]{0,1,2:T(8,128)} %constant.361) | copy-start | bytes 24580
  50.0 10.6 %collective-permute-start.2 = (f32[6,64,128]{2,1,0:T(8,128)S(1)}, f32[6,64,128]{2,1,0:T(8,128)S(1)}, u32[]{:S(2)}, u32[]{:S(2)}) collective-permute-start(f32[6,64,128]{2,1,0:T(8,128)S(1)} %get-tuple-element.28), channel_id=1, source_target_pairs={{0,1},{1,2},{2,3},{3,4},{4,5},{5,6},{6,7},{7,8},{8,9},{9,10},{10,1... | collective-permute-start | bytes 589832 | tf_op jit(solution)/shard_map/ppermute | solution.py:71
  53.2 8.5 %collective-permute-start.3 = (f32[6,64,128]{2,1,0:T(8,128)S(1)}, f32[6,64,128]{2,1,0:T(8,128)S(1)}, u32[]{:S(2)}, u32[]{:S(2)}) collective-permute-start(f32[6,64,128]{2,1,0:T(8,128)S(1)} %get-tuple-element.29), channel_id=1, source_target_pairs={{1,0},{2,1},{3,2},{4,3},{5,4},{6,5},{7,6},{8,7},{9,8},{10,9},{11,1... | collective-permute-start | bytes 589832 | tf_op jit(solution)/shard_map/ppermute | solution.py:71
  64.4 9.0 %collective-permute-start.7 = (f32[1,2,2,32,64]{4,3,2,1,0:T(8,128)S(1)}, f32[1,2,2,32,64]{4,3,2,1,0:T(8,128)S(1)}, u32[]{:S(2)}, u32[]{:S(2)}) collective-permute-start(f32[1,2,2,32,64]{4,3,2,1,0:T(8,128)S(1)} %maximum_bitcast_fusion), channel_id=1, source_target_pairs={{1,0},{2,1},{3,2},{4,3},{5,4},{6,5},{7,6},{8,7},{9,8},{10,9},{11,1... | collective-permute-start | bytes 98312 | tf_op jit(solution)/shard_map/ppermute | solution.py:71
  70.9 8.3 %collective-permute-start.4 = (f32[1,2,2,32,64]{4,3,2,1,0:T(8,128)S(1)}, f32[1,2,2,32,64]{4,3,2,1,0:T(8,128)S(1)}, u32[]{:S(2)}, u32[]{:S(2)}) collective-permute-start(f32[1,2,2,32,64]{4,3,2,1,0:T(8,128)S(1)} %maximum_bitcast_fusion), channel_id=1, source_target_pairs={{0,1},{1,2},{2,3},{3,4},{4,5},{5,6},{6,7},{7,8},{8,9},{9,10},{10,1... | collective-permute-start | bytes 98312 | tf_op jit(solution)/shard_map/ppermute | solution.py:71
  79.2 8.4 %collective-permute-start.8 = (f32[2,2,2,32,64]{4,3,2,1,0:T(8,128)S(1)}, f32[2,2,2,32,64]{4,3,2,1,0:T(8,128)S(1)}, u32[]{:S(2)}, u32[]{:S(2)}) collective-permute-start(f32[2,2,2,32,64]{4,3,2,1,0:T(8,128)S(1)} %get-tuple-element.34), channel_id=1, source_target_pairs={{2,0},{3,1},{4,2},{5,3},{6,4},{7,5},{8,6},{9,7},{10,8},{11,9},{12,... | collective-permute-start | bytes 196616 | tf_op jit(solution)/shard_map/ppermute | solution.py:71
  81.1 9.3 %collective-permute-start.5 = (f32[2,2,2,32,64]{4,3,2,1,0:T(8,128)S(1)}, f32[2,2,2,32,64]{4,3,2,1,0:T(8,128)S(1)}, u32[]{:S(2)}, u32[]{:S(2)}) collective-permute-start(f32[2,2,2,32,64]{4,3,2,1,0:T(8,128)S(1)} %get-tuple-element.35), channel_id=1, source_target_pairs={{0,2},{1,3},{2,4},{3,5},{4,6},{5,7},{6,8},{7,9},{8,10},{9,11},{10,... | collective-permute-start | bytes 196616 | tf_op jit(solution)/shard_map/ppermute | solution.py:71
  90.4 17.9 %collective-permute-start.6 = (f32[4,2,2,32,64]{4,3,2,1,0:T(8,128)S(1)}, f32[4,2,2,32,64]{4,3,2,1,0:T(8,128)S(1)}, u32[]{:S(2)}, u32[]{:S(2)}) collective-permute-start(f32[4,2,2,32,64]{4,3,2,1,0:T(8,128)S(1)} %get-tuple-element.33), channel_id=1, source_target_pairs={{0,4},{1,5},{2,6},{3,7},{4,8},{5,9},{6,10},{7,11},{8,12},{9,13},{1... | collective-permute-start | bytes 393224 | tf_op jit(solution)/shard_map/ppermute | solution.py:71
  105.7 10.4 %collective-permute-start.9 = (f32[4,2,2,32,64]{4,3,2,1,0:T(8,128)S(1)}, f32[4,2,2,32,64]{4,3,2,1,0:T(8,128)S(1)}, u32[]{:S(2)}, u32[]{:S(2)}) collective-permute-start(f32[4,2,2,32,64]{4,3,2,1,0:T(8,128)S(1)} %get-tuple-element.32), channel_id=1, source_target_pairs={{4,0},{5,1},{6,2},{7,3},{8,4},{9,5},{10,6},{11,7},{12,8},{13,9},{1... | collective-permute-start | bytes 393224 | tf_op jit(solution)/shard_map/ppermute | solution.py:71
  122.5 3.6 %copy-start.31 = (f32[11,17,32]{2,1,0:T(8,128)S(1)}, f32[11,17,32]{2,1,0:T(8,128)}, u32[]{:S(2)}) copy-start(f32[11,17,32]{2,1,0:T(8,128)} %fusion.152) | copy-start | bytes 71812
  122.5 3.6 %copy-start.55 = (pred[7]{0:T(512)(128)(4,1)S(1)}, pred[7]{0:T(512)(128)(4,1)}, u32[]{:S(2)}) copy-start(pred[7]{0:T(512)(128)(4,1)} %compare_and_fusion.2) | copy-start | bytes 25
  122.5 3.7 %copy-start.56 = (f32[16,32,1]{1,0,2:T(8,128)S(1)}, f32[16,32,1]{1,0,2:T(8,128)}, u32[]{:S(2)}) copy-start(f32[16,32,1]{1,0,2:T(8,128)} %constant.363) | copy-start | bytes 6148
  122.5 3.8 %copy-start.58 = (pred[5]{0:T(512)(128)(4,1)S(1)}, pred[5]{0:T(512)(128)(4,1)}, u32[]{:S(2)}) copy-start(pred[5]{0:T(512)(128)(4,1)} %compare_and_fusion.3) | copy-start | bytes 19
  124.9 3.0 %copy-start.23 = (f32[26,32,64]{2,1,0:T(8,128)S(1)}, f32[26,32,64]{2,1,0:T(8,128)}, u32[]{:S(2)}) copy-start(f32[26,32,64]{2,1,0:T(8,128)} %copy-done.22) | copy-start | bytes 638980
  124.9 3.0 %copy-start.52 = (pred[8]{0:T(512)(128)(4,1)S(1)}, pred[8]{0:T(512)(128)(4,1)}, u32[]{:S(2)}) copy-start(pred[8]{0:T(512)(128)(4,1)} %compare_and_fusion.6) | copy-start | bytes 28
  (45 other events, 70.4 us)

commit v12 on v11

--- a/solution.py
+++ b/solution.py
@@ -172,8 +172,8 @@
     ext = jnp.where((gidx < 0)[:, None, None], lo_plane, ext)
     ext = jnp.where((gidx >= coarse_total)[:, None, None], hi_plane, ext)
 
-    pro = along_x(ext, prolong_matrix(cx).astype(jnp.bfloat16), precision=lax.Precision.DEFAULT)
-    pro = along_y(pro, prolong_matrix(cy), GRID)
+    pro = along_y(ext, prolong_matrix(cy).astype(jnp.bfloat16), precision=lax.Precision.DEFAULT)
+    pro = along_x(pro, prolong_matrix(cx), GRID)
     inner = pro[1:-1]
     even = 0.75 * inner + 0.25 * pro[:-2]
     odd = 0.75 * inner + 0.25 * pro[2:]

time: 142 us -> 139 us (0.979)
  other arithmetic: 30.6 us -> 33 us
  matrix products: 16.1 us -> 13.8 us
  waiting for transfers between devices: 24.7 us -> 23 us
    dot_general x1, matrix products: 3.62 us -> 1.76 us  [on_device(): jnp.dot(along_rows.reshape(k0_planes * fy, MX), cols_table, precision=GRID)]
    another operation x1, local copies, waits for them, and re-layouts: 2.08 us -> 0.24 us  [on_device(): log_perm = jnp.stack((even, odd), axis=1).reshape(2 * (n_ext - 2), fy, fx)]
    and x15, other arithmetic: 6.22 us -> 7.98 us  [plane_mask(): return ((g >= 0) & (g < total))[:, None, None]]
    ppermute x10, waiting for transfers between devices: 24.7 us -> 23 us  [shift_from(): return lax.ppermute(block, 'slab', pairs)]
    unnamed x123 -> x137, local copies, waits for them, and re-layouts: 10.1 us -> 10.7 us
  transfers between devices with their start and end apart: 10 -> 10, of which waited for: 9 -> 9; matrix products, arithmetic and copies ran while one was open for 7% -> 8% of each run, Pallas kernels for 0% -> 0%
where the time goes in v12:
time: 139 us; the launch traced here: 138 us
  starting transfers between devices  48.3 us (35%)
  other arithmetic  33 us (24%)
  waiting for transfers between devices  23 us (17%)
  local copies, waits for them, and re-layouts  14.7 us (11%)
  matrix products  13.8 us (10%)
  between operations  3.53 us (3%)
  blocking collectives  2.18 us (2%)
    ppermute x10, starting transfers between devices, shift_from(): return lax.ppermute(block, 'slab', pairs)  48.3 us
    ppermute x10, waiting for transfers between devices, shift_from(): return lax.ppermute(block, 'slab', pairs)  23 us
    unnamed x137, local copies, waits for them, and re-layouts  10.7 us
    select_n x11, other arithmetic, mask(): jnp.where(plane_mask(self.first + self.halo - h, u.shape[0], self.total),...  10 us
    and x15, other arithmetic, plane_mask(): return ((g >= 0) & (g < total))[:, None, None]  7.98 us
    dot_general x10, matrix products, along_x(): jnp.einsum('zyx,xw->zyw', values, jnp.asarray(matrix), precision=precisio...  6.05 us
    reduce_sum x6, other arithmetic, restrict_sum(): values = values.reshape(nz // 2, 2, ny, nx).sum(axis=1)  5.41 us
    dot_general x10, matrix products, along_y(): jnp.einsum('zyx,yv->zvx', values, jnp.asarray(matrix), precision=precisio...  4.04 us
  transfers between devices with their start and end apart: 10, of which 9 were waited for; matrix products, arithmetic and copies ran while one was open for 8% of the time, Pallas kernels for 0%

profile of v12, /device:TPU:24, one launch (start us, length us, event | category | flops | bytes accessed | tf_op | source)
XLA Modules:
  0.0 138.4 jit_solution(12919646699413727814)
XLA Ops:
  4.1 2.2 %all_gather.3 = bf16[8,4,64,128]{3,2,1,0:T(8,128)(2,1)S(1)} all-gather(bf16[4,4,64,128]{3,2,1,0:T(8,128)(2,1)S(1)} %gather_fusion), channel_id=1, replica_groups=mesh['chain'=2,'slab'=64] {'chain'}, dimensions={0}, use_global_device_ids=true | all-gather | bytes 786432 | tf_op jit(solution)/shard_map/all_gather | solution.py:147
  7.2 3.4 %collective-permute-start = (f32[512,256]{1,0:T(8,128)S(1)}, f32[512,256]{1,0:T(8,128)S(1)}, u32[]{:S(2)}, u32[]{:S(2)}) collective-permute-start(f32[512,256]{1,0:T(8,128)S(1)} %get-tuple-element.30), channel_id=1, source_target_pairs={{0,1},{1,2},{2,3},{3,4},{4,5},{5,6},{6,7},{7,8},{8,9},{9,10},{10,1... | collective-permute-start | bytes 1572872 | tf_op jit(solution)/shard_map/ppermute | solution.py:71
  10.6 4.6 %collective-permute-start.1 = (f32[512,256]{1,0:T(8,128)S(1)}, f32[512,256]{1,0:T(8,128)S(1)}, u32[]{:S(2)}, u32[]{:S(2)}) collective-permute-start(f32[512,256]{1,0:T(8,128)S(1)} %get-tuple-element.31), channel_id=1, source_target_pairs={{1,0},{2,1},{3,2},{4,3},{5,4},{6,5},{7,6},{8,7},{9,8},{10,9},{11,1... | collective-permute-start | bytes 1572872 | tf_op jit(solution)/shard_map/ppermute | solution.py:71
  22.0 1.6 %convolution_bitcast_fusion.1 = f32[20,128,64]{1,2,0:T(8,128)} fusion(f32[20,16,64]{2,0,1:T(8,128)S(1)} %fusion.126, s32[128]{0:T(128)S(1)} %multiply_add_fusion.2, s32[16]{0:T(128)S(1)} %iota_add_fusion.2), kind=kOutput, calls=%fused_computation.74 | convolution fusion | flops 15757312 | bytes 737856 | tf_op jit(solution)/shard_map/zbe,by->zye/dot_general | solution.py:189
  23.5 1.7 %collective-permute-done = f32[512,256]{1,0:T(8,128)S(1)} collective-permute-done((f32[512,256]{1,0:T(8,128)S(1)}, f32[512,256]{1,0:T(8,128)S(1)}, u32[]{:S(2)}, u32[]{:S(2)}) %collective-permute-start) | collective-permute-done | bytes 524320 | tf_op jit(solution)/shard_map/ppermute | solution.py:71
  29.6 1.8 %fusion.3 = f32[20,128,256]{2,1,0:T(8,128)S(1)} fusion(f32[10,2,128,256]{3,2,1,0:T(8,128)S(1)} %copy.28, f32[20,128,64]{1,2,0:T(8,128)S(1)} %copy-done.29, pred[20]{0:T(512)(128)(4,1)S(1)} %compare_and_fusion.12, s32[256]{0:T(256)S(1)} %multiply_add_fusion, s32[64]{0:T(128)S(1)} %iota_add_fusion), kind=kOutput, calls=%fused_computation.8 | convolution fusion | flops 253198336 | bytes 5899540 | tf_op jit(solution)/shard_map/dot_general | solution.py:190
  32.8 2.0 %fusion.312 = f32[10,128,128]{2,1,0:T(8,128)S(1)} fusion(f32[10,128,256]{2,1,0:T(8,128)} %reduce_sum.54, f32[256,128,1]{1,0,2:T(8,128)S(1)} %copy-done.33), kind=kOutput, calls=%fused_computation.535 | convolution fusion | flops 251658240 | bytes 2097152 | tf_op jit(solution)/shard_map/zyx,xw->zyw/dot_general | solution.py:45
  39.9 1.5 %divide_select_fusion = (f32[14,128,256]{2,1,0:T(8,128)S(1)}, f32[14,128,256]{2,1,0:T(8,128)S(1)}, f32[14,128,256]{2,1,0:T(8,128)S(1)}) fusion(pred[14]{0:T(512)(128)(4,1)S(1)} %copy-done.62, f32[3,128,256]{2,1,0:T(8,128)S(1)} %bitcast.153, f32[8,128,256]{2,1,0:T(8,128)S(1)} %copy-done.15, f32[3,128,256]{2,1,0:T(8,128)S(1)} %bitcast.152, ...), kind=kLoop, calls=%fused_computation.22 | loop fusion | flops 4587520 | bytes 18350094 | tf_op jit(solution)/shard_map/jit(_where)/select_n | solution.py:112
  42.0 2.3 %fusion.19 = f32[12,128,256]{2,1,0:T(8,128)S(1)} fusion(f32[12,128,256]{2,1,0:T(8,128)S(1)} %slice.1360, f32[14,128,257]{2,1,0:T(8,128)S(1)} %fusion.1, f32[14,129,256]{2,1,0:T(8,128)S(1)} %add_multiply_fusion, f32[14,128,256]{2,1,0:T(8,128)S(1)} %get-tuple-element.11, f32[15,128,256]{2,1,0:T(8,128)S(1)} %fusion.4, ...), kind=kLoop, calls=%fused_computation.46 | loop fusion | flops 7077888 | bytes 18874380 | tf_op jit(solution)/shard_map/jit(_where)/select_n | solution.py:112
  46.6 3.2 %collective-permute-start.2 = (f32[6,64,128]{2,1,0:T(8,128)S(1)}, f32[6,64,128]{2,1,0:T(8,128)S(1)}, u32[]{:S(2)}, u32[]{:S(2)}) collective-permute-start(f32[6,64,128]{2,1,0:T(8,128)S(1)} %get-tuple-element.28), channel_id=1, source_target_pairs={{0,1},{1,2},{2,3},{3,4},{4,5},{5,6},{6,7},{7,8},{8,9},{9,10},{10,1... | collective-permute-start | bytes 589832 | tf_op jit(solution)/shard_map/ppermute | solution.py:71
  49.9 5.4 %collective-permute-start.3 = (f32[6,64,128]{2,1,0:T(8,128)S(1)}, f32[6,64,128]{2,1,0:T(8,128)S(1)}, u32[]{:S(2)}, u32[]{:S(2)}) collective-permute-start(f32[6,64,128]{2,1,0:T(8,128)S(1)} %get-tuple-element.29), channel_id=1, source_target_pairs={{1,0},{2,1},{3,2},{4,3},{5,4},{6,5},{7,6},{8,7},{9,8},{10,9},{11,1... | collective-permute-start | bytes 589832 | tf_op jit(solution)/shard_map/ppermute | solution.py:71
  55.6 1.6 %collective-permute-done.2 = f32[6,64,128]{2,1,0:T(8,128)S(1)} collective-permute-done((f32[6,64,128]{2,1,0:T(8,128)S(1)}, f32[6,64,128]{2,1,0:T(8,128)S(1)}, u32[]{:S(2)}, u32[]{:S(2)}) %collective-permute-start.2) | collective-permute-done | bytes 196640 | tf_op jit(solution)/shard_map/ppermute | solution.py:71
  61.4 6.5 %collective-permute-start.7 = (f32[1,2,2,32,64]{4,3,2,1,0:T(8,128)S(1)}, f32[1,2,2,32,64]{4,3,2,1,0:T(8,128)S(1)}, u32[]{:S(2)}, u32[]{:S(2)}) collective-permute-start(f32[1,2,2,32,64]{4,3,2,1,0:T(8,128)S(1)} %maximum_bitcast_fusion), channel_id=1, source_target_pairs={{1,0},{2,1},{3,2},{4,3},{5,4},{6,5},{7,6},{8,7},{9,8},{10,9},{11,1... | collective-permute-start | bytes 98312 | tf_op jit(solution)/shard_map/ppermute | solution.py:71
  67.9 1.9 %collective-permute-start.4 = (f32[1,2,2,32,64]{4,3,2,1,0:T(8,128)S(1)}, f32[1,2,2,32,64]{4,3,2,1,0:T(8,128)S(1)}, u32[]{:S(2)}, u32[]{:S(2)}) collective-permute-start(f32[1,2,2,32,64]{4,3,2,1,0:T(8,128)S(1)} %maximum_bitcast_fusion), channel_id=1, source_target_pairs={{0,1},{1,2},{2,3},{3,4},{4,5},{5,6},{6,7},{7,8},{8,9},{9,10},{10,1... | collective-permute-start | bytes 98312 | tf_op jit(solution)/shard_map/ppermute | solution.py:71
  70.4 5.8 %collective-permute-done.4 = f32[1,2,2,32,64]{4,3,2,1,0:T(8,128)S(1)} collective-permute-done((f32[1,2,2,32,64]{4,3,2,1,0:T(8,128)S(1)}, f32[1,2,2,32,64]{4,3,2,1,0:T(8,128)S(1)}, u32[]{:S(2)}, u32[]{:S(2)}) %collective-permute-start.4) | collective-permute-done | bytes 32800 | tf_op jit(solution)/shard_map/ppermute | solution.py:71
  76.2 1.9 %collective-permute-start.8 = (f32[2,2,2,32,64]{4,3,2,1,0:T(8,128)S(1)}, f32[2,2,2,32,64]{4,3,2,1,0:T(8,128)S(1)}, u32[]{:S(2)}, u32[]{:S(2)}) collective-permute-start(f32[2,2,2,32,64]{4,3,2,1,0:T(8,128)S(1)} %get-tuple-element.34), channel_id=1, source_target_pairs={{2,0},{3,1},{4,2},{5,3},{6,4},{7,5},{8,6},{9,7},{10,8},{11,9},{12,... | collective-permute-start | bytes 196616 | tf_op jit(solution)/shard_map/ppermute | solution.py:71
  78.1 5.4 %collective-permute-start.5 = (f32[2,2,2,32,64]{4,3,2,1,0:T(8,128)S(1)}, f32[2,2,2,32,64]{4,3,2,1,0:T(8,128)S(1)}, u32[]{:S(2)}, u32[]{:S(2)}) collective-permute-start(f32[2,2,2,32,64]{4,3,2,1,0:T(8,128)S(1)} %get-tuple-element.35), channel_id=1, source_target_pairs={{0,2},{1,3},{2,4},{3,5},{4,6},{5,7},{6,8},{7,9},{8,10},{9,11},{10,... | collective-permute-start | bytes 196616 | tf_op jit(solution)/shard_map/ppermute | solution.py:71
  84.5 2.8 %collective-permute-done.5 = f32[2,2,2,32,64]{4,3,2,1,0:T(8,128)S(1)} collective-permute-done((f32[2,2,2,32,64]{4,3,2,1,0:T(8,128)S(1)}, f32[2,2,2,32,64]{4,3,2,1,0:T(8,128)S(1)}, u32[]{:S(2)}, u32[]{:S(2)}) %collective-permute-start.5) | collective-permute-done | bytes 65568 | tf_op jit(solution)/shard_map/ppermute | solution.py:71
  87.4 14.0 %collective-permute-start.6 = (f32[4,2,2,32,64]{4,3,2,1,0:T(8,128)S(1)}, f32[4,2,2,32,64]{4,3,2,1,0:T(8,128)S(1)}, u32[]{:S(2)}, u32[]{:S(2)}) collective-permute-start(f32[4,2,2,32,64]{4,3,2,1,0:T(8,128)S(1)} %get-tuple-element.33), channel_id=1, source_target_pairs={{0,4},{1,5},{2,6},{3,7},{4,8},{5,9},{6,10},{7,11},{8,12},{9,13},{1... | collective-permute-start | bytes 393224 | tf_op jit(solution)/shard_map/ppermute | solution.py:71
  102.7 1.9 %collective-permute-start.9 = (f32[4,2,2,32,64]{4,3,2,1,0:T(8,128)S(1)}, f32[4,2,2,32,64]{4,3,2,1,0:T(8,128)S(1)}, u32[]{:S(2)}, u32[]{:S(2)}) collective-permute-start(f32[4,2,2,32,64]{4,3,2,1,0:T(8,128)S(1)} %get-tuple-element.32), channel_id=1, source_target_pairs={{4,0},{5,1},{6,2},{7,3},{8,4},{9,5},{10,6},{11,7},{12,8},{13,9},{1... | collective-permute-start | bytes 393224 | tf_op jit(solution)/shard_map/ppermute | solution.py:71
  105.4 7.6 %collective-permute-done.9 = f32[4,2,2,32,64]{4,3,2,1,0:T(8,128)S(1)} collective-permute-done((f32[4,2,2,32,64]{4,3,2,1,0:T(8,128)S(1)}, f32[4,2,2,32,64]{4,3,2,1,0:T(8,128)S(1)}, u32[]{:S(2)}, u32[]{:S(2)}) %collective-permute-start.9) | collective-permute-done | bytes 131104 | tf_op jit(solution)/shard_map/ppermute | solution.py:71
  117.9 1.7 %reduce_sum.58 = f32[11,32,64]{2,1,0:T(8,128)} reduce(f32[11,2,32,64]{3,2,1,0:T(8,128)} %bitcast.154, f32[]{:T(128)} %constant.129.clone.1), dimensions={1}, to_apply=%region_5.6 | reduce | flops 22528 | bytes 270340 | tf_op jit(solution)/shard_map/reduce_sum | solution.py:56
  133.1 2.0 %fusion.38 = f32[10,128,256]{2,1,0:T(8,128)S(1)} fusion(f32[10,128,256]{2,1,0:T(8,128)S(1)} %slice.1538, f32[14,128,257]{2,1,0:T(8,128)S(1)} %copy-done.5, f32[14,129,256]{2,1,0:T(8,128)S(1)} %add_multiply_fusion, f32[12,128,256]{2,1,0:T(8,128)S(1)} %bitcast_add_fusion.1, f32[15,128,256]{2,1,0:T(8,128)S(1)} %copy-done.3, f32[14,128,256]{2,1,0:T(8,128)S(1)} %copy-done.7, ...), kind=kLoop, calls=%fused_computation.72 | loop fusion | flops 5898240 | bytes 15728650 | tf_op jit(solution)/shard_map/jit(_where)/select_n | solution.py:112
  136.3 2.2 %select_bitcast_fusion = f32[1,8,128,256]{3,2,1,0:T(8,128)} fusion(f32[8,128,256]{2,1,0:T(8,128)S(1)} %slice.1549, f32[8,128,256]{2,1,0:T(8,128)S(1)} %copy-done.16, f32[10,128,256]{2,1,0:T(8,128)S(1)} %fusion.38, f32[14,128,257]{2,1,0:T(8,128)S(1)} %copy-done.5, f32[14,129,256]{2,1,0:T(8,128)S(1)} %add_multiply_fusion, f32[15,128,256]{2,1,0:T(8,128)S(1)} %copy-done.3, ...), kind=kLoop, calls=%fused_computation.122 | loop fusion | flops 4718592 | bytes 12582920 | tf_op jit(solution)/shard_map/broadcast_in_dim | solution.py:257
  (269 shorter events, 50.0 us)
Async XLA Ops:
  0.0 3.5 %copy-start = (bf16[4,4,4,64,128]{4,3,2,1,0:T(8,128)(2,1)S(1)}, bf16[4,4,4,64,128]{4,3,2,1,0:T(8,128)(2,1)}, u32[]{:S(2)}) copy-start(bf16[4,4,4,64,128]{4,3,2,1,0:T(8,128)(2,1)} %param.25) | copy-start | bytes 3145732
  0.0 7.0 %copy-start.14 = (f32[8,128,256]{2,1,0:T(8,128)S(1)}, f32[8,128,256]{2,1,0:T(8,128)}, u32[]{:S(2)}) copy-start(f32[8,128,256]{2,1,0:T(8,128)} %param.29) | copy-start | bytes 3145732
  7.1 14.4 %copy-start.41 = (f32[1,32,16,64]{3,2,1,0:T(8,128)S(1)}, f32[1,32,16,64]{3,2,1,0:T(8,128)}, u32[]{:S(2)}) copy-start(f32[1,32,16,64]{3,2,1,0:T(8,128)} %param.28) | copy-start | bytes 393220
  7.2 19.3 %copy-start.50 = (bf16[64,128,1]{1,0,2:T(8,128)(2,1)S(1)}, bf16[64,128,1]{1,0,2:T(8,128)(2,1)}, u32[]{:S(2)}) copy-start(bf16[64,128,1]{1,0,2:T(8,128)(2,1)} %constant.357) | copy-start | bytes 49156
  7.2 18.0 %collective-permute-start = (f32[512,256]{1,0:T(8,128)S(1)}, f32[512,256]{1,0:T(8,128)S(1)}, u32[]{:S(2)}, u32[]{:S(2)}) collective-permute-start(f32[512,256]{1,0:T(8,128)S(1)} %get-tuple-element.30), channel_id=1, source_target_pairs={{0,1},{1,2},{2,3},{3,4},{4,5},{5,6},{6,7},{7,8},{8,9},{9,10},{10,1... | collective-permute-start | bytes 1572872 | tf_op jit(solution)/shard_map/ppermute | solution.py:71
  10.6 15.7 %collective-permute-start.1 = (f32[512,256]{1,0:T(8,128)S(1)}, f32[512,256]{1,0:T(8,128)S(1)}, u32[]{:S(2)}, u32[]{:S(2)}) collective-permute-start(f32[512,256]{1,0:T(8,128)S(1)} %get-tuple-element.31), channel_id=1, source_target_pairs={{1,0},{2,1},{3,2},{4,3},{5,4},{6,5},{7,6},{8,7},{9,8},{10,9},{11,1... | collective-permute-start | bytes 1572872 | tf_op jit(solution)/shard_map/ppermute | solution.py:71
  21.6 5.6 %copy-start.46 = (f32[128,256,1]{1,0,2:T(8,128)S(1)}, f32[128,256,1]{1,0,2:T(8,128)}, u32[]{:S(2)}) copy-start(f32[128,256,1]{1,0,2:T(8,128)} %constant.358) | copy-start | bytes 393220
  36.8 7.7 %copy-start.2 = (f32[15,128,256]{2,1,0:T(8,128)}, f32[15,128,256]{2,1,0:T(8,128)S(1)}, u32[]{:S(2)}) copy-start(f32[15,128,256]{2,1,0:T(8,128)S(1)} %fusion.4) | copy-start | bytes 5898244
  37.8 6.7 %copy-start.4 = (f32[14,128,257]{2,1,0:T(8,128)}, f32[14,128,257]{2,1,0:T(8,128)S(1)}, u32[]{:S(2)}) copy-start(f32[14,128,257]{2,1,0:T(8,128)S(1)} %fusion.1) | copy-start | bytes 5526532
  41.4 3.1 %copy-start.6 = (f32[14,128,256]{2,1,0:T(8,128)}, f32[14,128,256]{2,1,0:T(8,128)S(1)}, u32[]{:S(2)}) copy-start(f32[14,128,256]{2,1,0:T(8,128)S(1)} %get-tuple-element.12) | copy-start | bytes 5505028
  46.0 9.3 %copy-start.42 = (f32[2,64,128]{2,1,0:T(8,128)S(1)}, f32[2,64,128]{2,1,0:T(8,128)}, u32[]{:S(2)}) copy-start(f32[2,64,128]{2,1,0:T(8,128)} %bitcast_reduce_fusion.1) | copy-start | bytes 196612
  46.0 9.5 %copy-start.40 = (f32[64,32,1]{0,1,2:T(8,128)S(1)}, f32[64,32,1]{0,1,2:T(8,128)}, u32[]{:S(2)}) copy-start(f32[64,32,1]{0,1,2:T(8,128)} %constant.361) | copy-start | bytes 24580
  46.6 10.6 %collective-permute-start.2 = (f32[6,64,128]{2,1,0:T(8,128)S(1)}, f32[6,64,128]{2,1,0:T(8,128)S(1)}, u32[]{:S(2)}, u32[]{:S(2)}) collective-permute-start(f32[6,64,128]{2,1,0:T(8,128)S(1)} %get-tuple-element.28), channel_id=1, source_target_pairs={{0,1},{1,2},{2,3},{3,4},{4,5},{5,6},{6,7},{7,8},{8,9},{9,10},{10,1... | collective-permute-start | bytes 589832 | tf_op jit(solution)/shard_map/ppermute | solution.py:71
  49.9 8.5 %collective-permute-start.3 = (f32[6,64,128]{2,1,0:T(8,128)S(1)}, f32[6,64,128]{2,1,0:T(8,128)S(1)}, u32[]{:S(2)}, u32[]{:S(2)}) collective-permute-start(f32[6,64,128]{2,1,0:T(8,128)S(1)} %get-tuple-element.29), channel_id=1, source_target_pairs={{1,0},{2,1},{3,2},{4,3},{5,4},{6,5},{7,6},{8,7},{9,8},{10,9},{11,1... | collective-permute-start | bytes 589832 | tf_op jit(solution)/shard_map/ppermute | solution.py:71
  61.4 9.0 %collective-permute-start.7 = (f32[1,2,2,32,64]{4,3,2,1,0:T(8,128)S(1)}, f32[1,2,2,32,64]{4,3,2,1,0:T(8,128)S(1)}, u32[]{:S(2)}, u32[]{:S(2)}) collective-permute-start(f32[1,2,2,32,64]{4,3,2,1,0:T(8,128)S(1)} %maximum_bitcast_fusion), channel_id=1, source_target_pairs={{1,0},{2,1},{3,2},{4,3},{5,4},{6,5},{7,6},{8,7},{9,8},{10,9},{11,1... | collective-permute-start | bytes 98312 | tf_op jit(solution)/shard_map/ppermute | solution.py:71
  67.9 8.3 %collective-permute-start.4 = (f32[1,2,2,32,64]{4,3,2,1,0:T(8,128)S(1)}, f32[1,2,2,32,64]{4,3,2,1,0:T(8,128)S(1)}, u32[]{:S(2)}, u32[]{:S(2)}) collective-permute-start(f32[1,2,2,32,64]{4,3,2,1,0:T(8,128)S(1)} %maximum_bitcast_fusion), channel_id=1, source_target_pairs={{0,1},{1,2},{2,3},{3,4},{4,5},{5,6},{6,7},{7,8},{8,9},{9,10},{10,1... | collective-permute-start | bytes 98312 | tf_op jit(solution)/shard_map/ppermute | solution.py:71
  76.2 8.4 %collective-permute-start.8 = (f32[2,2,2,32,64]{4,3,2,1,0:T(8,128)S(1)}, f32[2,2,2,32,64]{4,3,2,1,0:T(8,128)S(1)}, u32[]{:S(2)}, u32[]{:S(2)}) collective-permute-start(f32[2,2,2,32,64]{4,3,2,1,0:T(8,128)S(1)} %get-tuple-element.34), channel_id=1, source_target_pairs={{2,0},{3,1},{4,2},{5,3},{6,4},{7,5},{8,6},{9,7},{10,8},{11,9},{12,... | collective-permute-start | bytes 196616 | tf_op jit(solution)/shard_map/ppermute | solution.py:71
  78.1 9.3 %collective-permute-start.5 = (f32[2,2,2,32,64]{4,3,2,1,0:T(8,128)S(1)}, f32[2,2,2,32,64]{4,3,2,1,0:T(8,128)S(1)}, u32[]{:S(2)}, u32[]{:S(2)}) collective-permute-start(f32[2,2,2,32,64]{4,3,2,1,0:T(8,128)S(1)} %get-tuple-element.35), channel_id=1, source_target_pairs={{0,2},{1,3},{2,4},{3,5},{4,6},{5,7},{6,8},{7,9},{8,10},{9,11},{10,... | collective-permute-start | bytes 196616 | tf_op jit(solution)/shard_map/ppermute | solution.py:71
  87.4 17.9 %collective-permute-start.6 = (f32[4,2,2,32,64]{4,3,2,1,0:T(8,128)S(1)}, f32[4,2,2,32,64]{4,3,2,1,0:T(8,128)S(1)}, u32[]{:S(2)}, u32[]{:S(2)}) collective-permute-start(f32[4,2,2,32,64]{4,3,2,1,0:T(8,128)S(1)} %get-tuple-element.33), channel_id=1, source_target_pairs={{0,4},{1,5},{2,6},{3,7},{4,8},{5,9},{6,10},{7,11},{8,12},{9,13},{1... | collective-permute-start | bytes 393224 | tf_op jit(solution)/shard_map/ppermute | solution.py:71
  102.7 10.4 %collective-permute-start.9 = (f32[4,2,2,32,64]{4,3,2,1,0:T(8,128)S(1)}, f32[4,2,2,32,64]{4,3,2,1,0:T(8,128)S(1)}, u32[]{:S(2)}, u32[]{:S(2)}) collective-permute-start(f32[4,2,2,32,64]{4,3,2,1,0:T(8,128)S(1)} %get-tuple-element.32), channel_id=1, source_target_pairs={{4,0},{5,1},{6,2},{7,3},{8,4},{9,5},{10,6},{11,7},{12,8},{13,9},{1... | collective-permute-start | bytes 393224 | tf_op jit(solution)/shard_map/ppermute | solution.py:71
  119.6 3.6 %copy-start.32 = (f32[11,17,32]{2,1,0:T(8,128)S(1)}, f32[11,17,32]{2,1,0:T(8,128)}, u32[]{:S(2)}) copy-start(f32[11,17,32]{2,1,0:T(8,128)} %fusion.151) | copy-start | bytes 71812
  119.7 3.6 %copy-start.60 = (pred[7]{0:T(512)(128)(4,1)S(1)}, pred[7]{0:T(512)(128)(4,1)}, u32[]{:S(2)}) copy-start(pred[7]{0:T(512)(128)(4,1)} %compare_and_fusion.2) | copy-start | bytes 25
  119.7 3.7 %copy-start.63 = (f32[16,32,1]{1,0,2:T(8,128)S(1)}, f32[16,32,1]{1,0,2:T(8,128)}, u32[]{:S(2)}) copy-start(f32[16,32,1]{1,0,2:T(8,128)} %constant.363) | copy-start | bytes 6148
  119.7 3.8 %copy-start.65 = (pred[5]{0:T(512)(128)(4,1)S(1)}, pred[5]{0:T(512)(128)(4,1)}, u32[]{:S(2)}) copy-start(pred[5]{0:T(512)(128)(4,1)} %compare_and_fusion.3) | copy-start | bytes 19
  (52 other events, 83.0 us)

commit v13 on v11

--- a/solution.py
+++ b/solution.py
@@ -172,12 +172,13 @@
     ext = jnp.where((gidx < 0)[:, None, None], lo_plane, ext)
     ext = jnp.where((gidx >= coarse_total)[:, None, None], hi_plane, ext)
 
-    pro = along_x(ext, prolong_matrix(cx).astype(jnp.bfloat16), precision=lax.Precision.DEFAULT)
+    wide = ext.astype(jnp.float32)
+    inner = wide[1:-1]
+    even = 0.75 * inner + 0.25 * wide[:-2]
+    odd = 0.75 * inner + 0.25 * wide[2:]
+    pro = jnp.stack((even, odd), axis=1).reshape(2 * (n_ext - 2), cy, cx)
     pro = along_y(pro, prolong_matrix(cy), GRID)
-    inner = pro[1:-1]
-    even = 0.75 * inner + 0.25 * pro[:-2]
-    odd = 0.75 * inner + 0.25 * pro[2:]
-    log_perm = jnp.stack((even, odd), axis=1).reshape(2 * (n_ext - 2), fy, fx)
+    log_perm = along_x(pro, prolong_matrix(cx), GRID)
     k0_first = 2 * (g0 + 1)
     k0_planes = log_perm.shape[0]
 

time: 142 us -> 144 us (1.014)
    another operation x1 -> x0, local copies, waits for them, and re-layouts: 2.08 us -> none  [on_device(): log_perm = jnp.stack((even, odd), axis=1).reshape(2 * (n_ext - 2), fy, fx)]
    and x15, other arithmetic: 6.22 us -> 4.43 us  [plane_mask(): return ((g >= 0) & (g < total))[:, None, None]]
    select_n x11, other arithmetic: 10.1 us -> 11.7 us  [mask(): jnp.where(plane_mask(self.first + self.halo - h, u.shape[0], self.total),...]
    unnamed x123 -> x119, local copies, waits for them, and re-layouts: 10.1 us -> 11.6 us
where the time goes in v13:
time: 144 us; the launch traced here: 143 us
  starting transfers between devices  48.4 us (34%)
  other arithmetic  31.4 us (22%)
  waiting for transfers between devices  24.3 us (17%)
  local copies, waits for them, and re-layouts  17.1 us (12%)
  matrix products  15.8 us (11%)
  between operations  3.43 us (2%)
  blocking collectives  2.18 us (2%)
    ppermute x10, starting transfers between devices, shift_from(): return lax.ppermute(block, 'slab', pairs)  48.4 us
    ppermute x10, waiting for transfers between devices, shift_from(): return lax.ppermute(block, 'slab', pairs)  24.3 us
    select_n x11, other arithmetic, mask(): jnp.where(plane_mask(self.first + self.halo - h, u.shape[0], self.total),...  11.7 us
    unnamed x119, local copies, waits for them, and re-layouts  11.6 us
    dot_general x10, matrix products, along_x(): jnp.einsum('zyx,xw->zyw', values, jnp.asarray(matrix), precision=precisio...  6.83 us
    reduce_sum x6, other arithmetic, restrict_sum(): values = values.reshape(nz // 2, 2, ny, nx).sum(axis=1)  5.26 us
    dot_general x10, matrix products, along_y(): jnp.einsum('zyx,yv->zvx', values, jnp.asarray(matrix), precision=precisio...  4.89 us
    and x15, other arithmetic, plane_mask(): return ((g >= 0) & (g < total))[:, None, None]  4.43 us
  transfers between devices with their start and end apart: 10, of which 9 were waited for; matrix products, arithmetic and copies ran while one was open for 7% of the time, Pallas kernels for 0%

profile of v13, /device:TPU:24, one launch (start us, length us, event | category | flops | bytes accessed | tf_op | source)
XLA Modules:
  0.0 142.6 jit_solution(16623671767437525526)
XLA Ops:
  4.1 2.2 %all_gather.3 = bf16[8,4,64,128]{3,2,1,0:T(8,128)(2,1)S(1)} all-gather(bf16[4,4,64,128]{3,2,1,0:T(8,128)(2,1)S(1)} %gather_fusion), channel_id=1, replica_groups=mesh['chain'=2,'slab'=64] {'chain'}, dimensions={0}, use_global_device_ids=true | all-gather | bytes 786432 | tf_op jit(solution)/shard_map/all_gather | solution.py:147
  7.2 3.4 %collective-permute-start = (f32[512,256]{1,0:T(8,128)S(1)}, f32[512,256]{1,0:T(8,128)S(1)}, u32[]{:S(2)}, u32[]{:S(2)}) collective-permute-start(f32[512,256]{1,0:T(8,128)S(1)} %get-tuple-element.30), channel_id=1, source_target_pairs={{0,1},{1,2},{2,3},{3,4},{4,5},{5,6},{6,7},{7,8},{8,9},{9,10},{10,1... | collective-permute-start | bytes 1572872 | tf_op jit(solution)/shard_map/ppermute | solution.py:71
  10.6 4.6 %collective-permute-start.1 = (f32[512,256]{1,0:T(8,128)S(1)}, f32[512,256]{1,0:T(8,128)}, u32[]{:S(2)}, u32[]{:S(2)}) collective-permute-start(f32[512,256]{1,0:T(8,128)S(1)} %get-tuple-element.31), channel_id=1, source_target_pairs={{1,0},{2,1},{3,2},{4,3},{5,4},{6,5},{7,6},{8,7},{9,8},{10,9},{11,1... | collective-permute-start | bytes 1572872 | tf_op jit(solution)/shard_map/ppermute | solution.py:71
  19.2 3.0 %fusion.205 = f32[20,128,256]{2,1,0:T(8,128)} fusion(f32[20,128,64]{1,2,0:T(8,128)S(1)} %convolution_bitcast_fusion.1, s32[256]{0:T(256)S(1)} %multiply_add_fusion, s32[64]{0:T(128)S(1)} %iota_add_fusion), kind=kOutput, calls=%fused_computation.374 | convolution fusion | flops 251887616 | bytes 3278080 | tf_op jit(solution)/shard_map/dot_general | solution.py:191
  22.1 3.0 %collective-permute-done = f32[512,256]{1,0:T(8,128)S(1)} collective-permute-done((f32[512,256]{1,0:T(8,128)S(1)}, f32[512,256]{1,0:T(8,128)S(1)}, u32[]{:S(2)}, u32[]{:S(2)}) %collective-permute-start) | collective-permute-done | bytes 524320 | tf_op jit(solution)/shard_map/ppermute | solution.py:71
  29.5 2.9 %exponential_select_fusion = f32[20,128,256]{2,1,0:T(8,128)} fusion(f32[20,128,256]{2,1,0:T(8,128)S(1)} %copy-done.25, f32[20,128,128]{1,2,0:T(8,128)S(1)} %convolution_bitcast_fusion, f32[128,256,1]{1,0,2:T(8,128)S(1)} %copy-done.46, pred[20]{0:T(512)(128)(4,1)S(1)} %compare_and_fusion.12), kind=kOutput, calls=%fused_computation.5 | convolution fusion | flops 504627200 | bytes 6684692 | tf_op jit(solution)/shard_map/zyx,xw->zyw/dot_general | solution.py:45
  32.4 2.1 %reduce_sum.54 = f32[10,128,256]{2,1,0:T(8,128)S(1)} reduce(f32[10,2,128,256]{3,2,1,0:T(8,128)} %bitcast.142, f32[]{:T(128)} %constant.129.clone.1), dimensions={1}, to_apply=%region_1.2 | reduce | flops 327680 | bytes 3932164 | tf_op jit(solution)/shard_map/reduce_sum | solution.py:56
  40.7 2.4 %divide_select_fusion = (f32[14,128,256]{2,1,0:T(8,128)S(1)}, f32[14,128,256]{2,1,0:T(8,128)S(1)}, f32[14,128,256]{2,1,0:T(8,128)}) fusion(pred[14]{0:T(512)(128)(4,1)S(1)} %compare_and_fusion.13, f32[3,128,256]{2,1,0:T(8,128)S(1)} %bitcast.152, f32[8,128,256]{2,1,0:T(8,128)S(1)} %copy-done.19, f32[3,128,256]{2,1,0:T(8,128)S(1)} %bitcast.151, ...), kind=kLoop, calls=%fused_computation.19 | loop fusion | flops 4587520 | bytes 18350094 | tf_op jit(solution)/shard_map/jit(_where)/select_n | solution.py:112
  43.3 2.0 %copy-done.21 = f32[14,128,256]{2,1,0:T(8,128)S(1)} copy-done((f32[14,128,256]{2,1,0:T(8,128)S(1)}, f32[14,128,256]{2,1,0:T(8,128)}, u32[]{:S(2)}) %copy-start.21) | copy-done | bytes 1835032
  45.3 2.3 %fusion.17 = f32[12,128,256]{2,1,0:T(8,128)S(1)} fusion(f32[12,128,256]{2,1,0:T(8,128)S(1)} %slice.1360, f32[14,128,257]{2,1,0:T(8,128)S(1)} %fusion.1, f32[14,129,256]{2,1,0:T(8,128)S(1)} %add_multiply_fusion, f32[14,128,256]{2,1,0:T(8,128)S(1)} %get-tuple-element.11, f32[15,128,256]{2,1,0:T(8,128)S(1)} %fusion.2, ...), kind=kLoop, calls=%fused_computation.43 | loop fusion | flops 7077888 | bytes 18874380 | tf_op jit(solution)/shard_map/jit(_where)/select_n | solution.py:112
  49.6 3.3 %collective-permute-start.2 = (f32[6,64,128]{2,1,0:T(8,128)S(1)}, f32[6,64,128]{2,1,0:T(8,128)S(1)}, u32[]{:S(2)}, u32[]{:S(2)}) collective-permute-start(f32[6,64,128]{2,1,0:T(8,128)S(1)} %get-tuple-element.28), channel_id=1, source_target_pairs={{0,1},{1,2},{2,3},{3,4},{4,5},{5,6},{6,7},{7,8},{8,9},{9,10},{10,1... | collective-permute-start | bytes 589832 | tf_op jit(solution)/shard_map/ppermute | solution.py:71
  53.0 5.4 %collective-permute-start.3 = (f32[6,64,128]{2,1,0:T(8,128)S(1)}, f32[6,64,128]{2,1,0:T(8,128)S(1)}, u32[]{:S(2)}, u32[]{:S(2)}) collective-permute-start(f32[6,64,128]{2,1,0:T(8,128)S(1)} %get-tuple-element.29), channel_id=1, source_target_pairs={{1,0},{2,1},{3,2},{4,3},{5,4},{6,5},{7,6},{8,7},{9,8},{10,9},{11,1... | collective-permute-start | bytes 589832 | tf_op jit(solution)/shard_map/ppermute | solution.py:71
  64.1 6.5 %collective-permute-start.7 = (f32[1,2,2,32,64]{4,3,2,1,0:T(8,128)S(1)}, f32[1,2,2,32,64]{4,3,2,1,0:T(8,128)S(1)}, u32[]{:S(2)}, u32[]{:S(2)}) collective-permute-start(f32[1,2,2,32,64]{4,3,2,1,0:T(8,128)S(1)} %maximum_bitcast_fusion), channel_id=1, source_target_pairs={{1,0},{2,1},{3,2},{4,3},{5,4},{6,5},{7,6},{8,7},{9,8},{10,9},{11,1... | collective-permute-start | bytes 98312 | tf_op jit(solution)/shard_map/ppermute | solution.py:71
  70.6 1.9 %collective-permute-start.4 = (f32[1,2,2,32,64]{4,3,2,1,0:T(8,128)S(1)}, f32[1,2,2,32,64]{4,3,2,1,0:T(8,128)S(1)}, u32[]{:S(2)}, u32[]{:S(2)}) collective-permute-start(f32[1,2,2,32,64]{4,3,2,1,0:T(8,128)S(1)} %maximum_bitcast_fusion), channel_id=1, source_target_pairs={{0,1},{1,2},{2,3},{3,4},{4,5},{5,6},{6,7},{7,8},{8,9},{9,10},{10,1... | collective-permute-start | bytes 98312 | tf_op jit(solution)/shard_map/ppermute | solution.py:71
  73.1 5.7 %collective-permute-done.4 = f32[1,2,2,32,64]{4,3,2,1,0:T(8,128)S(1)} collective-permute-done((f32[1,2,2,32,64]{4,3,2,1,0:T(8,128)S(1)}, f32[1,2,2,32,64]{4,3,2,1,0:T(8,128)S(1)}, u32[]{:S(2)}, u32[]{:S(2)}) %collective-permute-start.4) | collective-permute-done | bytes 32800 | tf_op jit(solution)/shard_map/ppermute | solution.py:71
  78.9 1.9 %collective-permute-start.8 = (f32[2,2,2,32,64]{4,3,2,1,0:T(8,128)S(1)}, f32[2,2,2,32,64]{4,3,2,1,0:T(8,128)S(1)}, u32[]{:S(2)}, u32[]{:S(2)}) collective-permute-start(f32[2,2,2,32,64]{4,3,2,1,0:T(8,128)S(1)} %get-tuple-element.34), channel_id=1, source_target_pairs={{2,0},{3,1},{4,2},{5,3},{6,4},{7,5},{8,6},{9,7},{10,8},{11,9},{12,... | collective-permute-start | bytes 196616 | tf_op jit(solution)/shard_map/ppermute | solution.py:71
  80.8 5.4 %collective-permute-start.5 = (f32[2,2,2,32,64]{4,3,2,1,0:T(8,128)S(1)}, f32[2,2,2,32,64]{4,3,2,1,0:T(8,128)S(1)}, u32[]{:S(2)}, u32[]{:S(2)}) collective-permute-start(f32[2,2,2,32,64]{4,3,2,1,0:T(8,128)S(1)} %get-tuple-element.35), channel_id=1, source_target_pairs={{0,2},{1,3},{2,4},{3,5},{4,6},{5,7},{6,8},{7,9},{8,10},{9,11},{10,... | collective-permute-start | bytes 196616 | tf_op jit(solution)/shard_map/ppermute | solution.py:71
  87.2 2.8 %collective-permute-done.5 = f32[2,2,2,32,64]{4,3,2,1,0:T(8,128)S(1)} collective-permute-done((f32[2,2,2,32,64]{4,3,2,1,0:T(8,128)S(1)}, f32[2,2,2,32,64]{4,3,2,1,0:T(8,128)S(1)}, u32[]{:S(2)}, u32[]{:S(2)}) %collective-permute-start.5) | collective-permute-done | bytes 65568 | tf_op jit(solution)/shard_map/ppermute | solution.py:71
  90.1 14.0 %collective-permute-start.6 = (f32[4,2,2,32,64]{4,3,2,1,0:T(8,128)S(1)}, f32[4,2,2,32,64]{4,3,2,1,0:T(8,128)S(1)}, u32[]{:S(2)}, u32[]{:S(2)}) collective-permute-start(f32[4,2,2,32,64]{4,3,2,1,0:T(8,128)S(1)} %get-tuple-element.33), channel_id=1, source_target_pairs={{0,4},{1,5},{2,6},{3,7},{4,8},{5,9},{6,10},{7,11},{8,12},{9,13},{1... | collective-permute-start | bytes 393224 | tf_op jit(solution)/shard_map/ppermute | solution.py:71
  105.4 1.9 %collective-permute-start.9 = (f32[4,2,2,32,64]{4,3,2,1,0:T(8,128)S(1)}, f32[4,2,2,32,64]{4,3,2,1,0:T(8,128)S(1)}, u32[]{:S(2)}, u32[]{:S(2)}) collective-permute-start(f32[4,2,2,32,64]{4,3,2,1,0:T(8,128)S(1)} %get-tuple-element.32), channel_id=1, source_target_pairs={{4,0},{5,1},{6,2},{7,3},{8,4},{9,5},{10,6},{11,7},{12,8},{13,9},{1... | collective-permute-start | bytes 393224 | tf_op jit(solution)/shard_map/ppermute | solution.py:71
  108.1 7.6 %collective-permute-done.9 = f32[4,2,2,32,64]{4,3,2,1,0:T(8,128)S(1)} collective-permute-done((f32[4,2,2,32,64]{4,3,2,1,0:T(8,128)S(1)}, f32[4,2,2,32,64]{4,3,2,1,0:T(8,128)S(1)}, u32[]{:S(2)}, u32[]{:S(2)}) %collective-permute-start.9) | collective-permute-done | bytes 131104 | tf_op jit(solution)/shard_map/ppermute | solution.py:71
  121.2 1.7 %reduce_sum.58 = f32[11,32,64]{2,1,0:T(8,128)} reduce(f32[11,2,32,64]{3,2,1,0:T(8,128)} %bitcast.153, f32[]{:T(128)} %constant.129.clone.1), dimensions={1}, to_apply=%region_5.6 | reduce | flops 22528 | bytes 270340 | tf_op jit(solution)/shard_map/reduce_sum | solution.py:56
  137.2 2.0 %fusion.32 = f32[10,128,256]{2,1,0:T(8,128)S(1)} fusion(f32[10,128,256]{2,1,0:T(8,128)S(1)} %slice.1538, f32[14,128,257]{2,1,0:T(8,128)S(1)} %copy-done.4, f32[14,129,256]{2,1,0:T(8,128)S(1)} %add_multiply_fusion, f32[12,128,256]{2,1,0:T(8,128)S(1)} %bitcast_add_fusion, f32[15,128,256]{2,1,0:T(8,128)S(1)} %copy-done.2, f32[14,128,256]{2,1,0:T(8,128)S(1)} %copy-done.7, ...), kind=kLoop, calls=%fused_computation.63 | loop fusion | flops 5898240 | bytes 15728650 | tf_op jit(solution)/shard_map/jit(_where)/select_n | solution.py:112
  140.4 2.2 %select_bitcast_fusion = f32[1,8,128,256]{3,2,1,0:T(8,128)} fusion(f32[8,128,256]{2,1,0:T(8,128)S(1)} %slice.1549, f32[8,128,256]{2,1,0:T(8,128)S(1)} %copy-done.20, f32[10,128,256]{2,1,0:T(8,128)S(1)} %fusion.32, f32[14,128,257]{2,1,0:T(8,128)S(1)} %copy-done.4, f32[14,129,256]{2,1,0:T(8,128)S(1)} %add_multiply_fusion, f32[15,128,256]{2,1,0:T(8,128)S(1)} %copy-done.2, ...), kind=kLoop, calls=%fused_computation.112 | loop fusion | flops 4718592 | bytes 12582920 | tf_op jit(solution)/shard_map/broadcast_in_dim | solution.py:258
  (251 shorter events, 48.9 us)
Async XLA Ops:
  0.0 7.0 %copy-start.18 = (f32[8,128,256]{2,1,0:T(8,128)S(1)}, f32[8,128,256]{2,1,0:T(8,128)}, u32[]{:S(2)}) copy-start(f32[8,128,256]{2,1,0:T(8,128)} %param.29) | copy-start | bytes 3145732
  7.1 11.0 %copy-start.44 = (f32[1,32,16,64]{3,2,1,0:T(8,128)S(1)}, f32[1,32,16,64]{3,2,1,0:T(8,128)}, u32[]{:S(2)}) copy-start(f32[1,32,16,64]{3,2,1,0:T(8,128)} %param.28) | copy-start | bytes 393220
  7.2 18.0 %collective-permute-start = (f32[512,256]{1,0:T(8,128)S(1)}, f32[512,256]{1,0:T(8,128)S(1)}, u32[]{:S(2)}, u32[]{:S(2)}) collective-permute-start(f32[512,256]{1,0:T(8,128)S(1)} %get-tuple-element.30), channel_id=1, source_target_pairs={{0,1},{1,2},{2,3},{3,4},{4,5},{5,6},{6,7},{7,8},{8,9},{9,10},{10,1... | collective-permute-start | bytes 1572872 | tf_op jit(solution)/shard_map/ppermute | solution.py:71
  10.6 15.7 %collective-permute-start.1 = (f32[512,256]{1,0:T(8,128)S(1)}, f32[512,256]{1,0:T(8,128)}, u32[]{:S(2)}, u32[]{:S(2)}) collective-permute-start(f32[512,256]{1,0:T(8,128)S(1)} %get-tuple-element.31), channel_id=1, source_target_pairs={{1,0},{2,1},{3,2},{4,3},{5,4},{6,5},{7,6},{8,7},{9,8},{10,9},{11,1... | collective-permute-start | bytes 1572872 | tf_op jit(solution)/shard_map/ppermute | solution.py:71
  36.6 11.1 %copy-start.1 = (f32[15,128,256]{2,1,0:T(8,128)}, f32[15,128,256]{2,1,0:T(8,128)S(1)}, u32[]{:S(2)}) copy-start(f32[15,128,256]{2,1,0:T(8,128)S(1)} %fusion.2) | copy-start | bytes 5898244
  38.4 9.4 %copy-start.3 = (f32[14,128,257]{2,1,0:T(8,128)}, f32[14,128,257]{2,1,0:T(8,128)S(1)}, u32[]{:S(2)}) copy-start(f32[14,128,257]{2,1,0:T(8,128)S(1)} %fusion.1) | copy-start | bytes 5526532
  43.1 4.6 %copy-start.6 = (f32[14,128,256]{2,1,0:T(8,128)}, f32[14,128,256]{2,1,0:T(8,128)S(1)}, u32[]{:S(2)}) copy-start(f32[14,128,256]{2,1,0:T(8,128)S(1)} %get-tuple-element.12) | copy-start | bytes 5505028
  49.0 9.6 %copy-start.43 = (f32[64,32,1]{0,1,2:T(8,128)S(1)}, f32[64,32,1]{0,1,2:T(8,128)}, u32[]{:S(2)}) copy-start(f32[64,32,1]{0,1,2:T(8,128)} %constant.361) | copy-start | bytes 24580
  49.6 10.7 %collective-permute-start.2 = (f32[6,64,128]{2,1,0:T(8,128)S(1)}, f32[6,64,128]{2,1,0:T(8,128)S(1)}, u32[]{:S(2)}, u32[]{:S(2)}) collective-permute-start(f32[6,64,128]{2,1,0:T(8,128)S(1)} %get-tuple-element.28), channel_id=1, source_target_pairs={{0,1},{1,2},{2,3},{3,4},{4,5},{5,6},{6,7},{7,8},{8,9},{9,10},{10,1... | collective-permute-start | bytes 589832 | tf_op jit(solution)/shard_map/ppermute | solution.py:71
  53.0 8.5 %collective-permute-start.3 = (f32[6,64,128]{2,1,0:T(8,128)S(1)}, f32[6,64,128]{2,1,0:T(8,128)S(1)}, u32[]{:S(2)}, u32[]{:S(2)}) collective-permute-start(f32[6,64,128]{2,1,0:T(8,128)S(1)} %get-tuple-element.29), channel_id=1, source_target_pairs={{1,0},{2,1},{3,2},{4,3},{5,4},{6,5},{7,6},{8,7},{9,8},{10,9},{11,1... | collective-permute-start | bytes 589832 | tf_op jit(solution)/shard_map/ppermute | solution.py:71
  64.1 9.0 %collective-permute-start.7 = (f32[1,2,2,32,64]{4,3,2,1,0:T(8,128)S(1)}, f32[1,2,2,32,64]{4,3,2,1,0:T(8,128)S(1)}, u32[]{:S(2)}, u32[]{:S(2)}) collective-permute-start(f32[1,2,2,32,64]{4,3,2,1,0:T(8,128)S(1)} %maximum_bitcast_fusion), channel_id=1, source_target_pairs={{1,0},{2,1},{3,2},{4,3},{5,4},{6,5},{7,6},{8,7},{9,8},{10,9},{11,1... | collective-permute-start | bytes 98312 | tf_op jit(solution)/shard_map/ppermute | solution.py:71
  70.6 8.3 %collective-permute-start.4 = (f32[1,2,2,32,64]{4,3,2,1,0:T(8,128)S(1)}, f32[1,2,2,32,64]{4,3,2,1,0:T(8,128)S(1)}, u32[]{:S(2)}, u32[]{:S(2)}) collective-permute-start(f32[1,2,2,32,64]{4,3,2,1,0:T(8,128)S(1)} %maximum_bitcast_fusion), channel_id=1, source_target_pairs={{0,1},{1,2},{2,3},{3,4},{4,5},{5,6},{6,7},{7,8},{8,9},{9,10},{10,1... | collective-permute-start | bytes 98312 | tf_op jit(solution)/shard_map/ppermute | solution.py:71
  78.9 8.4 %collective-permute-start.8 = (f32[2,2,2,32,64]{4,3,2,1,0:T(8,128)S(1)}, f32[2,2,2,32,64]{4,3,2,1,0:T(8,128)S(1)}, u32[]{:S(2)}, u32[]{:S(2)}) collective-permute-start(f32[2,2,2,32,64]{4,3,2,1,0:T(8,128)S(1)} %get-tuple-element.34), channel_id=1, source_target_pairs={{2,0},{3,1},{4,2},{5,3},{6,4},{7,5},{8,6},{9,7},{10,8},{11,9},{12,... | collective-permute-start | bytes 196616 | tf_op jit(solution)/shard_map/ppermute | solution.py:71
  80.8 9.3 %collective-permute-start.5 = (f32[2,2,2,32,64]{4,3,2,1,0:T(8,128)S(1)}, f32[2,2,2,32,64]{4,3,2,1,0:T(8,128)S(1)}, u32[]{:S(2)}, u32[]{:S(2)}) collective-permute-start(f32[2,2,2,32,64]{4,3,2,1,0:T(8,128)S(1)} %get-tuple-element.35), channel_id=1, source_target_pairs={{0,2},{1,3},{2,4},{3,5},{4,6},{5,7},{6,8},{7,9},{8,10},{9,11},{10,... | collective-permute-start | bytes 196616 | tf_op jit(solution)/shard_map/ppermute | solution.py:71
  90.1 17.9 %collective-permute-start.6 = (f32[4,2,2,32,64]{4,3,2,1,0:T(8,128)S(1)}, f32[4,2,2,32,64]{4,3,2,1,0:T(8,128)S(1)}, u32[]{:S(2)}, u32[]{:S(2)}) collective-permute-start(f32[4,2,2,32,64]{4,3,2,1,0:T(8,128)S(1)} %get-tuple-element.33), channel_id=1, source_target_pairs={{0,4},{1,5},{2,6},{3,7},{4,8},{5,9},{6,10},{7,11},{8,12},{9,13},{1... | collective-permute-start | bytes 393224 | tf_op jit(solution)/shard_map/ppermute | solution.py:71
  105.4 10.4 %collective-permute-start.9 = (f32[4,2,2,32,64]{4,3,2,1,0:T(8,128)S(1)}, f32[4,2,2,32,64]{4,3,2,1,0:T(8,128)S(1)}, u32[]{:S(2)}, u32[]{:S(2)}) collective-permute-start(f32[4,2,2,32,64]{4,3,2,1,0:T(8,128)S(1)} %get-tuple-element.32), channel_id=1, source_target_pairs={{4,0},{5,1},{6,2},{7,3},{8,4},{9,5},{10,6},{11,7},{12,8},{13,9},{1... | collective-permute-start | bytes 393224 | tf_op jit(solution)/shard_map/ppermute | solution.py:71
  122.9 3.8 %copy-start.36 = (f32[12,16,32]{2,1,0:T(8,128)S(1)}, f32[12,16,32]{2,1,0:T(8,128)}, u32[]{:S(2)}) copy-start(f32[12,16,32]{2,1,0:T(8,128)} %fusion.182) | copy-start | bytes 73732
  122.9 3.8 %copy-start.37 = (f32[11,17,32]{2,1,0:T(8,128)S(1)}, f32[11,17,32]{2,1,0:T(8,128)}, u32[]{:S(2)}) copy-start(f32[11,17,32]{2,1,0:T(8,128)} %fusion.145) | copy-start | bytes 71812
  122.9 4.7 %copy-start.54 = (f32[16,32,1]{1,0,2:T(8,128)S(1)}, f32[16,32,1]{1,0,2:T(8,128)}, u32[]{:S(2)}) copy-start(f32[16,32,1]{1,0,2:T(8,128)} %constant.363) | copy-start | bytes 6148
  122.9 4.7 %copy-start.56 = (pred[5]{0:T(512)(128)(4,1)S(1)}, pred[5]{0:T(512)(128)(4,1)}, u32[]{:S(2)}) copy-start(pred[5]{0:T(512)(128)(4,1)} %compare_and_fusion.3) | copy-start | bytes 19
  124.1 3.8 %copy-start.47 = (f32[32,64,1]{1,0,2:T(8,128)S(1)}, f32[32,64,1]{1,0,2:T(8,128)}, u32[]{:S(2)}) copy-start(f32[32,64,1]{1,0,2:T(8,128)} %constant.364) | copy-start | bytes 24580
  125.3 3.8 %copy-start.11 = (f32[27,32,64]{2,1,0:T(8,128)S(1)}, f32[27,32,64]{2,1,0:T(8,128)}, u32[]{:S(2)}) copy-start(f32[27,32,64]{2,1,0:T(8,128)} %copy-done.10) | copy-start | bytes 663556
  125.3 3.8 %copy-start.13 = (f32[26,33,64]{2,1,0:T(8,128)S(1)}, f32[26,33,64]{2,1,0:T(8,128)}, u32[]{:S(2)}) copy-start(f32[26,33,64]{2,1,0:T(8,128)} %copy-done.12) | copy-start | bytes 658948
  125.4 3.8 %copy-start.28 = (f32[26,32,64]{2,1,0:T(8,128)S(1)}, f32[26,32,64]{2,1,0:T(8,128)}, u32[]{:S(2)}) copy-start(f32[26,32,64]{2,1,0:T(8,128)} %copy-done.27) | copy-start | bytes 638980
  (43 other events, 70.6 us)
